TPU v7x, 32 devices: a whole 2x2x4 slice. The times are simulated.
32 devices in a mesh: row: 8 (over y, x, core), col: 4 (over z).
Axes of the slice: x: 2, y: 2, z: 4, core: 2. Of those that a mesh axis runs over, the one named last changes fastest.
Arguments:
- pair_rep: bfloat16 [128, 128, 128], P(('row', 'col')), may hold values from -16 to 16
- tile_mask: int32 [1, 1], replicated, may hold values from 0 to 1, as said below
- chain_ids: int32 [128], replicated, may hold values from 0 to 3, never falling along the last dimension, each value on 1 to 64 neighbouring positions
- chain_bias: float32 [2, 4], replicated, may hold values from -6 to 6
- row_project: bfloat16 [128, 512], replicated, may hold values from -0.5 to 0.5
- row_bias_proj: bfloat16 [128, 4], replicated, may hold values from -36 to 36
- row_output: bfloat16 [128, 128], replicated, may hold values from -0.5 to 0.5
- col_project: bfloat16 [128, 512], replicated, may hold values from -0.5 to 0.5
- col_bias_proj: bfloat16 [128, 4], replicated, may hold values from -36 to 36
- col_output: bfloat16 [128, 128], replicated, may hold values from -0.5 to 0.5
- tri_left: bfloat16 [128, 256], replicated, may hold values from -0.5 to 0.5
- tri_right: bfloat16 [128, 256], replicated, may hold values from -0.5 to 0.5
- tri_gate: bfloat16 [128, 128], replicated, may hold values from -0.5 to 0.5
- tri_output: bfloat16 [128, 128], replicated, may hold values from -1.5 to 1.5
Outputs:
- pair_out: bfloat16 [128, 128, 128], P('row', 'col')
Inputs may be any that keep to these rules, and one draw needn't show every extreme that they name: `tile_mask`: every diagonal entry is 1. `chain_ids`: chain numbers never fall along the residues.
All inputs are finite; a program needn't handle non-finite values.
Results may differ from a plain program's by a relative error of at most 0.018.
Values may be sent and summed in bfloat16 or wider, within the bound.
No kernel may reach another device: no remote copies, remote signals or barrier semaphores. Data moves between devices by JAX's collectives and lax.ppermute only.
A program may use at most 64 MiB of HBM per device.

v0:
```python
import jax
import jax.numpy as jnp
from jax import lax
from jax.sharding import PartitionSpec as P


def layer_norm(values):
    values = values.astype(jnp.float32)
    center = values - jnp.mean(values, axis=-1, keepdims=True)
    spread = jnp.mean(center * center, axis=-1, keepdims=True)
    return center * lax.rsqrt(spread + 1e-05)


def tile_rows(positions, tile_table, length):
    tile_count = tile_table.shape[0]
    tile_width = length // tile_count
    onehot = (positions[:, None] // tile_width == jnp.arange(tile_count)[None, :]).astype(
        jnp.float32
    )
    picked = jnp.dot(onehot, tile_table.astype(jnp.float32))
    spread_out = jnp.broadcast_to(picked[:, :, None], (positions.shape[0], tile_count, tile_width))
    return spread_out.reshape(positions.shape[0], length) > 0.5


def tile_pairs(row_pos, col_pos, tile_table, length):
    tile_count = tile_table.shape[0]
    tile_width = length // tile_count
    row_hot = (row_pos[:, None] // tile_width == jnp.arange(tile_count)[None, :]).astype(
        jnp.float32
    )
    col_hot = (col_pos[:, None] // tile_width == jnp.arange(tile_count)[None, :]).astype(
        jnp.float32
    )
    return jnp.dot(jnp.dot(row_hot, tile_table.astype(jnp.float32)), col_hot.T)


def attend_lines(
    queries,
    key_rows,
    value_rows,
    gate_pre,
    bias_all,
    key_ok,
    chain_ids,
    chain_add,
    line_dim,
    flipped,
):
    line_count = queries.shape[line_dim]
    length = queries.shape[1 - line_dim]
    head_count = queries.shape[2]
    head_size = queries.shape[3]
    width_all = head_count * head_size
    query_rows = min(128, length)
    per_line = length // query_rows
    scaling = head_size ** (-0.5)

    def one_block(block_index):
        line_index = block_index // per_line
        offset = block_index % per_line * query_rows
        query_line = lax.dynamic_index_in_dim(queries, line_index, line_dim, keepdims=False)
        query_block = lax.dynamic_slice_in_dim(query_line, offset, query_rows, 0)
        key_line = lax.dynamic_index_in_dim(key_rows, line_index, line_dim, keepdims=False)
        value_line = lax.dynamic_index_in_dim(value_rows, line_index, line_dim, keepdims=False)
        scores = (
            jnp.einsum("qhd,khd->hqk", query_block, key_line, preferred_element_type=jnp.float32)
            * scaling
        )
        if flipped:
            bias_block = lax.dynamic_slice_in_dim(bias_all, offset, query_rows, 2).transpose(
                0, 2, 1
            )
        else:
            bias_block = lax.dynamic_slice_in_dim(bias_all, offset, query_rows, 1)
        scores = scores + bias_block
        chain_block = lax.dynamic_slice_in_dim(chain_ids, offset, query_rows, 0)
        same_chain = (chain_block[:, None] == chain_ids[None, :]).astype(jnp.float32)
        scores = scores + chain_add[:, None, None] * same_chain[None]
        usable = lax.dynamic_index_in_dim(key_ok, line_index, 0, keepdims=False)
        scores = jnp.where(usable[None, None, :], scores, -1000000000.0)
        row_peak = jnp.max(scores, axis=-1, keepdims=True)
        weights = jnp.exp(scores - row_peak)
        attention = (weights / jnp.sum(weights, axis=-1, keepdims=True)).astype(jnp.bfloat16)
        mixed_rows = jnp.einsum(
            "hqk,khd->qhd", attention, value_line, preferred_element_type=jnp.float32
        ).reshape(query_rows, width_all)
        gate_line = lax.dynamic_index_in_dim(gate_pre, line_index, line_dim, keepdims=False)
        gate_block = lax.dynamic_slice_in_dim(gate_line, offset, query_rows, 0)
        return (mixed_rows * jax.nn.sigmoid(gate_block)).astype(jnp.bfloat16)

    outputs = lax.map(one_block, jnp.arange(line_count * per_line, dtype=jnp.int32))
    outputs = outputs.reshape(line_count, length, width_all)
    if line_dim == 1:
        outputs = outputs.transpose(1, 0, 2)
    return outputs


def tri_acts(normed, weights, allowed):
    channels = normed.shape[-1]
    projected = jnp.dot(normed.reshape(-1, channels), weights, preferred_element_type=jnp.float32)
    projected = projected.reshape(normed.shape[0], normed.shape[1], 2 * channels)
    return (
        jax.nn.sigmoid(projected[..., channels:]) * projected[..., :channels] * allowed[..., None]
    ).astype(jnp.bfloat16)


def shards(
    pair_rep,
    tile_mask,
    chain_ids,
    chain_bias,
    row_project,
    row_bias_proj,
    row_output,
    col_project,
    col_bias_proj,
    col_output,
    tri_left,
    tri_right,
    tri_gate,
    tri_output,
):
    n_row = lax.axis_size("row")
    n_col = lax.axis_size("col")
    device_count = n_row * n_col
    rows_here, length, channels = pair_rep.shape
    head_count = row_bias_proj.shape[1]
    head_size = channels // head_count
    row_index = lax.axis_index("row")
    col_index = lax.axis_index("col")
    device_index = row_index * n_col + col_index
    local_lines = device_index * rows_here + jnp.arange(rows_here, dtype=jnp.int32)
    normed = layer_norm(pair_rep).astype(jnp.bfloat16)
    flat_rows = normed.reshape(rows_here * length, channels)
    bias_rows = jnp.dot(flat_rows, row_bias_proj, preferred_element_type=jnp.float32)
    bias_rows = bias_rows.reshape(rows_here, length, head_count).transpose(2, 0, 1)
    bias_all = lax.all_gather(bias_rows, ("row", "col"), axis=1, tiled=True)
    projected = jnp.dot(flat_rows, row_project, preferred_element_type=jnp.float32).reshape(
        rows_here, length, 4 * channels
    )
    qkv_rows = (
        projected[..., : 3 * channels]
        .astype(jnp.bfloat16)
        .reshape(rows_here, length, 3, head_count, head_size)
    )
    key_ok = tile_rows(local_lines, tile_mask, length)
    mixed_rows = attend_lines(
        qkv_rows[:, :, 0],
        qkv_rows[:, :, 1],
        qkv_rows[:, :, 2],
        projected[..., 3 * channels :],
        bias_all,
        key_ok,
        chain_ids,
        chain_bias[0],
        0,
        False,
    )
    update = jnp.dot(
        mixed_rows.reshape(-1, channels), row_output, preferred_element_type=jnp.float32
    ).reshape(rows_here, length, channels)
    first_pair = (pair_rep.astype(jnp.float32) + update).astype(jnp.bfloat16)
    normed_first = layer_norm(first_pair).astype(jnp.bfloat16)
    bias_next = jnp.dot(
        normed_first.reshape(-1, channels), col_bias_proj, preferred_element_type=jnp.float32
    )
    bias_next = bias_next.reshape(rows_here, length, head_count).transpose(2, 0, 1)
    bias_cols = lax.all_gather(bias_next, ("row", "col"), axis=1, tiled=True)
    columns = lax.all_to_all(first_pair, ("row", "col"), split_axis=1, concat_axis=0, tiled=True)
    normed_cols = layer_norm(columns).astype(jnp.bfloat16)
    projected_cols = jnp.dot(
        normed_cols.reshape(-1, channels), col_project, preferred_element_type=jnp.float32
    ).reshape(length, rows_here, 4 * channels)
    qkv_cols = (
        projected_cols[..., : 3 * channels]
        .astype(jnp.bfloat16)
        .reshape(length, rows_here, 3, head_count, head_size)
    )
    col_ok = tile_rows(local_lines, tile_mask.T, length)
    mixed_cols = attend_lines(
        qkv_cols[:, :, 0],
        qkv_cols[:, :, 1],
        qkv_cols[:, :, 2],
        projected_cols[..., 3 * channels :],
        bias_cols,
        col_ok,
        chain_ids,
        chain_bias[1],
        1,
        True,
    )
    update_cols = jnp.dot(
        mixed_cols.reshape(-1, channels), col_output, preferred_element_type=jnp.float32
    ).reshape(length, rows_here, channels)
    second_pair = (columns.astype(jnp.float32) + update_cols).astype(jnp.bfloat16)
    normed_second = layer_norm(second_pair).astype(jnp.bfloat16)
    edge_mask = tile_pairs(jnp.arange(length, dtype=jnp.int32), local_lines, tile_mask, length)
    left_all = tri_acts(normed_second, tri_left, edge_mask)
    right_all = tri_acts(normed_second, tri_right, edge_mask)
    block_rows = length // n_row
    block_cols = length // n_col

    def one_round(round_index, loop_state):
        product_sum, own_block = loop_state
        left_col = lax.dynamic_index_in_dim(left_all, round_index, 1, keepdims=False)
        right_col = lax.dynamic_index_in_dim(right_all, round_index, 1, keepdims=False)
        raw_col = lax.dynamic_index_in_dim(second_pair, round_index, 1, keepdims=False)
        left_send = jnp.broadcast_to(
            left_col.reshape(n_row, 1, block_rows, channels), (n_row, n_col, block_rows, channels)
        )
        raw_send = jnp.broadcast_to(
            raw_col.reshape(n_row, 1, block_rows, channels), (n_row, n_col, block_rows, channels)
        )
        right_send = jnp.broadcast_to(
            right_col.reshape(1, n_col, block_cols, channels), (n_row, n_col, block_cols, channels)
        )
        outgoing = jnp.concatenate([left_send, raw_send, right_send], axis=2).reshape(
            device_count, 2 * block_rows + block_cols, channels
        )
        received = lax.all_to_all(outgoing, ("row", "col"), split_axis=0, concat_axis=0, tiled=True)
        left_act = received[:, :block_rows].transpose(1, 0, 2)
        right_act = received[:, 2 * block_rows :].transpose(1, 0, 2)
        product_sum = product_sum + jnp.einsum(
            "ikc,jkc->ijc", left_act, right_act, preferred_element_type=jnp.float32
        )
        own_piece = lax.dynamic_slice_in_dim(
            received[:, block_rows : 2 * block_rows], col_index * n_row, n_row, 0
        )
        own_block = lax.dynamic_update_index_in_dim(own_block, own_piece, round_index, 1)
        return (product_sum, own_block)

    initial = (
        jnp.zeros((block_rows, block_cols, channels), jnp.float32),
        jnp.zeros((n_row, rows_here, block_rows, channels), jnp.bfloat16),
    )
    product_sum, own_block = lax.fori_loop(0, rows_here, one_round, initial)
    own_pair = own_block.transpose(2, 0, 1, 3).reshape(block_rows, block_cols, channels)
    normed_own = layer_norm(own_pair).astype(jnp.bfloat16)
    gate_values = jax.nn.sigmoid(
        jnp.dot(normed_own.reshape(-1, channels), tri_gate, preferred_element_type=jnp.float32)
    ).reshape(block_rows, block_cols, channels)
    centered = layer_norm(product_sum).astype(jnp.bfloat16)
    update_tri = jnp.dot(
        centered.reshape(-1, channels), tri_output, preferred_element_type=jnp.float32
    ).reshape(block_rows, block_cols, channels)
    return (own_pair.astype(jnp.float32) + gate_values * update_tri).astype(jnp.bfloat16)


def solution(mesh):
    return jax.shard_map(
        shards,
        mesh=mesh,
        in_specs=(
            P(("row", "col"), None, None),
            P(),
            P(),
            P(),
            P(),
            P(),
            P(),
            P(),
            P(),
            P(),
            P(),
            P(),
            P(),
            P(),
        ),
        out_specs=P("row", "col", None),
        check_vma=False,
    )
```

profile of v0, /device:TPU:0, one launch (start us, length us, event | category | flops | bytes accessed | tf_op | source)
XLA Modules:
  0.0 283.7 jit_solution(12374093587075202309)
XLA Ops:
  0.0 1.1 copy.107
  1.6 0.9 copy-done.1
  3.2 0.6 copy-done.11
  3.9 0.7 copy-done.13
  4.7 71.8 %all_gather.6 = f32[4,128,128]{2,0,1:T(4,128)S(1)} all-gather(f32[4,4,128]{2,0,1:T(4,128)S(1)} %convolution_bitcast_fusion.2), channel_id=1, replica_groups=mesh['row'=8,'col'=4] {'row','col'}, dimensions={1}, use_global_device_ids=true | all-gather | bytes 270336 | tf_op jit(solution)/shard_map/all_gather | solution.py:137
  77.1 0.8 slice-done
  77.9 14.2 %while.42 = (s32[]{:T(128)}, bf16[4,128,128]{1,2,0:T(8,128)(2,1)S(1)}, s32[4]{0:T(128)S(1)}, bf16[4,128,4,32]{1,3,2,0:T(8,128)(2,1)S(1)}, pred[4,128]{1,0:T(4,12...) while((s32[]{:T(128)}, ...), condition=%wide.region_5.6_spmd, body=%wide.region_2.5_spmd.sunk | while | flops 9159427 | bytes 2038731 | solution.py:91
  77.9 0.7 dynamic_slice.179
  81.4 0.7 dynamic_slice.179
  85.0 0.7 dynamic_slice.179
  88.5 0.7 dynamic_slice.179
  92.4 0.8 copy.115
  93.2 0.7 copy-done.14
  94.0 65.4 %all_gather.7 = f32[4,128,128]{2,0,1:T(4,128)S(1)} all-gather(f32[4,4,128]{2,0,1:T(4,128)S(1)} %convolution_bitcast_fusion.1), channel_id=1, replica_groups=mesh['row'=8,'col'=4] {'row','col'}, dimensions={1}, use_global_device_ids=true | all-gather | bytes 270336 | tf_op jit(solution)/shard_map/all_gather | solution.py:168
  159.5 2.6 all-to-all-start.1
  162.2 8.2 %all-to-all-done.1 = bf16[4,128,128]{2,0,1:T(4,128)(2,1)S(1)} async-done(((bf16[4,128,128]{2,0,1:T(4,128)(2,1)}), bf16[4,128,128]{2,0,1:T(4,128)(2,1)S(1)}, u32[]{:S(2)}, u32[]{:S(2)}) %all-to-all-start.1) | async-done | bytes 131104 | tf_op jit(solution)/shard_map/all_to_all | solution.py:169
  172.3 0.8 copy-done.5
  173.9 13.4 %while.43 = (s32[]{:T(128)}, bf16[4,128,128]{1,2,0:T(8,128)(2,1)S(1)}, s32[4]{0:T(128)S(1)}, bf16[128,4,4,32]{0,3,2,1:T(8,128)(2,1)S(1)}, pred[4,128]{1,0:T(4,12...) while((s32[]{:T(128)}, ...), condition=%wide.region_13.14_spmd, body=%wide.region_10.13_spmd.sunk | while | flops 9159427 | bytes 2038731 | solution.py:91
  173.9 0.6 dynamic_slice.185
  177.2 0.6 dynamic_slice.185
  180.6 0.6 dynamic_slice.185
  183.9 0.6 dynamic_slice.185
  187.6 0.8 copy-done.6
  188.6 0.6 copy-done.7
  189.7 90.2 %while.44 = (s32[]{:T(128)}, f32[16,32,128]{1,0,2:T(8,128)S(1)}, bf16[8,4,16,128]{3,2,0,1:T(8,128)(2,1)S(1)}, bf16[128,4,128]{2,0,1:T(8,128)(2,1)S(1)}, bf16[128...) while((s32[]{:T(128)}, f32[16,32,128]{1,0,2:T(8,128)S(1)}, ...), condition=%wide.region_17.18_spmd.clone, body=%wide.region_16.17_spmd.clone.sunk | while | flops 5898243 | bytes 7373015 | solution.py:236
  190.4 0.9 pad_maximum_fusion.2
  191.3 2.6 all-to-all-start
  193.9 14.2 %all-to-all-done = bf16[32,64,128]{2,1,0:T(8,128)(2,1)S(1)} async-done(((bf16[32,64,128]{2,1,0:T(8,128)(2,1)}), bf16[32,64,128]{2,1,0:T(8,128)(2,1)S(1)}, u32[]{:S(2)}, u32[]{:S(2)}) %all-to-all-start) | async-done | bytes 524320 | tf_op jit(solution)/shard_map/while/body/eval_jaxpr/all_to_all | solution.py:220
  208.7 1.4 copy.177
  211.2 0.5 copy-done.2
  211.8 0.9 pad_maximum_fusion.2
  212.7 4.1 %all-to-all-start = ((bf16[32,64,128]{2,1,0:T(8,128)(2,1)}), bf16[32,64,128]{2,1,0:T(8,128)(2,1)S(1)}, u32[]{:S(2)}, u32[]{:S(2)}) async-start(bf16[32,64,128]{2,1,0:T(8,128)(2,1)} %bitcast.188), calls=%async_computation | async-start | bytes 1048576 | tf_op jit(solution)/shard_map/while/body/eval_jaxpr/all_to_all | solution.py:220
  216.8 14.2 %all-to-all-done = bf16[32,64,128]{2,1,0:T(8,128)(2,1)S(1)} async-done(((bf16[32,64,128]{2,1,0:T(8,128)(2,1)}), bf16[32,64,128]{2,1,0:T(8,128)(2,1)S(1)}, u32[]{:S(2)}, u32[]{:S(2)}) %all-to-all-start) | async-done | bytes 524320 | tf_op jit(solution)/shard_map/while/body/eval_jaxpr/all_to_all | solution.py:220
  231.6 1.4 copy.177
  233.1 0.5 fusion.145
  234.1 0.5 copy-done.2
  234.7 0.9 pad_maximum_fusion.2
  235.6 4.2 %all-to-all-start = ((bf16[32,64,128]{2,1,0:T(8,128)(2,1)}), bf16[32,64,128]{2,1,0:T(8,128)(2,1)S(1)}, u32[]{:S(2)}, u32[]{:S(2)}) async-start(bf16[32,64,128]{2,1,0:T(8,128)(2,1)} %bitcast.188), calls=%async_computation | async-start | bytes 1048576 | tf_op jit(solution)/shard_map/while/body/eval_jaxpr/all_to_all | solution.py:220
  239.7 14.2 %all-to-all-done = bf16[32,64,128]{2,1,0:T(8,128)(2,1)S(1)} async-done(((bf16[32,64,128]{2,1,0:T(8,128)(2,1)}), bf16[32,64,128]{2,1,0:T(8,128)(2,1)S(1)}, u32[]{:S(2)}, u32[]{:S(2)}) %all-to-all-start) | async-done | bytes 524320 | tf_op jit(solution)/shard_map/while/body/eval_jaxpr/all_to_all | solution.py:220
  254.5 1.4 copy.177
  256.0 0.5 fusion.145
  257.0 0.5 copy-done.2
  257.6 0.9 pad_maximum_fusion.2
  258.5 4.2 %all-to-all-start = ((bf16[32,64,128]{2,1,0:T(8,128)(2,1)}), bf16[32,64,128]{2,1,0:T(8,128)(2,1)S(1)}, u32[]{:S(2)}, u32[]{:S(2)}) async-start(bf16[32,64,128]{2,1,0:T(8,128)(2,1)} %bitcast.188), calls=%async_computation | async-start | bytes 1048576 | tf_op jit(solution)/shard_map/while/body/eval_jaxpr/all_to_all | solution.py:220
  262.7 14.2 %all-to-all-done = bf16[32,64,128]{2,1,0:T(8,128)(2,1)S(1)} async-done(((bf16[32,64,128]{2,1,0:T(8,128)(2,1)}), bf16[32,64,128]{2,1,0:T(8,128)(2,1)S(1)}, u32[]{:S(2)}, u32[]{:S(2)}) %all-to-all-start) | async-done | bytes 524320 | tf_op jit(solution)/shard_map/while/body/eval_jaxpr/all_to_all | solution.py:220
  277.4 1.4 copy.177
  281.4 0.6 copy-done.12
  282.8 1.0 fusion.41
  (206 shorter events, 19.6 us)
Async XLA Ops:
  0.0 1.2 copy-start
  1.5 1.0 copy-start.1
  3.2 0.7 copy-start.11
  3.9 0.7 copy-start.13
  76.9 1.0 slice-start
  77.0 0.8 copy-start.4
  77.9 14.2 %copy-start.10 = (bf16[128,128]{1,0:T(8,128)(2,1)S(1)}, bf16[128,128]{1,0:T(8,128)(2,1)}, u32[]{:S(2)}) copy-start(bf16[128,128]{1,0:T(8,128)(2,1)} %param.26) | copy-start | bytes 98308
  93.2 0.7 copy-start.14
  159.5 11.0 %all-to-all-start.1 = ((bf16[4,128,128]{2,0,1:T(4,128)(2,1)}), bf16[4,128,128]{2,0,1:T(4,128)(2,1)S(1)}, u32[]{:S(2)}, u32[]{:S(2)}) async-start(bf16[4,128,128]{2,0,1:T(4,128)(2,1)} %copy.115), calls=%async_computation.1 | async-start | bytes 262144 | tf_op jit(solution)/shard_map/all_to_all | solution.py:169
  172.2 0.9 copy-start.5
  173.9 13.4 %copy-start.8 = (bf16[128,128]{1,0:T(8,128)(2,1)S(1)}, bf16[128,128]{1,0:T(8,128)(2,1)}, u32[]{:S(2)}) copy-start(bf16[128,128]{1,0:T(8,128)(2,1)} %param.29) | copy-start | bytes 98308
  187.5 0.8 copy-start.6
  188.4 0.8 copy-start.7
  189.7 0.7 copy-start.2
  191.3 16.9 %all-to-all-start = ((bf16[32,64,128]{2,1,0:T(8,128)(2,1)}), bf16[32,64,128]{2,1,0:T(8,128)(2,1)S(1)}, u32[]{:S(2)}, u32[]{:S(2)}) async-start(bf16[32,64,128]{2,1,0:T(8,128)(2,1)} %bitcast.188), calls=%async_computation | async-start | bytes 1048576 | tf_op jit(solution)/shard_map/while/body/eval_jaxpr/all_to_all | solution.py:220
  210.1 0.9 copy-start.3
  211.0 0.7 copy-start.2
  212.7 18.4 %all-to-all-start = ((bf16[32,64,128]{2,1,0:T(8,128)(2,1)}), bf16[32,64,128]{2,1,0:T(8,128)(2,1)S(1)}, u32[]{:S(2)}, u32[]{:S(2)}) async-start(bf16[32,64,128]{2,1,0:T(8,128)(2,1)} %bitcast.188), calls=%async_computation | async-start | bytes 1048576 | tf_op jit(solution)/shard_map/while/body/eval_jaxpr/all_to_all | solution.py:220
  233.0 0.9 copy-start.3
  234.0 0.7 copy-start.2
  235.6 18.4 %all-to-all-start = ((bf16[32,64,128]{2,1,0:T(8,128)(2,1)}), bf16[32,64,128]{2,1,0:T(8,128)(2,1)S(1)}, u32[]{:S(2)}, u32[]{:S(2)}) async-start(bf16[32,64,128]{2,1,0:T(8,128)(2,1)} %bitcast.188), calls=%async_computation | async-start | bytes 1048576 | tf_op jit(solution)/shard_map/while/body/eval_jaxpr/all_to_all | solution.py:220
  256.0 0.9 copy-start.3
  256.9 0.7 copy-start.2
  258.5 18.4 %all-to-all-start = ((bf16[32,64,128]{2,1,0:T(8,128)(2,1)}), bf16[32,64,128]{2,1,0:T(8,128)(2,1)S(1)}, u32[]{:S(2)}, u32[]{:S(2)}) async-start(bf16[32,64,128]{2,1,0:T(8,128)(2,1)} %bitcast.188), calls=%async_computation | async-start | bytes 1048576 | tf_op jit(solution)/shard_map/while/body/eval_jaxpr/all_to_all | solution.py:220
  278.9 0.9 copy-start.3
  281.3 0.8 copy-start.12
  282.0 0.8 copy-start.9
where the time goes:
time: 286 us; the launch traced here: 284 us
  blocking collectives  137 us (48%)
  waiting for transfers between devices  65.2 us (23%)
  local copies, waits for them, and re-layouts  29.6 us (10%)
  starting transfers between devices  17.7 us (6%)
  loops' own time  16.9 us (6%)
  matrix products  8.77 us (3%)
  other arithmetic  7.16 us (3%)
    all_gather x1, blocking collectives, shards(): bias_all = lax.all_gather(bias_rows, ('row', 'col'), axis=1, tiled=True)  71.8 us
    all_gather x1, blocking collectives, shards(): bias_cols = lax.all_gather(bias_next, ('row', 'col'), axis=1, tiled=True)  65.4 us
    all_to_all x4, waiting for transfers between devices, one_round(): lax.all_to_all(outgoing, ('row', 'col'), split_axis=0, concat_axis=0, til...  57 us
    another operation x2, loops' own time, attend_lines(): lax.map(one_block, jnp.arange(line_count * per_line, dtype=jnp.int32))  16.5 us
    all_to_all x4, starting transfers between devices, one_round(): lax.all_to_all(outgoing, ('row', 'col'), split_axis=0, concat_axis=0, til...  15.1 us
    while x24, local copies, waits for them, and re-layouts  11.2 us
    all_to_all x1, waiting for transfers between devices, shards(): lax.all_to_all(first_pair, ('row', 'col'), split_axis=1, concat_axis=0, t...  8.24 us
    unnamed x27, local copies, waits for them, and re-layouts  7.08 us
  transfers between devices with their start and end apart: 5, of which 5 were waited for; matrix products, arithmetic and copies ran while one was open for 0% of the time, Pallas kernels for 0%

commit v1 on v0

--- a/solution.py
+++ b/solution.py
@@ -104,6 +104,14 @@
     ).astype(jnp.bfloat16)
 
 
+def gather_lines(piece):
+    device_count = lax.axis_size("row") * lax.axis_size("col")
+    sent = jnp.broadcast_to(piece[None], (device_count,) + piece.shape)
+    got = lax.all_to_all(sent, ("row", "col"), 0, 0, tiled=True)
+    heads, rows_here, length = piece.shape
+    return got.transpose(1, 0, 2, 3).reshape(heads, device_count * rows_here, length)
+
+
 def shards(
     pair_rep,
     tile_mask,
@@ -129,12 +137,15 @@
     row_index = lax.axis_index("row")
     col_index = lax.axis_index("col")
     device_index = row_index * n_col + col_index
+    block_rows = length // n_row
+    block_cols = length // n_col
     local_lines = device_index * rows_here + jnp.arange(rows_here, dtype=jnp.int32)
+    local_cols = col_index * block_cols + row_index * rows_here + jnp.arange(rows_here, dtype=jnp.int32)
     normed = layer_norm(pair_rep).astype(jnp.bfloat16)
     flat_rows = normed.reshape(rows_here * length, channels)
     bias_rows = jnp.dot(flat_rows, row_bias_proj, preferred_element_type=jnp.float32)
     bias_rows = bias_rows.reshape(rows_here, length, head_count).transpose(2, 0, 1)
-    bias_all = lax.all_gather(bias_rows, ("row", "col"), axis=1, tiled=True)
+    bias_all = gather_lines(bias_rows)
     projected = jnp.dot(flat_rows, row_project, preferred_element_type=jnp.float32).reshape(
         rows_here, length, 4 * channels
     )
@@ -165,8 +176,13 @@
         normed_first.reshape(-1, channels), col_bias_proj, preferred_element_type=jnp.float32
     )
     bias_next = bias_next.reshape(rows_here, length, head_count).transpose(2, 0, 1)
-    bias_cols = lax.all_gather(bias_next, ("row", "col"), axis=1, tiled=True)
-    columns = lax.all_to_all(first_pair, ("row", "col"), split_axis=1, concat_axis=0, tiled=True)
+    bias_cols = gather_lines(bias_next)
+    first_sent = (
+        first_pair.reshape(rows_here, n_col, n_row, rows_here, channels)
+        .transpose(0, 2, 1, 3, 4)
+        .reshape(rows_here, length, channels)
+    )
+    columns = lax.all_to_all(first_sent, ("row", "col"), split_axis=1, concat_axis=0, tiled=True)
     normed_cols = layer_norm(columns).astype(jnp.bfloat16)
     projected_cols = jnp.dot(
         normed_cols.reshape(-1, channels), col_project, preferred_element_type=jnp.float32
@@ -176,7 +192,7 @@
         .astype(jnp.bfloat16)
         .reshape(length, rows_here, 3, head_count, head_size)
     )
-    col_ok = tile_rows(local_lines, tile_mask.T, length)
+    col_ok = tile_rows(local_cols, tile_mask.T, length)
     mixed_cols = attend_lines(
         qkv_cols[:, :, 0],
         qkv_cols[:, :, 1],
@@ -194,47 +210,31 @@
     ).reshape(length, rows_here, channels)
     second_pair = (columns.astype(jnp.float32) + update_cols).astype(jnp.bfloat16)
     normed_second = layer_norm(second_pair).astype(jnp.bfloat16)
-    edge_mask = tile_pairs(jnp.arange(length, dtype=jnp.int32), local_lines, tile_mask, length)
+    edge_mask = tile_pairs(jnp.arange(length, dtype=jnp.int32), local_cols, tile_mask, length)
     left_all = tri_acts(normed_second, tri_left, edge_mask)
     right_all = tri_acts(normed_second, tri_right, edge_mask)
-    block_rows = length // n_row
-    block_cols = length // n_col
-
-    def one_round(round_index, loop_state):
-        product_sum, own_block = loop_state
-        left_col = lax.dynamic_index_in_dim(left_all, round_index, 1, keepdims=False)
-        right_col = lax.dynamic_index_in_dim(right_all, round_index, 1, keepdims=False)
-        raw_col = lax.dynamic_index_in_dim(second_pair, round_index, 1, keepdims=False)
-        left_send = jnp.broadcast_to(
-            left_col.reshape(n_row, 1, block_rows, channels), (n_row, n_col, block_rows, channels)
-        )
-        raw_send = jnp.broadcast_to(
-            raw_col.reshape(n_row, 1, block_rows, channels), (n_row, n_col, block_rows, channels)
-        )
-        right_send = jnp.broadcast_to(
-            right_col.reshape(1, n_col, block_cols, channels), (n_row, n_col, block_cols, channels)
-        )
-        outgoing = jnp.concatenate([left_send, raw_send, right_send], axis=2).reshape(
-            device_count, 2 * block_rows + block_cols, channels
-        )
-        received = lax.all_to_all(outgoing, ("row", "col"), split_axis=0, concat_axis=0, tiled=True)
-        left_act = received[:, :block_rows].transpose(1, 0, 2)
-        right_act = received[:, 2 * block_rows :].transpose(1, 0, 2)
-        product_sum = product_sum + jnp.einsum(
-            "ikc,jkc->ijc", left_act, right_act, preferred_element_type=jnp.float32
-        )
-        own_piece = lax.dynamic_slice_in_dim(
-            received[:, block_rows : 2 * block_rows], col_index * n_row, n_row, 0
-        )
-        own_block = lax.dynamic_update_index_in_dim(own_block, own_piece, round_index, 1)
-        return (product_sum, own_block)
-
-    initial = (
-        jnp.zeros((block_rows, block_cols, channels), jnp.float32),
-        jnp.zeros((n_row, rows_here, block_rows, channels), jnp.bfloat16),
-    )
-    product_sum, own_block = lax.fori_loop(0, rows_here, one_round, initial)
-    own_pair = own_block.transpose(2, 0, 1, 3).reshape(block_rows, block_cols, channels)
+    raw_got = lax.all_to_all(
+        second_pair.reshape(n_row, block_rows, rows_here, channels), "row", 0, 0, tiled=True
+    )
+    own_pair = raw_got.transpose(1, 0, 2, 3).reshape(block_rows, block_cols, channels)
+    left_send = jnp.broadcast_to(
+        left_all.reshape(n_row, 1, block_rows, rows_here, channels),
+        (n_row, n_col, block_rows, rows_here, channels),
+    )
+    right_send = jnp.broadcast_to(
+        right_all.reshape(1, n_col, block_cols, rows_here, channels),
+        (n_row, n_col, block_cols, rows_here, channels),
+    )
+    outgoing = jnp.concatenate([left_send, right_send], axis=2).reshape(
+        device_count, block_rows + block_cols, rows_here, channels
+    )
+    received = lax.all_to_all(outgoing, ("row", "col"), split_axis=0, concat_axis=0, tiled=True)
+    product_sum = jnp.einsum(
+        "sikc,sjkc->ijc",
+        received[:, :block_rows],
+        received[:, block_rows:],
+        preferred_element_type=jnp.float32,
+    )
     normed_own = layer_norm(own_pair).astype(jnp.bfloat16)
     gate_values = jax.nn.sigmoid(
         jnp.dot(normed_own.reshape(-1, channels), tri_gate, preferred_element_type=jnp.float32)

time: 286 us -> 143 us (0.50)
  blocking collectives: 137 us -> 0 us
  local copies, waits for them, and re-layouts: 29.6 us -> 22.6 us
  waiting for transfers between devices: 65.2 us -> 60.9 us
  matrix products: 8.77 us -> 13 us
    all_gather x2 -> x0, blocking collectives: 137 us -> none  [the longest x1 71.8 us: shards(): bias_all = lax.all_gather(bias_rows, ('row', 'col'), axis=1, tiled=True)]
    while x24 -> x0, local copies, waits for them, and re-layouts: 11.2 us -> none
    all_to_all x5, waiting for transfers between devices: 65.2 us -> 60.9 us  [the longest x1 33.7 us: shards(): lax.all_to_all(outgoing, ('row', 'col'), split_axis=0, concat_axis=0, til...]
    unnamed x27 -> x26, local copies, waits for them, and re-layouts: 7.08 us -> 10.1 us
  transfers between devices with their start and end apart: 5 -> 5, of which waited for: 5 -> 5; matrix products, arithmetic and copies ran while one was open for 0% -> 6% of each run, Pallas kernels for 0% -> 0%
where the time goes in v1:
time: 143 us; the launch traced here: 141 us
  waiting for transfers between devices  60.9 us (43%)
  local copies, waits for them, and re-layouts  22.6 us (16%)
  starting transfers between devices  18.9 us (13%)
  loops' own time  16.5 us (12%)
  matrix products  13 us (9%)
  other arithmetic  7.65 us (5%)
    all_to_all x1, waiting for transfers between devices, shards(): lax.all_to_all(outgoing, ('row', 'col'), split_axis=0, concat_axis=0, til...  33.7 us
    another operation x2, loops' own time, attend_lines(): lax.map(one_block, jnp.arange(line_count * per_line, dtype=jnp.int32))  16.5 us
    all_to_all x2, waiting for transfers between devices, gather_lines(): got = lax.all_to_all(sent, ('row', 'col'), 0, 0, tiled=True)  15.4 us
    unnamed x26, local copies, waits for them, and re-layouts  10.1 us
    all_to_all x2, starting transfers between devices, gather_lines(): got = lax.all_to_all(sent, ('row', 'col'), 0, 0, tiled=True)  9.91 us
    all_to_all x1, waiting for transfers between devices, shards(): lax.all_to_all(first_sent, ('row', 'col'), split_axis=1, concat_axis=0, t...  8.03 us
    dynamic_slice x8, local copies, waits for them, and re-layouts, attend_lines(): lax.map(one_block, jnp.arange(line_count * per_line, dtype=jnp.int32))  5.01 us
    all_to_all x1, waiting for transfers between devices, shards(): lax.all_to_all(second_pair.reshape(n_row, block_rows, rows_here, channels...  3.78 us
  transfers between devices with their start and end apart: 5, of which 5 were waited for; matrix products, arithmetic and copies ran while one was open for 6% of the time, Pallas kernels for 0%

profile of v1, /device:TPU:0, one launch (start us, length us, event | category | flops | bytes accessed | tf_op | source)
XLA Modules:
  0.0 140.8 jit_solution(1615348873690497271)
XLA Ops:
  0.0 1.1 convert_reduce_fusion
  1.1 1.1 fusion.48
  2.2 1.2 convolution_bitcast_fusion.2
  3.5 0.7 broadcast_in_dim.69
  4.2 7.3 %all-to-all-start = ((f32[32,4,4,128]{3,2,1,0:T(4,128)}), f32[32,4,4,128]{3,2,1,0:T(4,128)S(1)}, u32[]{:S(2)}, u32[]{:S(2)}) async-start(f32[32,4,4,128]{3,2,1,0:T(4,128)} %broadcast_in_dim.69), calls=%async_computation | async-start | bytes 524288 | tf_op jit(solution)/shard_map/all_to_all | solution.py:110
  12.2 1.3 fusion.70
  14.0 7.7 %all-to-all-done = f32[32,4,4,128]{3,2,1,0:T(4,128)S(1)} async-done(((f32[32,4,4,128]{3,2,1,0:T(4,128)}), f32[32,4,4,128]{3,2,1,0:T(4,128)S(1)}, u32[]{:S(2)}, u32[]{:S(2)}) %all-to-all-start) | async-done | bytes 262176 | tf_op jit(solution)/shard_map/all_to_all | solution.py:110
  22.1 14.2 %while.24 = (s32[]{:T(128)}, bf16[4,128,128]{1,2,0:T(8,128)(2,1)S(1)}, s32[4]{0:T(128)S(1)}, bf16[4,128,4,32]{1,3,2,0:T(8,128)(2,1)S(1)}, pred[4,128]{1,0:T(4,12...) while((s32[]{:T(128)}, ...), condition=%wide.region_5.6_spmd, body=%wide.region_2.5_spmd.sunk | while | flops 9159427 | bytes 2038723 | solution.py:91
  22.1 0.7 dynamic_slice.131
  25.7 0.7 dynamic_slice.131
  28.5 0.2 fusion.127
  29.2 0.7 dynamic_slice.131
  32.8 0.7 dynamic_slice.131
  36.3 0.3 convert_reduce_fusion.2
  37.0 0.8 copy.147
  37.7 2.7 %all-to-all-start.1 = ((bf16[4,128,128]{2,0,1:T(4,128)(2,1)}), bf16[4,128,128]{2,0,1:T(4,128)(2,1)S(1)}, u32[]{:S(2)}, u32[]{:S(2)}) async-start(bf16[4,128,128]{2,0,1:T(4,128)(2,1)} %copy.147), calls=%async_computation.1 | async-start | bytes 262144 | tf_op jit(solution)/shard_map/all_to_all | solution.py:185
  40.4 0.3 convolution_bitcast_fusion.1
  40.8 8.0 %all-to-all-done.1 = bf16[4,128,128]{2,0,1:T(4,128)(2,1)S(1)} async-done(((bf16[4,128,128]{2,0,1:T(4,128)(2,1)}), bf16[4,128,128]{2,0,1:T(4,128)(2,1)S(1)}, u32[]{:S(2)}, u32[]{:S(2)}) %all-to-all-start.1) | async-done | bytes 131104 | tf_op jit(solution)/shard_map/all_to_all | solution.py:185
  48.8 0.7 broadcast_in_dim.70
  49.5 2.6 %all-to-all-start.2 = ((f32[32,4,4,128]{3,2,1,0:T(4,128)}), f32[32,4,4,128]{3,2,1,0:T(4,128)S(1)}, u32[]{:S(2)}, u32[]{:S(2)}) async-start(f32[32,4,4,128]{3,2,1,0:T(4,128)} %broadcast_in_dim.70), calls=%async_computation.2 | async-start | bytes 524288 | tf_op jit(solution)/shard_map/all_to_all | solution.py:110
  52.4 0.4 multiply_reduce_fusion.2
  52.8 0.3 copy.151
  53.1 0.3 copy.154
  53.9 0.4 fusion.64
  54.6 7.7 %all-to-all-done.2 = f32[32,4,4,128]{3,2,1,0:T(4,128)S(1)} async-done(((f32[32,4,4,128]{3,2,1,0:T(4,128)}), f32[32,4,4,128]{3,2,1,0:T(4,128)S(1)}, u32[]{:S(2)}, u32[]{:S(2)}) %all-to-all-start.2) | async-done | bytes 262176 | tf_op jit(solution)/shard_map/all_to_all | solution.py:110
  62.5 13.3 %while.25 = (s32[]{:T(128)}, bf16[4,128,128]{1,2,0:T(8,128)(2,1)S(1)}, s32[4]{0:T(128)S(1)}, bf16[128,4,4,32]{0,3,2,1:T(8,128)(2,1)S(1)}, pred[4,128]{1,0:T(4,12...) while((s32[]{:T(128)}, ...), condition=%wide.region_13.14_spmd, body=%wide.region_10.13_spmd.sunk | while | flops 9159427 | bytes 2038723 | solution.py:91
  62.5 0.6 dynamic_slice.137
  65.9 0.6 dynamic_slice.137
  68.5 0.2 fusion.135
  69.2 0.6 dynamic_slice.137
  71.8 0.2 fusion.135
  72.5 0.6 dynamic_slice.137
  75.9 0.3 convert_reduce_fusion.1
  76.5 0.3 fusion.78
  76.8 0.3 fusion.80
  77.4 0.8 copy.160
  78.1 3.4 %all-to-all-start.3 = ((bf16[8,16,4,128]{3,2,1,0:T(4,128)(2,1)}), bf16[8,16,4,128]{3,2,1,0:T(4,128)(2,1)S(1)}, u32[]{:S(2)}, u32[]{:S(2)}) async-start(bf16[8,16,4,128]{3,2,1,0:T(4,128)(2,1)} %copy.160), calls=%async_computation.3 | async-start | bytes 262144 | tf_op jit(solution)/shard_map/all_to_all | solution.py:216
  81.9 1.3 pad_maximum_fusion
  83.2 3.8 %all-to-all-done.3 = bf16[8,16,4,128]{3,2,1,0:T(4,128)(2,1)S(1)} async-done(((bf16[8,16,4,128]{3,2,1,0:T(4,128)(2,1)}), bf16[8,16,4,128]{3,2,1,0:T(4,128)(2,1)S(1)}, u32[]{:S(2)}, u32[]{:S(2)}) %all-to-all-start.3) | async-done | bytes 131104 | tf_op jit(solution)/shard_map/all_to_all | solution.py:216
  87.0 3.0 %all-to-all-start.4 = ((bf16[32,48,4,128]{3,1,2,0:T(8,128)(2,1)}), bf16[32,48,4,128]{3,1,2,0:T(8,128)(2,1)S(1)}, u32[]{:S(2)}, u32[]{:S(2)}) async-start(bf16[32,48,4,128]{3,1,2,0:T(8,128)(2,1)} %bitcast.57), calls=%async_computation.4 | async-start | bytes 3145728 | tf_op jit(solution)/shard_map/all_to_all | solution.py:231
  90.6 0.4 multiply_reduce_fusion.1
  91.6 0.3 fusion.37
  91.9 33.7 %all-to-all-done.4 = bf16[32,48,4,128]{3,1,2,0:T(8,128)(2,1)S(1)} async-done(((bf16[32,48,4,128]{3,1,2,0:T(8,128)(2,1)}), bf16[32,48,4,128]{3,1,2,0:T(8,128)(2,1)S(1)}, u32[]{:S(2)}, u32[]{:S(2)}) %all-to-all-start.4) | async-done | bytes 1572896 | tf_op jit(solution)/shard_map/all_to_all | solution.py:231
  125.7 6.4 %copy.181 = bf16[32,32,4,128]{1,0,2,3:T(8,128)(2,1)} copy(bf16[32,32,4,128]{3,1,2,0:T(8,128)(2,1)S(1)} %slice.89) | data formatting | bytes 2097152
  132.1 3.2 %copy.180 = bf16[32,16,4,128]{0,1,2,3:T(8,128)(2,1)S(1)} copy(bf16[32,16,4,128]{3,1,2,0:T(8,128)(2,1)S(1)} %slice.88) | data formatting | bytes 1048576
  135.3 3.7 %fusion.97 = (f32[16,32]{1,0:T(8,128)S(1)}, f32[16,32,128]{1,0,2:T(8,128)S(1)}) fusion(bf16[32,16,4,128]{0,1,2,3:T(8,128)(2,1)S(1)} %copy.180, bf16[32,32,4,128]{1,0,2,3:T(8,128)(2,1)} %copy.181), kind=kOutput, calls=%fused_computation.169 | convolution fusion | flops 16842240 | bytes 1837056 | tf_op jit(solution)/shard_map/sikc,sjkc->ijc/dot_general | solution.py:232
  139.4 0.4 copy-done.7
  139.8 1.0 fusion.40
  (149 shorter events, 10.0 us)
Async XLA Ops:
  0.0 12.2 %copy-start = (bf16[128,512]{1,0:T(8,128)(2,1)S(1)}, bf16[128,512]{1,0:T(8,128)(2,1)}, u32[]{:S(2)}) copy-start(bf16[128,512]{1,0:T(8,128)(2,1)} %param.22) | copy-start | bytes 393220
  0.0 13.5 %copy-start.9 = (f32[2,4]{1,0:T(2,128)S(1)}, f32[2,4]{1,0:T(2,128)}, u32[]{:S(2)}) copy-start(f32[2,4]{1,0:T(2,128)} %param.21) | copy-start | bytes 100
  4.2 17.6 %all-to-all-start = ((f32[32,4,4,128]{3,2,1,0:T(4,128)}), f32[32,4,4,128]{3,2,1,0:T(4,128)S(1)}, u32[]{:S(2)}, u32[]{:S(2)}) async-start(f32[32,4,4,128]{3,2,1,0:T(4,128)} %broadcast_in_dim.69), calls=%async_computation | async-start | bytes 524288 | tf_op jit(solution)/shard_map/all_to_all | solution.py:110
  13.5 8.5 %copy-start.2 = (s32[128]{0:T(128)S(1)}, s32[128]{0:T(128)}, u32[]{:S(2)}) copy-start(s32[128]{0:T(128)} %param.20) | copy-start | bytes 1540
  22.1 14.2 %copy-start.1 = (bf16[4,128,128]{2,1,0:T(8,128)(2,1)S(1)}, bf16[4,128,128]{2,1,0:T(8,128)(2,1)}, u32[]{:S(2)}) copy-start(bf16[4,128,128]{2,1,0:T(8,128)(2,1)} %param.18) | copy-start | bytes 393220
  22.1 14.2 %copy-start.8 = (bf16[128,128]{1,0:T(8,128)(2,1)S(1)}, bf16[128,128]{1,0:T(8,128)(2,1)}, u32[]{:S(2)}) copy-start(bf16[128,128]{1,0:T(8,128)(2,1)} %param.24) | copy-start | bytes 98308
  22.1 18.4 %copy-start.11 = (bf16[128,4]{0,1:T(4,128)(2,1)S(1)}, bf16[128,4]{0,1:T(4,128)(2,1)}, u32[]{:S(2)}) copy-start(bf16[128,4]{0,1:T(4,128)(2,1)} %param.26) | copy-start | bytes 3076
  36.9 17.0 %copy-start.3 = (bf16[128,512]{1,0:T(8,128)(2,1)S(1)}, bf16[128,512]{1,0:T(8,128)(2,1)}, u32[]{:S(2)}) copy-start(bf16[128,512]{1,0:T(8,128)(2,1)} %param.25) | copy-start | bytes 393220
  37.7 11.0 %all-to-all-start.1 = ((bf16[4,128,128]{2,0,1:T(4,128)(2,1)}), bf16[4,128,128]{2,0,1:T(4,128)(2,1)S(1)}, u32[]{:S(2)}, u32[]{:S(2)}) async-start(bf16[4,128,128]{2,0,1:T(4,128)(2,1)} %copy.147), calls=%async_computation.1 | async-start | bytes 262144 | tf_op jit(solution)/shard_map/all_to_all | solution.py:185
  49.5 12.8 %all-to-all-start.2 = ((f32[32,4,4,128]{3,2,1,0:T(4,128)}), f32[32,4,4,128]{3,2,1,0:T(4,128)S(1)}, u32[]{:S(2)}, u32[]{:S(2)}) async-start(f32[32,4,4,128]{3,2,1,0:T(4,128)} %broadcast_in_dim.70), calls=%async_computation.2 | async-start | bytes 524288 | tf_op jit(solution)/shard_map/all_to_all | solution.py:110
  62.5 13.4 %copy-start.6 = (bf16[128,128]{1,0:T(8,128)(2,1)S(1)}, bf16[128,128]{1,0:T(8,128)(2,1)}, u32[]{:S(2)}) copy-start(bf16[128,128]{1,0:T(8,128)(2,1)} %param.27) | copy-start | bytes 98308
  62.5 14.0 %copy-start.4 = (bf16[128,256]{1,0:T(8,128)(2,1)S(1)}, bf16[128,256]{1,0:T(8,128)(2,1)}, u32[]{:S(2)}) copy-start(bf16[128,256]{1,0:T(8,128)(2,1)} %param.29) | copy-start | bytes 196612
  62.5 14.3 %copy-start.5 = (bf16[128,256]{1,0:T(8,128)(2,1)S(1)}, bf16[128,256]{1,0:T(8,128)(2,1)}, u32[]{:S(2)}) copy-start(bf16[128,256]{1,0:T(8,128)(2,1)} %param.28) | copy-start | bytes 196612
  78.1 8.8 %all-to-all-start.3 = ((bf16[8,16,4,128]{3,2,1,0:T(4,128)(2,1)}), bf16[8,16,4,128]{3,2,1,0:T(4,128)(2,1)S(1)}, u32[]{:S(2)}, u32[]{:S(2)}) async-start(bf16[8,16,4,128]{3,2,1,0:T(4,128)(2,1)} %copy.160), calls=%async_computation.3 | async-start | bytes 262144 | tf_op jit(solution)/shard_map/all_to_all | solution.py:216
  87.0 4.6 %copy-start.10 = (bf16[128,128]{1,0:T(8,128)(2,1)S(1)}, bf16[128,128]{1,0:T(8,128)(2,1)}, u32[]{:S(2)}) copy-start(bf16[128,128]{1,0:T(8,128)(2,1)} %param.30) | copy-start | bytes 98308
  87.0 38.6 %all-to-all-start.4 = ((bf16[32,48,4,128]{3,1,2,0:T(8,128)(2,1)}), bf16[32,48,4,128]{3,1,2,0:T(8,128)(2,1)S(1)}, u32[]{:S(2)}, u32[]{:S(2)}) async-start(bf16[32,48,4,128]{3,1,2,0:T(8,128)(2,1)} %bitcast.57), calls=%async_computation.4 | async-start | bytes 3145728 | tf_op jit(solution)/shard_map/all_to_all | solution.py:231
  139.1 0.8 copy-start.7

commit v2 on v1

--- a/solution.py
+++ b/solution.py
@@ -46,24 +46,26 @@
     line_dim,
     flipped,
 ):
-    line_count = queries.shape[line_dim]
     length = queries.shape[1 - line_dim]
     head_count = queries.shape[2]
     head_size = queries.shape[3]
     width_all = head_count * head_size
     query_rows = min(128, length)
-    per_line = length // query_rows
+    blocks = length // query_rows
     scaling = head_size ** (-0.5)
-
-    def one_block(block_index):
-        line_index = block_index // per_line
-        offset = block_index % per_line * query_rows
-        query_line = lax.dynamic_index_in_dim(queries, line_index, line_dim, keepdims=False)
-        query_block = lax.dynamic_slice_in_dim(query_line, offset, query_rows, 0)
-        key_line = lax.dynamic_index_in_dim(key_rows, line_index, line_dim, keepdims=False)
-        value_line = lax.dynamic_index_in_dim(value_rows, line_index, line_dim, keepdims=False)
+    spec_q = "lqhd" if line_dim == 0 else "qlhd"
+    spec_k = "lkhd" if line_dim == 0 else "klhd"
+    usable = key_ok[:, None, None, :]
+
+    def one_block(offset):
+        query_block = lax.dynamic_slice_in_dim(queries, offset, query_rows, 1 - line_dim)
         scores = (
-            jnp.einsum("qhd,khd->hqk", query_block, key_line, preferred_element_type=jnp.float32)
+            jnp.einsum(
+                f"{spec_q},{spec_k}->lhqk",
+                query_block,
+                key_rows,
+                preferred_element_type=jnp.float32,
+            )
             * scaling
         )
         if flipped:
@@ -72,27 +74,27 @@
             )
         else:
             bias_block = lax.dynamic_slice_in_dim(bias_all, offset, query_rows, 1)
-        scores = scores + bias_block
+        scores = scores + bias_block[None]
         chain_block = lax.dynamic_slice_in_dim(chain_ids, offset, query_rows, 0)
         same_chain = (chain_block[:, None] == chain_ids[None, :]).astype(jnp.float32)
-        scores = scores + chain_add[:, None, None] * same_chain[None]
-        usable = lax.dynamic_index_in_dim(key_ok, line_index, 0, keepdims=False)
-        scores = jnp.where(usable[None, None, :], scores, -1000000000.0)
+        scores = scores + (chain_add[:, None, None] * same_chain[None])[None]
+        scores = jnp.where(usable, scores, -1000000000.0)
         row_peak = jnp.max(scores, axis=-1, keepdims=True)
         weights = jnp.exp(scores - row_peak)
         attention = (weights / jnp.sum(weights, axis=-1, keepdims=True)).astype(jnp.bfloat16)
         mixed_rows = jnp.einsum(
-            "hqk,khd->qhd", attention, value_line, preferred_element_type=jnp.float32
-        ).reshape(query_rows, width_all)
-        gate_line = lax.dynamic_index_in_dim(gate_pre, line_index, line_dim, keepdims=False)
-        gate_block = lax.dynamic_slice_in_dim(gate_line, offset, query_rows, 0)
+            f"lhqk,{spec_k}->{spec_q}", attention, value_rows, preferred_element_type=jnp.float32
+        )
+        mixed_rows = mixed_rows.reshape(mixed_rows.shape[:2] + (width_all,))
+        gate_block = lax.dynamic_slice_in_dim(gate_pre, offset, query_rows, 1 - line_dim)
         return (mixed_rows * jax.nn.sigmoid(gate_block)).astype(jnp.bfloat16)
 
-    outputs = lax.map(one_block, jnp.arange(line_count * per_line, dtype=jnp.int32))
-    outputs = outputs.reshape(line_count, length, width_all)
-    if line_dim == 1:
-        outputs = outputs.transpose(1, 0, 2)
-    return outputs
+    if blocks == 1:
+        return one_block(0)
+    outputs = lax.map(one_block, jnp.arange(blocks, dtype=jnp.int32) * query_rows)
+    if line_dim == 0:
+        outputs = outputs.transpose(1, 0, 2, 3)
+    return outputs.reshape(gate_pre.shape[:2] + (width_all,))
 
 
 def tri_acts(normed, weights, allowed):
@@ -176,13 +178,28 @@
         normed_first.reshape(-1, channels), col_bias_proj, preferred_element_type=jnp.float32
     )
     bias_next = bias_next.reshape(rows_here, length, head_count).transpose(2, 0, 1)
-    bias_cols = gather_lines(bias_next)
-    first_sent = (
+    pair_chunks = (
         first_pair.reshape(rows_here, n_col, n_row, rows_here, channels)
-        .transpose(0, 2, 1, 3, 4)
-        .reshape(rows_here, length, channels)
-    )
-    columns = lax.all_to_all(first_sent, ("row", "col"), split_axis=1, concat_axis=0, tiled=True)
+        .transpose(2, 1, 0, 3, 4)
+        .reshape(device_count, rows_here * rows_here * channels)
+        .astype(jnp.float32)
+    )
+    bias_chunks = jnp.broadcast_to(
+        bias_next.reshape(1, -1), (device_count, head_count * rows_here * length)
+    )
+    merged = lax.all_to_all(
+        jnp.concatenate([pair_chunks, bias_chunks], axis=1), ("row", "col"), 0, 0, tiled=True
+    )
+    pair_size = rows_here * rows_here * channels
+    columns = (
+        merged[:, :pair_size].astype(jnp.bfloat16).reshape(length, rows_here, channels)
+    )
+    bias_cols = (
+        merged[:, pair_size:]
+        .reshape(device_count, head_count, rows_here, length)
+        .transpose(1, 0, 2, 3)
+        .reshape(head_count, length, length)
+    )
     normed_cols = layer_norm(columns).astype(jnp.bfloat16)
     projected_cols = jnp.dot(
         normed_cols.reshape(-1, channels), col_project, preferred_element_type=jnp.float32

time: 143 us -> 121 us (0.85)
  loops' own time: 16.5 us -> 0 us
  local copies, waits for them, and re-layouts: 22.6 us -> 18 us
  matrix products: 13 us -> 17.3 us
  starting transfers between devices: 18.9 us -> 16.8 us
  waiting for transfers between devices: 60.9 us -> 59.4 us
    another operation x2 -> x0, loops' own time: 16.5 us -> none  [attend_lines(): lax.map(one_block, jnp.arange(line_count * per_line, dtype=jnp.int32))]
    all_to_all x2 -> x1, waiting for transfers between devices: 15.4 us -> 7.75 us  [gather_lines(): got = lax.all_to_all(sent, ('row', 'col'), 0, 0, tiled=True)]
    all_to_all x1, waiting for transfers between devices: 8.03 us -> 14.1 us  [shards(): lax.all_to_all(jnp.concatenate([pair_chunks, bias_chunks], axis=1), ('row...]
    dynamic_slice x24 -> x0, local copies, waits for them, and re-layouts: 5.76 us -> none  [the longest x8 5.01 us: attend_lines(): lax.map(one_block, jnp.arange(line_count * per_line, dtype=jnp.int32))]
    sub x0 -> x2, matrix products: none -> 3.08 us  [one_block(): weights = jnp.exp(scores - row_peak)]
    all_to_all x2 -> x1, starting transfers between devices: 9.91 us -> 7.33 us  [gather_lines(): got = lax.all_to_all(sent, ('row', 'col'), 0, 0, tiled=True)]
    unnamed x26 -> x23, local copies, waits for them, and re-layouts: 10.1 us -> 10.8 us
    dot_general x16 -> x4, matrix products: 3.49 us -> 3.38 us  [the longest x2 2.7 us: one_block(): jnp.einsum(f'{spec_q},{spec_k}->lhqk', query_block, key_rows, preferred_e...]
  transfers between devices with their start and end apart: 5 -> 4, of which waited for: 5 -> 4; matrix products, arithmetic and copies ran while one was open for 6% -> 4% of each run, Pallas kernels for 0% -> 0%
where the time goes in v2:
time: 121 us; the launch traced here: 119 us
  waiting for transfers between devices  59.4 us (49%)
  local copies, waits for them, and re-layouts  18 us (15%)
  matrix products  17.3 us (14%)
  starting transfers between devices  16.8 us (14%)
  other arithmetic  6.46 us (5%)
    all_to_all x1, waiting for transfers between devices, shards(): lax.all_to_all(outgoing, ('row', 'col'), split_axis=0, concat_axis=0, til...  33.7 us
    all_to_all x1, waiting for transfers between devices, shards(): lax.all_to_all(jnp.concatenate([pair_chunks, bias_chunks], axis=1), ('row...  14.1 us
    unnamed x23, local copies, waits for them, and re-layouts  10.8 us
    all_to_all x1, waiting for transfers between devices, gather_lines(): got = lax.all_to_all(sent, ('row', 'col'), 0, 0, tiled=True)  7.75 us
    all_to_all x1, starting transfers between devices, gather_lines(): got = lax.all_to_all(sent, ('row', 'col'), 0, 0, tiled=True)  7.33 us
    all_to_all x1, waiting for transfers between devices, shards(): lax.all_to_all(second_pair.reshape(n_row, block_rows, rows_here, channels...  3.84 us
    dot_general x1, matrix products, shards(): jnp.einsum('sikc,sjkc->ijc', received[:, :block_rows], received[:, block_...  3.72 us
    all_to_all x1, starting transfers between devices, shards(): lax.all_to_all(second_pair.reshape(n_row, block_rows, rows_here, channels...  3.65 us
  transfers between devices with their start and end apart: 4, of which 4 were waited for; matrix products, arithmetic and copies ran while one was open for 4% of the time, Pallas kernels for 0%

profile of v2, /device:TPU:0, one launch (start us, length us, event | category | flops | bytes accessed | tf_op | source)
XLA Modules:
  0.0 119.1 jit_solution(6508885538040972159)
XLA Ops:
  0.0 1.1 convert_reduce_fusion
  1.1 1.1 fusion.27
  2.2 1.2 %convolution_bitcast_fusion.2 = f32[4,4,128]{2,0,1:T(4,128)S(1)} fusion(bf16[4,128,128]{2,1,0:T(8,128)(2,1)} %param.14, f32[4,128]{1,0:T(4,128)S(1)} %add_rsqrt_fusion.5, f32[4,128]{1,0:T(4,128)S(1)} %broadcast_multiply_fusion.8, bf16[128,4]{0,1:T(4,128)(2,1)} %param.19), kind=kOutput, calls=%fused_computation.29 | convolution fusion | flops 786432 | bytes 144384 | tf_op jit(solution)/shard_map/dot_general | solution.py:148
  3.5 0.7 broadcast_in_dim.33
  4.2 7.3 %all-to-all-start = ((f32[32,4,4,128]{3,2,1,0:T(4,128)}), f32[32,4,4,128]{3,2,1,0:T(4,128)S(1)}, u32[]{:S(2)}, u32[]{:S(2)}) async-start(f32[32,4,4,128]{3,2,1,0:T(4,128)} %broadcast_in_dim.33), calls=%async_computation | async-start | bytes 524288 | tf_op jit(solution)/shard_map/all_to_all | solution.py:112
  12.2 1.3 %fusion.57 = f32[4,128,512]{2,1,0:T(8,128)S(1)} fusion(bf16[128,512]{1,0:T(8,128)(2,1)S(1)} %copy-done, bf16[4,128,128]{2,1,0:T(8,128)(2,1)} %param.14, f32[4,128]{1,0:T(4,128)S(1)} %add_rsqrt_fusion.5, f32[4,128]{1,0:T(4,128)S(1)} %broadcast_multiply_fusion.8), kind=kOutput, calls=%fused_computation.98 | convolution fusion | flops 67371008 | bytes 1314816 | tf_op jit(solution)/shard_map/dot_general | solution.py:151
  13.6 0.2 copy.150
  14.0 7.7 %all-to-all-done = f32[32,4,4,128]{3,2,1,0:T(4,128)S(1)} async-done(((f32[32,4,4,128]{3,2,1,0:T(4,128)}), f32[32,4,4,128]{3,2,1,0:T(4,128)S(1)}, u32[]{:S(2)}, u32[]{:S(2)}) %all-to-all-start) | async-done | bytes 262176 | tf_op jit(solution)/shard_map/all_to_all | solution.py:112
  21.8 0.8 copy.156
  22.6 1.3 %fusion.8 = f32[4,4,128,128]{2,3,1,0:T(8,128)S(1)} fusion(f32[4,128,128]{1,2,0:T(8,128)S(1)} %get-tuple-element.6, f32[4,128,128]{1,2,0:T(8,128)} %copy.156, pred[4]{0:T(512)(128)(4,1)S(1)} %get-tuple-element.18, bf16[4,128,3,4,32]{1,4,3,2,0:T(8,128)(2,1)S(1)} %bitcast.139), kind=kOutput, calls=%fused_computation.12 | convolution fusion | flops 17825792 | bytes 1835520 | tf_op jit(solution)/shard_map/lqhd,lkhd->lhqk/dot_general | solution.py:63
  24.0 1.5 %fusion.90 = f32[4,4,128]{2,1,0:T(4,128)S(1)} fusion(f32[4,128,128]{1,2,0:T(8,128)S(1)} %get-tuple-element.6, f32[4,128,128]{1,2,0:T(8,128)} %copy.156, pred[4]{0:T(512)(128)(4,1)S(1)} %get-tuple-element.18, bf16[4,128,3,4,32]{1,4,3,2,0:T(8,128)(2,1)S(1)} %bitcast.140), kind=kOutput, calls=%fused_computation.161 | convolution fusion | flops 18350208 | bytes 795136 | tf_op jit(solution)/shard_map/sub | solution.py:83
  25.5 0.3 fusion.21
  26.0 0.4 copy-done.1
  26.4 1.1 fusion.91
  27.5 0.2 multiply_reduce_fusion.3
  27.8 0.3 convolution_bitcast_fusion.1
  28.3 1.3 %copy.161 = f32[32,1,4096]{2,1,0:T(1,128)} copy(f32[32,1,4096]{2,0,1:T(8,128)S(1)} %maximum_bitcast_fusion) | data formatting | bytes 1048576 | tf_op jit(solution)/shard_map/all_to_all | solution.py:190
  29.7 2.7 %all-to-all-start.1 = ((f32[32,1,4096]{2,1,0:T(1,128)}), f32[32,1,4096]{2,1,0:T(1,128)S(1)}, u32[]{:S(2)}, u32[]{:S(2)}) async-start(f32[32,1,4096]{2,1,0:T(1,128)} %copy.161), calls=%async_computation.1 | async-start | bytes 1048576 | tf_op jit(solution)/shard_map/all_to_all | solution.py:190
  32.4 14.1 %all-to-all-done.1 = f32[32,1,4096]{2,1,0:T(1,128)S(1)} async-done(((f32[32,1,4096]{2,1,0:T(1,128)}), f32[32,1,4096]{2,1,0:T(1,128)S(1)}, u32[]{:S(2)}, u32[]{:S(2)}) %all-to-all-start.1) | async-done | bytes 524320 | tf_op jit(solution)/shard_map/all_to_all | solution.py:190
  46.6 0.3 copy.209
  47.1 0.2 reduce_sum.131
  47.4 0.4 multiply_reduce_fusion.2
  47.7 0.3 multiply_convert_fusion.2
  48.1 0.3 fusion.55
  48.4 0.2 copy.167
  48.9 0.7 copy.171
  49.6 1.3 %fusion.11 = f32[4,4,128,128]{2,3,1,0:T(8,128)S(1)} fusion(f32[4,128,128]{1,2,0:T(8,128)S(1)} %get-tuple-element.5, f32[4,128,128]{1,2,0:T(8,128)} %bitcast.27, pred[4]{0:T(512)(128)(4,1)S(1)} %get-tuple-element.17, bf16[128,4,3,4,32]{0,4,3,2,1:T(8,128)(2,1)S(1)} %bitcast.142), kind=kOutput, calls=%fused_computation.15 | convolution fusion | flops 17825792 | bytes 1835520 | tf_op jit(solution)/shard_map/qlhd,klhd->lhqk/dot_general | solution.py:63
  50.9 1.5 %fusion.92 = f32[4,4,128]{2,1,0:T(4,128)S(1)} fusion(f32[4,128,128]{1,2,0:T(8,128)S(1)} %get-tuple-element.5, f32[4,128,128]{1,2,0:T(8,128)} %bitcast.27, pred[4]{0:T(512)(128)(4,1)S(1)} %get-tuple-element.17, bf16[128,4,3,4,32]{0,4,3,2,1:T(8,128)(2,1)S(1)} %bitcast.143), kind=kOutput, calls=%fused_computation.163 | convolution fusion | flops 18350208 | bytes 795136 | tf_op jit(solution)/shard_map/sub | solution.py:83
  52.5 0.3 fusion.22
  53.0 1.1 convert_reduce_fusion.1
  54.0 0.2 fusion.29
  54.3 0.3 fusion.66
  54.6 0.3 fusion.68
  55.2 0.8 copy.175
  55.9 3.6 %all-to-all-start.2 = ((bf16[8,16,4,128]{3,2,1,0:T(4,128)(2,1)}), bf16[8,16,4,128]{3,2,1,0:T(4,128)(2,1)S(1)}, u32[]{:S(2)}, u32[]{:S(2)}) async-start(bf16[8,16,4,128]{3,2,1,0:T(4,128)(2,1)} %copy.175), calls=%async_computation.2 | async-start | bytes 262144 | tf_op jit(solution)/shard_map/all_to_all | solution.py:233
  59.6 0.2 broadcast_in_dim.41
  59.9 1.3 %pad_maximum_fusion = bf16[8,4,48,4,128]{4,2,3,1,0:T(8,128)(2,1)} fusion(bf16[8,4,32,4,128]{4,2,3,1,0:T(8,128)(2,1)S(1)} %broadcast_in_dim.41, bf16[8,4,16,4,128]{4,2,3,1,0:T(8,128)(2,1)S(1)} %broadcast_in_dim.39), kind=kLoop, calls=%fused_computation.2 | loop fusion | flops 3145728 | bytes 3145728 | tf_op jit(solution)/shard_map/concatenate | solution.py:245
  61.3 3.8 %all-to-all-done.2 = bf16[8,16,4,128]{3,2,1,0:T(4,128)(2,1)S(1)} async-done(((bf16[8,16,4,128]{3,2,1,0:T(4,128)(2,1)}), bf16[8,16,4,128]{3,2,1,0:T(4,128)(2,1)S(1)}, u32[]{:S(2)}, u32[]{:S(2)}) %all-to-all-start.2) | async-done | bytes 131104 | tf_op jit(solution)/shard_map/all_to_all | solution.py:233
  65.1 3.1 %all-to-all-start.3 = ((bf16[32,48,4,128]{3,1,2,0:T(8,128)(2,1)}), bf16[32,48,4,128]{3,1,2,0:T(8,128)(2,1)S(1)}, u32[]{:S(2)}, u32[]{:S(2)}) async-start(bf16[32,48,4,128]{3,1,2,0:T(8,128)(2,1)} %bitcast.42), calls=%async_computation.3 | async-start | bytes 3145728 | tf_op jit(solution)/shard_map/all_to_all | solution.py:248
  68.2 0.2 fusion.53
  68.8 0.4 multiply_reduce_fusion.1
  69.8 0.3 fusion.15
  70.2 33.7 %all-to-all-done.3 = bf16[32,48,4,128]{3,1,2,0:T(8,128)(2,1)S(1)} async-done(((bf16[32,48,4,128]{3,1,2,0:T(8,128)(2,1)}), bf16[32,48,4,128]{3,1,2,0:T(8,128)(2,1)S(1)}, u32[]{:S(2)}, u32[]{:S(2)}) %all-to-all-start.3) | async-done | bytes 1572896 | tf_op jit(solution)/shard_map/all_to_all | solution.py:248
  103.9 6.4 %copy.199 = bf16[32,32,4,128]{1,0,2,3:T(8,128)(2,1)} copy(bf16[32,32,4,128]{3,1,2,0:T(8,128)(2,1)S(1)} %slice.100) | data formatting | bytes 2097152
  110.4 3.2 %copy.198 = bf16[32,16,4,128]{0,1,2,3:T(8,128)(2,1)S(1)} copy(bf16[32,16,4,128]{3,1,2,0:T(8,128)(2,1)S(1)} %slice.99) | data formatting | bytes 1048576
  113.6 3.7 %fusion.93 = (f32[16,32]{1,0:T(8,128)S(1)}, f32[16,32,128]{1,0,2:T(8,128)S(1)}) fusion(bf16[32,16,4,128]{0,1,2,3:T(8,128)(2,1)S(1)} %copy.198, bf16[32,32,4,128]{1,0,2,3:T(8,128)(2,1)} %copy.199), kind=kOutput, calls=%fused_computation.164 | convolution fusion | flops 16842240 | bytes 1837056 | tf_op jit(solution)/shard_map/sikc,sjkc->ijc/dot_general | solution.py:249
  117.7 0.4 copy-done.5
  118.1 1.0 fusion.19
  (69 shorter events, 3.1 us)
Async XLA Ops:
  0.0 12.2 %copy-start = (bf16[128,512]{1,0:T(8,128)(2,1)S(1)}, bf16[128,512]{1,0:T(8,128)(2,1)}, u32[]{:S(2)}) copy-start(bf16[128,512]{1,0:T(8,128)(2,1)} %param.18) | copy-start | bytes 393220
  0.0 13.5 %copy-start.8 = (f32[2,4]{1,0:T(2,128)S(1)}, f32[2,4]{1,0:T(2,128)}, u32[]{:S(2)}) copy-start(f32[2,4]{1,0:T(2,128)} %param.17) | copy-start | bytes 100
  0.0 13.8 %copy-start.6 = (s32[128]{0:T(128)S(1)}, s32[128]{0:T(128)}, u32[]{:S(2)}) copy-start(s32[128]{0:T(128)} %param.16) | copy-start | bytes 1540
  4.2 17.6 %all-to-all-start = ((f32[32,4,4,128]{3,2,1,0:T(4,128)}), f32[32,4,4,128]{3,2,1,0:T(4,128)S(1)}, u32[]{:S(2)}, u32[]{:S(2)}) async-start(f32[32,4,4,128]{3,2,1,0:T(4,128)} %broadcast_in_dim.33), calls=%async_computation | async-start | bytes 524288 | tf_op jit(solution)/shard_map/all_to_all | solution.py:112
  25.5 0.9 copy-start.1
  25.9 1.9 %copy-start.7 = (bf16[128,4]{0,1:T(4,128)(2,1)S(1)}, bf16[128,4]{0,1:T(4,128)(2,1)}, u32[]{:S(2)}) copy-start(bf16[128,4]{0,1:T(4,128)(2,1)} %param.22) | copy-start | bytes 3076
  29.7 16.9 %all-to-all-start.1 = ((f32[32,1,4096]{2,1,0:T(1,128)}), f32[32,1,4096]{2,1,0:T(1,128)S(1)}, u32[]{:S(2)}, u32[]{:S(2)}) async-start(f32[32,1,4096]{2,1,0:T(1,128)} %copy.161), calls=%async_computation.1 | async-start | bytes 1048576 | tf_op jit(solution)/shard_map/all_to_all | solution.py:190
  32.3 15.8 %copy-start.2 = (bf16[128,512]{1,0:T(8,128)(2,1)S(1)}, bf16[128,512]{1,0:T(8,128)(2,1)}, u32[]{:S(2)}) copy-start(bf16[128,512]{1,0:T(8,128)(2,1)} %param.21) | copy-start | bytes 393220
  52.8 1.5 %copy-start.3 = (bf16[128,256]{1,0:T(8,128)(2,1)S(1)}, bf16[128,256]{1,0:T(8,128)(2,1)}, u32[]{:S(2)}) copy-start(bf16[128,256]{1,0:T(8,128)(2,1)} %param.25) | copy-start | bytes 196612
  52.8 1.8 %copy-start.4 = (bf16[128,256]{1,0:T(8,128)(2,1)S(1)}, bf16[128,256]{1,0:T(8,128)(2,1)}, u32[]{:S(2)}) copy-start(bf16[128,256]{1,0:T(8,128)(2,1)} %param.24) | copy-start | bytes 196612
  55.9 9.1 %all-to-all-start.2 = ((bf16[8,16,4,128]{3,2,1,0:T(4,128)(2,1)}), bf16[8,16,4,128]{3,2,1,0:T(4,128)(2,1)S(1)}, u32[]{:S(2)}, u32[]{:S(2)}) async-start(bf16[8,16,4,128]{3,2,1,0:T(4,128)(2,1)} %copy.175), calls=%async_computation.2 | async-start | bytes 262144 | tf_op jit(solution)/shard_map/all_to_all | solution.py:233
  65.1 4.7 %copy-start.9 = (bf16[128,128]{1,0:T(8,128)(2,1)S(1)}, bf16[128,128]{1,0:T(8,128)(2,1)}, u32[]{:S(2)}) copy-start(bf16[128,128]{1,0:T(8,128)(2,1)} %param.26) | copy-start | bytes 98308
  65.1 38.8 %all-to-all-start.3 = ((bf16[32,48,4,128]{3,1,2,0:T(8,128)(2,1)}), bf16[32,48,4,128]{3,1,2,0:T(8,128)(2,1)S(1)}, u32[]{:S(2)}, u32[]{:S(2)}) async-start(bf16[32,48,4,128]{3,1,2,0:T(8,128)(2,1)} %bitcast.42), calls=%async_computation.3 | async-start | bytes 3145728 | tf_op jit(solution)/shard_map/all_to_all | solution.py:248
  117.3 0.8 copy-start.5

commit v3 on v2

--- a/solution.py
+++ b/solution.py
@@ -234,24 +234,22 @@
         second_pair.reshape(n_row, block_rows, rows_here, channels), "row", 0, 0, tiled=True
     )
     own_pair = raw_got.transpose(1, 0, 2, 3).reshape(block_rows, block_cols, channels)
-    left_send = jnp.broadcast_to(
-        left_all.reshape(n_row, 1, block_rows, rows_here, channels),
-        (n_row, n_col, block_rows, rows_here, channels),
-    )
-    right_send = jnp.broadcast_to(
-        right_all.reshape(1, n_col, block_cols, rows_here, channels),
-        (n_row, n_col, block_cols, rows_here, channels),
-    )
-    outgoing = jnp.concatenate([left_send, right_send], axis=2).reshape(
-        device_count, block_rows + block_cols, rows_here, channels
-    )
-    received = lax.all_to_all(outgoing, ("row", "col"), split_axis=0, concat_axis=0, tiled=True)
-    product_sum = jnp.einsum(
-        "sikc,sjkc->ijc",
-        received[:, :block_rows],
-        received[:, block_rows:],
+    channels_here = channels // device_count
+    edges = jnp.stack([left_all, right_all], axis=0).transpose(3, 0, 1, 2)
+    edges_got = lax.all_to_all(edges, ("row", "col"), 0, 3, tiled=True)
+    product_part = jnp.einsum(
+        "cik,cjk->cij",
+        edges_got[:, 0],
+        edges_got[:, 1],
         preferred_element_type=jnp.float32,
     )
+    product_sent = (
+        product_part.reshape(channels_here, n_row, block_rows, n_col, block_cols)
+        .transpose(1, 3, 0, 2, 4)
+        .reshape(device_count, channels_here, block_rows, block_cols)
+    )
+    product_got = lax.all_to_all(product_sent, ("row", "col"), 0, 1, tiled=True)
+    product_sum = product_got.reshape(channels, block_rows, block_cols).transpose(1, 2, 0)
     normed_own = layer_norm(own_pair).astype(jnp.bfloat16)
     gate_values = jax.nn.sigmoid(
         jnp.dot(normed_own.reshape(-1, channels), tri_gate, preferred_element_type=jnp.float32)

time: 121 us -> 92.8 us (0.77)
  waiting for transfers between devices: 59.4 us -> 41.1 us
  matrix products: 17.3 us -> 6.7 us
  starting transfers between devices: 16.8 us -> 19.4 us
    all_to_all x1 -> x2, waiting for transfers between devices: 33.7 us -> 17.7 us  [the longest x1 9.73 us: shards(): edges_got = lax.all_to_all(edges, ('row', 'col'), 0, 3, tiled=True)]
    dot_general x1, matrix products: 3.72 us -> 0.23 us  [shards(): jnp.einsum('cik,cjk->cij', edges_got[:, 0], edges_got[:, 1], preferred_el...]
    all_to_all x1 -> x2, starting transfers between devices: 3.13 us -> 5.77 us  [the longest x1 2.93 us: shards(): edges_got = lax.all_to_all(edges, ('row', 'col'), 0, 3, tiled=True)]
    dot_general x2, matrix products: 2.7 us -> 0.8 us  [one_block(): jnp.einsum(f'{spec_q},{spec_k}->lhqk', query_block, key_rows, preferred_e...]
    sub x2, matrix products: 3.08 us -> 1.19 us  [one_block(): weights = jnp.exp(scores - row_peak)]
    all_to_all x1, waiting for transfers between devices: 3.84 us -> 2.4 us  [shards(): lax.all_to_all(second_pair.reshape(n_row, block_rows, rows_here, channels...]
    unnamed x23 -> x33, local copies, waits for them, and re-layouts: 10.8 us -> 9.47 us
    concatenate x1 -> x0, other arithmetic: 1.3 us -> none  [shards(): jnp.concatenate([left_send, right_send], axis=2)]
  transfers between devices with their start and end apart: 4 -> 5, of which waited for: 4 -> 5; matrix products, arithmetic and copies ran while one was open for 4% -> 6% of each run, Pallas kernels for 0% -> 0%
where the time goes in v3:
time: 92.8 us; the launch traced here: 91.8 us
  waiting for transfers between devices  41.1 us (44%)
  starting transfers between devices  19.4 us (21%)
  local copies, waits for them, and re-layouts  17 us (18%)
  matrix products  6.7 us (7%)
  other arithmetic  6.39 us (7%)
  between operations  1.18 us (1%)
    all_to_all x1, waiting for transfers between devices, shards(): lax.all_to_all(jnp.concatenate([pair_chunks, bias_chunks], axis=1), ('row...  14.1 us
    all_to_all x1, waiting for transfers between devices, shards(): edges_got = lax.all_to_all(edges, ('row', 'col'), 0, 3, tiled=True)  9.73 us
    unnamed x33, local copies, waits for them, and re-layouts  9.47 us
    all_to_all x1, waiting for transfers between devices, shards(): product_got = lax.all_to_all(product_sent, ('row', 'col'), 0, 1, tiled=True)  7.97 us
    all_to_all x1, starting transfers between devices, gather_lines(): got = lax.all_to_all(sent, ('row', 'col'), 0, 0, tiled=True)  7.33 us
    all_to_all x1, waiting for transfers between devices, gather_lines(): got = lax.all_to_all(sent, ('row', 'col'), 0, 0, tiled=True)  6.88 us
    all_to_all x1, starting transfers between devices, shards(): lax.all_to_all(second_pair.reshape(n_row, block_rows, rows_here, channels...  3.65 us
    all_to_all x1, starting transfers between devices, shards(): edges_got = lax.all_to_all(edges, ('row', 'col'), 0, 3, tiled=True)  2.93 us
  transfers between devices with their start and end apart: 5, of which 5 were waited for; matrix products, arithmetic and copies ran while one was open for 6% of the time, Pallas kernels for 0%

profile of v3, /device:TPU:0, one launch (start us, length us, event | category | flops | bytes accessed | tf_op | source)
XLA Modules:
  0.0 91.8 jit_solution(5748596570785014932)
XLA Ops:
  0.0 1.1 %convert_reduce_fusion = f32[4,128]{1,0:T(4,128)S(1)} fusion(bf16[4,128,128]{2,1,0:T(8,128)(2,1)} %param.14), kind=kLoop, calls=%fused_computation.42 | loop fusion | flops 130560 | bytes 133120 | tf_op jit(solution)/shard_map/reduce_sum | solution.py:9
  1.4 0.7 copy-done.14
  2.4 0.7 broadcast_in_dim.25
  3.1 7.3 %all-to-all-start = ((f32[32,4,4,128]{3,2,1,0:T(4,128)}), f32[32,4,4,128]{3,2,1,0:T(4,128)S(1)}, u32[]{:S(2)}, u32[]{:S(2)}) async-start(f32[32,4,4,128]{3,2,1,0:T(4,128)} %broadcast_in_dim.25), calls=%async_computation | async-start | bytes 524288 | tf_op jit(solution)/shard_map/all_to_all | solution.py:112
  10.4 0.7 copy-done.10
  11.8 0.4 fusion.58
  12.5 0.4 copy-done.8
  13.0 0.8 broadcast_multiply_fusion
  13.8 6.9 %all-to-all-done = f32[32,4,4,128]{3,2,1,0:T(4,128)S(1)} async-done(((f32[32,4,4,128]{3,2,1,0:T(4,128)}), f32[32,4,4,128]{3,2,1,0:T(4,128)S(1)}, u32[]{:S(2)}, u32[]{:S(2)}) %all-to-all-start) | async-done | bytes 262176 | tf_op jit(solution)/shard_map/all_to_all | solution.py:112
  20.8 0.6 fusion.93
  21.4 0.4 fusion.8
  21.8 0.3 fusion.21
  22.3 0.6 copy-done.11
  23.7 0.7 copy-done.9
  24.8 1.3 %copy.164 = f32[32,1,4096]{2,1,0:T(1,128)} copy(f32[32,1,4096]{2,0,1:T(8,128)S(1)} %maximum_bitcast_fusion) | data formatting | bytes 1048576 | tf_op jit(solution)/shard_map/all_to_all | solution.py:190
  26.1 2.7 %all-to-all-start.1 = ((f32[32,1,4096]{2,1,0:T(1,128)}), f32[32,1,4096]{2,1,0:T(1,128)S(1)}, u32[]{:S(2)}, u32[]{:S(2)}) async-start(f32[32,1,4096]{2,1,0:T(1,128)} %copy.164), calls=%async_computation.1 | async-start | bytes 1048576 | tf_op jit(solution)/shard_map/all_to_all | solution.py:190
  28.9 14.1 %all-to-all-done.1 = f32[32,1,4096]{2,1,0:T(1,128)S(1)} async-done(((f32[32,1,4096]{2,1,0:T(1,128)}), f32[32,1,4096]{2,1,0:T(1,128)S(1)}, u32[]{:S(2)}, u32[]{:S(2)}) %all-to-all-start.1) | async-done | bytes 524320 | tf_op jit(solution)/shard_map/all_to_all | solution.py:190
  44.0 0.4 multiply_reduce_fusion.2
  44.4 0.3 multiply_convert_fusion.2
  44.7 0.6 copy-done.4
  45.9 0.7 copy-done.2
  46.6 0.6 fusion.95
  47.2 0.4 copy-done.3
  47.6 0.4 fusion.11
  48.0 0.3 fusion.22
  48.5 0.6 copy-done.12
  49.4 0.8 copy.178
  50.1 3.6 %all-to-all-start.2 = ((bf16[8,16,4,128]{3,2,1,0:T(4,128)(2,1)}), bf16[8,16,4,128]{3,2,1,0:T(4,128)(2,1)S(1)}, u32[]{:S(2)}, u32[]{:S(2)}) async-start(bf16[8,16,4,128]{3,2,1,0:T(4,128)(2,1)} %copy.178), calls=%async_computation.2 | async-start | bytes 262144 | tf_op jit(solution)/shard_map/all_to_all | solution.py:233
  54.1 0.6 copy-done.5
  54.6 0.3 fusion.71
  55.0 0.5 copy-done.6
  55.5 0.3 fusion.69
  56.0 0.9 copy.186
  56.9 2.4 %all-to-all-done.2 = bf16[8,16,4,128]{3,2,1,0:T(4,128)(2,1)S(1)} async-done(((bf16[8,16,4,128]{3,2,1,0:T(4,128)(2,1)}), bf16[8,16,4,128]{3,2,1,0:T(4,128)(2,1)S(1)}, u32[]{:S(2)}, u32[]{:S(2)}) %all-to-all-start.2) | async-done | bytes 131104 | tf_op jit(solution)/shard_map/all_to_all | solution.py:233
  59.3 2.9 %all-to-all-start.3 = ((bf16[128,2,128,4]{2,3,1,0:T(4,128)(2,1)}), bf16[128,2,128,4]{2,3,1,0:T(4,128)(2,1)S(1)}, u32[]{:S(2)}, u32[]{:S(2)}) async-start(bf16[128,2,128,4]{2,3,1,0:T(4,128)(2,1)} %copy.186), calls=%async_computation.3 | async-start | bytes 524288 | tf_op jit(solution)/shard_map/all_to_all | solution.py:239
  62.7 9.7 %all-to-all-done.3 = bf16[128,2,128,4]{2,3,1,0:T(4,128)(2,1)S(1)} async-done(((bf16[128,2,128,4]{2,3,1,0:T(4,128)(2,1)}), bf16[128,2,128,4]{2,3,1,0:T(4,128)(2,1)S(1)}, u32[]{:S(2)}, u32[]{:S(2)}) %all-to-all-start.3) | async-done | bytes 262176 | tf_op jit(solution)/shard_map/all_to_all | solution.py:239
  72.9 0.4 reshape.397
  73.5 1.2 %reshape.415 = f32[32,1,2048]{2,1,0:T(1,128)} reshape(f32[32,4,16,32]{3,2,1,0:T(8,128)S(1)} %bitcast.155) | data formatting | bytes 524288
  74.7 2.8 %all-to-all-start.4 = ((f32[32,1,2048]{2,1,0:T(1,128)}), f32[32,1,2048]{2,1,0:T(1,128)S(1)}, u32[]{:S(2)}, u32[]{:S(2)}) async-start(f32[32,1,2048]{2,1,0:T(1,128)} %reshape.415), calls=%async_computation.4 | async-start | bytes 524288 | tf_op jit(solution)/shard_map/all_to_all | solution.py:251
  77.5 0.4 multiply_reduce_fusion.1
  78.6 0.6 copy-done.13
  79.3 0.3 fusion.15
  79.6 8.0 %all-to-all-done.4 = f32[32,1,2048]{2,1,0:T(1,128)S(1)} async-done(((f32[32,1,2048]{2,1,0:T(1,128)}), f32[32,1,2048]{2,1,0:T(1,128)S(1)}, u32[]{:S(2)}, u32[]{:S(2)}) %all-to-all-start.4) | async-done | bytes 262176 | tf_op jit(solution)/shard_map/all_to_all | solution.py:251
  87.6 0.5 broadcast.515
  88.1 1.3 %reduce.2 = f32[32,2048]{1,0:T(8,128)S(1)} reduce(f32[32,1,2048]{2,1,0:T(1,128)S(1)} %all-to-all-done.4, f32[]{:T(128)} %broadcast.515), dimensions={1}, to_apply=%all_to_all.43.reduce_sub_computation | reduce | bytes 524292 | tf_op jit(solution)/shard_map/all_to_all | solution.py:251
  89.4 0.3 reshape.416
  90.2 0.6 copy-done.7
  90.8 1.0 %fusion.19 = bf16[16,32,128]{2,1,0:T(8,128)(2,1)} fusion(f32[16,32,128]{2,1,0:T(8,128)S(1)} %bitcast.167, f32[16,32,128]{2,1,0:T(8,128)S(1)} %bitcast.176, bf16[16,32,128]{1,0,2:T(8,128)(2,1)S(1)} %multiply_convert_fusion, bf16[128,128]{1,0:T(8,128)(2,1)S(1)} %copy-done.7), kind=kOutput, calls=%fused_computation.25 | convolution fusion | flops 16973824 | bytes 819200 | tf_op jit(solution)/shard_map/dot_general | solution.py:258
  (83 shorter events, 7.1 us)
Async XLA Ops:
  0.0 11.8 %copy-start = (bf16[128,512]{1,0:T(8,128)(2,1)S(1)}, bf16[128,512]{1,0:T(8,128)(2,1)}, u32[]{:S(2)}) copy-start(bf16[128,512]{1,0:T(8,128)(2,1)} %param.18) | copy-start | bytes 393220
  0.0 1.1 %copy-start.1 = (bf16[4,128,128]{2,1,0:T(8,128)(2,1)S(1)}, bf16[4,128,128]{2,1,0:T(8,128)(2,1)}, u32[]{:S(2)}) copy-start(bf16[4,128,128]{2,1,0:T(8,128)(2,1)} %param.14) | copy-start | bytes 393220
  1.4 0.7 copy-start.14
  3.1 17.6 %all-to-all-start = ((f32[32,4,4,128]{3,2,1,0:T(4,128)}), f32[32,4,4,128]{3,2,1,0:T(4,128)S(1)}, u32[]{:S(2)}, u32[]{:S(2)}) async-start(f32[32,4,4,128]{3,2,1,0:T(4,128)} %broadcast_in_dim.25), calls=%async_computation | async-start | bytes 524288 | tf_op jit(solution)/shard_map/all_to_all | solution.py:112
  10.4 0.7 copy-start.10
  12.2 0.7 copy-start.8
  22.2 0.8 copy-start.11
  23.7 0.7 copy-start.9
  26.1 16.9 %all-to-all-start.1 = ((f32[32,1,4096]{2,1,0:T(1,128)}), f32[32,1,4096]{2,1,0:T(1,128)S(1)}, u32[]{:S(2)}, u32[]{:S(2)}) async-start(f32[32,1,4096]{2,1,0:T(1,128)} %copy.164), calls=%async_computation.1 | async-start | bytes 1048576 | tf_op jit(solution)/shard_map/all_to_all | solution.py:190
  44.4 0.9 copy-start.4
  45.7 1.0 %copy-start.2 = (f32[4,128,128]{1,2,0:T(8,128)S(1)}, f32[4,128,128]{1,2,0:T(8,128)}, u32[]{:S(2)}) copy-start(f32[4,128,128]{1,2,0:T(8,128)} %get-tuple-element.5) | copy-start | bytes 786436
  46.6 0.9 %copy-start.3 = (f32[4,128,128]{1,2,0:T(8,128)S(1)}, f32[4,128,128]{1,2,0:T(8,128)}, u32[]{:S(2)}) copy-start(f32[4,128,128]{1,2,0:T(8,128)} %get-tuple-element.5) | copy-start | bytes 786436
  48.3 0.8 copy-start.12
  50.1 9.1 %all-to-all-start.2 = ((bf16[8,16,4,128]{3,2,1,0:T(4,128)(2,1)}), bf16[8,16,4,128]{3,2,1,0:T(4,128)(2,1)S(1)}, u32[]{:S(2)}, u32[]{:S(2)}) async-start(bf16[8,16,4,128]{3,2,1,0:T(4,128)(2,1)} %copy.178), calls=%async_computation.2 | async-start | bytes 262144 | tf_op jit(solution)/shard_map/all_to_all | solution.py:233
  53.8 0.8 copy-start.5
  54.6 0.8 copy-start.6
  59.3 13.2 %all-to-all-start.3 = ((bf16[128,2,128,4]{2,3,1,0:T(4,128)(2,1)}), bf16[128,2,128,4]{2,3,1,0:T(4,128)(2,1)S(1)}, u32[]{:S(2)}, u32[]{:S(2)}) async-start(bf16[128,2,128,4]{2,3,1,0:T(4,128)(2,1)} %copy.186), calls=%async_computation.3 | async-start | bytes 524288 | tf_op jit(solution)/shard_map/all_to_all | solution.py:239
  74.7 12.9 %all-to-all-start.4 = ((f32[32,1,2048]{2,1,0:T(1,128)}), f32[32,1,2048]{2,1,0:T(1,128)S(1)}, u32[]{:S(2)}, u32[]{:S(2)}) async-start(f32[32,1,2048]{2,1,0:T(1,128)} %reshape.415), calls=%async_computation.4 | async-start | bytes 524288 | tf_op jit(solution)/shard_map/all_to_all | solution.py:251
  78.5 0.8 copy-start.13
  90.1 0.8 copy-start.7

commit v4 on v3

--- a/solution.py
+++ b/solution.py
@@ -230,9 +230,15 @@
     edge_mask = tile_pairs(jnp.arange(length, dtype=jnp.int32), local_cols, tile_mask, length)
     left_all = tri_acts(normed_second, tri_left, edge_mask)
     right_all = tri_acts(normed_second, tri_right, edge_mask)
-    raw_got = lax.all_to_all(
-        second_pair.reshape(n_row, block_rows, rows_here, channels), "row", 0, 0, tiled=True
-    )
+    raw_chunks = second_pair.reshape(n_row, block_rows, rows_here, channels)
+    raw_pieces = [lax.dynamic_index_in_dim(raw_chunks, row_index, 0, keepdims=False)]
+    for shift in range(1, n_row):
+        piece = lax.dynamic_index_in_dim(raw_chunks, (row_index + shift) % n_row, 0, keepdims=False)
+        raw_pieces.append(
+            lax.ppermute(piece, "row", perm=[(r, (r + shift) % n_row) for r in range(n_row)])
+        )
+    sources = (row_index - jnp.arange(n_row, dtype=jnp.int32)) % n_row
+    raw_got = jnp.take(jnp.stack(raw_pieces, axis=0), sources, axis=0)
     own_pair = raw_got.transpose(1, 0, 2, 3).reshape(block_rows, block_cols, channels)
     channels_here = channels // device_count
     edges = jnp.stack([left_all, right_all], axis=0).transpose(3, 0, 1, 2)

time: 92.8 us -> 92.4 us (level)
  starting transfers between devices: 19.4 us -> 25.3 us
  waiting for transfers between devices: 41.1 us -> 35.5 us
    ppermute x0 -> x7, starting transfers between devices: none -> 7.53 us  [shards(): lax.ppermute(piece, 'row', perm=[(r, (r + shift) % n_row) for r in range(...]
    all_to_all x1, waiting for transfers between devices: 9.73 us -> 4.96 us  [shards(): edges_got = lax.all_to_all(edges, ('row', 'col'), 0, 3, tiled=True)]
    all_to_all x1 -> x0, starting transfers between devices: 3.65 us -> none  [shards(): lax.all_to_all(second_pair.reshape(n_row, block_rows, rows_here, channels...]
    all_to_all x1 -> x0, waiting for transfers between devices: 2.4 us -> none  [shards(): lax.all_to_all(second_pair.reshape(n_row, block_rows, rows_here, channels...]
    all_to_all x1, starting transfers between devices: 2.93 us -> 4.99 us  [shards(): edges_got = lax.all_to_all(edges, ('row', 'col'), 0, 3, tiled=True)]
    ppermute x0 -> x7, waiting for transfers between devices: none -> 1.5 us  [shards(): lax.ppermute(piece, 'row', perm=[(r, (r + shift) % n_row) for r in range(...]
    unnamed x33 -> x38, local copies, waits for them, and re-layouts: 9.47 us -> 9.18 us
  transfers between devices with their start and end apart: 5 -> 11, of which waited for: 5 -> 6; matrix products, arithmetic and copies ran while one was open for 6% -> 6% of each run, Pallas kernels for 0% -> 0%
where the time goes in v4:
time: 92.4 us; the launch traced here: 91.5 us
  waiting for transfers between devices  35.5 us (38%)
  starting transfers between devices  25.3 us (27%)
  local copies, waits for them, and re-layouts  16.2 us (18%)
  matrix products  6.7 us (7%)
  other arithmetic  6.39 us (7%)
  between operations  1.37 us (1%)
    all_to_all x1, waiting for transfers between devices, shards(): lax.all_to_all(jnp.concatenate([pair_chunks, bias_chunks], axis=1), ('row...  14 us
    unnamed x38, local copies, waits for them, and re-layouts  9.18 us
    all_to_all x1, waiting for transfers between devices, shards(): product_got = lax.all_to_all(product_sent, ('row', 'col'), 0, 1, tiled=True)  8.16 us
    ppermute x7, starting transfers between devices, shards(): lax.ppermute(piece, 'row', perm=[(r, (r + shift) % n_row) for r in range(...  7.53 us
    all_to_all x1, starting transfers between devices, gather_lines(): got = lax.all_to_all(sent, ('row', 'col'), 0, 0, tiled=True)  7.33 us
    all_to_all x1, waiting for transfers between devices, gather_lines(): got = lax.all_to_all(sent, ('row', 'col'), 0, 0, tiled=True)  6.88 us
    all_to_all x1, starting transfers between devices, shards(): edges_got = lax.all_to_all(edges, ('row', 'col'), 0, 3, tiled=True)  4.99 us
    all_to_all x1, waiting for transfers between devices, shards(): edges_got = lax.all_to_all(edges, ('row', 'col'), 0, 3, tiled=True)  4.96 us
  transfers between devices with their start and end apart: 11, of which 6 were waited for; matrix products, arithmetic and copies ran while one was open for 6% of the time, Pallas kernels for 0%

profile of v4, /device:TPU:0, one launch (start us, length us, event | category | flops | bytes accessed | tf_op | source)
XLA Modules:
  0.0 91.5 jit_solution(16894540452129866986)
XLA Ops:
  0.0 1.1 %convert_reduce_fusion = f32[4,128]{1,0:T(4,128)S(1)} fusion(bf16[4,128,128]{2,1,0:T(8,128)(2,1)} %param.14), kind=kLoop, calls=%fused_computation.43 | loop fusion | flops 130560 | bytes 133120 | tf_op jit(solution)/shard_map/reduce_sum | solution.py:9
  1.4 0.7 copy-done.13
  2.4 0.7 broadcast_in_dim.33
  3.1 7.3 %all-to-all-start = ((f32[32,4,4,128]{3,2,1,0:T(4,128)}), f32[32,4,4,128]{3,2,1,0:T(4,128)S(1)}, u32[]{:S(2)}, u32[]{:S(2)}) async-start(f32[32,4,4,128]{3,2,1,0:T(4,128)} %broadcast_in_dim.33), calls=%async_computation | async-start | bytes 524288 | tf_op jit(solution)/shard_map/all_to_all | solution.py:112
  10.4 0.7 copy-done.9
  11.8 0.4 fusion.58
  12.5 0.4 copy-done.7
  13.0 0.8 broadcast_multiply_fusion
  13.8 6.9 %all-to-all-done = f32[32,4,4,128]{3,2,1,0:T(4,128)S(1)} async-done(((f32[32,4,4,128]{3,2,1,0:T(4,128)}), f32[32,4,4,128]{3,2,1,0:T(4,128)S(1)}, u32[]{:S(2)}, u32[]{:S(2)}) %all-to-all-start) | async-done | bytes 262176 | tf_op jit(solution)/shard_map/all_to_all | solution.py:112
  20.8 0.6 fusion.98
  21.4 0.4 fusion.8
  21.8 0.3 fusion.21
  22.3 0.6 copy-done.10
  23.7 0.7 copy-done.8
  24.8 1.3 %copy.167 = f32[32,1,4096]{2,1,0:T(1,128)} copy(f32[32,1,4096]{2,0,1:T(8,128)S(1)} %maximum_bitcast_fusion) | data formatting | bytes 1048576 | tf_op jit(solution)/shard_map/all_to_all | solution.py:190
  26.1 2.7 %all-to-all-start.1 = ((f32[32,1,4096]{2,1,0:T(1,128)}), f32[32,1,4096]{2,1,0:T(1,128)S(1)}, u32[]{:S(2)}, u32[]{:S(2)}) async-start(f32[32,1,4096]{2,1,0:T(1,128)} %copy.167), calls=%async_computation.1 | async-start | bytes 1048576 | tf_op jit(solution)/shard_map/all_to_all | solution.py:190
  29.0 14.0 %all-to-all-done.1 = f32[32,1,4096]{2,1,0:T(1,128)S(1)} async-done(((f32[32,1,4096]{2,1,0:T(1,128)}), f32[32,1,4096]{2,1,0:T(1,128)S(1)}, u32[]{:S(2)}, u32[]{:S(2)}) %all-to-all-start.1) | async-done | bytes 524320 | tf_op jit(solution)/shard_map/all_to_all | solution.py:190
  44.0 0.4 multiply_reduce_fusion.2
  44.4 0.3 multiply_convert_fusion.2
  44.7 0.6 copy-done.3
  45.9 0.7 copy-done.2
  46.6 0.6 fusion.100
  47.2 0.4 fusion.11
  47.6 0.3 fusion.22
  48.1 0.6 copy-done.11
  49.1 1.3 %collective-permute-start = (bf16[16,4,128]{2,0,1:T(8,128)(2,1)S(1)}, bf16[16,4,128]{2,0,1:T(8,128)(2,1)S(1)}, u32[]{:S(2)}, u32[]{:S(2)}) collective-permute-start(bf16[16,4,128]{2,0,1:T(8,128)(2,1)S(1)} %get-tuple-element.11), channel_id=1, source_target_pairs={{0,4},{4,8},{8,12},{12,16},{16,20},{20,24},{24,28},{28,0},{1,5},{5... | collective-permute-start | bytes 49160 | tf_op jit(solution)/shard_map/ppermute | solution.py:238
  50.4 1.5 %collective-permute-start.1 = (bf16[16,4,128]{2,0,1:T(8,128)(2,1)S(1)}, bf16[16,4,128]{2,0,1:T(8,128)(2,1)S(1)}, u32[]{:S(2)}, u32[]{:S(2)}) collective-permute-start(bf16[16,4,128]{2,0,1:T(8,128)(2,1)S(1)} %get-tuple-element.10), channel_id=1, source_target_pairs={{0,8},{4,12},{8,16},{12,20},{16,24},{20,28},{24,0},{28,4},{1,9},{5... | collective-permute-start | bytes 49160 | tf_op jit(solution)/shard_map/ppermute | solution.py:238
  51.9 0.9 %collective-permute-start.2 = (bf16[16,4,128]{2,0,1:T(8,128)(2,1)S(1)}, bf16[16,4,128]{2,0,1:T(8,128)(2,1)S(1)}, u32[]{:S(2)}, u32[]{:S(2)}) collective-permute-start(bf16[16,4,128]{2,0,1:T(8,128)(2,1)S(1)} %get-tuple-element.9), channel_id=1, source_target_pairs={{0,12},{4,16},{8,20},{12,24},{16,28},{20,0},{24,4},{28,8},{1,13},{... | collective-permute-start | bytes 49160 | tf_op jit(solution)/shard_map/ppermute | solution.py:238
  52.8 0.7 collective-permute-start.3
  53.5 0.4 collective-permute-start.4
  54.1 0.6 copy-done.4
  55.1 0.5 copy-done.5
  56.1 0.9 copy.189
  57.0 5.0 %all-to-all-start.2 = ((bf16[128,2,128,4]{2,3,1,0:T(4,128)(2,1)}), bf16[128,2,128,4]{2,3,1,0:T(4,128)(2,1)S(1)}, u32[]{:S(2)}, u32[]{:S(2)}) async-start(bf16[128,2,128,4]{2,3,1,0:T(4,128)(2,1)} %copy.189), calls=%async_computation.2 | async-start | bytes 524288 | tf_op jit(solution)/shard_map/all_to_all | solution.py:245
  62.0 2.7 %collective-permute-start.5 = (bf16[16,4,128]{2,0,1:T(8,128)(2,1)S(1)}, bf16[16,4,128]{2,0,1:T(8,128)(2,1)S(1)}, u32[]{:S(2)}, u32[]{:S(2)}) collective-permute-start(bf16[16,4,128]{2,0,1:T(8,128)(2,1)S(1)} %get-tuple-element.6), channel_id=1, source_target_pairs={{0,24},{4,28},{8,0},{12,4},{16,8},{20,12},{24,16},{28,20},{1,25},{... | collective-permute-start | bytes 49160 | tf_op jit(solution)/shard_map/ppermute | solution.py:238
  64.8 1.3 %collective-permute-done.5 = bf16[16,4,128]{2,0,1:T(8,128)(2,1)S(1)} collective-permute-done((bf16[16,4,128]{2,0,1:T(8,128)(2,1)S(1)}, bf16[16,4,128]{2,0,1:T(8,128)(2,1)S(1)}, u32[]{:S(2)}, u32[]{:S(2)}) %collective-permute-start.5) | collective-permute-done | bytes 16416 | tf_op jit(solution)/shard_map/ppermute | solution.py:238
  66.3 0.6 gather_fusion
  67.2 5.0 %all-to-all-done.2 = bf16[128,2,128,4]{2,3,1,0:T(4,128)(2,1)S(1)} async-done(((bf16[128,2,128,4]{2,3,1,0:T(4,128)(2,1)}), bf16[128,2,128,4]{2,3,1,0:T(4,128)(2,1)S(1)}, u32[]{:S(2)}, u32[]{:S(2)}) %all-to-all-start.2) | async-done | bytes 262176 | tf_op jit(solution)/shard_map/all_to_all | solution.py:245
  72.7 0.4 reshape.451
  73.3 1.2 %reshape.477 = f32[32,1,2048]{2,1,0:T(1,128)} reshape(f32[32,4,16,32]{3,2,1,0:T(8,128)S(1)} %bitcast.187) | data formatting | bytes 524288
  74.4 2.8 %all-to-all-start.3 = ((f32[32,1,2048]{2,1,0:T(1,128)}), f32[32,1,2048]{2,1,0:T(1,128)S(1)}, u32[]{:S(2)}, u32[]{:S(2)}) async-start(f32[32,1,2048]{2,1,0:T(1,128)} %reshape.477), calls=%async_computation.3 | async-start | bytes 524288 | tf_op jit(solution)/shard_map/all_to_all | solution.py:257
  78.2 0.6 copy-done.12
  79.2 8.2 %all-to-all-done.3 = f32[32,1,2048]{2,1,0:T(1,128)S(1)} async-done(((f32[32,1,2048]{2,1,0:T(1,128)}), f32[32,1,2048]{2,1,0:T(1,128)S(1)}, u32[]{:S(2)}, u32[]{:S(2)}) %all-to-all-start.3) | async-done | bytes 262176 | tf_op jit(solution)/shard_map/all_to_all | solution.py:257
  87.3 0.5 broadcast.641
  87.8 1.3 %reduce.2 = f32[32,2048]{1,0:T(8,128)S(1)} reduce(f32[32,1,2048]{2,1,0:T(1,128)S(1)} %all-to-all-done.3, f32[]{:T(128)} %broadcast.641), dimensions={1}, to_apply=%all_to_all.39.reduce_sub_computation | reduce | bytes 524292 | tf_op jit(solution)/shard_map/all_to_all | solution.py:257
  89.1 0.3 reshape.478
  89.9 0.6 copy-done.6
  90.6 1.0 %fusion.19 = bf16[16,32,128]{2,1,0:T(8,128)(2,1)} fusion(f32[16,32,128]{2,1,0:T(8,128)S(1)} %bitcast.200, f32[16,32,128]{2,1,0:T(8,128)S(1)} %bitcast.209, bf16[16,32,128]{1,0,2:T(8,128)(2,1)S(1)} %multiply_convert_fusion, bf16[128,128]{1,0:T(8,128)(2,1)S(1)} %copy-done.6), kind=kOutput, calls=%fused_computation.26 | convolution fusion | flops 16973824 | bytes 819200 | tf_op jit(solution)/shard_map/dot_general | solution.py:264
  (103 shorter events, 8.4 us)
Async XLA Ops:
  0.0 11.8 %copy-start = (bf16[128,512]{1,0:T(8,128)(2,1)S(1)}, bf16[128,512]{1,0:T(8,128)(2,1)}, u32[]{:S(2)}) copy-start(bf16[128,512]{1,0:T(8,128)(2,1)} %param.18) | copy-start | bytes 393220
  0.0 1.1 %copy-start.1 = (bf16[4,128,128]{2,1,0:T(8,128)(2,1)S(1)}, bf16[4,128,128]{2,1,0:T(8,128)(2,1)}, u32[]{:S(2)}) copy-start(bf16[4,128,128]{2,1,0:T(8,128)(2,1)} %param.14) | copy-start | bytes 393220
  1.4 0.7 copy-start.13
  3.1 17.6 %all-to-all-start = ((f32[32,4,4,128]{3,2,1,0:T(4,128)}), f32[32,4,4,128]{3,2,1,0:T(4,128)S(1)}, u32[]{:S(2)}, u32[]{:S(2)}) async-start(f32[32,4,4,128]{3,2,1,0:T(4,128)} %broadcast_in_dim.33), calls=%async_computation | async-start | bytes 524288 | tf_op jit(solution)/shard_map/all_to_all | solution.py:112
  10.4 0.7 copy-start.9
  12.2 0.7 copy-start.7
  22.2 0.8 copy-start.10
  23.7 0.7 copy-start.8
  26.1 16.9 %all-to-all-start.1 = ((f32[32,1,4096]{2,1,0:T(1,128)}), f32[32,1,4096]{2,1,0:T(1,128)S(1)}, u32[]{:S(2)}, u32[]{:S(2)}) async-start(f32[32,1,4096]{2,1,0:T(1,128)} %copy.167), calls=%async_computation.1 | async-start | bytes 1048576 | tf_op jit(solution)/shard_map/all_to_all | solution.py:190
  44.4 0.9 copy-start.3
  45.7 1.0 %copy-start.2 = (f32[4,128,128]{1,2,0:T(8,128)S(1)}, f32[4,128,128]{1,2,0:T(8,128)}, u32[]{:S(2)}) copy-start(f32[4,128,128]{1,2,0:T(8,128)} %get-tuple-element.12) | copy-start | bytes 786436
  48.0 0.8 copy-start.11
  49.1 12.9 %collective-permute-start = (bf16[16,4,128]{2,0,1:T(8,128)(2,1)S(1)}, bf16[16,4,128]{2,0,1:T(8,128)(2,1)S(1)}, u32[]{:S(2)}, u32[]{:S(2)}) collective-permute-start(bf16[16,4,128]{2,0,1:T(8,128)(2,1)S(1)} %get-tuple-element.11), channel_id=1, source_target_pairs={{0,4},{4,8},{8,12},{12,16},{16,20},{20,24},{24,28},{28,0},{1,5},{5... | collective-permute-start | bytes 49160 | tf_op jit(solution)/shard_map/ppermute | solution.py:238
  50.4 14.3 %collective-permute-start.1 = (bf16[16,4,128]{2,0,1:T(8,128)(2,1)S(1)}, bf16[16,4,128]{2,0,1:T(8,128)(2,1)S(1)}, u32[]{:S(2)}, u32[]{:S(2)}) collective-permute-start(bf16[16,4,128]{2,0,1:T(8,128)(2,1)S(1)} %get-tuple-element.10), channel_id=1, source_target_pairs={{0,8},{4,12},{8,16},{12,20},{16,24},{20,28},{24,0},{28,4},{1,9},{5... | collective-permute-start | bytes 49160 | tf_op jit(solution)/shard_map/ppermute | solution.py:238
  51.9 12.9 %collective-permute-start.2 = (bf16[16,4,128]{2,0,1:T(8,128)(2,1)S(1)}, bf16[16,4,128]{2,0,1:T(8,128)(2,1)S(1)}, u32[]{:S(2)}, u32[]{:S(2)}) collective-permute-start(bf16[16,4,128]{2,0,1:T(8,128)(2,1)S(1)} %get-tuple-element.9), channel_id=1, source_target_pairs={{0,12},{4,16},{8,20},{12,24},{16,28},{20,0},{24,4},{28,8},{1,13},{... | collective-permute-start | bytes 49160 | tf_op jit(solution)/shard_map/ppermute | solution.py:238
  52.8 12.0 %collective-permute-start.3 = (bf16[16,4,128]{2,0,1:T(8,128)(2,1)S(1)}, bf16[16,4,128]{2,0,1:T(8,128)(2,1)S(1)}, u32[]{:S(2)}, u32[]{:S(2)}) collective-permute-start(bf16[16,4,128]{2,0,1:T(8,128)(2,1)S(1)} %get-tuple-element.8), channel_id=1, source_target_pairs={{0,16},{4,20},{8,24},{12,28},{16,0},{20,4},{24,8},{28,12},{1,17},{... | collective-permute-start | bytes 49160 | tf_op jit(solution)/shard_map/ppermute | solution.py:238
  53.5 11.3 %collective-permute-start.4 = (bf16[16,4,128]{2,0,1:T(8,128)(2,1)S(1)}, bf16[16,4,128]{2,0,1:T(8,128)(2,1)S(1)}, u32[]{:S(2)}, u32[]{:S(2)}) collective-permute-start(bf16[16,4,128]{2,0,1:T(8,128)(2,1)S(1)} %get-tuple-element.7), channel_id=1, source_target_pairs={{0,20},{4,24},{8,28},{12,0},{16,4},{20,8},{24,12},{28,16},{1,21},{... | collective-permute-start | bytes 49160 | tf_op jit(solution)/shard_map/ppermute | solution.py:238
  53.9 0.8 copy-start.4
  54.7 0.8 copy-start.5
  57.0 15.2 %all-to-all-start.2 = ((bf16[128,2,128,4]{2,3,1,0:T(4,128)(2,1)}), bf16[128,2,128,4]{2,3,1,0:T(4,128)(2,1)S(1)}, u32[]{:S(2)}, u32[]{:S(2)}) async-start(bf16[128,2,128,4]{2,3,1,0:T(4,128)(2,1)} %copy.189), calls=%async_computation.2 | async-start | bytes 524288 | tf_op jit(solution)/shard_map/all_to_all | solution.py:245
  62.0 4.2 %collective-permute-start.5 = (bf16[16,4,128]{2,0,1:T(8,128)(2,1)S(1)}, bf16[16,4,128]{2,0,1:T(8,128)(2,1)S(1)}, u32[]{:S(2)}, u32[]{:S(2)}) collective-permute-start(bf16[16,4,128]{2,0,1:T(8,128)(2,1)S(1)} %get-tuple-element.6), channel_id=1, source_target_pairs={{0,24},{4,28},{8,0},{12,4},{16,8},{20,12},{24,16},{28,20},{1,25},{... | collective-permute-start | bytes 49160 | tf_op jit(solution)/shard_map/ppermute | solution.py:238
  64.7 1.6 %collective-permute-start.6 = (bf16[16,4,128]{2,0,1:T(8,128)(2,1)S(1)}, bf16[16,4,128]{2,0,1:T(8,128)(2,1)S(1)}, u32[]{:S(2)}, u32[]{:S(2)}) collective-permute-start(bf16[16,4,128]{2,0,1:T(8,128)(2,1)S(1)} %get-tuple-element.5), channel_id=1, source_target_pairs={{0,28},{4,0},{8,4},{12,8},{16,12},{20,16},{24,20},{28,24},{1,29},{... | collective-permute-start | bytes 49160 | tf_op jit(solution)/shard_map/ppermute | solution.py:238
  74.4 12.9 %all-to-all-start.3 = ((f32[32,1,2048]{2,1,0:T(1,128)}), f32[32,1,2048]{2,1,0:T(1,128)S(1)}, u32[]{:S(2)}, u32[]{:S(2)}) async-start(f32[32,1,2048]{2,1,0:T(1,128)} %reshape.477), calls=%async_computation.3 | async-start | bytes 524288 | tf_op jit(solution)/shard_map/all_to_all | solution.py:257
  78.1 0.8 copy-start.12
  89.8 0.8 copy-start.6

commit v5 on v3

--- a/solution.py
+++ b/solution.py
@@ -8,6 +8,13 @@
     values = values.astype(jnp.float32)
     center = values - jnp.mean(values, axis=-1, keepdims=True)
     spread = jnp.mean(center * center, axis=-1, keepdims=True)
+    return center * lax.rsqrt(spread + 1e-05)
+
+
+def layer_norm_lead(values):
+    values = values.astype(jnp.float32)
+    center = values - jnp.mean(values, axis=0, keepdims=True)
+    spread = jnp.mean(center * center, axis=0, keepdims=True)
     return center * lax.rsqrt(spread + 1e-05)
 
 
@@ -230,12 +237,8 @@
     edge_mask = tile_pairs(jnp.arange(length, dtype=jnp.int32), local_cols, tile_mask, length)
     left_all = tri_acts(normed_second, tri_left, edge_mask)
     right_all = tri_acts(normed_second, tri_right, edge_mask)
-    raw_got = lax.all_to_all(
-        second_pair.reshape(n_row, block_rows, rows_here, channels), "row", 0, 0, tiled=True
-    )
-    own_pair = raw_got.transpose(1, 0, 2, 3).reshape(block_rows, block_cols, channels)
     channels_here = channels // device_count
-    edges = jnp.stack([left_all, right_all], axis=0).transpose(3, 0, 1, 2)
+    edges = jnp.stack([left_all, right_all, second_pair], axis=0).transpose(3, 0, 1, 2)
     edges_got = lax.all_to_all(edges, ("row", "col"), 0, 3, tiled=True)
     product_part = jnp.einsum(
         "cik,cjk->cij",
@@ -243,22 +246,32 @@
         edges_got[:, 1],
         preferred_element_type=jnp.float32,
     )
-    product_sent = (
-        product_part.reshape(channels_here, n_row, block_rows, n_col, block_cols)
-        .transpose(1, 3, 0, 2, 4)
-        .reshape(device_count, channels_here, block_rows, block_cols)
-    )
-    product_got = lax.all_to_all(product_sent, ("row", "col"), 0, 1, tiled=True)
-    product_sum = product_got.reshape(channels, block_rows, block_cols).transpose(1, 2, 0)
-    normed_own = layer_norm(own_pair).astype(jnp.bfloat16)
+    raw_part = (
+        edges_got[:, 2]
+        .reshape(channels_here, length, n_row, n_col, rows_here)
+        .transpose(0, 1, 3, 2, 4)
+        .reshape(channels_here, length, length)
+        .astype(jnp.float32)
+    )
+    back = jnp.stack([product_part, raw_part], axis=0)
+    back_sent = (
+        back.reshape(2, channels_here, n_row, block_rows, n_col, block_cols)
+        .transpose(2, 4, 0, 1, 3, 5)
+        .reshape(device_count, 2 * channels_here, block_rows * block_cols)
+    )
+    back_got = lax.all_to_all(back_sent, ("row", "col"), 0, 1, tiled=True).reshape(
+        device_count, 2, channels_here, block_rows * block_cols
+    )
+    product_sum = back_got[:, 0].reshape(channels, block_rows * block_cols)
+    own_pair = back_got[:, 1].reshape(channels, block_rows * block_cols).astype(jnp.bfloat16)
+    normed_own = layer_norm_lead(own_pair).astype(jnp.bfloat16)
     gate_values = jax.nn.sigmoid(
-        jnp.dot(normed_own.reshape(-1, channels), tri_gate, preferred_element_type=jnp.float32)
-    ).reshape(block_rows, block_cols, channels)
-    centered = layer_norm(product_sum).astype(jnp.bfloat16)
-    update_tri = jnp.dot(
-        centered.reshape(-1, channels), tri_output, preferred_element_type=jnp.float32
-    ).reshape(block_rows, block_cols, channels)
-    return (own_pair.astype(jnp.float32) + gate_values * update_tri).astype(jnp.bfloat16)
+        jnp.einsum("cn,cd->nd", normed_own, tri_gate, preferred_element_type=jnp.float32)
+    )
+    centered = layer_norm_lead(product_sum).astype(jnp.bfloat16)
+    update_tri = jnp.einsum("cn,cd->nd", centered, tri_output, preferred_element_type=jnp.float32)
+    result = own_pair.T.astype(jnp.float32) + gate_values * update_tri
+    return result.astype(jnp.bfloat16).reshape(block_rows, block_cols, channels)
 
 
 def solution(mesh):

time: 92.8 us -> 98.1 us (1.057)
  blocking collectives: 0 us -> 33.7 us
  waiting for transfers between devices: 41.1 us -> 21.2 us
  starting transfers between devices: 19.4 us -> 9.98 us
  local copies, waits for them, and re-layouts: 17 us -> 14.1 us
  other arithmetic: 6.39 us -> 8.34 us
  matrix products: 6.7 us -> 8.39 us
    all_to_all x0 -> x2, blocking collectives: none -> 33.7 us  [the longest x1 17.9 us: shards(): lax.all_to_all(back_sent, ('row', 'col'), 0, 1, tiled=True)]
    all_to_all x3 -> x0, waiting for transfers between devices: 20.1 us -> none  [the longest x1 9.73 us: shards(): edges_got = lax.all_to_all(edges, ('row', 'col'), 0, 3, tiled=True)]
    all_to_all x3 -> x0, starting transfers between devices: 9.42 us -> none  [the longest x1 3.65 us: shards(): lax.all_to_all(second_pair.reshape(n_row, block_rows, rows_here, channels...]
    unnamed x33 -> x23, local copies, waits for them, and re-layouts: 9.47 us -> 1.01 us
    transpose x1 -> x2, other arithmetic: 0.03 us -> 3.94 us  [the longest x1 3.9 us: shards(): back_sent = back.reshape(2, channels_here, n_row, block_rows, n_col, bloc...]
    convert_element_type x1 -> x5, local copies, waits for them, and re-layouts: 0.06 us -> 2.44 us  [the longest x2 2.05 us: shards(): raw_part = edges_got[:, 2].reshape(channels_here, length, n_row, n_col, r...]
    transpose x1 -> x2, local copies, waits for them, and re-layouts: 0.87 us -> 3.06 us  [the longest x1 2.84 us: shards(): back_sent = back.reshape(2, channels_here, n_row, block_rows, n_col, bloc...]
    another operation x0 -> x3, local copies, waits for them, and re-layouts: none -> 1.44 us  [the longest x2 1.35 us: shards(): back = jnp.stack([product_part, raw_part], axis=0)]
  transfers between devices with their start and end apart: 5 -> 2, of which waited for: 5 -> 2; matrix products, arithmetic and copies ran while one was open for 6% -> 3% of each run, Pallas kernels for 0% -> 0%
where the time goes in v5:
time: 98.1 us; the launch traced here: 96.8 us
  blocking collectives  33.7 us (34%)
  waiting for transfers between devices  21.2 us (22%)
  local copies, waits for them, and re-layouts  14.1 us (14%)
  starting transfers between devices  9.98 us (10%)
  matrix products  8.39 us (9%)
  other arithmetic  8.34 us (9%)
  between operations  1.19 us (1%)
    all_to_all x1, blocking collectives, shards(): lax.all_to_all(back_sent, ('row', 'col'), 0, 1, tiled=True)  17.9 us
    all_to_all x1, blocking collectives, shards(): edges_got = lax.all_to_all(edges, ('row', 'col'), 0, 3, tiled=True)  15.8 us
    all_to_all x1, waiting for transfers between devices, shards(): lax.all_to_all(jnp.concatenate([pair_chunks, bias_chunks], axis=1), ('row...  14.1 us
    all_to_all x1, starting transfers between devices, gather_lines(): got = lax.all_to_all(sent, ('row', 'col'), 0, 0, tiled=True)  7.33 us
    all_to_all x1, waiting for transfers between devices, gather_lines(): got = lax.all_to_all(sent, ('row', 'col'), 0, 0, tiled=True)  7.01 us
    transpose x1, other arithmetic, shards(): back_sent = back.reshape(2, channels_here, n_row, block_rows, n_col, bloc...  3.9 us
    transpose x1, local copies, waits for them, and re-layouts, shards(): back_sent = back.reshape(2, channels_here, n_row, block_rows, n_col, bloc...  2.84 us
    all_to_all x1, starting transfers between devices, shards(): lax.all_to_all(jnp.concatenate([pair_chunks, bias_chunks], axis=1), ('row...  2.66 us
  transfers between devices with their start and end apart: 2, of which 2 were waited for; matrix products, arithmetic and copies ran while one was open for 3% of the time, Pallas kernels for 0%

profile of v5, /device:TPU:0, one launch (start us, length us, event | category | flops | bytes accessed | tf_op | source)
XLA Modules:
  0.0 96.8 jit_solution(15606777032999133771)
XLA Ops:
  0.0 1.1 %convert_reduce_fusion = f32[4,128]{1,0:T(4,128)S(1)} fusion(bf16[4,128,128]{2,1,0:T(8,128)(2,1)} %param.14), kind=kLoop, calls=%fused_computation.39 | loop fusion | flops 130560 | bytes 133120 | tf_op jit(solution)/shard_map/reduce_sum | solution.py:9
  1.1 1.1 %fusion.26 = f32[4,128]{1,0:T(4,128)S(1)} fusion(bf16[4,128,128]{2,1,0:T(8,128)(2,1)} %param.14, f32[4,128]{1,0:T(4,128)S(1)} %broadcast_multiply_fusion.8), kind=kLoop, calls=%fused_computation.46 | loop fusion | flops 261632 | bytes 135168 | tf_op jit(solution)/shard_map/reduce_sum | solution.py:10
  2.2 1.2 %convolution_bitcast_fusion.1 = f32[4,4,128]{2,0,1:T(4,128)S(1)} fusion(bf16[4,128,128]{2,1,0:T(8,128)(2,1)} %param.14, f32[4,128]{1,0:T(4,128)S(1)} %add_rsqrt_fusion.5, f32[4,128]{1,0:T(4,128)S(1)} %broadcast_multiply_fusion.8, bf16[128,4]{0,1:T(4,128)(2,1)} %param.19), kind=kOutput, calls=%fused_computation.28 | convolution fusion | flops 786432 | bytes 144384 | tf_op jit(solution)/shard_map/dot_general | solution.py:155
  3.5 0.7 broadcast_in_dim.25
  4.2 7.3 %all-to-all-start = ((f32[32,4,4,128]{3,2,1,0:T(4,128)}), f32[32,4,4,128]{3,2,1,0:T(4,128)S(1)}, u32[]{:S(2)}, u32[]{:S(2)}) async-start(f32[32,4,4,128]{3,2,1,0:T(4,128)} %broadcast_in_dim.25), calls=%async_computation | async-start | bytes 524288 | tf_op jit(solution)/shard_map/all_to_all | solution.py:119
  12.2 0.8 slice_bitcast_fusion.24
  13.0 1.3 %fusion.57 = f32[4,128,512]{2,1,0:T(8,128)S(1)} fusion(bf16[128,512]{1,0:T(8,128)(2,1)S(1)} %copy-done, bf16[4,128,128]{2,1,0:T(8,128)(2,1)} %param.14, f32[4,128]{1,0:T(4,128)S(1)} %add_rsqrt_fusion.5, f32[4,128]{1,0:T(4,128)S(1)} %broadcast_multiply_fusion.8), kind=kOutput, calls=%fused_computation.101 | convolution fusion | flops 67371008 | bytes 1314816 | tf_op jit(solution)/shard_map/dot_general | solution.py:158
  14.3 0.2 copy.171
  14.7 7.0 %all-to-all-done = f32[32,4,4,128]{3,2,1,0:T(4,128)S(1)} async-done(((f32[32,4,4,128]{3,2,1,0:T(4,128)}), f32[32,4,4,128]{3,2,1,0:T(4,128)S(1)}, u32[]{:S(2)}, u32[]{:S(2)}) %all-to-all-start) | async-done | bytes 262176 | tf_op jit(solution)/shard_map/all_to_all | solution.py:119
  21.9 0.6 fusion.94
  22.5 0.4 fusion.8
  23.0 0.3 fusion.20
  23.5 0.4 copy-done.1
  23.9 0.3 fusion.95
  24.2 0.2 multiply_reduce_fusion.3
  24.4 0.3 convolution_bitcast_fusion
  25.0 1.3 %copy.182 = f32[32,1,4096]{2,1,0:T(1,128)} copy(f32[32,1,4096]{2,0,1:T(8,128)S(1)} %maximum_bitcast_fusion.1) | data formatting | bytes 1048576 | tf_op jit(solution)/shard_map/all_to_all | solution.py:197
  26.3 2.7 %all-to-all-start.1 = ((f32[32,1,4096]{2,1,0:T(1,128)}), f32[32,1,4096]{2,1,0:T(1,128)S(1)}, u32[]{:S(2)}, u32[]{:S(2)}) async-start(f32[32,1,4096]{2,1,0:T(1,128)} %copy.182), calls=%async_computation.1 | async-start | bytes 1048576 | tf_op jit(solution)/shard_map/all_to_all | solution.py:197
  29.1 14.1 %all-to-all-done.1 = f32[32,1,4096]{2,1,0:T(1,128)S(1)} async-done(((f32[32,1,4096]{2,1,0:T(1,128)}), f32[32,1,4096]{2,1,0:T(1,128)S(1)}, u32[]{:S(2)}, u32[]{:S(2)}) %all-to-all-start.1) | async-done | bytes 524320 | tf_op jit(solution)/shard_map/all_to_all | solution.py:197
  43.2 0.3 copy.231
  43.6 0.2 reshape.396
  44.0 0.2 reduce_sum.131
  44.3 0.4 multiply_reduce_fusion.2
  44.6 0.3 multiply_convert_fusion.2
  45.0 0.3 fusion.55
  45.4 0.2 copy.188
  45.6 0.6 fusion.96
  46.2 0.4 fusion.11
  46.6 0.3 fusion.21
  47.1 0.3 copy-done.9
  47.4 0.3 convert_reduce_fusion.1
  47.7 0.2 fusion.28
  47.9 0.3 fusion.70
  48.3 0.3 fusion.72
  48.8 0.2 copy.198
  49.0 15.8 %all_to_all.44 = bf16[128,3,128,4]{2,3,1,0:T(4,128)(2,1)S(1)} all-to-all(bf16[128,3,128,4]{2,3,1,0:T(4,128)(2,1)S(1)} %copy.198), channel_id=1, replica_groups=mesh['row'=8,'col'=4] {'row','col'}, dimensions={0} | all-to-all | bytes 786432 | tf_op jit(solution)/shard_map/all_to_all | solution.py:242
  64.9 0.3 copy.200
  65.3 0.2 fusion.54
  65.6 0.4 stack.23
  66.0 0.9 copy.204
  67.0 2.0 %reshape.397 = f32[1,4,8,16,4,32]{3,2,5,4,1,0:T(8,128)} reshape(f32[4,128,4,8,4]{1,4,3,2,0:T(4,128)S(1)} %copy.203) | data formatting | bytes 524288 | tf_op jit(solution)/shard_map/convert_element_type | solution.py:254
  69.0 3.9 %maximum_bitcast_fusion = f32[8,4,2,4,16,32]{4,0,5,1,3,2:T(8,128)} fusion(f32[1,4,8,16,4,32]{3,2,5,4,1,0:T(8,128)} %reshape.397, f32[1,4,8,16,4,32]{3,2,5,4,1,0:T(8,128)S(1)} %copy.204), kind=kLoop, calls=%fused_computation.2 | loop fusion | flops 131072 | bytes 1048576 | tf_op jit(solution)/shard_map/transpose | solution.py:259
  72.9 2.8 %copy.205 = f32[8,4,2,4,16,32]{5,4,3,2,1,0:T(8,128)S(1)} copy(f32[8,4,2,4,16,32]{4,0,5,1,3,2:T(8,128)} %maximum_bitcast_fusion) | data formatting | bytes 1048576 | tf_op jit(solution)/shard_map/transpose | solution.py:259
  75.7 0.8 reshape.392
  76.5 17.9 %all_to_all.45 = f32[32,8,512]{2,1,0:T(8,128)S(1)} all-to-all(f32[32,8,512]{2,1,0:T(8,128)S(1)} %reshape.392), channel_id=1, replica_groups=mesh['row'=8,'col'=4] {'row','col'}, dimensions={0} | all-to-all | bytes 1048576 | tf_op jit(solution)/shard_map/all_to_all | solution.py:262
  94.4 0.3 copy.206
  95.6 0.3 fusion.15
  95.9 0.9 fusion.19
  (68 shorter events, 2.6 us)
Async XLA Ops:
  0.0 12.9 %copy-start = (bf16[128,512]{1,0:T(8,128)(2,1)S(1)}, bf16[128,512]{1,0:T(8,128)(2,1)}, u32[]{:S(2)}) copy-start(bf16[128,512]{1,0:T(8,128)(2,1)} %param.18) | copy-start | bytes 393220
  0.0 14.5 %copy-start.6 = (s32[128]{0:T(128)S(1)}, s32[128]{0:T(128)}, u32[]{:S(2)}) copy-start(s32[128]{0:T(128)} %param.16) | copy-start | bytes 1540
  4.2 17.6 %all-to-all-start = ((f32[32,4,4,128]{3,2,1,0:T(4,128)}), f32[32,4,4,128]{3,2,1,0:T(4,128)S(1)}, u32[]{:S(2)}, u32[]{:S(2)}) async-start(f32[32,4,4,128]{3,2,1,0:T(4,128)} %broadcast_in_dim.25), calls=%async_computation | async-start | bytes 524288 | tf_op jit(solution)/shard_map/all_to_all | solution.py:119
  23.0 0.9 copy-start.1
  23.0 0.9 copy-start.8
  23.3 1.1 %copy-start.7 = (bf16[128,4]{0,1:T(4,128)(2,1)S(1)}, bf16[128,4]{0,1:T(4,128)(2,1)}, u32[]{:S(2)}) copy-start(bf16[128,4]{0,1:T(4,128)(2,1)} %param.22) | copy-start | bytes 3076
  26.3 16.9 %all-to-all-start.1 = ((f32[32,1,4096]{2,1,0:T(1,128)}), f32[32,1,4096]{2,1,0:T(1,128)S(1)}, u32[]{:S(2)}, u32[]{:S(2)}) async-start(f32[32,1,4096]{2,1,0:T(1,128)} %copy.182), calls=%async_computation.1 | async-start | bytes 1048576 | tf_op jit(solution)/shard_map/all_to_all | solution.py:197
  43.5 1.4 %copy-start.2 = (bf16[128,512]{1,0:T(8,128)(2,1)S(1)}, bf16[128,512]{1,0:T(8,128)(2,1)}, u32[]{:S(2)}) copy-start(bf16[128,512]{1,0:T(8,128)(2,1)} %param.21) | copy-start | bytes 393220
  46.6 0.8 copy-start.9
  46.9 1.0 %copy-start.3 = (bf16[128,256]{1,0:T(8,128)(2,1)S(1)}, bf16[128,256]{1,0:T(8,128)(2,1)}, u32[]{:S(2)}) copy-start(bf16[128,256]{1,0:T(8,128)(2,1)} %param.25) | copy-start | bytes 196612
  47.0 1.3 %copy-start.4 = (bf16[128,256]{1,0:T(8,128)(2,1)S(1)}, bf16[128,256]{1,0:T(8,128)(2,1)}, u32[]{:S(2)}) copy-start(bf16[128,256]{1,0:T(8,128)(2,1)} %param.24) | copy-start | bytes 196612
  94.7 0.9 copy-start.10
  95.0 1.0 copy-start.5

commit v6 on v4

--- a/solution.py
+++ b/solution.py
@@ -8,6 +8,13 @@
     values = values.astype(jnp.float32)
     center = values - jnp.mean(values, axis=-1, keepdims=True)
     spread = jnp.mean(center * center, axis=-1, keepdims=True)
+    return center * lax.rsqrt(spread + 1e-05)
+
+
+def layer_norm_lead(values):
+    values = values.astype(jnp.float32)
+    center = values - jnp.mean(values, axis=0, keepdims=True)
+    spread = jnp.mean(center * center, axis=0, keepdims=True)
     return center * lax.rsqrt(spread + 1e-05)
 
 
@@ -108,9 +115,10 @@
 
 def gather_lines(piece):
     device_count = lax.axis_size("row") * lax.axis_size("col")
-    sent = jnp.broadcast_to(piece[None], (device_count,) + piece.shape)
+    heads, rows_here, length = piece.shape
+    sent = jnp.broadcast_to(piece.reshape(1, 1, -1), (device_count, 1, piece.size))
     got = lax.all_to_all(sent, ("row", "col"), 0, 0, tiled=True)
-    heads, rows_here, length = piece.shape
+    got = got.reshape(device_count, heads, rows_here, length)
     return got.transpose(1, 0, 2, 3).reshape(heads, device_count * rows_here, length)
 
 
@@ -255,16 +263,15 @@
         .reshape(device_count, channels_here, block_rows, block_cols)
     )
     product_got = lax.all_to_all(product_sent, ("row", "col"), 0, 1, tiled=True)
-    product_sum = product_got.reshape(channels, block_rows, block_cols).transpose(1, 2, 0)
+    product_sum = product_got.reshape(channels, block_rows * block_cols)
     normed_own = layer_norm(own_pair).astype(jnp.bfloat16)
     gate_values = jax.nn.sigmoid(
         jnp.dot(normed_own.reshape(-1, channels), tri_gate, preferred_element_type=jnp.float32)
-    ).reshape(block_rows, block_cols, channels)
-    centered = layer_norm(product_sum).astype(jnp.bfloat16)
-    update_tri = jnp.dot(
-        centered.reshape(-1, channels), tri_output, preferred_element_type=jnp.float32
-    ).reshape(block_rows, block_cols, channels)
-    return (own_pair.astype(jnp.float32) + gate_values * update_tri).astype(jnp.bfloat16)
+    )
+    centered = layer_norm_lead(product_sum).astype(jnp.bfloat16)
+    update_tri = jnp.einsum("cn,cd->nd", centered, tri_output, preferred_element_type=jnp.float32)
+    result = own_pair.reshape(-1, channels).astype(jnp.float32) + gate_values * update_tri
+    return result.astype(jnp.bfloat16).reshape(block_rows, block_cols, channels)
 
 
 def solution(mesh):

time: 92.4 us -> 92.8 us (level)
    unnamed x38 -> x37, local copies, waits for them, and re-layouts: 9.18 us -> 9.14 us
where the time goes in v6:
time: 92.8 us; the launch traced here: 91.9 us
  waiting for transfers between devices  35.5 us (38%)
  starting transfers between devices  25.3 us (27%)
  local copies, waits for them, and re-layouts  16.9 us (18%)
  matrix products  6.61 us (7%)
  other arithmetic  6.26 us (7%)
  between operations  1.34 us (1%)
    all_to_all x1, waiting for transfers between devices, shards(): lax.all_to_all(jnp.concatenate([pair_chunks, bias_chunks], axis=1), ('row...  14 us
    unnamed x37, local copies, waits for them, and re-layouts  9.14 us
    all_to_all x1, waiting for transfers between devices, shards(): product_got = lax.all_to_all(product_sent, ('row', 'col'), 0, 1, tiled=True)  8.16 us
    ppermute x7, starting transfers between devices, shards(): lax.ppermute(piece, 'row', perm=[(r, (r + shift) % n_row) for r in range(...  7.53 us
    all_to_all x1, starting transfers between devices, gather_lines(): got = lax.all_to_all(sent, ('row', 'col'), 0, 0, tiled=True)  7.33 us
    all_to_all x1, waiting for transfers between devices, gather_lines(): got = lax.all_to_all(sent, ('row', 'col'), 0, 0, tiled=True)  6.88 us
    all_to_all x1, starting transfers between devices, shards(): edges_got = lax.all_to_all(edges, ('row', 'col'), 0, 3, tiled=True)  4.99 us
    all_to_all x1, waiting for transfers between devices, shards(): edges_got = lax.all_to_all(edges, ('row', 'col'), 0, 3, tiled=True)  4.95 us
  transfers between devices with their start and end apart: 11, of which 6 were waited for; matrix products, arithmetic and copies ran while one was open for 6% of the time, Pallas kernels for 0%

profile of v6, /device:TPU:0, one launch (start us, length us, event | category | flops | bytes accessed | tf_op | source)
XLA Modules:
  0.0 91.9 jit_solution(2305627593094377254)
XLA Ops:
  0.0 1.1 %convert_reduce_fusion = f32[4,128]{1,0:T(4,128)S(1)} fusion(bf16[4,128,128]{2,1,0:T(8,128)(2,1)} %param.14), kind=kLoop, calls=%fused_computation.39 | loop fusion | flops 130560 | bytes 133120 | tf_op jit(solution)/shard_map/reduce_sum | solution.py:9
  1.4 0.7 copy-done.13
  2.4 0.8 broadcast_in_dim.36
  3.2 7.3 %all-to-all-start = ((f32[32,1,2048]{2,1,0:T(1,128)}), f32[32,1,2048]{2,1,0:T(1,128)S(1)}, u32[]{:S(2)}, u32[]{:S(2)}) async-start(f32[32,1,2048]{2,1,0:T(1,128)} %broadcast_in_dim.36), calls=%async_computation | async-start | bytes 524288 | tf_op jit(solution)/shard_map/all_to_all | solution.py:120
  10.6 0.7 copy-done.9
  11.9 0.4 fusion.57
  12.6 0.4 copy-done.7
  13.1 0.8 broadcast_multiply_fusion
  13.9 6.9 %all-to-all-done = f32[32,1,2048]{2,1,0:T(1,128)S(1)} async-done(((f32[32,1,2048]{2,1,0:T(1,128)}), f32[32,1,2048]{2,1,0:T(1,128)S(1)}, u32[]{:S(2)}, u32[]{:S(2)}) %all-to-all-start) | async-done | bytes 262176 | tf_op jit(solution)/shard_map/all_to_all | solution.py:120
  20.9 0.6 fusion.98
  21.5 0.4 fusion.8
  21.9 0.3 fusion.20
  22.4 0.6 copy-done.10
  23.8 0.7 copy-done.8
  24.9 1.3 %copy.160 = f32[32,1,4096]{2,1,0:T(1,128)} copy(f32[32,1,4096]{2,0,1:T(8,128)S(1)} %maximum_bitcast_fusion) | data formatting | bytes 1048576 | tf_op jit(solution)/shard_map/all_to_all | solution.py:198
  26.2 2.7 %all-to-all-start.1 = ((f32[32,1,4096]{2,1,0:T(1,128)}), f32[32,1,4096]{2,1,0:T(1,128)S(1)}, u32[]{:S(2)}, u32[]{:S(2)}) async-start(f32[32,1,4096]{2,1,0:T(1,128)} %copy.160), calls=%async_computation.1 | async-start | bytes 1048576 | tf_op jit(solution)/shard_map/all_to_all | solution.py:198
  29.1 14.0 %all-to-all-done.1 = f32[32,1,4096]{2,1,0:T(1,128)S(1)} async-done(((f32[32,1,4096]{2,1,0:T(1,128)}), f32[32,1,4096]{2,1,0:T(1,128)S(1)}, u32[]{:S(2)}, u32[]{:S(2)}) %all-to-all-start.1) | async-done | bytes 524320 | tf_op jit(solution)/shard_map/all_to_all | solution.py:198
  44.1 0.4 multiply_reduce_fusion.2
  44.8 0.6 copy-done.3
  46.0 0.7 copy-done.2
  46.7 0.6 fusion.100
  47.3 0.4 fusion.11
  47.7 0.3 fusion.21
  48.2 0.6 copy-done.11
  49.2 1.3 %collective-permute-start = (bf16[16,4,128]{2,0,1:T(8,128)(2,1)S(1)}, bf16[16,4,128]{2,0,1:T(8,128)(2,1)S(1)}, u32[]{:S(2)}, u32[]{:S(2)}) collective-permute-start(bf16[16,4,128]{2,0,1:T(8,128)(2,1)S(1)} %get-tuple-element.11), channel_id=1, source_target_pairs={{0,4},{4,8},{8,12},{12,16},{16,20},{20,24},{24,28},{28,0},{1,5},{5... | collective-permute-start | bytes 49160 | tf_op jit(solution)/shard_map/ppermute | solution.py:246
  50.5 1.5 %collective-permute-start.1 = (bf16[16,4,128]{2,0,1:T(8,128)(2,1)S(1)}, bf16[16,4,128]{2,0,1:T(8,128)(2,1)S(1)}, u32[]{:S(2)}, u32[]{:S(2)}) collective-permute-start(bf16[16,4,128]{2,0,1:T(8,128)(2,1)S(1)} %get-tuple-element.10), channel_id=1, source_target_pairs={{0,8},{4,12},{8,16},{12,20},{16,24},{20,28},{24,0},{28,4},{1,9},{5... | collective-permute-start | bytes 49160 | tf_op jit(solution)/shard_map/ppermute | solution.py:246
  51.9 0.9 collective-permute-start.2
  52.9 0.7 collective-permute-start.3
  53.6 0.4 collective-permute-start.4
  54.2 0.6 copy-done.4
  55.1 0.5 copy-done.5
  56.2 0.9 copy.180
  57.1 5.0 %all-to-all-start.2 = ((bf16[128,2,128,4]{2,3,1,0:T(4,128)(2,1)}), bf16[128,2,128,4]{2,3,1,0:T(4,128)(2,1)S(1)}, u32[]{:S(2)}, u32[]{:S(2)}) async-start(bf16[128,2,128,4]{2,3,1,0:T(4,128)(2,1)} %copy.180), calls=%async_computation.2 | async-start | bytes 524288 | tf_op jit(solution)/shard_map/all_to_all | solution.py:253
  62.1 2.7 %collective-permute-start.5 = (bf16[16,4,128]{2,0,1:T(8,128)(2,1)S(1)}, bf16[16,4,128]{2,0,1:T(8,128)(2,1)S(1)}, u32[]{:S(2)}, u32[]{:S(2)}) collective-permute-start(bf16[16,4,128]{2,0,1:T(8,128)(2,1)S(1)} %get-tuple-element.6), channel_id=1, source_target_pairs={{0,24},{4,28},{8,0},{12,4},{16,8},{20,12},{24,16},{28,20},{1,25},{... | collective-permute-start | bytes 49160 | tf_op jit(solution)/shard_map/ppermute | solution.py:246
  64.9 1.3 %collective-permute-done.5 = bf16[16,4,128]{2,0,1:T(8,128)(2,1)S(1)} collective-permute-done((bf16[16,4,128]{2,0,1:T(8,128)(2,1)S(1)}, bf16[16,4,128]{2,0,1:T(8,128)(2,1)S(1)}, u32[]{:S(2)}, u32[]{:S(2)}) %collective-permute-start.5) | collective-permute-done | bytes 16416 | tf_op jit(solution)/shard_map/ppermute | solution.py:246
  66.4 0.6 gather_fusion
  67.3 5.0 %all-to-all-done.2 = bf16[128,2,128,4]{2,3,1,0:T(4,128)(2,1)S(1)} async-done(((bf16[128,2,128,4]{2,3,1,0:T(4,128)(2,1)}), bf16[128,2,128,4]{2,3,1,0:T(4,128)(2,1)S(1)}, u32[]{:S(2)}, u32[]{:S(2)}) %all-to-all-start.2) | async-done | bytes 262176 | tf_op jit(solution)/shard_map/all_to_all | solution.py:253
  72.8 0.4 reshape.471
  73.4 1.2 %reshape.496 = f32[32,1,2048]{2,1,0:T(1,128)} reshape(f32[32,4,16,32]{3,2,1,0:T(8,128)S(1)} %bitcast.178) | data formatting | bytes 524288
  74.5 2.8 %all-to-all-start.3 = ((f32[32,1,2048]{2,1,0:T(1,128)}), f32[32,1,2048]{2,1,0:T(1,128)S(1)}, u32[]{:S(2)}, u32[]{:S(2)}) async-start(f32[32,1,2048]{2,1,0:T(1,128)} %reshape.496), calls=%async_computation.3 | async-start | bytes 524288 | tf_op jit(solution)/shard_map/all_to_all | solution.py:265
  78.3 0.6 copy-done.12
  79.2 8.2 %all-to-all-done.3 = f32[32,1,2048]{2,1,0:T(1,128)S(1)} async-done(((f32[32,1,2048]{2,1,0:T(1,128)}), f32[32,1,2048]{2,1,0:T(1,128)S(1)}, u32[]{:S(2)}, u32[]{:S(2)}) %all-to-all-start.3) | async-done | bytes 262176 | tf_op jit(solution)/shard_map/all_to_all | solution.py:265
  87.4 0.5 broadcast.641
  87.9 1.3 %reduce.4 = f32[32,2048]{1,0:T(8,128)S(1)} reduce(f32[32,1,2048]{2,1,0:T(1,128)S(1)} %all-to-all-done.3, f32[]{:T(128)} %broadcast.641), dimensions={1}, to_apply=%all_to_all.39.reduce_sub_computation | reduce | bytes 524292 | tf_op jit(solution)/shard_map/all_to_all | solution.py:265
  89.2 0.3 reshape.497
  89.5 0.4 reshape.473
  90.5 0.6 copy-done.6
  91.1 0.9 fusion.19
  (104 shorter events, 8.8 us)
Async XLA Ops:
  0.0 11.9 %copy-start = (bf16[128,512]{1,0:T(8,128)(2,1)S(1)}, bf16[128,512]{1,0:T(8,128)(2,1)}, u32[]{:S(2)}) copy-start(bf16[128,512]{1,0:T(8,128)(2,1)} %param.18) | copy-start | bytes 393220
  0.0 1.1 %copy-start.1 = (bf16[4,128,128]{2,1,0:T(8,128)(2,1)S(1)}, bf16[4,128,128]{2,1,0:T(8,128)(2,1)}, u32[]{:S(2)}) copy-start(bf16[4,128,128]{2,1,0:T(8,128)(2,1)} %param.14) | copy-start | bytes 393220
  1.4 0.7 copy-start.13
  3.2 17.6 %all-to-all-start = ((f32[32,1,2048]{2,1,0:T(1,128)}), f32[32,1,2048]{2,1,0:T(1,128)S(1)}, u32[]{:S(2)}, u32[]{:S(2)}) async-start(f32[32,1,2048]{2,1,0:T(1,128)} %broadcast_in_dim.36), calls=%async_computation | async-start | bytes 524288 | tf_op jit(solution)/shard_map/all_to_all | solution.py:120
  10.5 0.7 copy-start.9
  12.3 0.7 copy-start.7
  22.3 0.8 copy-start.10
  23.8 0.7 copy-start.8
  26.2 16.9 %all-to-all-start.1 = ((f32[32,1,4096]{2,1,0:T(1,128)}), f32[32,1,4096]{2,1,0:T(1,128)S(1)}, u32[]{:S(2)}, u32[]{:S(2)}) async-start(f32[32,1,4096]{2,1,0:T(1,128)} %copy.160), calls=%async_computation.1 | async-start | bytes 1048576 | tf_op jit(solution)/shard_map/all_to_all | solution.py:198
  44.5 0.9 copy-start.3
  45.8 1.0 %copy-start.2 = (f32[4,128,128]{1,2,0:T(8,128)S(1)}, f32[4,128,128]{1,2,0:T(8,128)}, u32[]{:S(2)}) copy-start(f32[4,128,128]{1,2,0:T(8,128)} %get-tuple-element.13) | copy-start | bytes 786436
  48.1 0.8 copy-start.11
  49.2 12.9 %collective-permute-start = (bf16[16,4,128]{2,0,1:T(8,128)(2,1)S(1)}, bf16[16,4,128]{2,0,1:T(8,128)(2,1)S(1)}, u32[]{:S(2)}, u32[]{:S(2)}) collective-permute-start(bf16[16,4,128]{2,0,1:T(8,128)(2,1)S(1)} %get-tuple-element.11), channel_id=1, source_target_pairs={{0,4},{4,8},{8,12},{12,16},{16,20},{20,24},{24,28},{28,0},{1,5},{5... | collective-permute-start | bytes 49160 | tf_op jit(solution)/shard_map/ppermute | solution.py:246
  50.5 14.3 %collective-permute-start.1 = (bf16[16,4,128]{2,0,1:T(8,128)(2,1)S(1)}, bf16[16,4,128]{2,0,1:T(8,128)(2,1)S(1)}, u32[]{:S(2)}, u32[]{:S(2)}) collective-permute-start(bf16[16,4,128]{2,0,1:T(8,128)(2,1)S(1)} %get-tuple-element.10), channel_id=1, source_target_pairs={{0,8},{4,12},{8,16},{12,20},{16,24},{20,28},{24,0},{28,4},{1,9},{5... | collective-permute-start | bytes 49160 | tf_op jit(solution)/shard_map/ppermute | solution.py:246
  51.9 12.9 %collective-permute-start.2 = (bf16[16,4,128]{2,0,1:T(8,128)(2,1)S(1)}, bf16[16,4,128]{2,0,1:T(8,128)(2,1)S(1)}, u32[]{:S(2)}, u32[]{:S(2)}) collective-permute-start(bf16[16,4,128]{2,0,1:T(8,128)(2,1)S(1)} %get-tuple-element.9), channel_id=1, source_target_pairs={{0,12},{4,16},{8,20},{12,24},{16,28},{20,0},{24,4},{28,8},{1,13},{... | collective-permute-start | bytes 49160 | tf_op jit(solution)/shard_map/ppermute | solution.py:246
  52.9 12.0 %collective-permute-start.3 = (bf16[16,4,128]{2,0,1:T(8,128)(2,1)S(1)}, bf16[16,4,128]{2,0,1:T(8,128)(2,1)S(1)}, u32[]{:S(2)}, u32[]{:S(2)}) collective-permute-start(bf16[16,4,128]{2,0,1:T(8,128)(2,1)S(1)} %get-tuple-element.8), channel_id=1, source_target_pairs={{0,16},{4,20},{8,24},{12,28},{16,0},{20,4},{24,8},{28,12},{1,17},{... | collective-permute-start | bytes 49160 | tf_op jit(solution)/shard_map/ppermute | solution.py:246
  53.6 11.3 %collective-permute-start.4 = (bf16[16,4,128]{2,0,1:T(8,128)(2,1)S(1)}, bf16[16,4,128]{2,0,1:T(8,128)(2,1)S(1)}, u32[]{:S(2)}, u32[]{:S(2)}) collective-permute-start(bf16[16,4,128]{2,0,1:T(8,128)(2,1)S(1)} %get-tuple-element.7), channel_id=1, source_target_pairs={{0,20},{4,24},{8,28},{12,0},{16,4},{20,8},{24,12},{28,16},{1,21},{... | collective-permute-start | bytes 49160 | tf_op jit(solution)/shard_map/ppermute | solution.py:246
  54.0 0.8 copy-start.4
  54.8 0.8 copy-start.5
  57.1 15.2 %all-to-all-start.2 = ((bf16[128,2,128,4]{2,3,1,0:T(4,128)(2,1)}), bf16[128,2,128,4]{2,3,1,0:T(4,128)(2,1)S(1)}, u32[]{:S(2)}, u32[]{:S(2)}) async-start(bf16[128,2,128,4]{2,3,1,0:T(4,128)(2,1)} %copy.180), calls=%async_computation.2 | async-start | bytes 524288 | tf_op jit(solution)/shard_map/all_to_all | solution.py:253
  62.1 4.2 %collective-permute-start.5 = (bf16[16,4,128]{2,0,1:T(8,128)(2,1)S(1)}, bf16[16,4,128]{2,0,1:T(8,128)(2,1)S(1)}, u32[]{:S(2)}, u32[]{:S(2)}) collective-permute-start(bf16[16,4,128]{2,0,1:T(8,128)(2,1)S(1)} %get-tuple-element.6), channel_id=1, source_target_pairs={{0,24},{4,28},{8,0},{12,4},{16,8},{20,12},{24,16},{28,20},{1,25},{... | collective-permute-start | bytes 49160 | tf_op jit(solution)/shard_map/ppermute | solution.py:246
  64.8 1.6 %collective-permute-start.6 = (bf16[16,4,128]{2,0,1:T(8,128)(2,1)S(1)}, bf16[16,4,128]{2,0,1:T(8,128)(2,1)S(1)}, u32[]{:S(2)}, u32[]{:S(2)}) collective-permute-start(bf16[16,4,128]{2,0,1:T(8,128)(2,1)S(1)} %get-tuple-element.5), channel_id=1, source_target_pairs={{0,28},{4,0},{8,4},{12,8},{16,12},{20,16},{24,20},{28,24},{1,29},{... | collective-permute-start | bytes 49160 | tf_op jit(solution)/shard_map/ppermute | solution.py:246
  74.5 12.9 %all-to-all-start.3 = ((f32[32,1,2048]{2,1,0:T(1,128)}), f32[32,1,2048]{2,1,0:T(1,128)S(1)}, u32[]{:S(2)}, u32[]{:S(2)}) async-start(f32[32,1,2048]{2,1,0:T(1,128)} %reshape.496), calls=%async_computation.3 | async-start | bytes 524288 | tf_op jit(solution)/shard_map/all_to_all | solution.py:265
  78.1 0.8 copy-start.12
  90.3 0.8 copy-start.6

commit v7 on v6

--- a/solution.py
+++ b/solution.py
@@ -138,6 +138,14 @@
     tri_gate,
     tri_output,
 ):
+    slab_parts = [row_project, col_project, tri_left, tri_right, tri_gate, row_output, col_output, tri_output]
+    slab = lax.optimization_barrier(jnp.concatenate(slab_parts, axis=1))
+    cuts = [0]
+    for part in slab_parts:
+        cuts.append(cuts[-1] + part.shape[1])
+    (row_project, col_project, tri_left, tri_right, tri_gate, row_output, col_output, tri_output) = [
+        slab[:, cuts[n] : cuts[n + 1]] for n in range(len(slab_parts))
+    ]
     n_row = lax.axis_size("row")
     n_col = lax.axis_size("col")
     device_count = n_row * n_col

time: 92.8 us -> 94.5 us (1.018)
  matrix products: 6.61 us -> 12.3 us
  waiting for transfers between devices: 35.5 us -> 30.4 us
  starting transfers between devices: 25.3 us -> 26.6 us
    all_to_all x1, waiting for transfers between devices: 6.88 us -> 1.93 us  [gather_lines(): got = lax.all_to_all(sent, ('row', 'col'), 0, 0, tiled=True)]
    dot_general x2, matrix products: 0.64 us -> 2.33 us  [tri_acts(): jnp.dot(normed.reshape(-1, channels), weights, preferred_element_type=jnp...]
    all_to_all x1, starting transfers between devices: 2.66 us -> 3.92 us  [shards(): lax.all_to_all(jnp.concatenate([pair_chunks, bias_chunks], axis=1), ('row...]
    unnamed x37 -> x44, local copies, waits for them, and re-layouts: 9.14 us -> 9.23 us
  transfers between devices with their start and end apart: 11 -> 11, of which waited for: 6 -> 6; matrix products, arithmetic and copies ran while one was open for 6% -> 5% of each run, Pallas kernels for 0% -> 0%
where the time goes in v7:
time: 94.5 us; the launch traced here: 93.3 us
  waiting for transfers between devices  30.4 us (32%)
  starting transfers between devices  26.6 us (28%)
  local copies, waits for them, and re-layouts  17 us (18%)
  matrix products  12.3 us (13%)
  other arithmetic  5.6 us (6%)
  between operations  1.34 us (1%)
    all_to_all x1, waiting for transfers between devices, shards(): lax.all_to_all(jnp.concatenate([pair_chunks, bias_chunks], axis=1), ('row...  14 us
    unnamed x44, local copies, waits for them, and re-layouts  9.23 us
    all_to_all x1, waiting for transfers between devices, shards(): product_got = lax.all_to_all(product_sent, ('row', 'col'), 0, 1, tiled=True)  8.05 us
    ppermute x7, starting transfers between devices, shards(): lax.ppermute(piece, 'row', perm=[(r, (r + shift) % n_row) for r in range(...  7.54 us
    all_to_all x1, starting transfers between devices, gather_lines(): got = lax.all_to_all(sent, ('row', 'col'), 0, 0, tiled=True)  7.33 us
    all_to_all x1, starting transfers between devices, shards(): edges_got = lax.all_to_all(edges, ('row', 'col'), 0, 3, tiled=True)  4.98 us
    all_to_all x1, waiting for transfers between devices, shards(): edges_got = lax.all_to_all(edges, ('row', 'col'), 0, 3, tiled=True)  4.95 us
    all_to_all x1, starting transfers between devices, shards(): lax.all_to_all(jnp.concatenate([pair_chunks, bias_chunks], axis=1), ('row...  3.92 us
  transfers between devices with their start and end apart: 11, of which 6 were waited for; matrix products, arithmetic and copies ran while one was open for 5% of the time, Pallas kernels for 0%

profile of v7, /device:TPU:0, one launch (start us, length us, event | category | flops | bytes accessed | tf_op | source)
XLA Modules:
  0.0 93.3 jit_solution(11258681619430504893)
XLA Ops:
  0.0 1.1 %convert_reduce_fusion = f32[4,128]{1,0:T(4,128)S(1)} fusion(bf16[4,128,128]{2,1,0:T(8,128)(2,1)} %param.14), kind=kLoop, calls=%fused_computation.39 | loop fusion | flops 130560 | bytes 133120 | tf_op jit(solution)/shard_map/reduce_sum | solution.py:9
  1.7 0.8 broadcast_in_dim.36
  2.6 7.3 %all-to-all-start = ((f32[32,1,2048]{2,1,0:T(1,128)}), f32[32,1,2048]{2,1,0:T(1,128)S(1)}, u32[]{:S(2)}, u32[]{:S(2)}) async-start(f32[32,1,2048]{2,1,0:T(1,128)} %broadcast_in_dim.36), calls=%async_computation | async-start | bytes 524288 | tf_op jit(solution)/shard_map/all_to_all | solution.py:120
  9.9 0.9 copy-done.4
  10.8 0.8 copy-done.5
  11.7 0.8 copy-done.6
  12.5 0.8 copy-done.7
  13.3 0.7 copy-done.8
  14.0 0.7 copy-done.9
  14.8 0.7 copy-done.10
  15.5 0.7 copy-done.13
  16.9 0.4 fusion.56
  17.6 0.4 copy-done.11
  18.2 1.9 %all-to-all-done = f32[32,1,2048]{2,1,0:T(1,128)S(1)} async-done(((f32[32,1,2048]{2,1,0:T(1,128)}), f32[32,1,2048]{2,1,0:T(1,128)S(1)}, u32[]{:S(2)}, u32[]{:S(2)}) %all-to-all-start) | async-done | bytes 262176 | tf_op jit(solution)/shard_map/all_to_all | solution.py:120
  20.3 0.6 fusion.94
  20.9 0.4 fusion.8
  21.3 0.3 fusion.20
  21.8 1.1 %fusion.95 = (f32[4,128]{1,0:T(4,128)S(1)}, f32[4,128,128]{2,1,0:T(8,128)S(1)}) fusion(bf16[128,2048]{1,0:T(8,128)(2,1)} %copy-done.2, f32[4,128,128]{2,1,0:T(8,128)S(1)} %copy.157, f32[4,128,512]{2,1,0:T(8,128)S(1)} %fusion.56, bf16[4,128,128]{2,1,0:T(8,128)(2,1)S(1)} %copy-done.1), kind=kOutput, calls=%fused_computation.208 | convolution fusion | flops 17432064 | bytes 952320 | tf_op jit(solution)/shard_map/dot_general | solution.py:188
  23.3 0.7 copy-done.12
  24.4 1.4 %copy.160 = f32[32,1,4096]{2,1,0:T(1,128)} copy(f32[32,1,4096]{2,0,1:T(8,128)S(1)} %maximum_bitcast_fusion) | data formatting | bytes 1048576 | tf_op jit(solution)/shard_map/all_to_all | solution.py:206
  25.7 3.9 %all-to-all-start.1 = ((f32[32,1,4096]{2,1,0:T(1,128)}), f32[32,1,4096]{2,1,0:T(1,128)S(1)}, u32[]{:S(2)}, u32[]{:S(2)}) async-start(f32[32,1,4096]{2,1,0:T(1,128)} %copy.160), calls=%async_computation.1 | async-start | bytes 1048576 | tf_op jit(solution)/shard_map/all_to_all | solution.py:206
  29.9 14.0 %all-to-all-done.1 = f32[32,1,4096]{2,1,0:T(1,128)S(1)} async-done(((f32[32,1,4096]{2,1,0:T(1,128)}), f32[32,1,4096]{2,1,0:T(1,128)S(1)}, u32[]{:S(2)}, u32[]{:S(2)}) %all-to-all-start.1) | async-done | bytes 524320 | tf_op jit(solution)/shard_map/all_to_all | solution.py:206
  44.9 0.4 multiply_reduce_fusion.2
  45.6 1.2 %fusion.55 = f32[128,4,512]{2,0,1:T(8,128)S(1)} fusion(bf16[128,2048]{1,0:T(8,128)(2,1)} %copy-done.2, bf16[128,4,128]{2,1,0:T(4,128)(2,1)S(1)} %multiply_convert_fusion.2), kind=kOutput, calls=%fused_computation.96 | convolution fusion | flops 67108864 | bytes 1310720 | tf_op jit(solution)/shard_map/dot_general | solution.py:220
  47.1 0.6 fusion.96
  47.7 0.4 fusion.11
  48.6 1.1 %convert_reduce_fusion.1 = (f32[128,4]{0,1:T(4,128)S(1)}, bf16[128,4,128]{2,0,1:T(8,128)(2,1)S(1)}) fusion(bf16[128,2048]{1,0:T(8,128)(2,1)} %copy-done.2, f32[128,4,128]{2,0,1:T(8,128)S(1)} %copy.172, f32[128,4,512]{2,0,1:T(8,128)S(1)} %fusion.55, f32[128,4,128]{2,1,0:T(4,128)S(1)} %reshape.476), kind=kOutput, calls=%fused_computation.41 | convolution fusion | flops 17366528 | bytes 952320 | tf_op jit(solution)/shard_map/dot_general | solution.py:241
  49.9 1.2 %fusion.70 = f32[128,4,256]{2,0,1:T(8,128)S(1)} fusion(bf16[128,4,128]{2,0,1:T(8,128)(2,1)S(1)} %get-tuple-element.22, f32[128,4]{0,1:T(4,128)S(1)} %add_rsqrt_fusion.2, f32[128,4]{0,1:T(4,128)S(1)} %broadcast_multiply_fusion.5, bf16[128,2048]{1,0:T(8,128)(2,1)} %copy-done.2), kind=kOutput, calls=%fused_computation.117 | convolution fusion | flops 33816576 | bytes 724992 | tf_op jit(solution)/shard_map/dot_general | solution.py:109
  51.1 1.2 %fusion.68 = f32[128,4,256]{2,0,1:T(8,128)S(1)} fusion(bf16[128,4,128]{2,0,1:T(8,128)(2,1)S(1)} %get-tuple-element.22, f32[128,4]{0,1:T(4,128)S(1)} %add_rsqrt_fusion.2, f32[128,4]{0,1:T(4,128)S(1)} %broadcast_multiply_fusion.5, bf16[128,2048]{1,0:T(8,128)(2,1)} %copy-done.2), kind=kOutput, calls=%fused_computation.116 | convolution fusion | flops 33816576 | bytes 724992 | tf_op jit(solution)/shard_map/dot_general | solution.py:109
  52.3 1.3 %collective-permute-start = (bf16[16,4,128]{2,0,1:T(8,128)(2,1)S(1)}, bf16[16,4,128]{2,0,1:T(8,128)(2,1)S(1)}, u32[]{:S(2)}, u32[]{:S(2)}) collective-permute-start(bf16[16,4,128]{2,0,1:T(8,128)(2,1)S(1)} %get-tuple-element.11), channel_id=1, source_target_pairs={{0,4},{4,8},{8,12},{12,16},{16,20},{20,24},{24,28},{28,0},{1,5},{5... | collective-permute-start | bytes 49160 | tf_op jit(solution)/shard_map/ppermute | solution.py:254
  53.7 1.5 %collective-permute-start.1 = (bf16[16,4,128]{2,0,1:T(8,128)(2,1)S(1)}, bf16[16,4,128]{2,0,1:T(8,128)(2,1)S(1)}, u32[]{:S(2)}, u32[]{:S(2)}) collective-permute-start(bf16[16,4,128]{2,0,1:T(8,128)(2,1)S(1)} %get-tuple-element.10), channel_id=1, source_target_pairs={{0,8},{4,12},{8,16},{12,20},{16,24},{20,28},{24,0},{28,4},{1,9},{5... | collective-permute-start | bytes 49160 | tf_op jit(solution)/shard_map/ppermute | solution.py:254
  55.1 0.9 collective-permute-start.2
  56.1 0.8 collective-permute-start.3
  57.4 0.9 copy.180
  58.2 5.0 %all-to-all-start.2 = ((bf16[128,2,128,4]{2,3,1,0:T(4,128)(2,1)}), bf16[128,2,128,4]{2,3,1,0:T(4,128)(2,1)S(1)}, u32[]{:S(2)}, u32[]{:S(2)}) async-start(bf16[128,2,128,4]{2,3,1,0:T(4,128)(2,1)} %copy.180), calls=%async_computation.2 | async-start | bytes 524288 | tf_op jit(solution)/shard_map/all_to_all | solution.py:261
  63.2 2.7 %collective-permute-start.5 = (bf16[16,4,128]{2,0,1:T(8,128)(2,1)S(1)}, bf16[16,4,128]{2,0,1:T(8,128)(2,1)S(1)}, u32[]{:S(2)}, u32[]{:S(2)}) collective-permute-start(bf16[16,4,128]{2,0,1:T(8,128)(2,1)S(1)} %get-tuple-element.6), channel_id=1, source_target_pairs={{0,24},{4,28},{8,0},{12,4},{16,8},{20,12},{24,16},{28,20},{1,25},{... | collective-permute-start | bytes 49160 | tf_op jit(solution)/shard_map/ppermute | solution.py:254
  66.1 1.3 %collective-permute-done.5 = bf16[16,4,128]{2,0,1:T(8,128)(2,1)S(1)} collective-permute-done((bf16[16,4,128]{2,0,1:T(8,128)(2,1)S(1)}, bf16[16,4,128]{2,0,1:T(8,128)(2,1)S(1)}, u32[]{:S(2)}, u32[]{:S(2)}) %collective-permute-start.5) | collective-permute-done | bytes 16416 | tf_op jit(solution)/shard_map/ppermute | solution.py:254
  67.6 0.6 gather_fusion
  68.5 5.0 %all-to-all-done.2 = bf16[128,2,128,4]{2,3,1,0:T(4,128)(2,1)S(1)} async-done(((bf16[128,2,128,4]{2,3,1,0:T(4,128)(2,1)}), bf16[128,2,128,4]{2,3,1,0:T(4,128)(2,1)S(1)}, u32[]{:S(2)}, u32[]{:S(2)}) %all-to-all-start.2) | async-done | bytes 262176 | tf_op jit(solution)/shard_map/all_to_all | solution.py:261
  73.9 0.4 reshape.471
  74.5 1.2 %reshape.496 = f32[32,1,2048]{2,1,0:T(1,128)} reshape(f32[32,4,16,32]{3,2,1,0:T(8,128)S(1)} %bitcast.176) | data formatting | bytes 524288
  75.7 2.8 %all-to-all-start.3 = ((f32[32,1,2048]{2,1,0:T(1,128)}), f32[32,1,2048]{2,1,0:T(1,128)S(1)}, u32[]{:S(2)}, u32[]{:S(2)}) async-start(f32[32,1,2048]{2,1,0:T(1,128)} %reshape.496), calls=%async_computation.3 | async-start | bytes 524288 | tf_op jit(solution)/shard_map/all_to_all | solution.py:273
  79.4 1.1 %fusion.15 = f32[512,128]{1,0:T(8,128)S(1)} fusion(f32[512,128]{1,0:T(8,128)S(1)} %bitcast.193, f32[512]{0:T(512)S(1)} %rsqrt.58, f32[512]{0:T(512)S(1)} %div.121, bf16[128,2048]{1,0:T(8,128)(2,1)} %copy-done.2), kind=kOutput, calls=%fused_computation.22 | convolution fusion | flops 17170432 | bytes 561152 | tf_op jit(solution)/shard_map/dot_general | solution.py:277
  80.5 8.1 %all-to-all-done.3 = f32[32,1,2048]{2,1,0:T(1,128)S(1)} async-done(((f32[32,1,2048]{2,1,0:T(1,128)}), f32[32,1,2048]{2,1,0:T(1,128)S(1)}, u32[]{:S(2)}, u32[]{:S(2)}) %all-to-all-start.3) | async-done | bytes 262176 | tf_op jit(solution)/shard_map/all_to_all | solution.py:273
  88.6 0.5 broadcast.641
  89.1 1.3 %reduce.4 = f32[32,2048]{1,0:T(8,128)S(1)} reduce(f32[32,1,2048]{2,1,0:T(1,128)S(1)} %all-to-all-done.3, f32[]{:T(128)} %broadcast.641), dimensions={1}, to_apply=%all_to_all.39.reduce_sub_computation | reduce | bytes 524292 | tf_op jit(solution)/shard_map/all_to_all | solution.py:273
  90.7 0.4 reshape.473
  91.7 1.6 %fusion.19 = bf16[512,128]{1,0:T(8,128)(2,1)} fusion(f32[512,128]{1,0:T(8,128)S(1)} %bitcast.194, f32[512,128]{1,0:T(8,128)S(1)} %fusion.15, f32[128,512]{1,0:T(8,128)S(1)} %reshape.473, f32[512]{0:T(512)S(1)} %rsqrt.61, f32[512]{0:T(512)S(1)} %div.131, bf16[128,2048]{1,0:T(8,128)(2,1)} %copy-done.2), kind=kOutput, calls=%fused_computation.26 | convolution fusion | flops 17170432 | bytes 954368 | tf_op jit(solution)/shard_map/cn,cd->nd/dot_general | solution.py:280
  (112 shorter events, 8.2 us)
Async XLA Ops:
  0.0 1.4 %copy-start = (bf16[128,4]{0,1:T(4,128)(2,1)S(1)}, bf16[128,4]{0,1:T(4,128)(2,1)}, u32[]{:S(2)}) copy-start(bf16[128,4]{0,1:T(4,128)(2,1)} %param.19) | copy-start | bytes 3076
  0.0 1.1 %copy-start.1 = (bf16[4,128,128]{2,1,0:T(8,128)(2,1)S(1)}, bf16[4,128,128]{2,1,0:T(8,128)(2,1)}, u32[]{:S(2)}) copy-start(bf16[4,128,128]{2,1,0:T(8,128)(2,1)} %param.14) | copy-start | bytes 393220
  2.5 7.3 %copy-start.3 = (bf16[128,512]{1,0:T(8,128)(2,1)S(1)}, bf16[128,512]{1,0:T(8,128)(2,1)}, u32[]{:S(2)}) copy-start(bf16[128,512]{1,0:T(8,128)(2,1)} %param.18) | copy-start | bytes 393220
  2.6 17.6 %all-to-all-start = ((f32[32,1,2048]{2,1,0:T(1,128)}), f32[32,1,2048]{2,1,0:T(1,128)S(1)}, u32[]{:S(2)}, u32[]{:S(2)}) async-start(f32[32,1,2048]{2,1,0:T(1,128)} %broadcast_in_dim.36), calls=%async_computation | async-start | bytes 524288 | tf_op jit(solution)/shard_map/all_to_all | solution.py:120
  9.9 0.9 copy-start.4
  10.8 0.8 copy-start.5
  11.6 0.8 copy-start.6
  12.5 0.8 copy-start.7
  13.2 0.8 copy-start.8
  14.0 0.8 copy-start.9
  14.8 0.8 copy-start.10
  15.5 0.7 copy-start.13
  16.2 1.0 %copy-start.2 = (bf16[128,2048]{1,0:T(8,128)(2,1)}, bf16[128,2048]{1,0:T(8,128)(2,1)S(1)}, u32[]{:S(2)}) copy-start(bf16[128,2048]{1,0:T(8,128)(2,1)S(1)} %constant_dynamic-update-slice_fusion) | copy-start | bytes 1572868
  17.3 0.7 copy-start.11
  23.3 0.7 copy-start.12
  25.7 18.2 %all-to-all-start.1 = ((f32[32,1,4096]{2,1,0:T(1,128)}), f32[32,1,4096]{2,1,0:T(1,128)S(1)}, u32[]{:S(2)}, u32[]{:S(2)}) async-start(f32[32,1,4096]{2,1,0:T(1,128)} %copy.160), calls=%async_computation.1 | async-start | bytes 1048576 | tf_op jit(solution)/shard_map/all_to_all | solution.py:206
  52.3 10.9 %collective-permute-start = (bf16[16,4,128]{2,0,1:T(8,128)(2,1)S(1)}, bf16[16,4,128]{2,0,1:T(8,128)(2,1)S(1)}, u32[]{:S(2)}, u32[]{:S(2)}) collective-permute-start(bf16[16,4,128]{2,0,1:T(8,128)(2,1)S(1)} %get-tuple-element.11), channel_id=1, source_target_pairs={{0,4},{4,8},{8,12},{12,16},{16,20},{20,24},{24,28},{28,0},{1,5},{5... | collective-permute-start | bytes 49160 | tf_op jit(solution)/shard_map/ppermute | solution.py:254
  53.7 12.3 %collective-permute-start.1 = (bf16[16,4,128]{2,0,1:T(8,128)(2,1)S(1)}, bf16[16,4,128]{2,0,1:T(8,128)(2,1)S(1)}, u32[]{:S(2)}, u32[]{:S(2)}) collective-permute-start(bf16[16,4,128]{2,0,1:T(8,128)(2,1)S(1)} %get-tuple-element.10), channel_id=1, source_target_pairs={{0,8},{4,12},{8,16},{12,20},{16,24},{20,28},{24,0},{28,4},{1,9},{5... | collective-permute-start | bytes 49160 | tf_op jit(solution)/shard_map/ppermute | solution.py:254
  55.1 10.9 %collective-permute-start.2 = (bf16[16,4,128]{2,0,1:T(8,128)(2,1)S(1)}, bf16[16,4,128]{2,0,1:T(8,128)(2,1)S(1)}, u32[]{:S(2)}, u32[]{:S(2)}) collective-permute-start(bf16[16,4,128]{2,0,1:T(8,128)(2,1)S(1)} %get-tuple-element.9), channel_id=1, source_target_pairs={{0,12},{4,16},{8,20},{12,24},{16,28},{20,0},{24,4},{28,8},{1,13},{... | collective-permute-start | bytes 49160 | tf_op jit(solution)/shard_map/ppermute | solution.py:254
  56.1 10.0 %collective-permute-start.3 = (bf16[16,4,128]{2,0,1:T(8,128)(2,1)S(1)}, bf16[16,4,128]{2,0,1:T(8,128)(2,1)S(1)}, u32[]{:S(2)}, u32[]{:S(2)}) collective-permute-start(bf16[16,4,128]{2,0,1:T(8,128)(2,1)S(1)} %get-tuple-element.8), channel_id=1, source_target_pairs={{0,16},{4,20},{8,24},{12,28},{16,0},{20,4},{24,8},{28,12},{1,17},{... | collective-permute-start | bytes 49160 | tf_op jit(solution)/shard_map/ppermute | solution.py:254
  56.8 9.2 %collective-permute-start.4 = (bf16[16,4,128]{2,0,1:T(8,128)(2,1)S(1)}, bf16[16,4,128]{2,0,1:T(8,128)(2,1)S(1)}, u32[]{:S(2)}, u32[]{:S(2)}) collective-permute-start(bf16[16,4,128]{2,0,1:T(8,128)(2,1)S(1)} %get-tuple-element.7), channel_id=1, source_target_pairs={{0,20},{4,24},{8,28},{12,0},{16,4},{20,8},{24,12},{28,16},{1,21},{... | collective-permute-start | bytes 49160 | tf_op jit(solution)/shard_map/ppermute | solution.py:254
  58.2 15.2 %all-to-all-start.2 = ((bf16[128,2,128,4]{2,3,1,0:T(4,128)(2,1)}), bf16[128,2,128,4]{2,3,1,0:T(4,128)(2,1)S(1)}, u32[]{:S(2)}, u32[]{:S(2)}) async-start(bf16[128,2,128,4]{2,3,1,0:T(4,128)(2,1)} %copy.180), calls=%async_computation.2 | async-start | bytes 524288 | tf_op jit(solution)/shard_map/all_to_all | solution.py:261
  63.2 4.2 %collective-permute-start.5 = (bf16[16,4,128]{2,0,1:T(8,128)(2,1)S(1)}, bf16[16,4,128]{2,0,1:T(8,128)(2,1)S(1)}, u32[]{:S(2)}, u32[]{:S(2)}) collective-permute-start(bf16[16,4,128]{2,0,1:T(8,128)(2,1)S(1)} %get-tuple-element.6), channel_id=1, source_target_pairs={{0,24},{4,28},{8,0},{12,4},{16,8},{20,12},{24,16},{28,20},{1,25},{... | collective-permute-start | bytes 49160 | tf_op jit(solution)/shard_map/ppermute | solution.py:254
  66.0 1.6 %collective-permute-start.6 = (bf16[16,4,128]{2,0,1:T(8,128)(2,1)S(1)}, bf16[16,4,128]{2,0,1:T(8,128)(2,1)S(1)}, u32[]{:S(2)}, u32[]{:S(2)}) collective-permute-start(bf16[16,4,128]{2,0,1:T(8,128)(2,1)S(1)} %get-tuple-element.5), channel_id=1, source_target_pairs={{0,28},{4,0},{8,4},{12,8},{16,12},{20,16},{24,20},{28,24},{1,29},{... | collective-permute-start | bytes 49160 | tf_op jit(solution)/shard_map/ppermute | solution.py:254
  75.7 12.9 %all-to-all-start.3 = ((f32[32,1,2048]{2,1,0:T(1,128)}), f32[32,1,2048]{2,1,0:T(1,128)S(1)}, u32[]{:S(2)}, u32[]{:S(2)}) async-start(f32[32,1,2048]{2,1,0:T(1,128)} %reshape.496), calls=%async_computation.3 | async-start | bytes 524288 | tf_op jit(solution)/shard_map/all_to_all | solution.py:273

commit v8 on v4

--- a/solution.py
+++ b/solution.py
@@ -182,21 +182,23 @@
         first_pair.reshape(rows_here, n_col, n_row, rows_here, channels)
         .transpose(2, 1, 0, 3, 4)
         .reshape(device_count, rows_here * rows_here * channels)
-        .astype(jnp.float32)
-    )
-    bias_chunks = jnp.broadcast_to(
-        bias_next.reshape(1, -1), (device_count, head_count * rows_here * length)
-    )
+    )
+    bias_high = bias_next.astype(jnp.bfloat16)
+    bias_low = (bias_next - bias_high.astype(jnp.float32)).astype(jnp.bfloat16)
+    bias_words = jnp.stack([bias_high, bias_low], axis=0).reshape(1, -1)
+    bias_chunks = jnp.broadcast_to(bias_words, (device_count, bias_words.shape[1]))
     merged = lax.all_to_all(
         jnp.concatenate([pair_chunks, bias_chunks], axis=1), ("row", "col"), 0, 0, tiled=True
     )
     pair_size = rows_here * rows_here * channels
-    columns = (
-        merged[:, :pair_size].astype(jnp.bfloat16).reshape(length, rows_here, channels)
+    columns = merged[:, :pair_size].reshape(length, rows_here, channels)
+    bias_got = (
+        merged[:, pair_size:]
+        .reshape(device_count, 2, head_count, rows_here, length)
+        .astype(jnp.float32)
     )
     bias_cols = (
-        merged[:, pair_size:]
-        .reshape(device_count, head_count, rows_here, length)
+        (bias_got[:, 0] + bias_got[:, 1])
         .transpose(1, 0, 2, 3)
         .reshape(head_count, length, length)
     )

time: 92.4 us -> 90.6 us (0.981)
  waiting for transfers between devices: 35.5 us -> 33.5 us
    all_to_all x1, waiting for transfers between devices: 14 us -> 11.7 us  [shards(): lax.all_to_all(jnp.concatenate([pair_chunks, bias_chunks], axis=1), ('row...]
where the time goes in v8:
time: 90.6 us; the launch traced here: 89.8 us
  waiting for transfers between devices  33.5 us (37%)
  starting transfers between devices  25 us (28%)
  local copies, waits for them, and re-layouts  16.4 us (18%)
  other arithmetic  6.73 us (7%)
  matrix products  6.69 us (7%)
  between operations  1.43 us (2%)
    all_to_all x1, waiting for transfers between devices, shards(): lax.all_to_all(jnp.concatenate([pair_chunks, bias_chunks], axis=1), ('row...  11.7 us
    unnamed x38, local copies, waits for them, and re-layouts  9.96 us
    all_to_all x1, waiting for transfers between devices, shards(): product_got = lax.all_to_all(product_sent, ('row', 'col'), 0, 1, tiled=True)  8.16 us
    all_to_all x1, starting transfers between devices, gather_lines(): got = lax.all_to_all(sent, ('row', 'col'), 0, 0, tiled=True)  7.33 us
    all_to_all x1, waiting for transfers between devices, gather_lines(): got = lax.all_to_all(sent, ('row', 'col'), 0, 0, tiled=True)  7.21 us
    ppermute x7, starting transfers between devices, shards(): lax.ppermute(piece, 'row', perm=[(r, (r + shift) % n_row) for r in range(...  7.17 us
    all_to_all x1, starting transfers between devices, shards(): edges_got = lax.all_to_all(edges, ('row', 'col'), 0, 3, tiled=True)  5 us
    all_to_all x1, waiting for transfers between devices, shards(): edges_got = lax.all_to_all(edges, ('row', 'col'), 0, 3, tiled=True)  4.96 us
  transfers between devices with their start and end apart: 11, of which 6 were waited for; matrix products, arithmetic and copies ran while one was open for 6% of the time, Pallas kernels for 0%

profile of v8, /device:TPU:0, one launch (start us, length us, event | category | flops | bytes accessed | tf_op | source)
XLA Modules:
  0.0 89.8 jit_solution(16219553903482356163)
XLA Ops:
  0.0 1.1 %convert_reduce_fusion = f32[4,128]{1,0:T(4,128)S(1)} fusion(bf16[4,128,128]{2,1,0:T(8,128)(2,1)} %param.14), kind=kLoop, calls=%fused_computation.42 | loop fusion | flops 130560 | bytes 133120 | tf_op jit(solution)/shard_map/reduce_sum | solution.py:9
  1.4 0.7 copy-done.11
  2.4 0.7 broadcast_in_dim.33
  3.1 7.3 %all-to-all-start = ((f32[32,4,4,128]{3,2,1,0:T(4,128)}), f32[32,4,4,128]{3,2,1,0:T(4,128)S(1)}, u32[]{:S(2)}, u32[]{:S(2)}) async-start(f32[32,4,4,128]{3,2,1,0:T(4,128)} %broadcast_in_dim.33), calls=%async_computation | async-start | bytes 524288 | tf_op jit(solution)/shard_map/all_to_all | solution.py:112
  10.4 0.7 copy-done.7
  11.8 0.4 fusion.61
  12.6 0.6 copy-done.6
  13.4 7.2 %all-to-all-done = f32[32,4,4,128]{3,2,1,0:T(4,128)S(1)} async-done(((f32[32,4,4,128]{3,2,1,0:T(4,128)}), f32[32,4,4,128]{3,2,1,0:T(4,128)S(1)}, u32[]{:S(2)}, u32[]{:S(2)}) %all-to-all-start) | async-done | bytes 262176 | tf_op jit(solution)/shard_map/all_to_all | solution.py:112
  20.8 0.6 fusion.102
  21.4 0.4 fusion.8
  21.8 0.3 fusion.20
  22.3 0.6 copy-done.8
  23.7 0.7 copy-done.12
  24.7 0.6 broadcast.639
  25.3 0.9 %reduce.2 = bf16[32,6144]{1,0:T(8,128)(2,1)S(1)} reduce(bf16[32,1,6144]{2,0,1:T(8,128)(2,1)S(1)} %maximum_bitcast_fusion, bf16[]{:T(256)} %broadcast.639), dimensions={1}, to_apply=%copy.201.reduce_sub_computation | reduce | bytes 786434 | tf_op jit(solution)/shard_map/all_to_all | solution.py:190
  26.3 1.0 %reshape.478 = bf16[32,2,3072]{2,1,0:T(2,128)(2,1)} reshape(bf16[32,6144]{1,0:T(8,128)(2,1)S(1)} %reduce.2) | data formatting | bytes 786432
  27.3 2.7 %all-to-all-start.1 = ((bf16[32,2,3072]{2,1,0:T(2,128)(2,1)}), bf16[32,2,3072]{2,1,0:T(2,128)(2,1)S(1)}, u32[]{:S(2)}, u32[]{:S(2)}) async-start(bf16[32,2,3072]{2,1,0:T(2,128)(2,1)} %reshape.478), calls=%async_computation.1 | async-start | bytes 786432 | tf_op jit(solution)/shard_map/all_to_all | solution.py:190
  30.1 11.7 %all-to-all-done.1 = bf16[32,2,3072]{2,1,0:T(2,128)(2,1)S(1)} async-done(((bf16[32,2,3072]{2,1,0:T(2,128)(2,1)}), bf16[32,2,3072]{2,1,0:T(2,128)(2,1)S(1)}, u32[]{:S(2)}, u32[]{:S(2)}) %all-to-all-start.1) | async-done | bytes 393248 | tf_op jit(solution)/shard_map/all_to_all | solution.py:190
  42.4 0.4 reshape.457
  43.3 0.4 multiply_reduce_fusion.2
  43.7 0.3 multiply_convert_fusion.2
  44.1 0.6 copy-done.2
  45.2 0.6 fusion.103
  45.8 0.4 fusion.11
  46.2 0.3 fusion.21
  46.7 0.6 copy-done.9
  47.7 1.3 %collective-permute-start = (bf16[16,4,128]{2,0,1:T(8,128)(2,1)S(1)}, bf16[16,4,128]{2,0,1:T(8,128)(2,1)S(1)}, u32[]{:S(2)}, u32[]{:S(2)}) collective-permute-start(bf16[16,4,128]{2,0,1:T(8,128)(2,1)S(1)} %get-tuple-element.11), channel_id=1, source_target_pairs={{0,4},{4,8},{8,12},{12,16},{16,20},{20,24},{24,28},{28,0},{1,5},{5... | collective-permute-start | bytes 49160 | tf_op jit(solution)/shard_map/ppermute | solution.py:240
  49.0 1.2 %collective-permute-start.1 = (bf16[16,4,128]{2,0,1:T(8,128)(2,1)S(1)}, bf16[16,4,128]{2,0,1:T(8,128)(2,1)S(1)}, u32[]{:S(2)}, u32[]{:S(2)}) collective-permute-start(bf16[16,4,128]{2,0,1:T(8,128)(2,1)S(1)} %get-tuple-element.10), channel_id=1, source_target_pairs={{0,8},{4,12},{8,16},{12,20},{16,24},{20,28},{24,0},{28,4},{1,9},{5... | collective-permute-start | bytes 49160 | tf_op jit(solution)/shard_map/ppermute | solution.py:240
  50.1 1.0 %collective-permute-start.2 = (bf16[16,4,128]{2,0,1:T(8,128)(2,1)S(1)}, bf16[16,4,128]{2,0,1:T(8,128)(2,1)S(1)}, u32[]{:S(2)}, u32[]{:S(2)}) collective-permute-start(bf16[16,4,128]{2,0,1:T(8,128)(2,1)S(1)} %get-tuple-element.9), channel_id=1, source_target_pairs={{0,12},{4,16},{8,20},{12,24},{16,28},{20,0},{24,4},{28,8},{1,13},{... | collective-permute-start | bytes 49160 | tf_op jit(solution)/shard_map/ppermute | solution.py:240
  51.1 1.0 %collective-permute-start.3 = (bf16[16,4,128]{2,0,1:T(8,128)(2,1)S(1)}, bf16[16,4,128]{2,0,1:T(8,128)(2,1)S(1)}, u32[]{:S(2)}, u32[]{:S(2)}) collective-permute-start(bf16[16,4,128]{2,0,1:T(8,128)(2,1)S(1)} %get-tuple-element.8), channel_id=1, source_target_pairs={{0,16},{4,20},{8,24},{12,28},{16,0},{20,4},{24,8},{28,12},{1,17},{... | collective-permute-start | bytes 49160 | tf_op jit(solution)/shard_map/ppermute | solution.py:240
  52.4 0.6 copy-done.3
  53.3 0.5 copy-done.4
  54.3 0.9 copy.223
  55.2 5.0 %all-to-all-start.2 = ((bf16[128,2,128,4]{2,3,1,0:T(4,128)(2,1)}), bf16[128,2,128,4]{2,3,1,0:T(4,128)(2,1)S(1)}, u32[]{:S(2)}, u32[]{:S(2)}) async-start(bf16[128,2,128,4]{2,3,1,0:T(4,128)(2,1)} %copy.223), calls=%async_computation.2 | async-start | bytes 524288 | tf_op jit(solution)/shard_map/all_to_all | solution.py:247
  60.2 2.7 %collective-permute-start.5 = (bf16[16,4,128]{2,0,1:T(8,128)(2,1)S(1)}, bf16[16,4,128]{2,0,1:T(8,128)(2,1)S(1)}, u32[]{:S(2)}, u32[]{:S(2)}) collective-permute-start(bf16[16,4,128]{2,0,1:T(8,128)(2,1)S(1)} %get-tuple-element.6), channel_id=1, source_target_pairs={{0,24},{4,28},{8,0},{12,4},{16,8},{20,12},{24,16},{28,20},{1,25},{... | collective-permute-start | bytes 49160 | tf_op jit(solution)/shard_map/ppermute | solution.py:240
  63.0 1.3 %collective-permute-done.5 = bf16[16,4,128]{2,0,1:T(8,128)(2,1)S(1)} collective-permute-done((bf16[16,4,128]{2,0,1:T(8,128)(2,1)S(1)}, bf16[16,4,128]{2,0,1:T(8,128)(2,1)S(1)}, u32[]{:S(2)}, u32[]{:S(2)}) %collective-permute-start.5) | collective-permute-done | bytes 16416 | tf_op jit(solution)/shard_map/ppermute | solution.py:240
  64.6 0.6 gather_fusion
  65.5 5.0 %all-to-all-done.2 = bf16[128,2,128,4]{2,3,1,0:T(4,128)(2,1)S(1)} async-done(((bf16[128,2,128,4]{2,3,1,0:T(4,128)(2,1)}), bf16[128,2,128,4]{2,3,1,0:T(4,128)(2,1)S(1)}, u32[]{:S(2)}, u32[]{:S(2)}) %all-to-all-start.2) | async-done | bytes 262176 | tf_op jit(solution)/shard_map/all_to_all | solution.py:247
  70.9 0.4 reshape.453
  71.5 1.2 %reshape.480 = f32[32,1,2048]{2,1,0:T(1,128)} reshape(f32[32,4,16,32]{3,2,1,0:T(8,128)S(1)} %bitcast.198) | data formatting | bytes 524288
  72.7 2.8 %all-to-all-start.3 = ((f32[32,1,2048]{2,1,0:T(1,128)}), f32[32,1,2048]{2,1,0:T(1,128)S(1)}, u32[]{:S(2)}, u32[]{:S(2)}) async-start(f32[32,1,2048]{2,1,0:T(1,128)} %reshape.480), calls=%async_computation.3 | async-start | bytes 524288 | tf_op jit(solution)/shard_map/all_to_all | solution.py:259
  76.4 0.6 copy-done.10
  77.4 8.2 %all-to-all-done.3 = f32[32,1,2048]{2,1,0:T(1,128)S(1)} async-done(((f32[32,1,2048]{2,1,0:T(1,128)}), f32[32,1,2048]{2,1,0:T(1,128)S(1)}, u32[]{:S(2)}, u32[]{:S(2)}) %all-to-all-start.3) | async-done | bytes 262176 | tf_op jit(solution)/shard_map/all_to_all | solution.py:259
  85.6 0.5 broadcast.640
  86.1 1.3 %reduce.3 = f32[32,2048]{1,0:T(8,128)S(1)} reduce(f32[32,1,2048]{2,1,0:T(1,128)S(1)} %all-to-all-done.3, f32[]{:T(128)} %broadcast.640), dimensions={1}, to_apply=%all_to_all.39.reduce_sub_computation | reduce | bytes 524292 | tf_op jit(solution)/shard_map/all_to_all | solution.py:259
  87.3 0.3 reshape.481
  88.2 0.6 copy-done.5
  88.8 1.0 %fusion.18 = bf16[16,32,128]{2,1,0:T(8,128)(2,1)} fusion(f32[16,32,128]{2,1,0:T(8,128)S(1)} %bitcast.210, f32[16,32,128]{2,1,0:T(8,128)S(1)} %bitcast.219, bf16[16,32,128]{1,0,2:T(8,128)(2,1)S(1)} %multiply_convert_fusion, bf16[128,128]{1,0:T(8,128)(2,1)S(1)} %copy-done.5), kind=kOutput, calls=%fused_computation.25 | convolution fusion | flops 16973824 | bytes 819200 | tf_op jit(solution)/shard_map/dot_general | solution.py:266
  (106 shorter events, 8.7 us)
Async XLA Ops:
  0.0 11.8 %copy-start = (bf16[128,512]{1,0:T(8,128)(2,1)S(1)}, bf16[128,512]{1,0:T(8,128)(2,1)}, u32[]{:S(2)}) copy-start(bf16[128,512]{1,0:T(8,128)(2,1)} %param.18) | copy-start | bytes 393220
  0.0 1.1 %copy-start.1 = (bf16[4,128,128]{2,1,0:T(8,128)(2,1)S(1)}, bf16[4,128,128]{2,1,0:T(8,128)(2,1)}, u32[]{:S(2)}) copy-start(bf16[4,128,128]{2,1,0:T(8,128)(2,1)} %param.14) | copy-start | bytes 393220
  1.4 0.7 copy-start.11
  3.1 17.6 %all-to-all-start = ((f32[32,4,4,128]{3,2,1,0:T(4,128)}), f32[32,4,4,128]{3,2,1,0:T(4,128)S(1)}, u32[]{:S(2)}, u32[]{:S(2)}) async-start(f32[32,4,4,128]{3,2,1,0:T(4,128)} %broadcast_in_dim.33), calls=%async_computation | async-start | bytes 524288 | tf_op jit(solution)/shard_map/all_to_all | solution.py:112
  10.4 0.7 copy-start.7
  12.6 0.7 copy-start.6
  22.2 0.8 copy-start.8
  23.6 0.7 copy-start.12
  27.3 14.5 %all-to-all-start.1 = ((bf16[32,2,3072]{2,1,0:T(2,128)(2,1)}), bf16[32,2,3072]{2,1,0:T(2,128)(2,1)S(1)}, u32[]{:S(2)}, u32[]{:S(2)}) async-start(bf16[32,2,3072]{2,1,0:T(2,128)(2,1)} %reshape.478), calls=%async_computation.1 | async-start | bytes 786432 | tf_op jit(solution)/shard_map/all_to_all | solution.py:190
  43.7 0.9 %copy-start.2 = (bf16[128,512]{1,0:T(8,128)(2,1)S(1)}, bf16[128,512]{1,0:T(8,128)(2,1)}, u32[]{:S(2)}) copy-start(bf16[128,512]{1,0:T(8,128)(2,1)} %param.21) | copy-start | bytes 393220
  46.6 0.8 copy-start.9
  47.7 12.5 %collective-permute-start = (bf16[16,4,128]{2,0,1:T(8,128)(2,1)S(1)}, bf16[16,4,128]{2,0,1:T(8,128)(2,1)S(1)}, u32[]{:S(2)}, u32[]{:S(2)}) collective-permute-start(bf16[16,4,128]{2,0,1:T(8,128)(2,1)S(1)} %get-tuple-element.11), channel_id=1, source_target_pairs={{0,4},{4,8},{8,12},{12,16},{16,20},{20,24},{24,28},{28,0},{1,5},{5... | collective-permute-start | bytes 49160 | tf_op jit(solution)/shard_map/ppermute | solution.py:240
  49.0 14.0 %collective-permute-start.1 = (bf16[16,4,128]{2,0,1:T(8,128)(2,1)S(1)}, bf16[16,4,128]{2,0,1:T(8,128)(2,1)S(1)}, u32[]{:S(2)}, u32[]{:S(2)}) collective-permute-start(bf16[16,4,128]{2,0,1:T(8,128)(2,1)S(1)} %get-tuple-element.10), channel_id=1, source_target_pairs={{0,8},{4,12},{8,16},{12,20},{16,24},{20,28},{24,0},{28,4},{1,9},{5... | collective-permute-start | bytes 49160 | tf_op jit(solution)/shard_map/ppermute | solution.py:240
  50.1 12.9 %collective-permute-start.2 = (bf16[16,4,128]{2,0,1:T(8,128)(2,1)S(1)}, bf16[16,4,128]{2,0,1:T(8,128)(2,1)S(1)}, u32[]{:S(2)}, u32[]{:S(2)}) collective-permute-start(bf16[16,4,128]{2,0,1:T(8,128)(2,1)S(1)} %get-tuple-element.9), channel_id=1, source_target_pairs={{0,12},{4,16},{8,20},{12,24},{16,28},{20,0},{24,4},{28,8},{1,13},{... | collective-permute-start | bytes 49160 | tf_op jit(solution)/shard_map/ppermute | solution.py:240
  51.1 11.9 %collective-permute-start.3 = (bf16[16,4,128]{2,0,1:T(8,128)(2,1)S(1)}, bf16[16,4,128]{2,0,1:T(8,128)(2,1)S(1)}, u32[]{:S(2)}, u32[]{:S(2)}) collective-permute-start(bf16[16,4,128]{2,0,1:T(8,128)(2,1)S(1)} %get-tuple-element.8), channel_id=1, source_target_pairs={{0,16},{4,20},{8,24},{12,28},{16,0},{20,4},{24,8},{28,12},{1,17},{... | collective-permute-start | bytes 49160 | tf_op jit(solution)/shard_map/ppermute | solution.py:240
  52.1 10.9 %collective-permute-start.4 = (bf16[16,4,128]{2,0,1:T(8,128)(2,1)S(1)}, bf16[16,4,128]{2,0,1:T(8,128)(2,1)S(1)}, u32[]{:S(2)}, u32[]{:S(2)}) collective-permute-start(bf16[16,4,128]{2,0,1:T(8,128)(2,1)S(1)} %get-tuple-element.7), channel_id=1, source_target_pairs={{0,20},{4,24},{8,28},{12,0},{16,4},{20,8},{24,12},{28,16},{1,21},{... | collective-permute-start | bytes 49160 | tf_op jit(solution)/shard_map/ppermute | solution.py:240
  52.1 0.8 copy-start.3
  53.0 0.8 copy-start.4
  55.2 15.2 %all-to-all-start.2 = ((bf16[128,2,128,4]{2,3,1,0:T(4,128)(2,1)}), bf16[128,2,128,4]{2,3,1,0:T(4,128)(2,1)S(1)}, u32[]{:S(2)}, u32[]{:S(2)}) async-start(bf16[128,2,128,4]{2,3,1,0:T(4,128)(2,1)} %copy.223), calls=%async_computation.2 | async-start | bytes 524288 | tf_op jit(solution)/shard_map/all_to_all | solution.py:247
  60.2 4.2 %collective-permute-start.5 = (bf16[16,4,128]{2,0,1:T(8,128)(2,1)S(1)}, bf16[16,4,128]{2,0,1:T(8,128)(2,1)S(1)}, u32[]{:S(2)}, u32[]{:S(2)}) collective-permute-start(bf16[16,4,128]{2,0,1:T(8,128)(2,1)S(1)} %get-tuple-element.6), channel_id=1, source_target_pairs={{0,24},{4,28},{8,0},{12,4},{16,8},{20,12},{24,16},{28,20},{1,25},{... | collective-permute-start | bytes 49160 | tf_op jit(solution)/shard_map/ppermute | solution.py:240
  63.0 1.6 %collective-permute-start.6 = (bf16[16,4,128]{2,0,1:T(8,128)(2,1)S(1)}, bf16[16,4,128]{2,0,1:T(8,128)(2,1)S(1)}, u32[]{:S(2)}, u32[]{:S(2)}) collective-permute-start(bf16[16,4,128]{2,0,1:T(8,128)(2,1)S(1)} %get-tuple-element.5), channel_id=1, source_target_pairs={{0,28},{4,0},{8,4},{12,8},{16,12},{20,16},{24,20},{28,24},{1,29},{... | collective-permute-start | bytes 49160 | tf_op jit(solution)/shard_map/ppermute | solution.py:240
  72.7 12.9 %all-to-all-start.3 = ((f32[32,1,2048]{2,1,0:T(1,128)}), f32[32,1,2048]{2,1,0:T(1,128)S(1)}, u32[]{:S(2)}, u32[]{:S(2)}) async-start(f32[32,1,2048]{2,1,0:T(1,128)} %reshape.480), calls=%async_computation.3 | async-start | bytes 524288 | tf_op jit(solution)/shard_map/all_to_all | solution.py:259
  76.3 0.8 copy-start.10
  88.0 0.8 copy-start.5

commit v9 on v8

--- a/solution.py
+++ b/solution.py
@@ -233,14 +233,27 @@
     left_all = tri_acts(normed_second, tri_left, edge_mask)
     right_all = tri_acts(normed_second, tri_right, edge_mask)
     raw_chunks = second_pair.reshape(n_row, block_rows, rows_here, channels)
-    raw_pieces = [lax.dynamic_index_in_dim(raw_chunks, row_index, 0, keepdims=False)]
-    for shift in range(1, n_row):
-        piece = lax.dynamic_index_in_dim(raw_chunks, (row_index + shift) % n_row, 0, keepdims=False)
-        raw_pieces.append(
-            lax.ppermute(piece, "row", perm=[(r, (r + shift) % n_row) for r in range(n_row)])
-        )
-    sources = (row_index - jnp.arange(n_row, dtype=jnp.int32)) % n_row
-    raw_got = jnp.take(jnp.stack(raw_pieces, axis=0), sources, axis=0)
+    positions = jnp.arange(n_row, dtype=jnp.int32)
+    if n_row & (n_row - 1) == 0:
+        held = jnp.take(raw_chunks, (row_index + positions) % n_row, axis=0)
+        step = 1
+        while step < n_row:
+            moving = [p for p in range(n_row) if p & step]
+            came = lax.ppermute(
+                held[jnp.array(moving)], "row", perm=[(r, (r + step) % n_row) for r in range(n_row)]
+            )
+            held = held.at[jnp.array(moving)].set(came)
+            step *= 2
+        stacked = held
+    else:
+        raw_pieces = [lax.dynamic_index_in_dim(raw_chunks, row_index, 0, keepdims=False)]
+        for shift in range(1, n_row):
+            piece = lax.dynamic_index_in_dim(raw_chunks, (row_index + shift) % n_row, 0, keepdims=False)
+            raw_pieces.append(
+                lax.ppermute(piece, "row", perm=[(r, (r + shift) % n_row) for r in range(n_row)])
+            )
+        stacked = jnp.stack(raw_pieces, axis=0)
+    raw_got = jnp.take(stacked, (row_index - positions) % n_row, axis=0)
     own_pair = raw_got.transpose(1, 0, 2, 3).reshape(block_rows, block_cols, channels)
     channels_here = channels // device_count
     edges = jnp.stack([left_all, right_all], axis=0).transpose(3, 0, 1, 2)

time: 90.6 us -> 98.1 us (1.083)
  local copies, waits for them, and re-layouts: 16.4 us -> 22.8 us
  starting transfers between devices: 25 us -> 19.1 us
  other arithmetic: 6.73 us -> 10.8 us
  waiting for transfers between devices: 33.5 us -> 36.3 us
    ppermute x7 -> x3, waiting for transfers between devices: 1.5 us -> 5.84 us  [shards(): lax.ppermute(held[jnp.array(moving)], 'row', perm=[(r, (r + step) % n_row...]
    ppermute x7 -> x3, starting transfers between devices: 7.17 us -> 3.35 us  [shards(): lax.ppermute(held[jnp.array(moving)], 'row', perm=[(r, (r + step) % n_row...]
    all_to_all x1, waiting for transfers between devices: 4.96 us -> 8.6 us  [shards(): edges_got = lax.all_to_all(edges, ('row', 'col'), 0, 3, tiled=True)]
    all_to_all x1, waiting for transfers between devices: 11.7 us -> 8.45 us  [shards(): lax.all_to_all(jnp.concatenate([pair_chunks, bias_chunks], axis=1), ('row...]
    gather x1 -> x5, local copies, waits for them, and re-layouts: 0.57 us -> 3.09 us  [the longest x3 1.94 us: shards(): held[jnp.array(moving)]]
    all_to_all x1, starting transfers between devices: 5 us -> 2.92 us  [shards(): edges_got = lax.all_to_all(edges, ('row', 'col'), 0, 3, tiled=True)]
    unnamed x38 -> x53, local copies, waits for them, and re-layouts: 9.96 us -> 12 us
    all_to_all x1, waiting for transfers between devices: 7.21 us -> 5.23 us  [gather_lines(): got = lax.all_to_all(sent, ('row', 'col'), 0, 0, tiled=True)]
  transfers between devices with their start and end apart: 11 -> 7, of which waited for: 6 -> 6; matrix products, arithmetic and copies ran while one was open for 6% -> 10% of each run, Pallas kernels for 0% -> 0%
where the time goes in v9:
time: 98.1 us; the launch traced here: 97.1 us
  waiting for transfers between devices  36.3 us (37%)
  local copies, waits for them, and re-layouts  22.8 us (23%)
  starting transfers between devices  19.1 us (19%)
  other arithmetic  10.8 us (11%)
  matrix products  6.79 us (7%)
  between operations  1.32 us (1%)
    unnamed x53, local copies, waits for them, and re-layouts  12 us
    all_to_all x1, waiting for transfers between devices, shards(): edges_got = lax.all_to_all(edges, ('row', 'col'), 0, 3, tiled=True)  8.6 us
    all_to_all x1, waiting for transfers between devices, shards(): lax.all_to_all(jnp.concatenate([pair_chunks, bias_chunks], axis=1), ('row...  8.45 us
    all_to_all x1, waiting for transfers between devices, shards(): product_got = lax.all_to_all(product_sent, ('row', 'col'), 0, 1, tiled=True)  8.16 us
    all_to_all x1, starting transfers between devices, gather_lines(): got = lax.all_to_all(sent, ('row', 'col'), 0, 0, tiled=True)  7.33 us
    ppermute x3, waiting for transfers between devices, shards(): lax.ppermute(held[jnp.array(moving)], 'row', perm=[(r, (r + step) % n_row...  5.84 us
    all_to_all x1, waiting for transfers between devices, gather_lines(): got = lax.all_to_all(sent, ('row', 'col'), 0, 0, tiled=True)  5.23 us
    ppermute x3, starting transfers between devices, shards(): lax.ppermute(held[jnp.array(moving)], 'row', perm=[(r, (r + step) % n_row...  3.35 us
  transfers between devices with their start and end apart: 7, of which 6 were waited for; matrix products, arithmetic and copies ran while one was open for 10% of the time, Pallas kernels for 0%

profile of v9, /device:TPU:0, one launch (start us, length us, event | category | flops | bytes accessed | tf_op | source)
XLA Modules:
  0.0 97.1 jit_solution(156183993186726372)
XLA Ops:
  0.0 1.1 %convert_reduce_fusion = f32[4,128]{1,0:T(4,128)S(1)} fusion(bf16[4,128,128]{2,1,0:T(8,128)(2,1)} %param.22), kind=kLoop, calls=%fused_computation.49 | loop fusion | flops 130560 | bytes 133120 | tf_op jit(solution)/shard_map/reduce_sum | solution.py:9
  1.4 0.7 copy-done.22
  2.4 0.7 broadcast_in_dim.43
  3.1 7.3 %all-to-all-start = ((f32[32,4,4,128]{3,2,1,0:T(4,128)}), f32[32,4,4,128]{3,2,1,0:T(4,128)S(1)}, u32[]{:S(2)}, u32[]{:S(2)}) async-start(f32[32,4,4,128]{3,2,1,0:T(4,128)} %broadcast_in_dim.43), calls=%async_computation | async-start | bytes 524288 | tf_op jit(solution)/shard_map/all_to_all | solution.py:112
  10.5 0.6 compare_and_fusion.1
  11.1 0.6 compare_select_fusion
  13.9 0.6 compare_convert_fusion.1
  15.4 5.2 %all-to-all-done = f32[32,4,4,128]{3,2,1,0:T(4,128)S(1)} async-done(((f32[32,4,4,128]{3,2,1,0:T(4,128)}), f32[32,4,4,128]{3,2,1,0:T(4,128)S(1)}, u32[]{:S(2)}, u32[]{:S(2)}) %all-to-all-start) | async-done | bytes 262176 | tf_op jit(solution)/shard_map/all_to_all | solution.py:112
  20.8 0.6 fusion.101
  22.4 0.6 copy-done.19
  23.7 0.7 copy-done.23
  24.8 0.6 broadcast.578
  25.4 0.9 reduce.2
  26.3 1.0 %reshape.491 = bf16[32,2,3072]{2,1,0:T(2,128)(2,1)} reshape(bf16[32,6144]{1,0:T(8,128)(2,1)S(1)} %reduce.2) | data formatting | bytes 786432
  27.3 2.7 %all-to-all-start.1 = ((bf16[32,2,3072]{2,1,0:T(2,128)(2,1)}), bf16[32,2,3072]{2,1,0:T(2,128)(2,1)S(1)}, u32[]{:S(2)}, u32[]{:S(2)}) async-start(bf16[32,2,3072]{2,1,0:T(2,128)(2,1)} %reshape.491), calls=%async_computation.1 | async-start | bytes 786432 | tf_op jit(solution)/shard_map/all_to_all | solution.py:190
  30.0 0.6 copy-done.12
  30.7 0.6 pad_clamp_fusion.3
  31.3 0.6 pad_clamp_fusion.2
  32.0 0.7 copy-done.17
  32.7 0.7 copy-done.18
  33.4 8.5 %all-to-all-done.1 = bf16[32,2,3072]{2,1,0:T(2,128)(2,1)S(1)} async-done(((bf16[32,2,3072]{2,1,0:T(2,128)(2,1)}), bf16[32,2,3072]{2,1,0:T(2,128)(2,1)S(1)}, u32[]{:S(2)}, u32[]{:S(2)}) %all-to-all-start.1) | async-done | bytes 393248 | tf_op jit(solution)/shard_map/all_to_all | solution.py:190
  45.3 0.6 copy-done.14
  45.9 0.6 fusion.102
  47.4 0.6 copy-done.20
  48.3 0.6 gather_fusion.3
  49.1 0.7 gather_fusion
  49.8 1.3 %collective-permute-start = (bf16[4,16,4,128]{3,1,2,0:T(8,128)(2,1)S(1)}, bf16[4,16,4,128]{3,1,2,0:T(8,128)(2,1)S(1)}, u32[]{:S(2)}, u32[]{:S(2)}) collective-permute-start(bf16[4,16,4,128]{3,1,2,0:T(8,128)(2,1)S(1)} %gather_fusion), channel_id=1, source_target_pairs={{0,4},{4,8},{8,12},{12,16},{16,20},{20,24},{24,28},{28,0},{1,5},{5... | collective-permute-start | bytes 196616 | tf_op jit(solution)/shard_map/ppermute | solution.py:242
  51.3 0.6 copy-done.3
  53.1 1.4 %collective-permute-done = bf16[4,16,4,128]{3,1,2,0:T(8,128)(2,1)S(1)} collective-permute-done((bf16[4,16,4,128]{3,1,2,0:T(8,128)(2,1)S(1)}, bf16[4,16,4,128]{3,1,2,0:T(8,128)(2,1)S(1)}, u32[]{:S(2)}, u32[]{:S(2)}) %collective-permute-start) | collective-permute-done | bytes 65568 | tf_op jit(solution)/shard_map/ppermute | solution.py:242
  54.4 0.6 scatter_fusion
  55.1 0.7 gather_fusion.1
  55.8 0.6 collective-permute-start.1
  56.5 4.5 %collective-permute-done.1 = bf16[4,16,4,128]{3,1,2,0:T(8,128)(2,1)S(1)} collective-permute-done((bf16[4,16,4,128]{3,1,2,0:T(8,128)(2,1)S(1)}, bf16[4,16,4,128]{3,1,2,0:T(8,128)(2,1)S(1)}, u32[]{:S(2)}, u32[]{:S(2)}) %collective-permute-start.1) | collective-permute-done | bytes 65568 | tf_op jit(solution)/shard_map/ppermute | solution.py:242
  61.0 0.6 scatter_fusion.1
  61.7 0.6 gather_fusion.2
  62.2 1.5 %collective-permute-start.2 = (bf16[4,16,4,128]{3,1,2,0:T(8,128)(2,1)S(1)}, bf16[4,16,4,128]{3,1,2,0:T(8,128)(2,1)S(1)}, u32[]{:S(2)}, u32[]{:S(2)}) collective-permute-start(bf16[4,16,4,128]{3,1,2,0:T(8,128)(2,1)S(1)} %gather_fusion.2), channel_id=1, source_target_pairs={{0,16},{4,20},{8,24},{12,28},{16,0},{20,4},{24,8},{28,12},{1,17},{... | collective-permute-start | bytes 196616 | tf_op jit(solution)/shard_map/ppermute | solution.py:242
  63.8 0.9 copy.227
  64.6 2.9 %all-to-all-start.2 = ((bf16[128,2,128,4]{2,3,1,0:T(4,128)(2,1)}), bf16[128,2,128,4]{2,3,1,0:T(4,128)(2,1)S(1)}, u32[]{:S(2)}, u32[]{:S(2)}) async-start(bf16[128,2,128,4]{2,3,1,0:T(4,128)(2,1)} %copy.227), calls=%async_computation.2 | async-start | bytes 524288 | tf_op jit(solution)/shard_map/all_to_all | solution.py:260
  67.6 0.6 scatter_fusion.2
  68.2 0.6 gather_fusion.4
  69.2 8.6 %all-to-all-done.2 = bf16[128,2,128,4]{2,3,1,0:T(4,128)(2,1)S(1)} async-done(((bf16[128,2,128,4]{2,3,1,0:T(4,128)(2,1)}), bf16[128,2,128,4]{2,3,1,0:T(4,128)(2,1)S(1)}, u32[]{:S(2)}, u32[]{:S(2)}) %all-to-all-start.2) | async-done | bytes 262176 | tf_op jit(solution)/shard_map/all_to_all | solution.py:260
  78.9 1.2 %reshape.493 = f32[32,1,2048]{2,1,0:T(1,128)} reshape(f32[32,4,16,32]{3,2,1,0:T(8,128)S(1)} %bitcast.166) | data formatting | bytes 524288
  80.0 2.8 %all-to-all-start.3 = ((f32[32,1,2048]{2,1,0:T(1,128)}), f32[32,1,2048]{2,1,0:T(1,128)S(1)}, u32[]{:S(2)}, u32[]{:S(2)}) async-start(f32[32,1,2048]{2,1,0:T(1,128)} %reshape.493), calls=%async_computation.3 | async-start | bytes 524288 | tf_op jit(solution)/shard_map/all_to_all | solution.py:272
  83.8 0.6 copy-done.21
  84.8 8.2 %all-to-all-done.3 = f32[32,1,2048]{2,1,0:T(1,128)S(1)} async-done(((f32[32,1,2048]{2,1,0:T(1,128)}), f32[32,1,2048]{2,1,0:T(1,128)S(1)}, u32[]{:S(2)}, u32[]{:S(2)}) %all-to-all-start.3) | async-done | bytes 262176 | tf_op jit(solution)/shard_map/all_to_all | solution.py:272
  93.4 1.3 %reduce.3 = f32[32,2048]{1,0:T(8,128)S(1)} reduce(f32[32,1,2048]{2,1,0:T(1,128)S(1)} %all-to-all-done.3, f32[]{:T(128)} %broadcast.579), dimensions={1}, to_apply=%all_to_all.39.reduce_sub_computation | reduce | bytes 524292 | tf_op jit(solution)/shard_map/all_to_all | solution.py:272
  95.5 0.6 copy-done.5
  96.2 1.0 fusion.18
  (125 shorter events, 15.6 us)
Async XLA Ops:
  0.0 13.0 %copy-start = (bf16[128,512]{1,0:T(8,128)(2,1)S(1)}, bf16[128,512]{1,0:T(8,128)(2,1)}, u32[]{:S(2)}) copy-start(bf16[128,512]{1,0:T(8,128)(2,1)} %param.26) | copy-start | bytes 393220
  0.0 1.1 %copy-start.1 = (bf16[4,128,128]{2,1,0:T(8,128)(2,1)S(1)}, bf16[4,128,128]{2,1,0:T(8,128)(2,1)}, u32[]{:S(2)}) copy-start(bf16[4,128,128]{2,1,0:T(8,128)(2,1)} %param.22) | copy-start | bytes 393220
  1.4 0.7 copy-start.22
  3.1 17.6 %all-to-all-start = ((f32[32,4,4,128]{3,2,1,0:T(4,128)}), f32[32,4,4,128]{3,2,1,0:T(4,128)S(1)}, u32[]{:S(2)}, u32[]{:S(2)}) async-start(f32[32,4,4,128]{3,2,1,0:T(4,128)} %broadcast_in_dim.43), calls=%async_computation | async-start | bytes 524288 | tf_op jit(solution)/shard_map/all_to_all | solution.py:112
  11.7 0.7 copy-start.15
  14.6 0.7 copy-start.7
  22.2 0.8 copy-start.19
  23.7 0.7 copy-start.23
  27.3 14.5 %all-to-all-start.1 = ((bf16[32,2,3072]{2,1,0:T(2,128)(2,1)}), bf16[32,2,3072]{2,1,0:T(2,128)(2,1)S(1)}, u32[]{:S(2)}, u32[]{:S(2)}) async-start(bf16[32,2,3072]{2,1,0:T(2,128)(2,1)} %reshape.491), calls=%async_computation.1 | async-start | bytes 786432 | tf_op jit(solution)/shard_map/all_to_all | solution.py:190
  30.0 0.7 copy-start.12
  30.7 0.7 copy-start.10
  31.3 0.7 copy-start.8
  32.0 0.7 copy-start.17
  32.7 0.7 copy-start.18
  43.8 0.9 copy-start.2
  45.3 0.6 copy-start.14
  47.3 0.8 copy-start.20
  48.3 0.7 copy-start.16
  49.8 4.6 %collective-permute-start = (bf16[4,16,4,128]{3,1,2,0:T(8,128)(2,1)S(1)}, bf16[4,16,4,128]{3,1,2,0:T(8,128)(2,1)S(1)}, u32[]{:S(2)}, u32[]{:S(2)}) collective-permute-start(bf16[4,16,4,128]{3,1,2,0:T(8,128)(2,1)S(1)} %gather_fusion), channel_id=1, source_target_pairs={{0,4},{4,8},{8,12},{12,16},{16,20},{20,24},{24,28},{28,0},{1,5},{5... | collective-permute-start | bytes 196616 | tf_op jit(solution)/shard_map/ppermute | solution.py:242
  51.1 0.8 copy-start.3
  51.9 0.8 copy-start.4
  52.7 1.7 %copy-start.13 = (s32[4]{0:T(128)S(1)}, s32[4]{0:T(128)}, u32[]{:S(2)}) copy-start(s32[4]{0:T(128)} %constant.140) | copy-start | bytes 52
  55.8 5.2 %copy-start.11 = (s32[4]{0:T(128)S(1)}, s32[4]{0:T(128)}, u32[]{:S(2)}) copy-start(s32[4]{0:T(128)} %constant.142) | copy-start | bytes 52
  55.8 5.2 %collective-permute-start.1 = (bf16[4,16,4,128]{3,1,2,0:T(8,128)(2,1)S(1)}, bf16[4,16,4,128]{3,1,2,0:T(8,128)(2,1)S(1)}, u32[]{:S(2)}, u32[]{:S(2)}) collective-permute-start(bf16[4,16,4,128]{3,1,2,0:T(8,128)(2,1)S(1)} %gather_fusion.1), channel_id=1, source_target_pairs={{0,8},{4,12},{8,16},{12,20},{16,24},{20,28},{24,0},{28,4},{1,9},{5... | collective-permute-start | bytes 196616 | tf_op jit(solution)/shard_map/ppermute | solution.py:242
  62.2 5.3 %collective-permute-start.2 = (bf16[4,16,4,128]{3,1,2,0:T(8,128)(2,1)S(1)}, bf16[4,16,4,128]{3,1,2,0:T(8,128)(2,1)S(1)}, u32[]{:S(2)}, u32[]{:S(2)}) collective-permute-start(bf16[4,16,4,128]{3,1,2,0:T(8,128)(2,1)S(1)} %gather_fusion.2), channel_id=1, source_target_pairs={{0,16},{4,20},{8,24},{12,28},{16,0},{20,4},{24,8},{28,12},{1,17},{... | collective-permute-start | bytes 196616 | tf_op jit(solution)/shard_map/ppermute | solution.py:242
  64.6 2.9 %copy-start.9 = (s32[4]{0:T(128)S(1)}, s32[4]{0:T(128)}, u32[]{:S(2)}) copy-start(s32[4]{0:T(128)} %constant.144) | copy-start | bytes 52
  64.6 13.2 %all-to-all-start.2 = ((bf16[128,2,128,4]{2,3,1,0:T(4,128)(2,1)}), bf16[128,2,128,4]{2,3,1,0:T(4,128)(2,1)S(1)}, u32[]{:S(2)}, u32[]{:S(2)}) async-start(bf16[128,2,128,4]{2,3,1,0:T(4,128)(2,1)} %copy.227), calls=%async_computation.2 | async-start | bytes 524288 | tf_op jit(solution)/shard_map/all_to_all | solution.py:260
  68.2 0.6 copy-start.6
  80.0 12.9 %all-to-all-start.3 = ((f32[32,1,2048]{2,1,0:T(1,128)}), f32[32,1,2048]{2,1,0:T(1,128)S(1)}, u32[]{:S(2)}, u32[]{:S(2)}) async-start(f32[32,1,2048]{2,1,0:T(1,128)} %reshape.493), calls=%async_computation.3 | async-start | bytes 524288 | tf_op jit(solution)/shard_map/all_to_all | solution.py:272
  83.7 0.8 copy-start.21
  95.4 0.8 copy-start.5

commit v10 on v8

--- a/solution.py
+++ b/solution.py
@@ -178,22 +178,23 @@
         normed_first.reshape(-1, channels), col_bias_proj, preferred_element_type=jnp.float32
     )
     bias_next = bias_next.reshape(rows_here, length, head_count).transpose(2, 0, 1)
+    lanes = 128
     pair_chunks = (
         first_pair.reshape(rows_here, n_col, n_row, rows_here, channels)
         .transpose(2, 1, 0, 3, 4)
-        .reshape(device_count, rows_here * rows_here * channels)
+        .reshape(device_count, rows_here * rows_here * channels // lanes, lanes)
     )
     bias_high = bias_next.astype(jnp.bfloat16)
     bias_low = (bias_next - bias_high.astype(jnp.float32)).astype(jnp.bfloat16)
-    bias_words = jnp.stack([bias_high, bias_low], axis=0).reshape(1, -1)
-    bias_chunks = jnp.broadcast_to(bias_words, (device_count, bias_words.shape[1]))
+    bias_words = jnp.stack([bias_high, bias_low], axis=0).reshape(1, -1, lanes)
+    bias_chunks = jnp.broadcast_to(bias_words, (device_count,) + bias_words.shape[1:])
     merged = lax.all_to_all(
         jnp.concatenate([pair_chunks, bias_chunks], axis=1), ("row", "col"), 0, 0, tiled=True
     )
-    pair_size = rows_here * rows_here * channels
-    columns = merged[:, :pair_size].reshape(length, rows_here, channels)
+    pair_rows = pair_chunks.shape[1]
+    columns = merged[:, :pair_rows].reshape(length, rows_here, channels)
     bias_got = (
-        merged[:, pair_size:]
+        merged[:, pair_rows:]
         .reshape(device_count, 2, head_count, rows_here, length)
         .astype(jnp.float32)
     )
@@ -256,7 +257,9 @@
         .transpose(1, 3, 0, 2, 4)
         .reshape(device_count, channels_here, block_rows, block_cols)
     )
-    product_got = lax.all_to_all(product_sent, ("row", "col"), 0, 1, tiled=True)
+    product_got = lax.all_to_all(
+        product_sent.reshape(device_count, -1, lanes), ("row", "col"), 0, 0, tiled=True
+    )
     product_sum = product_got.reshape(channels, block_rows, block_cols).transpose(1, 2, 0)
     normed_own = layer_norm(own_pair).astype(jnp.bfloat16)
     gate_values = jax.nn.sigmoid(

time: 90.6 us -> 90.7 us (level)
  matrix products: 6.69 us -> 10.3 us
  local copies, waits for them, and re-layouts: 16.4 us -> 14.6 us
  other arithmetic: 6.73 us -> 5.07 us
    unnamed x38 -> x37, local copies, waits for them, and re-layouts: 9.96 us -> 6.3 us
    all_to_all x3 -> x0, other arithmetic: 2.22 us -> none  [the longest x1 1.26 us: shards(): product_got = lax.all_to_all(product_sent, ('row', 'col'), 0, 1, tiled=True)]
    dot_general x2, matrix products: 0.8 us -> 2.78 us  [one_block(): jnp.einsum(f'{spec_q},{spec_k}->lhqk', query_block, key_rows, preferred_e...]
    all_to_all x2 -> x0, local copies, waits for them, and re-layouts: 1.1 us -> none  [the longest x1 0.59 us: shards(): lax.all_to_all(jnp.concatenate([pair_chunks, bias_chunks], axis=1), ('row...]
    another operation x1 -> x2, local copies, waits for them, and re-layouts: 0.01 us -> 0.98 us  [the longest x1 0.98 us: shards(): product_sent.reshape(device_count, -1, lanes)]
    reshape x2, local copies, waits for them, and re-layouts: 0.26 us -> 1.22 us  [one_block(): mixed_rows = mixed_rows.reshape(mixed_rows.shape[:2] + (width_all,))]
    sub x2, matrix products: 1.19 us -> 2.14 us  [one_block(): weights = jnp.exp(scores - row_peak)]
where the time goes in v10:
time: 90.7 us; the launch traced here: 89.8 us
  waiting for transfers between devices  33.7 us (37%)
  starting transfers between devices  24.8 us (27%)
  local copies, waits for them, and re-layouts  14.6 us (16%)
  matrix products  10.3 us (11%)
  other arithmetic  5.07 us (6%)
  between operations  1.4 us (2%)
    all_to_all x1, waiting for transfers between devices, shards(): lax.all_to_all(jnp.concatenate([pair_chunks, bias_chunks], axis=1), ('row...  11.7 us
    all_to_all x1, waiting for transfers between devices, shards(): lax.all_to_all(product_sent.reshape(device_count, -1, lanes), ('row', 'co...  8.34 us
    all_to_all x1, starting transfers between devices, gather_lines(): got = lax.all_to_all(sent, ('row', 'col'), 0, 0, tiled=True)  7.33 us
    all_to_all x1, waiting for transfers between devices, gather_lines(): got = lax.all_to_all(sent, ('row', 'col'), 0, 0, tiled=True)  7.2 us
    ppermute x7, starting transfers between devices, shards(): lax.ppermute(piece, 'row', perm=[(r, (r + shift) % n_row) for r in range(...  7.17 us
    unnamed x37, local copies, waits for them, and re-layouts  6.3 us
    all_to_all x1, starting transfers between devices, shards(): edges_got = lax.all_to_all(edges, ('row', 'col'), 0, 3, tiled=True)  4.98 us
    all_to_all x1, waiting for transfers between devices, shards(): edges_got = lax.all_to_all(edges, ('row', 'col'), 0, 3, tiled=True)  4.96 us
  transfers between devices with their start and end apart: 11, of which 6 were waited for; matrix products, arithmetic and copies ran while one was open for 6% of the time, Pallas kernels for 0%

profile of v10, /device:TPU:0, one launch (start us, length us, event | category | flops | bytes accessed | tf_op | source)
XLA Modules:
  0.0 89.8 jit_solution(8467950021288086087)
XLA Ops:
  0.0 1.1 %convert_reduce_fusion = f32[4,128]{1,0:T(4,128)S(1)} fusion(bf16[4,128,128]{2,1,0:T(8,128)(2,1)} %param.14), kind=kLoop, calls=%fused_computation.42 | loop fusion | flops 130560 | bytes 133120 | tf_op jit(solution)/shard_map/reduce_sum | solution.py:9
  1.4 0.7 copy-done.13
  2.0 0.3 convolution_bitcast_fusion.1
  2.4 0.7 broadcast_in_dim.33
  3.1 7.3 %all-to-all-start = ((f32[32,4,4,128]{3,2,1,0:T(4,128)}), f32[32,4,4,128]{3,2,1,0:T(4,128)S(1)}, u32[]{:S(2)}, u32[]{:S(2)}) async-start(f32[32,4,4,128]{3,2,1,0:T(4,128)} %broadcast_in_dim.33), calls=%async_computation | async-start | bytes 524288 | tf_op jit(solution)/shard_map/all_to_all | solution.py:112
  10.5 0.7 copy-done.9
  11.8 0.4 fusion.61
  12.6 0.6 copy-done.8
  13.5 7.2 %all-to-all-done = f32[32,4,4,128]{3,2,1,0:T(4,128)S(1)} async-done(((f32[32,4,4,128]{3,2,1,0:T(4,128)}), f32[32,4,4,128]{3,2,1,0:T(4,128)S(1)}, u32[]{:S(2)}, u32[]{:S(2)}) %all-to-all-start) | async-done | bytes 262176 | tf_op jit(solution)/shard_map/all_to_all | solution.py:112
  20.7 0.8 copy.122
  21.6 1.5 %fusion.103 = f32[4,4,128]{2,1,0:T(4,128)S(1)} fusion(f32[4,128,128]{1,2,0:T(8,128)S(1)} %get-tuple-element.13, f32[4,128,128]{1,2,0:T(8,128)} %copy.122, pred[4]{0:T(512)(128)(4,1)S(1)} %get-tuple-element.25, bf16[4,128,3,4,32]{1,4,3,2,0:T(8,128)(2,1)S(1)} %bitcast.199), kind=kOutput, calls=%fused_computation.207 | convolution fusion | flops 18350208 | bytes 795136 | tf_op jit(solution)/shard_map/sub | solution.py:83
  23.1 1.4 %fusion.8 = f32[4,4,128,128]{2,3,1,0:T(8,128)S(1)} fusion(f32[4,128,128]{1,2,0:T(8,128)} %copy-done.3, f32[4,128,128]{1,2,0:T(8,128)} %copy.122, pred[4]{0:T(512)(128)(4,1)S(1)} %get-tuple-element.25, bf16[4,128,3,4,32]{1,4,3,2,0:T(8,128)(2,1)S(1)} %bitcast.200), kind=kOutput, calls=%fused_computation.11 | convolution fusion | flops 17825792 | bytes 1835520 | tf_op jit(solution)/shard_map/lqhd,lkhd->lhqk/dot_general | solution.py:63
  24.5 1.0 %fusion.20 = f32[4,4,32,128]{3,2,1,0:T(8,128)} fusion(f32[4,4,128]{2,1,0:T(4,128)S(1)} %fusion.103, bf16[4,128,3,4,32]{1,4,3,2,0:T(8,128)(2,1)S(1)} %bitcast.201, f32[4,4,128,128]{2,3,1,0:T(8,128)S(1)} %fusion.8), kind=kOutput, calls=%fused_computation.38 | convolution fusion | flops 17565824 | bytes 2498560 | tf_op jit(solution)/shard_map/lhqk,lkhd->lqhd/dot_general | solution.py:85
  25.6 1.1 %copy.124 = f32[4,128,128]{2,1,0:T(8,128)S(1)} copy(f32[4,128,128]{1,2,0:T(8,128)} %bitcast.218) | data formatting | bytes 524288 | tf_op jit(solution)/shard_map/reshape | solution.py:88
  27.3 0.7 copy-done.14
  27.9 0.3 convert_bitcast_fusion.1
  28.4 0.8 pad_maximum_fusion
  29.1 2.7 %all-to-all-start.1 = ((bf16[32,48,128]{2,1,0:T(8,128)(2,1)}), bf16[32,48,128]{2,1,0:T(8,128)(2,1)S(1)}, u32[]{:S(2)}, u32[]{:S(2)}) async-start(bf16[32,48,128]{2,1,0:T(8,128)(2,1)} %pad_maximum_fusion), calls=%async_computation.1 | async-start | bytes 786432 | tf_op jit(solution)/shard_map/all_to_all | solution.py:191
  32.0 11.7 %all-to-all-done.1 = bf16[32,48,128]{2,1,0:T(8,128)(2,1)S(1)} async-done(((bf16[32,48,128]{2,1,0:T(8,128)(2,1)}), bf16[32,48,128]{2,1,0:T(8,128)(2,1)S(1)}, u32[]{:S(2)}, u32[]{:S(2)}) %all-to-all-start.1) | async-done | bytes 393248 | tf_op jit(solution)/shard_map/all_to_all | solution.py:191
  43.7 0.3 copy.132
  44.9 0.3 multiply_convert_fusion.2
  45.2 0.6 copy-done.4
  46.4 0.6 fusion.104
  47.0 1.4 %fusion.11 = f32[4,4,128,128]{2,3,1,0:T(8,128)S(1)} fusion(f32[4,128,128]{1,2,0:T(8,128)S(1)} %get-tuple-element.12, f32[4,128,128]{1,2,0:T(8,128)} %bitcast.214, pred[4]{0:T(512)(128)(4,1)S(1)} %get-tuple-element.24, bf16[128,4,3,4,32]{0,4,3,2,1:T(8,128)(2,1)S(1)} %bitcast.203), kind=kOutput, calls=%fused_computation.14 | convolution fusion | flops 17825792 | bytes 1835520 | tf_op jit(solution)/shard_map/qlhd,klhd->lhqk/dot_general | solution.py:63
  48.3 0.3 fusion.21
  48.8 0.6 copy-done.11
  49.8 1.3 %collective-permute-start = (bf16[16,4,128]{2,0,1:T(8,128)(2,1)S(1)}, bf16[16,4,128]{2,0,1:T(8,128)(2,1)S(1)}, u32[]{:S(2)}, u32[]{:S(2)}) collective-permute-start(bf16[16,4,128]{2,0,1:T(8,128)(2,1)S(1)} %get-tuple-element.11), channel_id=1, source_target_pairs={{0,4},{4,8},{8,12},{12,16},{16,20},{20,24},{24,28},{28,0},{1,5},{5... | collective-permute-start | bytes 49160 | tf_op jit(solution)/shard_map/ppermute | solution.py:241
  51.0 1.2 %collective-permute-start.1 = (bf16[16,4,128]{2,0,1:T(8,128)(2,1)S(1)}, bf16[16,4,128]{2,0,1:T(8,128)(2,1)S(1)}, u32[]{:S(2)}, u32[]{:S(2)}) collective-permute-start(bf16[16,4,128]{2,0,1:T(8,128)(2,1)S(1)} %get-tuple-element.10), channel_id=1, source_target_pairs={{0,8},{4,12},{8,16},{12,20},{16,24},{20,28},{24,0},{28,4},{1,9},{5... | collective-permute-start | bytes 49160 | tf_op jit(solution)/shard_map/ppermute | solution.py:241
  52.2 1.0 %collective-permute-start.2 = (bf16[16,4,128]{2,0,1:T(8,128)(2,1)S(1)}, bf16[16,4,128]{2,0,1:T(8,128)(2,1)S(1)}, u32[]{:S(2)}, u32[]{:S(2)}) collective-permute-start(bf16[16,4,128]{2,0,1:T(8,128)(2,1)S(1)} %get-tuple-element.9), channel_id=1, source_target_pairs={{0,12},{4,16},{8,20},{12,24},{16,28},{20,0},{24,4},{28,8},{1,13},{... | collective-permute-start | bytes 49160 | tf_op jit(solution)/shard_map/ppermute | solution.py:241
  53.2 1.0 %collective-permute-start.3 = (bf16[16,4,128]{2,0,1:T(8,128)(2,1)S(1)}, bf16[16,4,128]{2,0,1:T(8,128)(2,1)S(1)}, u32[]{:S(2)}, u32[]{:S(2)}) collective-permute-start(bf16[16,4,128]{2,0,1:T(8,128)(2,1)S(1)} %get-tuple-element.8), channel_id=1, source_target_pairs={{0,16},{4,20},{8,24},{12,28},{16,0},{20,4},{24,8},{28,12},{1,17},{... | collective-permute-start | bytes 49160 | tf_op jit(solution)/shard_map/ppermute | solution.py:241
  54.5 0.6 copy-done.5
  55.1 0.3 fusion.75
  55.4 0.5 copy-done.6
  55.9 0.3 fusion.73
  56.4 0.9 copy.145
  57.3 5.0 %all-to-all-start.2 = ((bf16[128,2,128,4]{2,3,1,0:T(4,128)(2,1)}), bf16[128,2,128,4]{2,3,1,0:T(4,128)(2,1)S(1)}, u32[]{:S(2)}, u32[]{:S(2)}) async-start(bf16[128,2,128,4]{2,3,1,0:T(4,128)(2,1)} %copy.145), calls=%async_computation.2 | async-start | bytes 524288 | tf_op jit(solution)/shard_map/all_to_all | solution.py:248
  62.3 2.7 %collective-permute-start.5 = (bf16[16,4,128]{2,0,1:T(8,128)(2,1)S(1)}, bf16[16,4,128]{2,0,1:T(8,128)(2,1)S(1)}, u32[]{:S(2)}, u32[]{:S(2)}) collective-permute-start(bf16[16,4,128]{2,0,1:T(8,128)(2,1)S(1)} %get-tuple-element.6), channel_id=1, source_target_pairs={{0,24},{4,28},{8,0},{12,4},{16,8},{20,12},{24,16},{28,20},{1,25},{... | collective-permute-start | bytes 49160 | tf_op jit(solution)/shard_map/ppermute | solution.py:241
  65.1 1.3 %collective-permute-done.5 = bf16[16,4,128]{2,0,1:T(8,128)(2,1)S(1)} collective-permute-done((bf16[16,4,128]{2,0,1:T(8,128)(2,1)S(1)}, bf16[16,4,128]{2,0,1:T(8,128)(2,1)S(1)}, u32[]{:S(2)}, u32[]{:S(2)}) %collective-permute-start.5) | collective-permute-done | bytes 16416 | tf_op jit(solution)/shard_map/ppermute | solution.py:241
  66.6 0.6 gather_fusion
  67.6 5.0 %all-to-all-done.2 = bf16[128,2,128,4]{2,3,1,0:T(4,128)(2,1)S(1)} async-done(((bf16[128,2,128,4]{2,3,1,0:T(4,128)(2,1)}), bf16[128,2,128,4]{2,3,1,0:T(4,128)(2,1)S(1)}, u32[]{:S(2)}, u32[]{:S(2)}) %all-to-all-start.2) | async-done | bytes 262176 | tf_op jit(solution)/shard_map/all_to_all | solution.py:248
  73.0 0.4 reshape.461
  73.6 1.0 %reshape_reshape.3 = f32[32,16,128]{2,1,0:T(8,128)} reshape(f32[8,4,4,16,32]{4,3,2,1,0:T(8,128)S(1)} %bitcast.195) | data formatting | bytes 524288 | tf_op jit(solution)/shard_map/reshape;reshape | solution.py:261
  74.6 2.7 %all-to-all-start.3 = ((f32[32,16,128]{2,1,0:T(8,128)}), f32[32,16,128]{2,1,0:T(8,128)S(1)}, u32[]{:S(2)}, u32[]{:S(2)}) async-start(f32[32,16,128]{2,1,0:T(8,128)} %reshape_reshape.3), calls=%async_computation.3 | async-start | bytes 524288 | tf_op jit(solution)/shard_map/all_to_all | solution.py:260
  78.2 0.6 copy-done.12
  78.8 0.3 fusion.15
  79.1 8.3 %all-to-all-done.3 = f32[32,16,128]{2,1,0:T(8,128)S(1)} async-done(((f32[32,16,128]{2,1,0:T(8,128)}), f32[32,16,128]{2,1,0:T(8,128)S(1)}, u32[]{:S(2)}, u32[]{:S(2)}) %all-to-all-start.3) | async-done | bytes 262176 | tf_op jit(solution)/shard_map/all_to_all | solution.py:260
  88.2 0.6 copy-done.7
  88.9 1.0 %fusion.18 = bf16[16,32,128]{2,1,0:T(8,128)(2,1)} fusion(f32[16,32,128]{2,1,0:T(8,128)S(1)} %bitcast.206, f32[16,32,128]{2,1,0:T(8,128)S(1)} %bitcast.217, bf16[16,32,128]{1,0,2:T(8,128)(2,1)S(1)} %multiply_convert_fusion, bf16[128,128]{1,0:T(8,128)(2,1)S(1)} %copy-done.7), kind=kOutput, calls=%fused_computation.25 | convolution fusion | flops 16973824 | bytes 819200 | tf_op jit(solution)/shard_map/dot_general | solution.py:269
  (103 shorter events, 6.7 us)
Async XLA Ops:
  0.0 11.8 %copy-start = (bf16[128,512]{1,0:T(8,128)(2,1)S(1)}, bf16[128,512]{1,0:T(8,128)(2,1)}, u32[]{:S(2)}) copy-start(bf16[128,512]{1,0:T(8,128)(2,1)} %param.18) | copy-start | bytes 393220
  0.0 1.1 %copy-start.1 = (bf16[4,128,128]{2,1,0:T(8,128)(2,1)S(1)}, bf16[4,128,128]{2,1,0:T(8,128)(2,1)}, u32[]{:S(2)}) copy-start(bf16[4,128,128]{2,1,0:T(8,128)(2,1)} %param.14) | copy-start | bytes 393220
  1.4 0.7 copy-start.13
  3.1 17.6 %all-to-all-start = ((f32[32,4,4,128]{3,2,1,0:T(4,128)}), f32[32,4,4,128]{3,2,1,0:T(4,128)S(1)}, u32[]{:S(2)}, u32[]{:S(2)}) async-start(f32[32,4,4,128]{3,2,1,0:T(4,128)} %broadcast_in_dim.33), calls=%async_computation | async-start | bytes 524288 | tf_op jit(solution)/shard_map/all_to_all | solution.py:112
  10.4 0.7 copy-start.9
  12.6 0.7 copy-start.8
  13.5 8.1 %copy-start.3 = (f32[4,128,128]{1,2,0:T(8,128)}, f32[4,128,128]{1,2,0:T(8,128)S(1)}, u32[]{:S(2)}) copy-start(f32[4,128,128]{1,2,0:T(8,128)S(1)} %get-tuple-element.13) | copy-start | bytes 786436
  25.6 1.1 %copy-start.10 = (bf16[128,128]{1,0:T(8,128)(2,1)S(1)}, bf16[128,128]{1,0:T(8,128)(2,1)}, u32[]{:S(2)}) copy-start(bf16[128,128]{1,0:T(8,128)(2,1)} %param.20) | copy-start | bytes 98308
  27.2 0.7 copy-start.14
  29.1 14.5 %all-to-all-start.1 = ((bf16[32,48,128]{2,1,0:T(8,128)(2,1)}), bf16[32,48,128]{2,1,0:T(8,128)(2,1)S(1)}, u32[]{:S(2)}, u32[]{:S(2)}) async-start(bf16[32,48,128]{2,1,0:T(8,128)(2,1)} %pad_maximum_fusion), calls=%async_computation.1 | async-start | bytes 786432 | tf_op jit(solution)/shard_map/all_to_all | solution.py:191
  44.2 2.1 %copy-start.2 = (f32[4,32,4,128]{3,2,1,0:T(4,128)}, f32[4,32,4,128]{3,2,1,0:T(4,128)S(1)}, u32[]{:S(2)}) copy-start(f32[4,32,4,128]{3,2,1,0:T(4,128)S(1)} %copy.133) | copy-start | bytes 786436
  44.9 0.9 %copy-start.4 = (bf16[128,512]{1,0:T(8,128)(2,1)S(1)}, bf16[128,512]{1,0:T(8,128)(2,1)}, u32[]{:S(2)}) copy-start(bf16[128,512]{1,0:T(8,128)(2,1)} %param.21) | copy-start | bytes 393220
  48.7 0.8 copy-start.11
  49.8 12.5 %collective-permute-start = (bf16[16,4,128]{2,0,1:T(8,128)(2,1)S(1)}, bf16[16,4,128]{2,0,1:T(8,128)(2,1)S(1)}, u32[]{:S(2)}, u32[]{:S(2)}) collective-permute-start(bf16[16,4,128]{2,0,1:T(8,128)(2,1)S(1)} %get-tuple-element.11), channel_id=1, source_target_pairs={{0,4},{4,8},{8,12},{12,16},{16,20},{20,24},{24,28},{28,0},{1,5},{5... | collective-permute-start | bytes 49160 | tf_op jit(solution)/shard_map/ppermute | solution.py:241
  51.0 14.0 %collective-permute-start.1 = (bf16[16,4,128]{2,0,1:T(8,128)(2,1)S(1)}, bf16[16,4,128]{2,0,1:T(8,128)(2,1)S(1)}, u32[]{:S(2)}, u32[]{:S(2)}) collective-permute-start(bf16[16,4,128]{2,0,1:T(8,128)(2,1)S(1)} %get-tuple-element.10), channel_id=1, source_target_pairs={{0,8},{4,12},{8,16},{12,20},{16,24},{20,28},{24,0},{28,4},{1,9},{5... | collective-permute-start | bytes 49160 | tf_op jit(solution)/shard_map/ppermute | solution.py:241
  52.2 12.8 %collective-permute-start.2 = (bf16[16,4,128]{2,0,1:T(8,128)(2,1)S(1)}, bf16[16,4,128]{2,0,1:T(8,128)(2,1)S(1)}, u32[]{:S(2)}, u32[]{:S(2)}) collective-permute-start(bf16[16,4,128]{2,0,1:T(8,128)(2,1)S(1)} %get-tuple-element.9), channel_id=1, source_target_pairs={{0,12},{4,16},{8,20},{12,24},{16,28},{20,0},{24,4},{28,8},{1,13},{... | collective-permute-start | bytes 49160 | tf_op jit(solution)/shard_map/ppermute | solution.py:241
  53.2 11.9 %collective-permute-start.3 = (bf16[16,4,128]{2,0,1:T(8,128)(2,1)S(1)}, bf16[16,4,128]{2,0,1:T(8,128)(2,1)S(1)}, u32[]{:S(2)}, u32[]{:S(2)}) collective-permute-start(bf16[16,4,128]{2,0,1:T(8,128)(2,1)S(1)} %get-tuple-element.8), channel_id=1, source_target_pairs={{0,16},{4,20},{8,24},{12,28},{16,0},{20,4},{24,8},{28,12},{1,17},{... | collective-permute-start | bytes 49160 | tf_op jit(solution)/shard_map/ppermute | solution.py:241
  54.2 10.9 %collective-permute-start.4 = (bf16[16,4,128]{2,0,1:T(8,128)(2,1)S(1)}, bf16[16,4,128]{2,0,1:T(8,128)(2,1)S(1)}, u32[]{:S(2)}, u32[]{:S(2)}) collective-permute-start(bf16[16,4,128]{2,0,1:T(8,128)(2,1)S(1)} %get-tuple-element.7), channel_id=1, source_target_pairs={{0,20},{4,24},{8,28},{12,0},{16,4},{20,8},{24,12},{28,16},{1,21},{... | collective-permute-start | bytes 49160 | tf_op jit(solution)/shard_map/ppermute | solution.py:241
  54.2 0.8 copy-start.5
  55.1 0.8 copy-start.6
  57.3 15.2 %all-to-all-start.2 = ((bf16[128,2,128,4]{2,3,1,0:T(4,128)(2,1)}), bf16[128,2,128,4]{2,3,1,0:T(4,128)(2,1)S(1)}, u32[]{:S(2)}, u32[]{:S(2)}) async-start(bf16[128,2,128,4]{2,3,1,0:T(4,128)(2,1)} %copy.145), calls=%async_computation.2 | async-start | bytes 524288 | tf_op jit(solution)/shard_map/all_to_all | solution.py:248
  62.3 4.2 %collective-permute-start.5 = (bf16[16,4,128]{2,0,1:T(8,128)(2,1)S(1)}, bf16[16,4,128]{2,0,1:T(8,128)(2,1)S(1)}, u32[]{:S(2)}, u32[]{:S(2)}) collective-permute-start(bf16[16,4,128]{2,0,1:T(8,128)(2,1)S(1)} %get-tuple-element.6), channel_id=1, source_target_pairs={{0,24},{4,28},{8,0},{12,4},{16,8},{20,12},{24,16},{28,20},{1,25},{... | collective-permute-start | bytes 49160 | tf_op jit(solution)/shard_map/ppermute | solution.py:241
  65.0 1.6 %collective-permute-start.6 = (bf16[16,4,128]{2,0,1:T(8,128)(2,1)S(1)}, bf16[16,4,128]{2,0,1:T(8,128)(2,1)S(1)}, u32[]{:S(2)}, u32[]{:S(2)}) collective-permute-start(bf16[16,4,128]{2,0,1:T(8,128)(2,1)S(1)} %get-tuple-element.5), channel_id=1, source_target_pairs={{0,28},{4,0},{8,4},{12,8},{16,12},{20,16},{24,20},{28,24},{1,29},{... | collective-permute-start | bytes 49160 | tf_op jit(solution)/shard_map/ppermute | solution.py:241
  74.6 12.9 %all-to-all-start.3 = ((f32[32,16,128]{2,1,0:T(8,128)}), f32[32,16,128]{2,1,0:T(8,128)S(1)}, u32[]{:S(2)}, u32[]{:S(2)}) async-start(f32[32,16,128]{2,1,0:T(8,128)} %reshape_reshape.3), calls=%async_computation.3 | async-start | bytes 524288 | tf_op jit(solution)/shard_map/all_to_all | solution.py:260
  78.0 0.8 copy-start.12
  88.1 0.8 copy-start.7

commit v11 on v10

--- a/solution.py
+++ b/solution.py
@@ -56,6 +56,10 @@
     spec_q = "lqhd" if line_dim == 0 else "qlhd"
     spec_k = "lkhd" if line_dim == 0 else "klhd"
     usable = key_ok[:, None, None, :]
+    if flipped:
+        bias_all = bias_all.transpose(0, 2, 1)
+    same_all = (chain_ids[:, None] == chain_ids[None, :]).astype(jnp.float32)
+    bias_all = bias_all + chain_add[:, None, None] * same_all[None]
 
     def one_block(offset):
         query_block = lax.dynamic_slice_in_dim(queries, offset, query_rows, 1 - line_dim)
@@ -68,16 +72,8 @@
             )
             * scaling
         )
-        if flipped:
-            bias_block = lax.dynamic_slice_in_dim(bias_all, offset, query_rows, 2).transpose(
-                0, 2, 1
-            )
-        else:
-            bias_block = lax.dynamic_slice_in_dim(bias_all, offset, query_rows, 1)
+        bias_block = lax.dynamic_slice_in_dim(bias_all, offset, query_rows, 1)
         scores = scores + bias_block[None]
-        chain_block = lax.dynamic_slice_in_dim(chain_ids, offset, query_rows, 0)
-        same_chain = (chain_block[:, None] == chain_ids[None, :]).astype(jnp.float32)
-        scores = scores + (chain_add[:, None, None] * same_chain[None])[None]
         scores = jnp.where(usable, scores, -1000000000.0)
         row_peak = jnp.max(scores, axis=-1, keepdims=True)
         weights = jnp.exp(scores - row_peak)

time: 90.7 us -> 85.9 us (0.947)
  waiting for transfers between devices: 33.7 us -> 29 us
  starting transfers between devices: 24.8 us -> 28.1 us
  matrix products: 10.3 us -> 7.27 us
    all_to_all x1, waiting for transfers between devices: 4.96 us -> 0.01 us  [shards(): edges_got = lax.all_to_all(edges, ('row', 'col'), 0, 3, tiled=True)]
    all_to_all x1, starting transfers between devices: 2.66 us -> 5.77 us  [shards(): lax.all_to_all(product_sent.reshape(device_count, -1, lanes), ('row', 'co...]
    dot_general x2, matrix products: 2.78 us -> 0.73 us  [one_block(): jnp.einsum(f'{spec_q},{spec_k}->lhqk', query_block, key_rows, preferred_e...]
    ppermute x7, starting transfers between devices: 7.17 us -> 8.58 us  [shards(): lax.ppermute(piece, 'row', perm=[(r, (r + shift) % n_row) for r in range(...]
    all_to_all x1, starting transfers between devices: 4.98 us -> 3.81 us  [shards(): edges_got = lax.all_to_all(edges, ('row', 'col'), 0, 3, tiled=True)]
    sub x2, matrix products: 2.14 us -> 1.13 us  [one_block(): weights = jnp.exp(scores - row_peak)]
  transfers between devices with their start and end apart: 11 -> 11, of which waited for: 6 -> 4; matrix products, arithmetic and copies ran while one was open for 6% -> 4% of each run, Pallas kernels for 0% -> 0%
where the time goes in v11:
time: 85.9 us; the launch traced here: 85.1 us
  waiting for transfers between devices  29 us (34%)
  starting transfers between devices  28.1 us (33%)
  local copies, waits for them, and re-layouts  14.2 us (17%)
  matrix products  7.27 us (8%)
  other arithmetic  5.17 us (6%)
  between operations  1.39 us (2%)
    all_to_all x1, waiting for transfers between devices, shards(): lax.all_to_all(jnp.concatenate([pair_chunks, bias_chunks], axis=1), ('row...  11.7 us
    ppermute x7, starting transfers between devices, shards(): lax.ppermute(piece, 'row', perm=[(r, (r + shift) % n_row) for r in range(...  8.58 us
    all_to_all x1, waiting for transfers between devices, shards(): lax.all_to_all(product_sent.reshape(device_count, -1, lanes), ('row', 'co...  8.53 us
    all_to_all x1, waiting for transfers between devices, gather_lines(): got = lax.all_to_all(sent, ('row', 'col'), 0, 0, tiled=True)  7.35 us
    all_to_all x1, starting transfers between devices, gather_lines(): got = lax.all_to_all(sent, ('row', 'col'), 0, 0, tiled=True)  7.33 us
    unnamed x37, local copies, waits for them, and re-layouts  6.36 us
    all_to_all x1, starting transfers between devices, shards(): lax.all_to_all(product_sent.reshape(device_count, -1, lanes), ('row', 'co...  5.77 us
    all_to_all x1, starting transfers between devices, shards(): edges_got = lax.all_to_all(edges, ('row', 'col'), 0, 3, tiled=True)  3.81 us
  transfers between devices with their start and end apart: 11, of which 4 were waited for; matrix products, arithmetic and copies ran while one was open for 4% of the time, Pallas kernels for 0%

profile of v11, /device:TPU:0, one launch (start us, length us, event | category | flops | bytes accessed | tf_op | source)
XLA Modules:
  0.0 85.1 jit_solution(16144681690534049723)
XLA Ops:
  0.0 1.1 %convert_reduce_fusion = f32[4,128]{1,0:T(4,128)S(1)} fusion(bf16[4,128,128]{2,1,0:T(8,128)(2,1)} %param.14), kind=kLoop, calls=%fused_computation.40 | loop fusion | flops 130560 | bytes 133120 | tf_op jit(solution)/shard_map/reduce_sum | solution.py:9
  1.4 0.7 copy-done.13
  2.0 0.3 convolution_bitcast_fusion.1
  2.4 0.7 broadcast_in_dim.33
  3.1 7.3 %all-to-all-start = ((f32[32,4,4,128]{3,2,1,0:T(4,128)}), f32[32,4,4,128]{3,2,1,0:T(4,128)S(1)}, u32[]{:S(2)}, u32[]{:S(2)}) async-start(f32[32,4,4,128]{3,2,1,0:T(4,128)} %broadcast_in_dim.33), calls=%async_computation | async-start | bytes 524288 | tf_op jit(solution)/shard_map/all_to_all | solution.py:108
  11.2 0.4 fusion.59
  11.9 0.6 copy-done.9
  12.6 0.6 copy-done.8
  13.3 7.4 %all-to-all-done = f32[32,4,4,128]{3,2,1,0:T(4,128)S(1)} async-done(((f32[32,4,4,128]{3,2,1,0:T(4,128)}), f32[32,4,4,128]{3,2,1,0:T(4,128)S(1)}, u32[]{:S(2)}, u32[]{:S(2)}) %all-to-all-start) | async-done | bytes 262176 | tf_op jit(solution)/shard_map/all_to_all | solution.py:108
  20.9 0.4 fusion.7
  21.3 0.6 fusion.101
  21.9 0.3 fusion.18
  22.4 0.6 copy-done.10
  23.6 0.7 copy-done.14
  24.2 0.3 convert_bitcast_fusion.1
  24.7 0.8 pad_maximum_fusion
  25.5 2.7 %all-to-all-start.1 = ((bf16[32,48,128]{2,1,0:T(8,128)(2,1)}), bf16[32,48,128]{2,1,0:T(8,128)(2,1)S(1)}, u32[]{:S(2)}, u32[]{:S(2)}) async-start(bf16[32,48,128]{2,1,0:T(8,128)(2,1)} %pad_maximum_fusion), calls=%async_computation.1 | async-start | bytes 786432 | tf_op jit(solution)/shard_map/all_to_all | solution.py:187
  28.3 11.7 %all-to-all-done.1 = bf16[32,48,128]{2,1,0:T(8,128)(2,1)S(1)} async-done(((bf16[32,48,128]{2,1,0:T(8,128)(2,1)}), bf16[32,48,128]{2,1,0:T(8,128)(2,1)S(1)}, u32[]{:S(2)}, u32[]{:S(2)}) %all-to-all-start.1) | async-done | bytes 393248 | tf_op jit(solution)/shard_map/all_to_all | solution.py:187
  40.6 0.3 multiply_convert_fusion.2
  40.9 0.3 copy-done.2
  41.3 0.3 copy-done.4
  42.2 0.3 copy.138
  43.1 0.4 fusion.9
  43.5 0.6 fusion.102
  44.1 1.1 %fusion.19 = f32[4,4,32,128]{3,2,1,0:T(8,128)} fusion(f32[4,4,128]{2,1,0:T(4,128)S(1)} %fusion.102, bf16[128,4,3,4,32]{0,4,3,2,1:T(8,128)(2,1)S(1)} %bitcast.204, f32[4,4,128,128]{2,3,1,0:T(8,128)S(1)} %fusion.9), kind=kOutput, calls=%fused_computation.37 | convolution fusion | flops 17565824 | bytes 2498560 | tf_op jit(solution)/shard_map/lhqk,klhd->qlhd/dot_general | solution.py:81
  45.1 1.1 %copy.143 = f32[128,4,128]{2,0,1:T(8,128)S(1)} copy(f32[128,4,128]{0,2,1:T(8,128)} %bitcast.218) | data formatting | bytes 524288 | tf_op jit(solution)/shard_map/reshape | solution.py:84
  46.8 0.6 copy-done.5
  47.4 0.3 fusion.71
  47.7 0.5 copy-done.6
  48.3 0.3 fusion.73
  48.8 0.9 %copy.153 = bf16[128,2,128,4]{2,3,1,0:T(4,128)(2,1)} copy(bf16[128,2,128,4]{0,2,3,1:T(8,128)(2,1)S(1)} %maximum_bitcast_fusion) | data formatting | bytes 524288 | tf_op jit(solution)/shard_map/transpose | solution.py:243
  49.7 3.8 %all-to-all-start.2 = ((bf16[128,2,128,4]{2,3,1,0:T(4,128)(2,1)}), bf16[128,2,128,4]{2,3,1,0:T(4,128)(2,1)S(1)}, u32[]{:S(2)}, u32[]{:S(2)}) async-start(bf16[128,2,128,4]{2,3,1,0:T(4,128)(2,1)} %copy.153), calls=%async_computation.2 | async-start | bytes 524288 | tf_op jit(solution)/shard_map/all_to_all | solution.py:244
  53.5 0.3 collective-permute-start
  53.8 1.6 %collective-permute-start.1 = (bf16[16,4,128]{2,0,1:T(8,128)(2,1)S(1)}, bf16[16,4,128]{2,0,1:T(8,128)(2,1)S(1)}, u32[]{:S(2)}, u32[]{:S(2)}) collective-permute-start(bf16[16,4,128]{2,0,1:T(8,128)(2,1)S(1)} %get-tuple-element.10), channel_id=1, source_target_pairs={{0,8},{4,12},{8,16},{12,20},{16,24},{20,28},{24,0},{28,4},{1,9},{5... | collective-permute-start | bytes 49160 | tf_op jit(solution)/shard_map/ppermute | solution.py:237
  55.5 2.3 %collective-permute-start.2 = (bf16[16,4,128]{2,0,1:T(8,128)(2,1)S(1)}, bf16[16,4,128]{2,0,1:T(8,128)(2,1)S(1)}, u32[]{:S(2)}, u32[]{:S(2)}) collective-permute-start(bf16[16,4,128]{2,0,1:T(8,128)(2,1)S(1)} %get-tuple-element.9), channel_id=1, source_target_pairs={{0,12},{4,16},{8,20},{12,24},{16,28},{20,0},{24,4},{28,8},{1,13},{... | collective-permute-start | bytes 49160 | tf_op jit(solution)/shard_map/ppermute | solution.py:237
  57.7 0.6 collective-permute-start.3
  58.4 1.5 %collective-permute-start.5 = (bf16[16,4,128]{2,0,1:T(8,128)(2,1)S(1)}, bf16[16,4,128]{2,0,1:T(8,128)(2,1)S(1)}, u32[]{:S(2)}, u32[]{:S(2)}) collective-permute-start(bf16[16,4,128]{2,0,1:T(8,128)(2,1)S(1)} %get-tuple-element.6), channel_id=1, source_target_pairs={{0,24},{4,28},{8,0},{12,4},{16,8},{20,12},{24,16},{28,20},{1,25},{... | collective-permute-start | bytes 49160 | tf_op jit(solution)/shard_map/ppermute | solution.py:237
  59.9 2.2 %collective-permute-start.6 = (bf16[16,4,128]{2,0,1:T(8,128)(2,1)S(1)}, bf16[16,4,128]{2,0,1:T(8,128)(2,1)S(1)}, u32[]{:S(2)}, u32[]{:S(2)}) collective-permute-start(bf16[16,4,128]{2,0,1:T(8,128)(2,1)S(1)} %get-tuple-element.5), channel_id=1, source_target_pairs={{0,28},{4,0},{8,4},{12,8},{16,12},{20,16},{24,20},{28,24},{1,29},{... | collective-permute-start | bytes 49160 | tf_op jit(solution)/shard_map/ppermute | solution.py:237
  62.2 1.4 %collective-permute-done.6 = bf16[16,4,128]{2,0,1:T(8,128)(2,1)S(1)} collective-permute-done((bf16[16,4,128]{2,0,1:T(8,128)(2,1)S(1)}, bf16[16,4,128]{2,0,1:T(8,128)(2,1)S(1)}, u32[]{:S(2)}, u32[]{:S(2)}) %collective-permute-start.6) | collective-permute-done | bytes 16416 | tf_op jit(solution)/shard_map/ppermute | solution.py:237
  63.6 0.6 gather_fusion
  65.2 0.4 reshape.468
  65.8 1.0 %reshape_reshape.3 = f32[32,16,128]{2,1,0:T(8,128)} reshape(f32[8,4,4,16,32]{4,3,2,1,0:T(8,128)S(1)} %bitcast.195) | data formatting | bytes 524288 | tf_op jit(solution)/shard_map/reshape;reshape | solution.py:257
  66.8 5.8 %all-to-all-start.3 = ((f32[32,16,128]{2,1,0:T(8,128)}), f32[32,16,128]{2,1,0:T(8,128)S(1)}, u32[]{:S(2)}, u32[]{:S(2)}) async-start(f32[32,16,128]{2,1,0:T(8,128)} %reshape_reshape.3), calls=%async_computation.3 | async-start | bytes 524288 | tf_op jit(solution)/shard_map/all_to_all | solution.py:256
  73.3 0.6 copy-done.12
  73.9 0.3 fusion.13
  74.2 8.5 %all-to-all-done.3 = f32[32,16,128]{2,1,0:T(8,128)S(1)} async-done(((f32[32,16,128]{2,1,0:T(8,128)}), f32[32,16,128]{2,1,0:T(8,128)S(1)}, u32[]{:S(2)}, u32[]{:S(2)}) %all-to-all-start.3) | async-done | bytes 262176 | tf_op jit(solution)/shard_map/all_to_all | solution.py:256
  83.5 0.6 copy-done.7
  84.2 1.0 %fusion.16 = bf16[16,32,128]{2,1,0:T(8,128)(2,1)} fusion(f32[16,32,128]{2,1,0:T(8,128)S(1)} %bitcast.206, f32[16,32,128]{2,1,0:T(8,128)S(1)} %bitcast.216, bf16[16,32,128]{1,0,2:T(8,128)(2,1)S(1)} %multiply_convert_fusion, bf16[128,128]{1,0:T(8,128)(2,1)S(1)} %copy-done.7), kind=kOutput, calls=%fused_computation.23 | convolution fusion | flops 16973824 | bytes 819200 | tf_op jit(solution)/shard_map/dot_general | solution.py:265
  (106 shorter events, 7.1 us)
Async XLA Ops:
  0.0 11.2 %copy-start = (bf16[128,512]{1,0:T(8,128)(2,1)S(1)}, bf16[128,512]{1,0:T(8,128)(2,1)}, u32[]{:S(2)}) copy-start(bf16[128,512]{1,0:T(8,128)(2,1)} %param.18) | copy-start | bytes 393220
  0.0 1.1 %copy-start.1 = (bf16[4,128,128]{2,1,0:T(8,128)(2,1)S(1)}, bf16[4,128,128]{2,1,0:T(8,128)(2,1)}, u32[]{:S(2)}) copy-start(bf16[4,128,128]{2,1,0:T(8,128)(2,1)} %param.14) | copy-start | bytes 393220
  1.4 0.7 copy-start.13
  3.1 17.6 %all-to-all-start = ((f32[32,4,4,128]{3,2,1,0:T(4,128)}), f32[32,4,4,128]{3,2,1,0:T(4,128)S(1)}, u32[]{:S(2)}, u32[]{:S(2)}) async-start(f32[32,4,4,128]{3,2,1,0:T(4,128)} %broadcast_in_dim.33), calls=%async_computation | async-start | bytes 524288 | tf_op jit(solution)/shard_map/all_to_all | solution.py:108
  11.9 0.7 copy-start.9
  12.6 0.7 copy-start.8
  22.2 0.8 copy-start.10
  23.6 0.7 copy-start.14
  25.5 14.5 %all-to-all-start.1 = ((bf16[32,48,128]{2,1,0:T(8,128)(2,1)}), bf16[32,48,128]{2,1,0:T(8,128)(2,1)S(1)}, u32[]{:S(2)}, u32[]{:S(2)}) async-start(bf16[32,48,128]{2,1,0:T(8,128)(2,1)} %pad_maximum_fusion), calls=%async_computation.1 | async-start | bytes 786432 | tf_op jit(solution)/shard_map/all_to_all | solution.py:187
  40.6 0.7 copy-start.2
  40.6 1.0 %copy-start.4 = (bf16[128,512]{1,0:T(8,128)(2,1)S(1)}, bf16[128,512]{1,0:T(8,128)(2,1)}, u32[]{:S(2)}) copy-start(bf16[128,512]{1,0:T(8,128)(2,1)} %param.21) | copy-start | bytes 393220
  45.1 1.1 %copy-start.3 = (f32[32,16,128]{2,1,0:T(8,128)S(1)}, f32[32,16,128]{2,1,0:T(8,128)}, u32[]{:S(2)}) copy-start(f32[32,16,128]{2,1,0:T(8,128)} %copy-done.2) | copy-start | bytes 786436
  45.1 1.1 %copy-start.11 = (bf16[128,128]{1,0:T(8,128)(2,1)S(1)}, bf16[128,128]{1,0:T(8,128)(2,1)}, u32[]{:S(2)}) copy-start(bf16[128,128]{1,0:T(8,128)(2,1)} %param.23) | copy-start | bytes 98308
  46.6 0.8 copy-start.5
  47.4 0.8 copy-start.6
  49.7 15.0 %all-to-all-start.2 = ((bf16[128,2,128,4]{2,3,1,0:T(4,128)(2,1)}), bf16[128,2,128,4]{2,3,1,0:T(4,128)(2,1)S(1)}, u32[]{:S(2)}, u32[]{:S(2)}) async-start(bf16[128,2,128,4]{2,3,1,0:T(4,128)(2,1)} %copy.153), calls=%async_computation.2 | async-start | bytes 524288 | tf_op jit(solution)/shard_map/all_to_all | solution.py:244
  53.5 4.9 %collective-permute-start = (bf16[16,4,128]{2,0,1:T(8,128)(2,1)S(1)}, bf16[16,4,128]{2,0,1:T(8,128)(2,1)S(1)}, u32[]{:S(2)}, u32[]{:S(2)}) collective-permute-start(bf16[16,4,128]{2,0,1:T(8,128)(2,1)S(1)} %get-tuple-element.11), channel_id=1, source_target_pairs={{0,4},{4,8},{8,12},{12,16},{16,20},{20,24},{24,28},{28,0},{1,5},{5... | collective-permute-start | bytes 49160 | tf_op jit(solution)/shard_map/ppermute | solution.py:237
  53.8 6.0 %collective-permute-start.1 = (bf16[16,4,128]{2,0,1:T(8,128)(2,1)S(1)}, bf16[16,4,128]{2,0,1:T(8,128)(2,1)S(1)}, u32[]{:S(2)}, u32[]{:S(2)}) collective-permute-start(bf16[16,4,128]{2,0,1:T(8,128)(2,1)S(1)} %get-tuple-element.10), channel_id=1, source_target_pairs={{0,8},{4,12},{8,16},{12,20},{16,24},{20,28},{24,0},{28,4},{1,9},{5... | collective-permute-start | bytes 49160 | tf_op jit(solution)/shard_map/ppermute | solution.py:237
  55.5 6.7 %collective-permute-start.2 = (bf16[16,4,128]{2,0,1:T(8,128)(2,1)S(1)}, bf16[16,4,128]{2,0,1:T(8,128)(2,1)S(1)}, u32[]{:S(2)}, u32[]{:S(2)}) collective-permute-start(bf16[16,4,128]{2,0,1:T(8,128)(2,1)S(1)} %get-tuple-element.9), channel_id=1, source_target_pairs={{0,12},{4,16},{8,20},{12,24},{16,28},{20,0},{24,4},{28,8},{1,13},{... | collective-permute-start | bytes 49160 | tf_op jit(solution)/shard_map/ppermute | solution.py:237
  57.7 4.4 %collective-permute-start.3 = (bf16[16,4,128]{2,0,1:T(8,128)(2,1)S(1)}, bf16[16,4,128]{2,0,1:T(8,128)(2,1)S(1)}, u32[]{:S(2)}, u32[]{:S(2)}) collective-permute-start(bf16[16,4,128]{2,0,1:T(8,128)(2,1)S(1)} %get-tuple-element.8), channel_id=1, source_target_pairs={{0,16},{4,20},{8,24},{12,28},{16,0},{20,4},{24,8},{28,12},{1,17},{... | collective-permute-start | bytes 49160 | tf_op jit(solution)/shard_map/ppermute | solution.py:237
  58.3 3.9 %collective-permute-start.4 = (bf16[16,4,128]{2,0,1:T(8,128)(2,1)S(1)}, bf16[16,4,128]{2,0,1:T(8,128)(2,1)S(1)}, u32[]{:S(2)}, u32[]{:S(2)}) collective-permute-start(bf16[16,4,128]{2,0,1:T(8,128)(2,1)S(1)} %get-tuple-element.7), channel_id=1, source_target_pairs={{0,20},{4,24},{8,28},{12,0},{16,4},{20,8},{24,12},{28,16},{1,21},{... | collective-permute-start | bytes 49160 | tf_op jit(solution)/shard_map/ppermute | solution.py:237
  58.4 3.8 %collective-permute-start.5 = (bf16[16,4,128]{2,0,1:T(8,128)(2,1)S(1)}, bf16[16,4,128]{2,0,1:T(8,128)(2,1)S(1)}, u32[]{:S(2)}, u32[]{:S(2)}) collective-permute-start(bf16[16,4,128]{2,0,1:T(8,128)(2,1)S(1)} %get-tuple-element.6), channel_id=1, source_target_pairs={{0,24},{4,28},{8,0},{12,4},{16,8},{20,12},{24,16},{28,20},{1,25},{... | collective-permute-start | bytes 49160 | tf_op jit(solution)/shard_map/ppermute | solution.py:237
  59.9 3.7 %collective-permute-start.6 = (bf16[16,4,128]{2,0,1:T(8,128)(2,1)S(1)}, bf16[16,4,128]{2,0,1:T(8,128)(2,1)S(1)}, u32[]{:S(2)}, u32[]{:S(2)}) collective-permute-start(bf16[16,4,128]{2,0,1:T(8,128)(2,1)S(1)} %get-tuple-element.5), channel_id=1, source_target_pairs={{0,28},{4,0},{8,4},{12,8},{16,12},{20,16},{24,20},{28,24},{1,29},{... | collective-permute-start | bytes 49160 | tf_op jit(solution)/shard_map/ppermute | solution.py:237
  66.8 16.0 %all-to-all-start.3 = ((f32[32,16,128]{2,1,0:T(8,128)}), f32[32,16,128]{2,1,0:T(8,128)S(1)}, u32[]{:S(2)}, u32[]{:S(2)}) async-start(f32[32,16,128]{2,1,0:T(8,128)} %reshape_reshape.3), calls=%async_computation.3 | async-start | bytes 524288 | tf_op jit(solution)/shard_map/all_to_all | solution.py:256
  73.1 0.8 copy-start.12
  83.4 0.8 copy-start.7

commit v12 on v11

--- a/solution.py
+++ b/solution.py
@@ -229,15 +229,9 @@
     edge_mask = tile_pairs(jnp.arange(length, dtype=jnp.int32), local_cols, tile_mask, length)
     left_all = tri_acts(normed_second, tri_left, edge_mask)
     right_all = tri_acts(normed_second, tri_right, edge_mask)
-    raw_chunks = second_pair.reshape(n_row, block_rows, rows_here, channels)
-    raw_pieces = [lax.dynamic_index_in_dim(raw_chunks, row_index, 0, keepdims=False)]
-    for shift in range(1, n_row):
-        piece = lax.dynamic_index_in_dim(raw_chunks, (row_index + shift) % n_row, 0, keepdims=False)
-        raw_pieces.append(
-            lax.ppermute(piece, "row", perm=[(r, (r + shift) % n_row) for r in range(n_row)])
-        )
-    sources = (row_index - jnp.arange(n_row, dtype=jnp.int32)) % n_row
-    raw_got = jnp.take(jnp.stack(raw_pieces, axis=0), sources, axis=0)
+    raw_got = lax.all_to_all(
+        second_pair.reshape(n_row, block_rows, rows_here, channels), "row", 0, 0, tiled=True
+    )
     own_pair = raw_got.transpose(1, 0, 2, 3).reshape(block_rows, block_cols, channels)
     channels_here = channels // device_count
     edges = jnp.stack([left_all, right_all], axis=0).transpose(3, 0, 1, 2)

time: 85.9 us -> 88.6 us (1.031)
  waiting for transfers between devices: 29 us -> 41.5 us
  starting transfers between devices: 28.1 us -> 18.9 us
    all_to_all x1, waiting for transfers between devices: 0.01 us -> 9.24 us  [shards(): edges_got = lax.all_to_all(edges, ('row', 'col'), 0, 3, tiled=True)]
    ppermute x7 -> x0, starting transfers between devices: 8.58 us -> none  [shards(): lax.ppermute(piece, 'row', perm=[(r, (r + shift) % n_row) for r in range(...]
    all_to_all x0 -> x1, waiting for transfers between devices: none -> 4.35 us  [shards(): lax.all_to_all(second_pair.reshape(n_row, block_rows, rows_here, channels...]
    all_to_all x0 -> x1, starting transfers between devices: none -> 3.37 us  [shards(): lax.all_to_all(second_pair.reshape(n_row, block_rows, rows_here, channels...]
    all_to_all x1, starting transfers between devices: 5.77 us -> 2.66 us  [shards(): lax.all_to_all(product_sent.reshape(device_count, -1, lanes), ('row', 'co...]
    ppermute x7 -> x0, waiting for transfers between devices: 1.37 us -> none  [shards(): lax.ppermute(piece, 'row', perm=[(r, (r + shift) % n_row) for r in range(...]
    reshape x2, local copies, waits for them, and re-layouts: 1.26 us -> 0.27 us  [one_block(): mixed_rows = mixed_rows.reshape(mixed_rows.shape[:2] + (width_all,))]
    all_to_all x1, starting transfers between devices: 3.81 us -> 2.91 us  [shards(): edges_got = lax.all_to_all(edges, ('row', 'col'), 0, 3, tiled=True)]
  transfers between devices with their start and end apart: 11 -> 5, of which waited for: 4 -> 5; matrix products, arithmetic and copies ran while one was open for 4% -> 4% of each run, Pallas kernels for 0% -> 0%
where the time goes in v12:
time: 88.6 us; the launch traced here: 87.7 us
  waiting for transfers between devices  41.5 us (47%)
  starting transfers between devices  18.9 us (21%)
  local copies, waits for them, and re-layouts  14.4 us (16%)
  matrix products  6.56 us (7%)
  other arithmetic  5.16 us (6%)
  between operations  1.18 us (1%)
    all_to_all x1, waiting for transfers between devices, shards(): lax.all_to_all(jnp.concatenate([pair_chunks, bias_chunks], axis=1), ('row...  11.7 us
    all_to_all x1, waiting for transfers between devices, shards(): edges_got = lax.all_to_all(edges, ('row', 'col'), 0, 3, tiled=True)  9.24 us
    all_to_all x1, waiting for transfers between devices, shards(): lax.all_to_all(product_sent.reshape(device_count, -1, lanes), ('row', 'co...  8.64 us
    all_to_all x1, waiting for transfers between devices, gather_lines(): got = lax.all_to_all(sent, ('row', 'col'), 0, 0, tiled=True)  7.48 us
    all_to_all x1, starting transfers between devices, gather_lines(): got = lax.all_to_all(sent, ('row', 'col'), 0, 0, tiled=True)  7.33 us
    unnamed x30, local copies, waits for them, and re-layouts  7.11 us
    all_to_all x1, waiting for transfers between devices, shards(): lax.all_to_all(second_pair.reshape(n_row, block_rows, rows_here, channels...  4.35 us
    all_to_all x1, starting transfers between devices, shards(): lax.all_to_all(second_pair.reshape(n_row, block_rows, rows_here, channels...  3.37 us
  transfers between devices with their start and end apart: 5, of which 5 were waited for; matrix products, arithmetic and copies ran while one was open for 4% of the time, Pallas kernels for 0%

profile of v12, /device:TPU:0, one launch (start us, length us, event | category | flops | bytes accessed | tf_op | source)
XLA Modules:
  0.0 87.7 jit_solution(665996184860227028)
XLA Ops:
  0.0 1.1 %convert_reduce_fusion = f32[4,128]{1,0:T(4,128)S(1)} fusion(bf16[4,128,128]{2,1,0:T(8,128)(2,1)} %param.14), kind=kLoop, calls=%fused_computation.39 | loop fusion | flops 130560 | bytes 133120 | tf_op jit(solution)/shard_map/reduce_sum | solution.py:9
  1.4 0.7 copy-done.13
  2.0 0.3 convolution_bitcast_fusion.1
  2.4 0.7 broadcast_in_dim.25
  3.1 7.3 %all-to-all-start = ((f32[32,4,4,128]{3,2,1,0:T(4,128)}), f32[32,4,4,128]{3,2,1,0:T(4,128)S(1)}, u32[]{:S(2)}, u32[]{:S(2)}) async-start(f32[32,4,4,128]{3,2,1,0:T(4,128)} %broadcast_in_dim.25), calls=%async_computation | async-start | bytes 524288 | tf_op jit(solution)/shard_map/all_to_all | solution.py:108
  11.1 0.4 fusion.59
  11.8 0.6 copy-done.9
  12.4 0.6 copy-done.8
  13.2 7.5 %all-to-all-done = f32[32,4,4,128]{3,2,1,0:T(4,128)S(1)} async-done(((f32[32,4,4,128]{3,2,1,0:T(4,128)}), f32[32,4,4,128]{3,2,1,0:T(4,128)S(1)}, u32[]{:S(2)}, u32[]{:S(2)}) %all-to-all-start) | async-done | bytes 262176 | tf_op jit(solution)/shard_map/all_to_all | solution.py:108
  20.9 0.4 fusion.7
  21.3 0.6 fusion.96
  21.9 0.3 fusion.18
  22.4 0.6 copy-done.10
  23.0 0.3 convert_reduce_fusion.2
  23.6 0.7 copy-done.14
  24.2 0.3 convert_bitcast_fusion.1
  24.7 0.8 pad_maximum_fusion
  25.5 2.7 %all-to-all-start.1 = ((bf16[32,48,128]{2,1,0:T(8,128)(2,1)}), bf16[32,48,128]{2,1,0:T(8,128)(2,1)S(1)}, u32[]{:S(2)}, u32[]{:S(2)}) async-start(bf16[32,48,128]{2,1,0:T(8,128)(2,1)} %pad_maximum_fusion), calls=%async_computation.1 | async-start | bytes 786432 | tf_op jit(solution)/shard_map/all_to_all | solution.py:187
  28.2 11.7 %all-to-all-done.1 = bf16[32,48,128]{2,1,0:T(8,128)(2,1)S(1)} async-done(((bf16[32,48,128]{2,1,0:T(8,128)(2,1)}), bf16[32,48,128]{2,1,0:T(8,128)(2,1)S(1)}, u32[]{:S(2)}, u32[]{:S(2)}) %all-to-all-start.1) | async-done | bytes 393248 | tf_op jit(solution)/shard_map/all_to_all | solution.py:187
  40.6 0.3 multiply_convert_fusion.2
  40.9 0.3 copy-done.2
  41.3 0.3 copy-done.4
  41.6 0.3 fusion.57
  42.2 0.3 copy.170
  43.1 0.4 fusion.9
  43.5 0.6 fusion.97
  44.1 0.3 fusion.19
  44.5 0.8 copy-done.3
  45.4 0.3 convert_reduce_fusion.1
  45.9 0.6 copy-done.5
  46.5 0.3 fusion.71
  46.8 0.5 copy-done.6
  47.4 0.3 fusion.73
  47.7 0.8 copy.177
  48.4 3.4 %all-to-all-start.2 = ((bf16[8,16,4,128]{3,2,1,0:T(4,128)(2,1)}), bf16[8,16,4,128]{3,2,1,0:T(4,128)(2,1)S(1)}, u32[]{:S(2)}, u32[]{:S(2)}) async-start(bf16[8,16,4,128]{3,2,1,0:T(4,128)(2,1)} %copy.177), calls=%async_computation.2 | async-start | bytes 262144 | tf_op jit(solution)/shard_map/all_to_all | solution.py:232
  52.0 0.9 copy.185
  52.9 4.3 %all-to-all-done.2 = bf16[8,16,4,128]{3,2,1,0:T(4,128)(2,1)S(1)} async-done(((bf16[8,16,4,128]{3,2,1,0:T(4,128)(2,1)}), bf16[8,16,4,128]{3,2,1,0:T(4,128)(2,1)S(1)}, u32[]{:S(2)}, u32[]{:S(2)}) %all-to-all-start.2) | async-done | bytes 131104 | tf_op jit(solution)/shard_map/all_to_all | solution.py:232
  57.3 2.9 %all-to-all-start.3 = ((bf16[128,2,128,4]{2,3,1,0:T(4,128)(2,1)}), bf16[128,2,128,4]{2,3,1,0:T(4,128)(2,1)S(1)}, u32[]{:S(2)}, u32[]{:S(2)}) async-start(bf16[128,2,128,4]{2,3,1,0:T(4,128)(2,1)} %copy.185), calls=%async_computation.3 | async-start | bytes 524288 | tf_op jit(solution)/shard_map/all_to_all | solution.py:238
  60.6 0.4 multiply_reduce_fusion.1
  61.2 9.2 %all-to-all-done.3 = bf16[128,2,128,4]{2,3,1,0:T(4,128)(2,1)S(1)} async-done(((bf16[128,2,128,4]{2,3,1,0:T(4,128)(2,1)}), bf16[128,2,128,4]{2,3,1,0:T(4,128)(2,1)S(1)}, u32[]{:S(2)}, u32[]{:S(2)}) %all-to-all-start.3) | async-done | bytes 262176 | tf_op jit(solution)/shard_map/all_to_all | solution.py:238
  70.9 0.4 reshape.414
  71.5 1.0 %reshape_reshape.3 = f32[32,16,128]{2,1,0:T(8,128)} reshape(f32[8,4,4,16,32]{4,3,2,1,0:T(8,128)S(1)} %bitcast.163) | data formatting | bytes 524288 | tf_op jit(solution)/shard_map/reshape;reshape | solution.py:251
  72.5 2.7 %all-to-all-start.4 = ((f32[32,16,128]{2,1,0:T(8,128)}), f32[32,16,128]{2,1,0:T(8,128)S(1)}, u32[]{:S(2)}, u32[]{:S(2)}) async-start(f32[32,16,128]{2,1,0:T(8,128)} %reshape_reshape.3), calls=%async_computation.4 | async-start | bytes 524288 | tf_op jit(solution)/shard_map/all_to_all | solution.py:250
  75.7 0.6 copy-done.12
  76.4 0.3 fusion.13
  76.7 8.6 %all-to-all-done.4 = f32[32,16,128]{2,1,0:T(8,128)S(1)} async-done(((f32[32,16,128]{2,1,0:T(8,128)}), f32[32,16,128]{2,1,0:T(8,128)S(1)}, u32[]{:S(2)}, u32[]{:S(2)}) %all-to-all-start.4) | async-done | bytes 262176 | tf_op jit(solution)/shard_map/all_to_all | solution.py:250
  86.1 0.6 copy-done.7
  86.7 1.0 %fusion.16 = bf16[16,32,128]{2,1,0:T(8,128)(2,1)} fusion(f32[16,32,128]{2,1,0:T(8,128)S(1)} %bitcast.173, f32[16,32,128]{2,1,0:T(8,128)S(1)} %bitcast.183, bf16[16,32,128]{1,0,2:T(8,128)(2,1)S(1)} %multiply_convert_fusion, bf16[128,128]{1,0:T(8,128)(2,1)S(1)} %copy-done.7), kind=kOutput, calls=%fused_computation.22 | convolution fusion | flops 16973824 | bytes 819200 | tf_op jit(solution)/shard_map/dot_general | solution.py:259
  (84 shorter events, 6.1 us)
Async XLA Ops:
  0.0 11.1 %copy-start = (bf16[128,512]{1,0:T(8,128)(2,1)S(1)}, bf16[128,512]{1,0:T(8,128)(2,1)}, u32[]{:S(2)}) copy-start(bf16[128,512]{1,0:T(8,128)(2,1)} %param.18) | copy-start | bytes 393220
  0.0 1.1 %copy-start.1 = (bf16[4,128,128]{2,1,0:T(8,128)(2,1)S(1)}, bf16[4,128,128]{2,1,0:T(8,128)(2,1)}, u32[]{:S(2)}) copy-start(bf16[4,128,128]{2,1,0:T(8,128)(2,1)} %param.14) | copy-start | bytes 393220
  1.4 0.7 copy-start.13
  3.1 17.6 %all-to-all-start = ((f32[32,4,4,128]{3,2,1,0:T(4,128)}), f32[32,4,4,128]{3,2,1,0:T(4,128)S(1)}, u32[]{:S(2)}, u32[]{:S(2)}) async-start(f32[32,4,4,128]{3,2,1,0:T(4,128)} %broadcast_in_dim.25), calls=%async_computation | async-start | bytes 524288 | tf_op jit(solution)/shard_map/all_to_all | solution.py:108
  11.8 0.7 copy-start.9
  12.4 0.7 copy-start.8
  22.2 0.8 copy-start.10
  23.5 0.7 copy-start.14
  25.5 14.5 %all-to-all-start.1 = ((bf16[32,48,128]{2,1,0:T(8,128)(2,1)}), bf16[32,48,128]{2,1,0:T(8,128)(2,1)S(1)}, u32[]{:S(2)}, u32[]{:S(2)}) async-start(bf16[32,48,128]{2,1,0:T(8,128)(2,1)} %pad_maximum_fusion), calls=%async_computation.1 | async-start | bytes 786432 | tf_op jit(solution)/shard_map/all_to_all | solution.py:187
  40.6 0.7 copy-start.2
  40.6 1.0 %copy-start.4 = (bf16[128,512]{1,0:T(8,128)(2,1)S(1)}, bf16[128,512]{1,0:T(8,128)(2,1)}, u32[]{:S(2)}) copy-start(bf16[128,512]{1,0:T(8,128)(2,1)} %param.21) | copy-start | bytes 393220
  44.4 1.0 %copy-start.3 = (f32[32,16,128]{2,1,0:T(8,128)S(1)}, f32[32,16,128]{2,1,0:T(8,128)}, u32[]{:S(2)}) copy-start(f32[32,16,128]{2,1,0:T(8,128)} %copy-done.2) | copy-start | bytes 786436
  44.4 1.0 %copy-start.11 = (bf16[128,128]{1,0:T(8,128)(2,1)S(1)}, bf16[128,128]{1,0:T(8,128)(2,1)}, u32[]{:S(2)}) copy-start(bf16[128,128]{1,0:T(8,128)(2,1)} %param.23) | copy-start | bytes 98308
  45.7 0.8 copy-start.5
  46.5 0.8 copy-start.6
  48.4 8.8 %all-to-all-start.2 = ((bf16[8,16,4,128]{3,2,1,0:T(4,128)(2,1)}), bf16[8,16,4,128]{3,2,1,0:T(4,128)(2,1)S(1)}, u32[]{:S(2)}, u32[]{:S(2)}) async-start(bf16[8,16,4,128]{3,2,1,0:T(4,128)(2,1)} %copy.177), calls=%async_computation.2 | async-start | bytes 262144 | tf_op jit(solution)/shard_map/all_to_all | solution.py:232
  57.3 13.1 %all-to-all-start.3 = ((bf16[128,2,128,4]{2,3,1,0:T(4,128)(2,1)}), bf16[128,2,128,4]{2,3,1,0:T(4,128)(2,1)S(1)}, u32[]{:S(2)}, u32[]{:S(2)}) async-start(bf16[128,2,128,4]{2,3,1,0:T(4,128)(2,1)} %copy.185), calls=%async_computation.3 | async-start | bytes 524288 | tf_op jit(solution)/shard_map/all_to_all | solution.py:238
  72.5 12.9 %all-to-all-start.4 = ((f32[32,16,128]{2,1,0:T(8,128)}), f32[32,16,128]{2,1,0:T(8,128)S(1)}, u32[]{:S(2)}, u32[]{:S(2)}) async-start(f32[32,16,128]{2,1,0:T(8,128)} %reshape_reshape.3), calls=%async_computation.4 | async-start | bytes 524288 | tf_op jit(solution)/shard_map/all_to_all | solution.py:250
  75.6 0.8 copy-start.12
  86.0 0.8 copy-start.7

commit v13 on v11

--- a/solution.py
+++ b/solution.py
@@ -188,7 +188,12 @@
         jnp.concatenate([pair_chunks, bias_chunks], axis=1), ("row", "col"), 0, 0, tiled=True
     )
     pair_rows = pair_chunks.shape[1]
-    columns = merged[:, :pair_rows].reshape(length, rows_here, channels)
+    columns = (
+        merged[:, :pair_rows]
+        .reshape(device_count, rows_here, rows_here, channels)
+        .transpose(2, 0, 1, 3)
+        .reshape(rows_here, length, channels)
+    )
     bias_got = (
         merged[:, pair_rows:]
         .reshape(device_count, 2, head_count, rows_here, length)
@@ -202,11 +207,11 @@
     normed_cols = layer_norm(columns).astype(jnp.bfloat16)
     projected_cols = jnp.dot(
         normed_cols.reshape(-1, channels), col_project, preferred_element_type=jnp.float32
-    ).reshape(length, rows_here, 4 * channels)
+    ).reshape(rows_here, length, 4 * channels)
     qkv_cols = (
         projected_cols[..., : 3 * channels]
         .astype(jnp.bfloat16)
-        .reshape(length, rows_here, 3, head_count, head_size)
+        .reshape(rows_here, length, 3, head_count, head_size)
     )
     col_ok = tile_rows(local_cols, tile_mask.T, length)
     mixed_cols = attend_lines(
@@ -218,18 +223,18 @@
         col_ok,
         chain_ids,
         chain_bias[1],
-        1,
+        0,
         True,
     )
     update_cols = jnp.dot(
         mixed_cols.reshape(-1, channels), col_output, preferred_element_type=jnp.float32
-    ).reshape(length, rows_here, channels)
+    ).reshape(rows_here, length, channels)
     second_pair = (columns.astype(jnp.float32) + update_cols).astype(jnp.bfloat16)
     normed_second = layer_norm(second_pair).astype(jnp.bfloat16)
-    edge_mask = tile_pairs(jnp.arange(length, dtype=jnp.int32), local_cols, tile_mask, length)
+    edge_mask = tile_pairs(local_cols, jnp.arange(length, dtype=jnp.int32), tile_mask.T, length)
     left_all = tri_acts(normed_second, tri_left, edge_mask)
     right_all = tri_acts(normed_second, tri_right, edge_mask)
-    raw_chunks = second_pair.reshape(n_row, block_rows, rows_here, channels)
+    raw_chunks = second_pair.reshape(rows_here, n_row, block_rows, channels).transpose(1, 2, 0, 3)
     raw_pieces = [lax.dynamic_index_in_dim(raw_chunks, row_index, 0, keepdims=False)]
     for shift in range(1, n_row):
         piece = lax.dynamic_index_in_dim(raw_chunks, (row_index + shift) % n_row, 0, keepdims=False)
@@ -241,9 +246,9 @@
     own_pair = raw_got.transpose(1, 0, 2, 3).reshape(block_rows, block_cols, channels)
     channels_here = channels // device_count
     edges = jnp.stack([left_all, right_all], axis=0).transpose(3, 0, 1, 2)
-    edges_got = lax.all_to_all(edges, ("row", "col"), 0, 3, tiled=True)
+    edges_got = lax.all_to_all(edges, ("row", "col"), 0, 2, tiled=True)
     product_part = jnp.einsum(
-        "cik,cjk->cij",
+        "cki,ckj->cij",
         edges_got[:, 0],
         edges_got[:, 1],
         preferred_element_type=jnp.float32,

time: 85.9 us -> 85 us (0.990)
    reshape x2, local copies, waits for them, and re-layouts: 1.26 us -> 0.27 us  [one_block(): mixed_rows = mixed_rows.reshape(mixed_rows.shape[:2] + (width_all,))]
    unnamed x37 -> x38, local copies, waits for them, and re-layouts: 6.36 us -> 7.23 us
where the time goes in v13:
time: 85 us; the launch traced here: 84.2 us
  waiting for transfers between devices  29 us (34%)
  starting transfers between devices  28.1 us (33%)
  local copies, waits for them, and re-layouts  14.3 us (17%)
  matrix products  6.63 us (8%)
  other arithmetic  4.88 us (6%)
  between operations  1.35 us (2%)
    all_to_all x1, waiting for transfers between devices, shards(): lax.all_to_all(jnp.concatenate([pair_chunks, bias_chunks], axis=1), ('row...  11.6 us
    ppermute x7, starting transfers between devices, shards(): lax.ppermute(piece, 'row', perm=[(r, (r + shift) % n_row) for r in range(...  8.58 us
    all_to_all x1, waiting for transfers between devices, shards(): lax.all_to_all(product_sent.reshape(device_count, -1, lanes), ('row', 'co...  8.53 us
    all_to_all x1, waiting for transfers between devices, gather_lines(): got = lax.all_to_all(sent, ('row', 'col'), 0, 0, tiled=True)  7.48 us
    all_to_all x1, starting transfers between devices, gather_lines(): got = lax.all_to_all(sent, ('row', 'col'), 0, 0, tiled=True)  7.33 us
    unnamed x38, local copies, waits for them, and re-layouts  7.23 us
    all_to_all x1, starting transfers between devices, shards(): lax.all_to_all(product_sent.reshape(device_count, -1, lanes), ('row', 'co...  5.77 us
    all_to_all x1, starting transfers between devices, shards(): edges_got = lax.all_to_all(edges, ('row', 'col'), 0, 2, tiled=True)  3.8 us
  transfers between devices with their start and end apart: 11, of which 4 were waited for; matrix products, arithmetic and copies ran while one was open for 4% of the time, Pallas kernels for 0%

profile of v13, /device:TPU:0, one launch (start us, length us, event | category | flops | bytes accessed | tf_op | source)
XLA Modules:
  0.0 84.2 jit_solution(7983128946129549791)
XLA Ops:
  0.0 1.1 %convert_reduce_fusion = f32[4,128]{1,0:T(4,128)S(1)} fusion(bf16[4,128,128]{2,1,0:T(8,128)(2,1)} %param.14), kind=kLoop, calls=%fused_computation.40 | loop fusion | flops 130560 | bytes 133120 | tf_op jit(solution)/shard_map/reduce_sum | solution.py:9
  1.4 0.7 copy-done.13
  2.0 0.3 convolution_bitcast_fusion.1
  2.4 0.7 broadcast_in_dim.33
  3.1 7.3 %all-to-all-start = ((f32[32,4,4,128]{3,2,1,0:T(4,128)}), f32[32,4,4,128]{3,2,1,0:T(4,128)S(1)}, u32[]{:S(2)}, u32[]{:S(2)}) async-start(f32[32,4,4,128]{3,2,1,0:T(4,128)} %broadcast_in_dim.33), calls=%async_computation | async-start | bytes 524288 | tf_op jit(solution)/shard_map/all_to_all | solution.py:108
  11.1 0.4 fusion.60
  11.8 0.6 copy-done.9
  12.4 0.6 copy-done.8
  13.2 7.5 %all-to-all-done = f32[32,4,4,128]{3,2,1,0:T(4,128)S(1)} async-done(((f32[32,4,4,128]{3,2,1,0:T(4,128)}), f32[32,4,4,128]{3,2,1,0:T(4,128)S(1)}, u32[]{:S(2)}, u32[]{:S(2)}) %all-to-all-start) | async-done | bytes 262176 | tf_op jit(solution)/shard_map/all_to_all | solution.py:108
  20.9 0.4 fusion.7
  21.3 0.6 fusion.101
  21.9 0.3 fusion.18
  22.4 0.6 copy-done.10
  23.0 0.3 convert_reduce_fusion.2
  23.6 0.7 copy-done.14
  24.2 0.3 convert_bitcast_fusion.2
  24.7 0.8 pad_maximum_fusion
  25.4 2.7 %all-to-all-start.1 = ((bf16[32,48,128]{2,1,0:T(8,128)(2,1)}), bf16[32,48,128]{2,1,0:T(8,128)(2,1)S(1)}, u32[]{:S(2)}, u32[]{:S(2)}) async-start(bf16[32,48,128]{2,1,0:T(8,128)(2,1)} %pad_maximum_fusion), calls=%async_computation.1 | async-start | bytes 786432 | tf_op jit(solution)/shard_map/all_to_all | solution.py:187
  28.4 11.6 %all-to-all-done.1 = bf16[32,48,128]{2,1,0:T(8,128)(2,1)S(1)} async-done(((bf16[32,48,128]{2,1,0:T(8,128)(2,1)}), bf16[32,48,128]{2,1,0:T(8,128)(2,1)S(1)}, u32[]{:S(2)}, u32[]{:S(2)}) %all-to-all-start.1) | async-done | bytes 393248 | tf_op jit(solution)/shard_map/all_to_all | solution.py:187
  41.1 0.6 copy-done.2
  41.7 0.4 fusion.54
  43.2 0.4 fusion.9
  43.5 0.6 fusion.102
  44.1 0.3 fusion.19
  44.6 0.8 copy-done.3
  45.4 0.3 convert_reduce_fusion.1
  46.0 0.6 copy-done.5
  46.5 0.3 fusion.72
  46.9 0.5 copy-done.6
  47.4 0.3 fusion.74
  47.9 0.9 %copy.190 = bf16[128,2,4,128]{3,2,1,0:T(4,128)(2,1)} copy(bf16[128,2,4,128]{0,3,2,1:T(8,128)(2,1)S(1)} %maximum_bitcast_fusion) | data formatting | bytes 524288 | tf_op jit(solution)/shard_map/transpose | solution.py:248
  48.8 3.8 %all-to-all-start.2 = ((bf16[128,2,4,128]{3,2,1,0:T(4,128)(2,1)}), bf16[128,2,4,128]{3,2,1,0:T(4,128)(2,1)S(1)}, u32[]{:S(2)}, u32[]{:S(2)}) async-start(bf16[128,2,4,128]{3,2,1,0:T(4,128)(2,1)} %copy.190), calls=%async_computation.2 | async-start | bytes 524288 | tf_op jit(solution)/shard_map/all_to_all | solution.py:249
  52.6 0.3 collective-permute-start
  52.9 1.6 %collective-permute-start.1 = (bf16[16,4,128]{2,0,1:T(8,128)(2,1)S(1)}, bf16[16,4,128]{2,0,1:T(8,128)(2,1)S(1)}, u32[]{:S(2)}, u32[]{:S(2)}) collective-permute-start(bf16[16,4,128]{2,0,1:T(8,128)(2,1)S(1)} %get-tuple-element.12), channel_id=1, source_target_pairs={{0,8},{4,12},{8,16},{12,20},{16,24},{20,28},{24,0},{28,4},{1,9},{5... | collective-permute-start | bytes 49160 | tf_op jit(solution)/shard_map/ppermute | solution.py:242
  54.6 2.3 %collective-permute-start.2 = (bf16[16,4,128]{2,0,1:T(8,128)(2,1)S(1)}, bf16[16,4,128]{2,0,1:T(8,128)(2,1)S(1)}, u32[]{:S(2)}, u32[]{:S(2)}) collective-permute-start(bf16[16,4,128]{2,0,1:T(8,128)(2,1)S(1)} %get-tuple-element.11), channel_id=1, source_target_pairs={{0,12},{4,16},{8,20},{12,24},{16,28},{20,0},{24,4},{28,8},{1,13},{... | collective-permute-start | bytes 49160 | tf_op jit(solution)/shard_map/ppermute | solution.py:242
  56.8 0.6 collective-permute-start.3
  57.5 1.5 %collective-permute-start.5 = (bf16[16,4,128]{2,0,1:T(8,128)(2,1)S(1)}, bf16[16,4,128]{2,0,1:T(8,128)(2,1)S(1)}, u32[]{:S(2)}, u32[]{:S(2)}) collective-permute-start(bf16[16,4,128]{2,0,1:T(8,128)(2,1)S(1)} %get-tuple-element.8), channel_id=1, source_target_pairs={{0,24},{4,28},{8,0},{12,4},{16,8},{20,12},{24,16},{28,20},{1,25},{... | collective-permute-start | bytes 49160 | tf_op jit(solution)/shard_map/ppermute | solution.py:242
  59.0 2.2 %collective-permute-start.6 = (bf16[16,4,128]{2,0,1:T(8,128)(2,1)S(1)}, bf16[16,4,128]{2,0,1:T(8,128)(2,1)S(1)}, u32[]{:S(2)}, u32[]{:S(2)}) collective-permute-start(bf16[16,4,128]{2,0,1:T(8,128)(2,1)S(1)} %get-tuple-element.7), channel_id=1, source_target_pairs={{0,28},{4,0},{8,4},{12,8},{16,12},{20,16},{24,20},{28,24},{1,29},{... | collective-permute-start | bytes 49160 | tf_op jit(solution)/shard_map/ppermute | solution.py:242
  61.3 1.4 %collective-permute-done.6 = bf16[16,4,128]{2,0,1:T(8,128)(2,1)S(1)} collective-permute-done((bf16[16,4,128]{2,0,1:T(8,128)(2,1)S(1)}, bf16[16,4,128]{2,0,1:T(8,128)(2,1)S(1)}, u32[]{:S(2)}, u32[]{:S(2)}) %collective-permute-start.6) | collective-permute-done | bytes 16416 | tf_op jit(solution)/shard_map/ppermute | solution.py:242
  62.7 0.6 gather_fusion
  64.3 0.4 reshape.438
  64.9 1.0 %reshape_reshape.3 = f32[32,16,128]{2,1,0:T(8,128)} reshape(f32[8,4,4,16,32]{4,3,2,1,0:T(8,128)S(1)} %bitcast.231) | data formatting | bytes 524288 | tf_op jit(solution)/shard_map/reshape;reshape | solution.py:262
  65.9 5.8 %all-to-all-start.3 = ((f32[32,16,128]{2,1,0:T(8,128)}), f32[32,16,128]{2,1,0:T(8,128)S(1)}, u32[]{:S(2)}, u32[]{:S(2)}) async-start(f32[32,16,128]{2,1,0:T(8,128)} %reshape_reshape.3), calls=%async_computation.3 | async-start | bytes 524288 | tf_op jit(solution)/shard_map/all_to_all | solution.py:261
  72.4 0.6 copy-done.12
  73.0 0.3 fusion.13
  73.4 8.5 %all-to-all-done.3 = f32[32,16,128]{2,1,0:T(8,128)S(1)} async-done(((f32[32,16,128]{2,1,0:T(8,128)}), f32[32,16,128]{2,1,0:T(8,128)S(1)}, u32[]{:S(2)}, u32[]{:S(2)}) %all-to-all-start.3) | async-done | bytes 262176 | tf_op jit(solution)/shard_map/all_to_all | solution.py:261
  82.6 0.6 copy-done.7
  83.3 1.0 %fusion.16 = bf16[16,32,128]{2,1,0:T(8,128)(2,1)} fusion(f32[16,32,128]{2,1,0:T(8,128)S(1)} %bitcast.243, f32[16,32,128]{2,1,0:T(8,128)S(1)} %bitcast.254, bf16[16,32,128]{1,0,2:T(8,128)(2,1)S(1)} %multiply_convert_fusion, bf16[128,128]{1,0:T(8,128)(2,1)S(1)} %copy-done.7), kind=kOutput, calls=%fused_computation.23 | convolution fusion | flops 16973824 | bytes 819200 | tf_op jit(solution)/shard_map/dot_general | solution.py:270
  (109 shorter events, 7.1 us)
Async XLA Ops:
  0.0 11.1 %copy-start = (bf16[128,512]{1,0:T(8,128)(2,1)S(1)}, bf16[128,512]{1,0:T(8,128)(2,1)}, u32[]{:S(2)}) copy-start(bf16[128,512]{1,0:T(8,128)(2,1)} %param.18) | copy-start | bytes 393220
  0.0 1.1 %copy-start.1 = (bf16[4,128,128]{2,1,0:T(8,128)(2,1)S(1)}, bf16[4,128,128]{2,1,0:T(8,128)(2,1)}, u32[]{:S(2)}) copy-start(bf16[4,128,128]{2,1,0:T(8,128)(2,1)} %param.14) | copy-start | bytes 393220
  1.4 0.7 copy-start.13
  3.1 17.6 %all-to-all-start = ((f32[32,4,4,128]{3,2,1,0:T(4,128)}), f32[32,4,4,128]{3,2,1,0:T(4,128)S(1)}, u32[]{:S(2)}, u32[]{:S(2)}) async-start(f32[32,4,4,128]{3,2,1,0:T(4,128)} %broadcast_in_dim.33), calls=%async_computation | async-start | bytes 524288 | tf_op jit(solution)/shard_map/all_to_all | solution.py:108
  11.8 0.7 copy-start.9
  12.4 0.7 copy-start.8
  22.2 0.8 copy-start.10
  23.5 0.7 copy-start.14
  25.4 14.5 %all-to-all-start.1 = ((bf16[32,48,128]{2,1,0:T(8,128)(2,1)}), bf16[32,48,128]{2,1,0:T(8,128)(2,1)S(1)}, u32[]{:S(2)}, u32[]{:S(2)}) async-start(bf16[32,48,128]{2,1,0:T(8,128)(2,1)} %pad_maximum_fusion), calls=%async_computation.1 | async-start | bytes 786432 | tf_op jit(solution)/shard_map/all_to_all | solution.py:187
  40.8 0.9 %copy-start.4 = (bf16[128,512]{1,0:T(8,128)(2,1)S(1)}, bf16[128,512]{1,0:T(8,128)(2,1)}, u32[]{:S(2)}) copy-start(bf16[128,512]{1,0:T(8,128)(2,1)} %param.21) | copy-start | bytes 393220
  41.0 0.7 copy-start.2
  44.4 1.0 %copy-start.3 = (f32[4,32,4,128]{3,2,1,0:T(4,128)S(1)}, f32[4,32,4,128]{3,2,1,0:T(4,128)}, u32[]{:S(2)}) copy-start(f32[4,32,4,128]{3,2,1,0:T(4,128)} %copy-done.2) | copy-start | bytes 786436
  44.4 1.0 %copy-start.11 = (bf16[128,128]{1,0:T(8,128)(2,1)S(1)}, bf16[128,128]{1,0:T(8,128)(2,1)}, u32[]{:S(2)}) copy-start(bf16[128,128]{1,0:T(8,128)(2,1)} %param.23) | copy-start | bytes 98308
  45.7 0.8 %copy-start.5 = (bf16[128,256]{1,0:T(8,128)(2,1)S(1)}, bf16[128,256]{1,0:T(8,128)(2,1)}, u32[]{:S(2)}) copy-start(bf16[128,256]{1,0:T(8,128)(2,1)} %param.25) | copy-start | bytes 196612
  46.5 0.8 copy-start.6
  48.8 15.0 %all-to-all-start.2 = ((bf16[128,2,4,128]{3,2,1,0:T(4,128)(2,1)}), bf16[128,2,4,128]{3,2,1,0:T(4,128)(2,1)S(1)}, u32[]{:S(2)}, u32[]{:S(2)}) async-start(bf16[128,2,4,128]{3,2,1,0:T(4,128)(2,1)} %copy.190), calls=%async_computation.2 | async-start | bytes 524288 | tf_op jit(solution)/shard_map/all_to_all | solution.py:249
  52.6 4.9 %collective-permute-start = (bf16[16,4,128]{2,0,1:T(8,128)(2,1)S(1)}, bf16[16,4,128]{2,0,1:T(8,128)(2,1)S(1)}, u32[]{:S(2)}, u32[]{:S(2)}) collective-permute-start(bf16[16,4,128]{2,0,1:T(8,128)(2,1)S(1)} %get-tuple-element.13), channel_id=1, source_target_pairs={{0,4},{4,8},{8,12},{12,16},{16,20},{20,24},{24,28},{28,0},{1,5},{5... | collective-permute-start | bytes 49160 | tf_op jit(solution)/shard_map/ppermute | solution.py:242
  52.9 6.0 %collective-permute-start.1 = (bf16[16,4,128]{2,0,1:T(8,128)(2,1)S(1)}, bf16[16,4,128]{2,0,1:T(8,128)(2,1)S(1)}, u32[]{:S(2)}, u32[]{:S(2)}) collective-permute-start(bf16[16,4,128]{2,0,1:T(8,128)(2,1)S(1)} %get-tuple-element.12), channel_id=1, source_target_pairs={{0,8},{4,12},{8,16},{12,20},{16,24},{20,28},{24,0},{28,4},{1,9},{5... | collective-permute-start | bytes 49160 | tf_op jit(solution)/shard_map/ppermute | solution.py:242
  54.6 6.7 %collective-permute-start.2 = (bf16[16,4,128]{2,0,1:T(8,128)(2,1)S(1)}, bf16[16,4,128]{2,0,1:T(8,128)(2,1)S(1)}, u32[]{:S(2)}, u32[]{:S(2)}) collective-permute-start(bf16[16,4,128]{2,0,1:T(8,128)(2,1)S(1)} %get-tuple-element.11), channel_id=1, source_target_pairs={{0,12},{4,16},{8,20},{12,24},{16,28},{20,0},{24,4},{28,8},{1,13},{... | collective-permute-start | bytes 49160 | tf_op jit(solution)/shard_map/ppermute | solution.py:242
  56.8 4.4 %collective-permute-start.3 = (bf16[16,4,128]{2,0,1:T(8,128)(2,1)S(1)}, bf16[16,4,128]{2,0,1:T(8,128)(2,1)S(1)}, u32[]{:S(2)}, u32[]{:S(2)}) collective-permute-start(bf16[16,4,128]{2,0,1:T(8,128)(2,1)S(1)} %get-tuple-element.10), channel_id=1, source_target_pairs={{0,16},{4,20},{8,24},{12,28},{16,0},{20,4},{24,8},{28,12},{1,17},{... | collective-permute-start | bytes 49160 | tf_op jit(solution)/shard_map/ppermute | solution.py:242
  57.4 3.9 %collective-permute-start.4 = (bf16[16,4,128]{2,0,1:T(8,128)(2,1)S(1)}, bf16[16,4,128]{2,0,1:T(8,128)(2,1)S(1)}, u32[]{:S(2)}, u32[]{:S(2)}) collective-permute-start(bf16[16,4,128]{2,0,1:T(8,128)(2,1)S(1)} %get-tuple-element.9), channel_id=1, source_target_pairs={{0,20},{4,24},{8,28},{12,0},{16,4},{20,8},{24,12},{28,16},{1,21},{... | collective-permute-start | bytes 49160 | tf_op jit(solution)/shard_map/ppermute | solution.py:242
  57.5 3.8 %collective-permute-start.5 = (bf16[16,4,128]{2,0,1:T(8,128)(2,1)S(1)}, bf16[16,4,128]{2,0,1:T(8,128)(2,1)S(1)}, u32[]{:S(2)}, u32[]{:S(2)}) collective-permute-start(bf16[16,4,128]{2,0,1:T(8,128)(2,1)S(1)} %get-tuple-element.8), channel_id=1, source_target_pairs={{0,24},{4,28},{8,0},{12,4},{16,8},{20,12},{24,16},{28,20},{1,25},{... | collective-permute-start | bytes 49160 | tf_op jit(solution)/shard_map/ppermute | solution.py:242
  59.0 3.7 %collective-permute-start.6 = (bf16[16,4,128]{2,0,1:T(8,128)(2,1)S(1)}, bf16[16,4,128]{2,0,1:T(8,128)(2,1)S(1)}, u32[]{:S(2)}, u32[]{:S(2)}) collective-permute-start(bf16[16,4,128]{2,0,1:T(8,128)(2,1)S(1)} %get-tuple-element.7), channel_id=1, source_target_pairs={{0,28},{4,0},{8,4},{12,8},{16,12},{20,16},{24,20},{28,24},{1,29},{... | collective-permute-start | bytes 49160 | tf_op jit(solution)/shard_map/ppermute | solution.py:242
  65.9 16.0 %all-to-all-start.3 = ((f32[32,16,128]{2,1,0:T(8,128)}), f32[32,16,128]{2,1,0:T(8,128)S(1)}, u32[]{:S(2)}, u32[]{:S(2)}) async-start(f32[32,16,128]{2,1,0:T(8,128)} %reshape_reshape.3), calls=%async_computation.3 | async-start | bytes 524288 | tf_op jit(solution)/shard_map/all_to_all | solution.py:261
  72.3 0.8 copy-start.12
  82.5 0.8 copy-start.7

commit v14 on v13

--- a/solution.py
+++ b/solution.py
@@ -232,8 +232,17 @@
     second_pair = (columns.astype(jnp.float32) + update_cols).astype(jnp.bfloat16)
     normed_second = layer_norm(second_pair).astype(jnp.bfloat16)
     edge_mask = tile_pairs(local_cols, jnp.arange(length, dtype=jnp.int32), tile_mask.T, length)
-    left_all = tri_acts(normed_second, tri_left, edge_mask)
-    right_all = tri_acts(normed_second, tri_right, edge_mask)
+    both = jnp.dot(
+        normed_second.reshape(-1, channels),
+        jnp.concatenate([tri_left, tri_right], axis=1),
+        preferred_element_type=jnp.float32,
+    ).reshape(normed_second.shape[:2] + (4 * channels,))
+    left_all, right_all = (
+        (
+            jax.nn.sigmoid(half[..., channels:]) * half[..., :channels] * edge_mask[..., None]
+        ).astype(jnp.bfloat16)
+        for half in (both[..., : 2 * channels], both[..., 2 * channels :])
+    )
     raw_chunks = second_pair.reshape(rows_here, n_row, block_rows, channels).transpose(1, 2, 0, 3)
     raw_pieces = [lax.dynamic_index_in_dim(raw_chunks, row_index, 0, keepdims=False)]
     for shift in range(1, n_row):

time: 85 us -> 84.2 us (level)
  no operation moved by 1% of the time
where the time goes in v14:
time: 84.2 us; the launch traced here: 83.5 us
  waiting for transfers between devices  29 us (34%)
  starting transfers between devices  28.1 us (33%)
  local copies, waits for them, and re-layouts  13.8 us (16%)
  matrix products  6.35 us (8%)
  other arithmetic  4.88 us (6%)
  between operations  1.36 us (2%)
    all_to_all x1, waiting for transfers between devices, shards(): lax.all_to_all(jnp.concatenate([pair_chunks, bias_chunks], axis=1), ('row...  11.6 us
    ppermute x7, starting transfers between devices, shards(): lax.ppermute(piece, 'row', perm=[(r, (r + shift) % n_row) for r in range(...  8.58 us
    all_to_all x1, waiting for transfers between devices, shards(): lax.all_to_all(product_sent.reshape(device_count, -1, lanes), ('row', 'co...  8.53 us
    all_to_all x1, waiting for transfers between devices, gather_lines(): got = lax.all_to_all(sent, ('row', 'col'), 0, 0, tiled=True)  7.47 us
    all_to_all x1, starting transfers between devices, gather_lines(): got = lax.all_to_all(sent, ('row', 'col'), 0, 0, tiled=True)  7.33 us
    unnamed x38, local copies, waits for them, and re-layouts  6.74 us
    all_to_all x1, starting transfers between devices, shards(): lax.all_to_all(product_sent.reshape(device_count, -1, lanes), ('row', 'co...  5.77 us
    all_to_all x1, starting transfers between devices, shards(): edges_got = lax.all_to_all(edges, ('row', 'col'), 0, 2, tiled=True)  3.8 us
  transfers between devices with their start and end apart: 11, of which 4 were waited for; matrix products, arithmetic and copies ran while one was open for 4% of the time, Pallas kernels for 0%

profile of v14, /device:TPU:0, one launch (start us, length us, event | category | flops | bytes accessed | tf_op | source)
XLA Modules:
  0.0 83.5 jit_solution(3181368993616217490)
XLA Ops:
  0.0 1.1 %convert_reduce_fusion = f32[4,128]{1,0:T(4,128)S(1)} fusion(bf16[4,128,128]{2,1,0:T(8,128)(2,1)} %param.14), kind=kLoop, calls=%fused_computation.40 | loop fusion | flops 130560 | bytes 133120 | tf_op jit(solution)/shard_map/reduce_sum | solution.py:9
  1.4 0.7 copy-done.13
  2.0 0.3 convolution_bitcast_fusion.1
  2.4 0.7 broadcast_in_dim.33
  3.1 7.3 %all-to-all-start = ((f32[32,4,4,128]{3,2,1,0:T(4,128)}), f32[32,4,4,128]{3,2,1,0:T(4,128)S(1)}, u32[]{:S(2)}, u32[]{:S(2)}) async-start(f32[32,4,4,128]{3,2,1,0:T(4,128)} %broadcast_in_dim.33), calls=%async_computation | async-start | bytes 524288 | tf_op jit(solution)/shard_map/all_to_all | solution.py:108
  11.1 0.4 fusion.64
  11.8 0.6 copy-done.9
  12.5 0.6 copy-done.8
  13.2 7.5 %all-to-all-done = f32[32,4,4,128]{3,2,1,0:T(4,128)S(1)} async-done(((f32[32,4,4,128]{3,2,1,0:T(4,128)}), f32[32,4,4,128]{3,2,1,0:T(4,128)S(1)}, u32[]{:S(2)}, u32[]{:S(2)}) %all-to-all-start) | async-done | bytes 262176 | tf_op jit(solution)/shard_map/all_to_all | solution.py:108
  20.9 0.4 fusion.7
  21.3 0.6 fusion.102
  21.9 0.3 fusion.18
  22.4 0.6 copy-done.10
  23.0 0.3 convert_reduce_fusion.2
  23.6 0.7 copy-done.14
  24.2 0.3 convert_bitcast_fusion.2
  24.7 0.8 pad_maximum_fusion
  25.4 2.7 %all-to-all-start.1 = ((bf16[32,48,128]{2,1,0:T(8,128)(2,1)}), bf16[32,48,128]{2,1,0:T(8,128)(2,1)S(1)}, u32[]{:S(2)}, u32[]{:S(2)}) async-start(bf16[32,48,128]{2,1,0:T(8,128)(2,1)} %pad_maximum_fusion), calls=%async_computation.1 | async-start | bytes 786432 | tf_op jit(solution)/shard_map/all_to_all | solution.py:187
  28.4 11.6 %all-to-all-done.1 = bf16[32,48,128]{2,1,0:T(8,128)(2,1)S(1)} async-done(((bf16[32,48,128]{2,1,0:T(8,128)(2,1)}), bf16[32,48,128]{2,1,0:T(8,128)(2,1)S(1)}, u32[]{:S(2)}, u32[]{:S(2)}) %all-to-all-start.1) | async-done | bytes 393248 | tf_op jit(solution)/shard_map/all_to_all | solution.py:187
  40.2 0.3 multiply_reduce_fusion.2
  41.1 0.6 copy-done.2
  41.7 0.4 fusion.54
  43.2 0.4 fusion.9
  43.5 0.6 fusion.103
  44.1 0.3 fusion.19
  44.6 0.8 copy-done.3
  45.4 0.3 convert_reduce_fusion.1
  46.0 0.6 copy-done.5
  46.6 0.4 fusion.58
  47.2 0.9 %copy.190 = bf16[128,2,4,128]{3,2,1,0:T(4,128)(2,1)} copy(bf16[128,2,4,128]{0,3,2,1:T(8,128)(2,1)S(1)} %maximum_bitcast_fusion) | data formatting | bytes 524288 | tf_op jit(solution)/shard_map/transpose | solution.py:257
  48.0 3.8 %all-to-all-start.2 = ((bf16[128,2,4,128]{3,2,1,0:T(4,128)(2,1)}), bf16[128,2,4,128]{3,2,1,0:T(4,128)(2,1)S(1)}, u32[]{:S(2)}, u32[]{:S(2)}) async-start(bf16[128,2,4,128]{3,2,1,0:T(4,128)(2,1)} %copy.190), calls=%async_computation.2 | async-start | bytes 524288 | tf_op jit(solution)/shard_map/all_to_all | solution.py:258
  51.9 0.3 collective-permute-start
  52.2 1.6 %collective-permute-start.1 = (bf16[16,4,128]{2,0,1:T(8,128)(2,1)S(1)}, bf16[16,4,128]{2,0,1:T(8,128)(2,1)S(1)}, u32[]{:S(2)}, u32[]{:S(2)}) collective-permute-start(bf16[16,4,128]{2,0,1:T(8,128)(2,1)S(1)} %get-tuple-element.14), channel_id=1, source_target_pairs={{0,8},{4,12},{8,16},{12,20},{16,24},{20,28},{24,0},{28,4},{1,9},{5... | collective-permute-start | bytes 49160 | tf_op jit(solution)/shard_map/ppermute | solution.py:251
  53.8 2.3 %collective-permute-start.2 = (bf16[16,4,128]{2,0,1:T(8,128)(2,1)S(1)}, bf16[16,4,128]{2,0,1:T(8,128)(2,1)S(1)}, u32[]{:S(2)}, u32[]{:S(2)}) collective-permute-start(bf16[16,4,128]{2,0,1:T(8,128)(2,1)S(1)} %get-tuple-element.13), channel_id=1, source_target_pairs={{0,12},{4,16},{8,20},{12,24},{16,28},{20,0},{24,4},{28,8},{1,13},{... | collective-permute-start | bytes 49160 | tf_op jit(solution)/shard_map/ppermute | solution.py:251
  56.1 0.6 collective-permute-start.3
  56.8 1.5 %collective-permute-start.5 = (bf16[16,4,128]{2,0,1:T(8,128)(2,1)S(1)}, bf16[16,4,128]{2,0,1:T(8,128)(2,1)S(1)}, u32[]{:S(2)}, u32[]{:S(2)}) collective-permute-start(bf16[16,4,128]{2,0,1:T(8,128)(2,1)S(1)} %get-tuple-element.10), channel_id=1, source_target_pairs={{0,24},{4,28},{8,0},{12,4},{16,8},{20,12},{24,16},{28,20},{1,25},{... | collective-permute-start | bytes 49160 | tf_op jit(solution)/shard_map/ppermute | solution.py:251
  58.2 2.2 %collective-permute-start.6 = (bf16[16,4,128]{2,0,1:T(8,128)(2,1)S(1)}, bf16[16,4,128]{2,0,1:T(8,128)(2,1)S(1)}, u32[]{:S(2)}, u32[]{:S(2)}) collective-permute-start(bf16[16,4,128]{2,0,1:T(8,128)(2,1)S(1)} %get-tuple-element.9), channel_id=1, source_target_pairs={{0,28},{4,0},{8,4},{12,8},{16,12},{20,16},{24,20},{28,24},{1,29},{... | collective-permute-start | bytes 49160 | tf_op jit(solution)/shard_map/ppermute | solution.py:251
  60.6 1.4 %collective-permute-done.6 = bf16[16,4,128]{2,0,1:T(8,128)(2,1)S(1)} collective-permute-done((bf16[16,4,128]{2,0,1:T(8,128)(2,1)S(1)}, bf16[16,4,128]{2,0,1:T(8,128)(2,1)S(1)}, u32[]{:S(2)}, u32[]{:S(2)}) %collective-permute-start.6) | collective-permute-done | bytes 16416 | tf_op jit(solution)/shard_map/ppermute | solution.py:251
  61.9 0.6 gather_fusion
  62.8 0.3 multiply_reduce_fusion.1
  63.6 0.4 reshape.434
  64.1 1.0 %reshape_reshape.3 = f32[32,16,128]{2,1,0:T(8,128)} reshape(f32[8,4,4,16,32]{4,3,2,1,0:T(8,128)S(1)} %bitcast.228) | data formatting | bytes 524288 | tf_op jit(solution)/shard_map/reshape;reshape | solution.py:271
  65.1 5.8 %all-to-all-start.3 = ((f32[32,16,128]{2,1,0:T(8,128)}), f32[32,16,128]{2,1,0:T(8,128)S(1)}, u32[]{:S(2)}, u32[]{:S(2)}) async-start(f32[32,16,128]{2,1,0:T(8,128)} %reshape_reshape.3), calls=%async_computation.3 | async-start | bytes 524288 | tf_op jit(solution)/shard_map/all_to_all | solution.py:270
  71.6 0.6 copy-done.12
  72.3 0.3 fusion.13
  72.6 8.5 %all-to-all-done.3 = f32[32,16,128]{2,1,0:T(8,128)S(1)} async-done(((f32[32,16,128]{2,1,0:T(8,128)}), f32[32,16,128]{2,1,0:T(8,128)S(1)}, u32[]{:S(2)}, u32[]{:S(2)}) %all-to-all-start.3) | async-done | bytes 262176 | tf_op jit(solution)/shard_map/all_to_all | solution.py:270
  81.9 0.6 copy-done.7
  82.5 1.0 %fusion.16 = bf16[16,32,128]{2,1,0:T(8,128)(2,1)} fusion(f32[16,32,128]{2,1,0:T(8,128)S(1)} %bitcast.240, f32[16,32,128]{2,1,0:T(8,128)S(1)} %bitcast.251, bf16[16,32,128]{1,0,2:T(8,128)(2,1)S(1)} %multiply_convert_fusion, bf16[128,128]{1,0:T(8,128)(2,1)S(1)} %copy-done.7), kind=kOutput, calls=%fused_computation.23 | convolution fusion | flops 16973824 | bytes 819200 | tf_op jit(solution)/shard_map/dot_general | solution.py:279
  (108 shorter events, 6.5 us)
Async XLA Ops:
  0.0 11.1 %copy-start = (bf16[128,512]{1,0:T(8,128)(2,1)S(1)}, bf16[128,512]{1,0:T(8,128)(2,1)}, u32[]{:S(2)}) copy-start(bf16[128,512]{1,0:T(8,128)(2,1)} %param.18) | copy-start | bytes 393220
  0.0 1.1 %copy-start.1 = (bf16[4,128,128]{2,1,0:T(8,128)(2,1)S(1)}, bf16[4,128,128]{2,1,0:T(8,128)(2,1)}, u32[]{:S(2)}) copy-start(bf16[4,128,128]{2,1,0:T(8,128)(2,1)} %param.14) | copy-start | bytes 393220
  1.4 0.7 copy-start.13
  3.1 17.6 %all-to-all-start = ((f32[32,4,4,128]{3,2,1,0:T(4,128)}), f32[32,4,4,128]{3,2,1,0:T(4,128)S(1)}, u32[]{:S(2)}, u32[]{:S(2)}) async-start(f32[32,4,4,128]{3,2,1,0:T(4,128)} %broadcast_in_dim.33), calls=%async_computation | async-start | bytes 524288 | tf_op jit(solution)/shard_map/all_to_all | solution.py:108
  11.8 0.7 copy-start.9
  12.4 0.7 copy-start.8
  22.2 0.8 copy-start.10
  23.5 0.7 copy-start.14
  25.4 14.5 %all-to-all-start.1 = ((bf16[32,48,128]{2,1,0:T(8,128)(2,1)}), bf16[32,48,128]{2,1,0:T(8,128)(2,1)S(1)}, u32[]{:S(2)}, u32[]{:S(2)}) async-start(bf16[32,48,128]{2,1,0:T(8,128)(2,1)} %pad_maximum_fusion), calls=%async_computation.1 | async-start | bytes 786432 | tf_op jit(solution)/shard_map/all_to_all | solution.py:187
  40.8 0.9 %copy-start.4 = (bf16[128,512]{1,0:T(8,128)(2,1)S(1)}, bf16[128,512]{1,0:T(8,128)(2,1)}, u32[]{:S(2)}) copy-start(bf16[128,512]{1,0:T(8,128)(2,1)} %param.21) | copy-start | bytes 393220
  41.0 0.7 copy-start.2
  44.4 1.0 %copy-start.3 = (f32[4,32,4,128]{3,2,1,0:T(4,128)S(1)}, f32[4,32,4,128]{3,2,1,0:T(4,128)}, u32[]{:S(2)}) copy-start(f32[4,32,4,128]{3,2,1,0:T(4,128)} %copy-done.2) | copy-start | bytes 786436
  44.4 1.0 %copy-start.11 = (bf16[128,128]{1,0:T(8,128)(2,1)S(1)}, bf16[128,128]{1,0:T(8,128)(2,1)}, u32[]{:S(2)}) copy-start(bf16[128,128]{1,0:T(8,128)(2,1)} %param.23) | copy-start | bytes 98308
  45.7 0.8 %copy-start.5 = (bf16[128,256]{1,0:T(8,128)(2,1)S(1)}, bf16[128,256]{1,0:T(8,128)(2,1)}, u32[]{:S(2)}) copy-start(bf16[128,256]{1,0:T(8,128)(2,1)} %param.25) | copy-start | bytes 196612
  45.7 0.9 %copy-start.6 = (bf16[128,256]{1,0:T(8,128)(2,1)S(1)}, bf16[128,256]{1,0:T(8,128)(2,1)}, u32[]{:S(2)}) copy-start(bf16[128,256]{1,0:T(8,128)(2,1)} %param.24) | copy-start | bytes 196612
  48.0 15.0 %all-to-all-start.2 = ((bf16[128,2,4,128]{3,2,1,0:T(4,128)(2,1)}), bf16[128,2,4,128]{3,2,1,0:T(4,128)(2,1)S(1)}, u32[]{:S(2)}, u32[]{:S(2)}) async-start(bf16[128,2,4,128]{3,2,1,0:T(4,128)(2,1)} %copy.190), calls=%async_computation.2 | async-start | bytes 524288 | tf_op jit(solution)/shard_map/all_to_all | solution.py:258
  51.9 4.9 %collective-permute-start = (bf16[16,4,128]{2,0,1:T(8,128)(2,1)S(1)}, bf16[16,4,128]{2,0,1:T(8,128)(2,1)S(1)}, u32[]{:S(2)}, u32[]{:S(2)}) collective-permute-start(bf16[16,4,128]{2,0,1:T(8,128)(2,1)S(1)} %get-tuple-element.15), channel_id=1, source_target_pairs={{0,4},{4,8},{8,12},{12,16},{16,20},{20,24},{24,28},{28,0},{1,5},{5... | collective-permute-start | bytes 49160 | tf_op jit(solution)/shard_map/ppermute | solution.py:251
  52.2 6.0 %collective-permute-start.1 = (bf16[16,4,128]{2,0,1:T(8,128)(2,1)S(1)}, bf16[16,4,128]{2,0,1:T(8,128)(2,1)S(1)}, u32[]{:S(2)}, u32[]{:S(2)}) collective-permute-start(bf16[16,4,128]{2,0,1:T(8,128)(2,1)S(1)} %get-tuple-element.14), channel_id=1, source_target_pairs={{0,8},{4,12},{8,16},{12,20},{16,24},{20,28},{24,0},{28,4},{1,9},{5... | collective-permute-start | bytes 49160 | tf_op jit(solution)/shard_map/ppermute | solution.py:251
  53.8 6.7 %collective-permute-start.2 = (bf16[16,4,128]{2,0,1:T(8,128)(2,1)S(1)}, bf16[16,4,128]{2,0,1:T(8,128)(2,1)S(1)}, u32[]{:S(2)}, u32[]{:S(2)}) collective-permute-start(bf16[16,4,128]{2,0,1:T(8,128)(2,1)S(1)} %get-tuple-element.13), channel_id=1, source_target_pairs={{0,12},{4,16},{8,20},{12,24},{16,28},{20,0},{24,4},{28,8},{1,13},{... | collective-permute-start | bytes 49160 | tf_op jit(solution)/shard_map/ppermute | solution.py:251
  56.1 4.4 %collective-permute-start.3 = (bf16[16,4,128]{2,0,1:T(8,128)(2,1)S(1)}, bf16[16,4,128]{2,0,1:T(8,128)(2,1)S(1)}, u32[]{:S(2)}, u32[]{:S(2)}) collective-permute-start(bf16[16,4,128]{2,0,1:T(8,128)(2,1)S(1)} %get-tuple-element.12), channel_id=1, source_target_pairs={{0,16},{4,20},{8,24},{12,28},{16,0},{20,4},{24,8},{28,12},{1,17},{... | collective-permute-start | bytes 49160 | tf_op jit(solution)/shard_map/ppermute | solution.py:251
  56.6 3.9 %collective-permute-start.4 = (bf16[16,4,128]{2,0,1:T(8,128)(2,1)S(1)}, bf16[16,4,128]{2,0,1:T(8,128)(2,1)S(1)}, u32[]{:S(2)}, u32[]{:S(2)}) collective-permute-start(bf16[16,4,128]{2,0,1:T(8,128)(2,1)S(1)} %get-tuple-element.11), channel_id=1, source_target_pairs={{0,20},{4,24},{8,28},{12,0},{16,4},{20,8},{24,12},{28,16},{1,21},{... | collective-permute-start | bytes 49160 | tf_op jit(solution)/shard_map/ppermute | solution.py:251
  56.8 3.8 %collective-permute-start.5 = (bf16[16,4,128]{2,0,1:T(8,128)(2,1)S(1)}, bf16[16,4,128]{2,0,1:T(8,128)(2,1)S(1)}, u32[]{:S(2)}, u32[]{:S(2)}) collective-permute-start(bf16[16,4,128]{2,0,1:T(8,128)(2,1)S(1)} %get-tuple-element.10), channel_id=1, source_target_pairs={{0,24},{4,28},{8,0},{12,4},{16,8},{20,12},{24,16},{28,20},{1,25},{... | collective-permute-start | bytes 49160 | tf_op jit(solution)/shard_map/ppermute | solution.py:251
  58.2 3.7 %collective-permute-start.6 = (bf16[16,4,128]{2,0,1:T(8,128)(2,1)S(1)}, bf16[16,4,128]{2,0,1:T(8,128)(2,1)S(1)}, u32[]{:S(2)}, u32[]{:S(2)}) collective-permute-start(bf16[16,4,128]{2,0,1:T(8,128)(2,1)S(1)} %get-tuple-element.9), channel_id=1, source_target_pairs={{0,28},{4,0},{8,4},{12,8},{16,12},{20,16},{24,20},{28,24},{1,29},{... | collective-permute-start | bytes 49160 | tf_op jit(solution)/shard_map/ppermute | solution.py:251
  65.1 16.0 %all-to-all-start.3 = ((f32[32,16,128]{2,1,0:T(8,128)}), f32[32,16,128]{2,1,0:T(8,128)S(1)}, u32[]{:S(2)}, u32[]{:S(2)}) async-start(f32[32,16,128]{2,1,0:T(8,128)} %reshape_reshape.3), calls=%async_computation.3 | async-start | bytes 524288 | tf_op jit(solution)/shard_map/all_to_all | solution.py:270
  71.5 0.8 copy-start.12
  81.7 0.8 copy-start.7

commit v15 on v14

--- a/solution.py
+++ b/solution.py
@@ -243,6 +243,21 @@
         ).astype(jnp.bfloat16)
         for half in (both[..., : 2 * channels], both[..., 2 * channels :])
     )
+    channels_here = channels // device_count
+    edges = jnp.stack([left_all, right_all], axis=0).transpose(3, 0, 1, 2)
+    edges_got = lax.all_to_all(edges, ("row", "col"), 0, 2, tiled=True)
+    product_part = jnp.einsum(
+        "cki,ckj->cij",
+        edges_got[:, 0],
+        edges_got[:, 1],
+        preferred_element_type=jnp.float32,
+    )
+    product_sent = (
+        product_part.reshape(channels_here, n_row, block_rows, n_col, block_cols)
+        .transpose(1, 3, 0, 2, 4)
+        .reshape(device_count, channels_here, block_rows, block_cols)
+    )
+    product_sent, second_pair = lax.optimization_barrier((product_sent, second_pair))
     raw_chunks = second_pair.reshape(rows_here, n_row, block_rows, channels).transpose(1, 2, 0, 3)
     raw_pieces = [lax.dynamic_index_in_dim(raw_chunks, row_index, 0, keepdims=False)]
     for shift in range(1, n_row):
@@ -253,20 +268,6 @@
     sources = (row_index - jnp.arange(n_row, dtype=jnp.int32)) % n_row
     raw_got = jnp.take(jnp.stack(raw_pieces, axis=0), sources, axis=0)
     own_pair = raw_got.transpose(1, 0, 2, 3).reshape(block_rows, block_cols, channels)
-    channels_here = channels // device_count
-    edges = jnp.stack([left_all, right_all], axis=0).transpose(3, 0, 1, 2)
-    edges_got = lax.all_to_all(edges, ("row", "col"), 0, 2, tiled=True)
-    product_part = jnp.einsum(
-        "cki,ckj->cij",
-        edges_got[:, 0],
-        edges_got[:, 1],
-        preferred_element_type=jnp.float32,
-    )
-    product_sent = (
-        product_part.reshape(channels_here, n_row, block_rows, n_col, block_cols)
-        .transpose(1, 3, 0, 2, 4)
-        .reshape(device_count, channels_here, block_rows, block_cols)
-    )
     product_got = lax.all_to_all(
         product_sent.reshape(device_count, -1, lanes), ("row", "col"), 0, 0, tiled=True
     )

time: 84.2 us -> 83 us (0.986)
  starting transfers between devices: 28.1 us -> 25 us
  waiting for transfers between devices: 29 us -> 30.7 us
    all_to_all x1, waiting for transfers between devices: 0.01 us -> 10.1 us  [shards(): edges_got = lax.all_to_all(edges, ('row', 'col'), 0, 2, tiled=True)]
    all_to_all x1, waiting for transfers between devices: 8.53 us -> 0.01 us  [shards(): lax.all_to_all(product_sent.reshape(device_count, -1, lanes), ('row', 'co...]
    all_to_all x1, starting transfers between devices: 5.77 us -> 2.66 us  [shards(): lax.all_to_all(product_sent.reshape(device_count, -1, lanes), ('row', 'co...]
    reshape x0 -> x1, local copies, waits for them, and re-layouts: none -> 0.98 us  [shards(): product_sent.reshape(device_count, -1, lanes)]
    another operation x1 -> x0, local copies, waits for them, and re-layouts: 0.98 us -> none  [shards(): product_sent.reshape(device_count, -1, lanes)]
    unnamed x38 -> x34, local copies, waits for them, and re-layouts: 6.74 us -> 6.74 us
where the time goes in v15:
time: 83 us; the launch traced here: 82.1 us
  waiting for transfers between devices  30.7 us (37%)
  starting transfers between devices  25 us (30%)
  local copies, waits for them, and re-layouts  14 us (17%)
  matrix products  6.28 us (8%)
  other arithmetic  4.69 us (6%)
  between operations  1.37 us (2%)
    all_to_all x1, waiting for transfers between devices, shards(): lax.all_to_all(jnp.concatenate([pair_chunks, bias_chunks], axis=1), ('row...  11.8 us
    all_to_all x1, waiting for transfers between devices, shards(): edges_got = lax.all_to_all(edges, ('row', 'col'), 0, 2, tiled=True)  10.1 us
    ppermute x7, starting transfers between devices, shards(): lax.ppermute(piece, 'row', perm=[(r, (r + shift) % n_row) for r in range(...  8.58 us
    all_to_all x1, waiting for transfers between devices, gather_lines(): got = lax.all_to_all(sent, ('row', 'col'), 0, 0, tiled=True)  7.48 us
    all_to_all x1, starting transfers between devices, gather_lines(): got = lax.all_to_all(sent, ('row', 'col'), 0, 0, tiled=True)  7.33 us
    unnamed x34, local copies, waits for them, and re-layouts  6.74 us
    all_to_all x1, starting transfers between devices, shards(): edges_got = lax.all_to_all(edges, ('row', 'col'), 0, 2, tiled=True)  3.8 us
    all_to_all x1, starting transfers between devices, shards(): lax.all_to_all(jnp.concatenate([pair_chunks, bias_chunks], axis=1), ('row...  2.67 us
  transfers between devices with their start and end apart: 11, of which 4 were waited for; matrix products, arithmetic and copies ran while one was open for 4% of the time, Pallas kernels for 0%

profile of v15, /device:TPU:0, one launch (start us, length us, event | category | flops | bytes accessed | tf_op | source)
XLA Modules:
  0.0 82.1 jit_solution(3272182387500078161)
XLA Ops:
  0.0 1.1 %convert_reduce_fusion = f32[4,128]{1,0:T(4,128)S(1)} fusion(bf16[4,128,128]{2,1,0:T(8,128)(2,1)} %param.14), kind=kLoop, calls=%fused_computation.39 | loop fusion | flops 130560 | bytes 133120 | tf_op jit(solution)/shard_map/reduce_sum | solution.py:9
  1.4 0.7 copy-done.11
  2.0 0.3 convolution_bitcast_fusion.1
  2.4 0.7 broadcast_in_dim.33
  3.1 7.3 %all-to-all-start = ((f32[32,4,4,128]{3,2,1,0:T(4,128)}), f32[32,4,4,128]{3,2,1,0:T(4,128)S(1)}, u32[]{:S(2)}, u32[]{:S(2)}) async-start(f32[32,4,4,128]{3,2,1,0:T(4,128)} %broadcast_in_dim.33), calls=%async_computation | async-start | bytes 524288 | tf_op jit(solution)/shard_map/all_to_all | solution.py:108
  11.1 0.4 fusion.64
  11.8 0.6 copy-done.7
  12.4 0.6 copy-done.6
  13.2 7.5 %all-to-all-done = f32[32,4,4,128]{3,2,1,0:T(4,128)S(1)} async-done(((f32[32,4,4,128]{3,2,1,0:T(4,128)}), f32[32,4,4,128]{3,2,1,0:T(4,128)S(1)}, u32[]{:S(2)}, u32[]{:S(2)}) %all-to-all-start) | async-done | bytes 262176 | tf_op jit(solution)/shard_map/all_to_all | solution.py:108
  20.9 0.4 fusion.7
  21.3 0.6 fusion.102
  21.9 0.3 fusion.18
  22.4 0.6 copy-done.8
  23.0 0.3 convert_reduce_fusion.2
  23.6 0.7 copy-done.12
  24.2 0.3 convert_bitcast_fusion.2
  24.7 0.8 pad_maximum_fusion
  25.4 2.7 %all-to-all-start.1 = ((bf16[32,48,128]{2,1,0:T(8,128)(2,1)}), bf16[32,48,128]{2,1,0:T(8,128)(2,1)S(1)}, u32[]{:S(2)}, u32[]{:S(2)}) async-start(bf16[32,48,128]{2,1,0:T(8,128)(2,1)} %pad_maximum_fusion), calls=%async_computation.1 | async-start | bytes 786432 | tf_op jit(solution)/shard_map/all_to_all | solution.py:187
  28.2 11.8 %all-to-all-done.1 = bf16[32,48,128]{2,1,0:T(8,128)(2,1)S(1)} async-done(((bf16[32,48,128]{2,1,0:T(8,128)(2,1)}), bf16[32,48,128]{2,1,0:T(8,128)(2,1)S(1)}, u32[]{:S(2)}, u32[]{:S(2)}) %all-to-all-start.1) | async-done | bytes 393248 | tf_op jit(solution)/shard_map/all_to_all | solution.py:187
  40.2 0.3 multiply_reduce_fusion.2
  41.1 0.6 copy-done.2
  41.7 0.4 fusion.54
  43.2 0.4 fusion.9
  43.5 0.6 fusion.103
  44.3 0.3 fusion.19
  44.7 0.6 copy-done.9
  45.7 0.8 copy-done.3
  46.5 0.3 fusion.58
  47.0 0.9 %copy.191 = bf16[128,2,4,128]{3,2,1,0:T(4,128)(2,1)} copy(bf16[128,2,4,128]{0,3,2,1:T(8,128)(2,1)S(1)} %maximum_bitcast_fusion) | data formatting | bytes 524288 | tf_op jit(solution)/shard_map/transpose | solution.py:247
  47.9 3.8 %all-to-all-start.2 = ((bf16[128,2,4,128]{3,2,1,0:T(4,128)(2,1)}), bf16[128,2,4,128]{3,2,1,0:T(4,128)(2,1)S(1)}, u32[]{:S(2)}, u32[]{:S(2)}) async-start(bf16[128,2,4,128]{3,2,1,0:T(4,128)(2,1)} %copy.191), calls=%async_computation.2 | async-start | bytes 524288 | tf_op jit(solution)/shard_map/all_to_all | solution.py:248
  51.9 10.1 %all-to-all-done.2 = bf16[128,2,4,128]{3,2,1,0:T(4,128)(2,1)S(1)} async-done(((bf16[128,2,4,128]{3,2,1,0:T(4,128)(2,1)}), bf16[128,2,4,128]{3,2,1,0:T(4,128)(2,1)S(1)}, u32[]{:S(2)}, u32[]{:S(2)}) %all-to-all-start.2) | async-done | bytes 262176 | tf_op jit(solution)/shard_map/all_to_all | solution.py:248
  62.4 0.4 reshape.438
  63.0 1.0 %reshape.442 = f32[32,16,128]{2,1,0:T(8,128)} reshape(f32[32,4,16,32]{3,2,1,0:T(8,128)S(1)} %bitcast.224) | data formatting | bytes 524288 | tf_op jit(solution)/shard_map/reshape | solution.py:272
  64.0 2.7 %all-to-all-start.3 = ((f32[32,16,128]{2,1,0:T(8,128)}), f32[32,16,128]{2,1,0:T(8,128)S(1)}, u32[]{:S(2)}, u32[]{:S(2)}) async-start(f32[32,16,128]{2,1,0:T(8,128)} %reshape.442), calls=%async_computation.3 | async-start | bytes 524288 | tf_op jit(solution)/shard_map/all_to_all | solution.py:271
  66.8 0.3 collective-permute-start
  67.2 1.6 %collective-permute-start.1 = (bf16[16,4,128]{2,0,1:T(8,128)(2,1)S(1)}, bf16[16,4,128]{2,0,1:T(8,128)(2,1)S(1)}, u32[]{:S(2)}, u32[]{:S(2)}) collective-permute-start(bf16[16,4,128]{2,0,1:T(8,128)(2,1)S(1)} %get-tuple-element.16), channel_id=1, source_target_pairs={{0,8},{4,12},{8,16},{12,20},{16,24},{20,28},{24,0},{28,4},{1,9},{5... | collective-permute-start | bytes 49160 | tf_op jit(solution)/shard_map/ppermute | solution.py:266
  68.8 2.3 %collective-permute-start.2 = (bf16[16,4,128]{2,0,1:T(8,128)(2,1)S(1)}, bf16[16,4,128]{2,0,1:T(8,128)(2,1)S(1)}, u32[]{:S(2)}, u32[]{:S(2)}) collective-permute-start(bf16[16,4,128]{2,0,1:T(8,128)(2,1)S(1)} %get-tuple-element.15), channel_id=1, source_target_pairs={{0,12},{4,16},{8,20},{12,24},{16,28},{20,0},{24,4},{28,8},{1,13},{... | collective-permute-start | bytes 49160 | tf_op jit(solution)/shard_map/ppermute | solution.py:266
  71.0 0.6 collective-permute-start.3
  71.7 1.5 %collective-permute-start.5 = (bf16[16,4,128]{2,0,1:T(8,128)(2,1)S(1)}, bf16[16,4,128]{2,0,1:T(8,128)(2,1)S(1)}, u32[]{:S(2)}, u32[]{:S(2)}) collective-permute-start(bf16[16,4,128]{2,0,1:T(8,128)(2,1)S(1)} %get-tuple-element.18), channel_id=1, source_target_pairs={{0,24},{4,28},{8,0},{12,4},{16,8},{20,12},{24,16},{28,20},{1,25},{... | collective-permute-start | bytes 49160 | tf_op jit(solution)/shard_map/ppermute | solution.py:266
  73.2 2.2 %collective-permute-start.6 = (bf16[16,4,128]{2,0,1:T(8,128)(2,1)S(1)}, bf16[16,4,128]{2,0,1:T(8,128)(2,1)S(1)}, u32[]{:S(2)}, u32[]{:S(2)}) collective-permute-start(bf16[16,4,128]{2,0,1:T(8,128)(2,1)S(1)} %get-tuple-element.13), channel_id=1, source_target_pairs={{0,28},{4,0},{8,4},{12,8},{16,12},{20,16},{24,20},{28,24},{1,29},{... | collective-permute-start | bytes 49160 | tf_op jit(solution)/shard_map/ppermute | solution.py:266
  75.5 1.4 %collective-permute-done.6 = bf16[16,4,128]{2,0,1:T(8,128)(2,1)S(1)} collective-permute-done((bf16[16,4,128]{2,0,1:T(8,128)(2,1)S(1)}, bf16[16,4,128]{2,0,1:T(8,128)(2,1)S(1)}, u32[]{:S(2)}, u32[]{:S(2)}) %collective-permute-start.6) | collective-permute-done | bytes 16416 | tf_op jit(solution)/shard_map/ppermute | solution.py:266
  76.9 0.6 gather_fusion
  77.7 0.3 multiply_reduce_fusion.1
  78.7 0.6 copy-done.10
  79.4 0.3 fusion.13
  79.7 0.3 reshape.443
  80.5 0.6 copy-done.5
  81.1 1.0 %fusion.16 = bf16[16,32,128]{2,1,0:T(8,128)(2,1)} fusion(f32[16,32,128]{2,1,0:T(8,128)S(1)} %bitcast.236, f32[16,32,128]{2,1,0:T(8,128)S(1)} %bitcast.247, bf16[16,32,128]{1,0,2:T(8,128)(2,1)S(1)} %multiply_convert_fusion, bf16[128,128]{1,0:T(8,128)(2,1)S(1)} %copy-done.5), kind=kOutput, calls=%fused_computation.23 | convolution fusion | flops 16973824 | bytes 819200 | tf_op jit(solution)/shard_map/dot_general | solution.py:280
  (106 shorter events, 6.6 us)
Async XLA Ops:
  0.0 11.1 %copy-start = (bf16[128,512]{1,0:T(8,128)(2,1)S(1)}, bf16[128,512]{1,0:T(8,128)(2,1)}, u32[]{:S(2)}) copy-start(bf16[128,512]{1,0:T(8,128)(2,1)} %param.18) | copy-start | bytes 393220
  0.0 1.1 %copy-start.1 = (bf16[4,128,128]{2,1,0:T(8,128)(2,1)S(1)}, bf16[4,128,128]{2,1,0:T(8,128)(2,1)}, u32[]{:S(2)}) copy-start(bf16[4,128,128]{2,1,0:T(8,128)(2,1)} %param.14) | copy-start | bytes 393220
  1.4 0.7 copy-start.11
  3.1 17.6 %all-to-all-start = ((f32[32,4,4,128]{3,2,1,0:T(4,128)}), f32[32,4,4,128]{3,2,1,0:T(4,128)S(1)}, u32[]{:S(2)}, u32[]{:S(2)}) async-start(f32[32,4,4,128]{3,2,1,0:T(4,128)} %broadcast_in_dim.33), calls=%async_computation | async-start | bytes 524288 | tf_op jit(solution)/shard_map/all_to_all | solution.py:108
  11.8 0.7 copy-start.7
  12.4 0.7 copy-start.6
  22.2 0.8 copy-start.8
  23.5 0.7 copy-start.12
  25.4 14.5 %all-to-all-start.1 = ((bf16[32,48,128]{2,1,0:T(8,128)(2,1)}), bf16[32,48,128]{2,1,0:T(8,128)(2,1)S(1)}, u32[]{:S(2)}, u32[]{:S(2)}) async-start(bf16[32,48,128]{2,1,0:T(8,128)(2,1)} %pad_maximum_fusion), calls=%async_computation.1 | async-start | bytes 786432 | tf_op jit(solution)/shard_map/all_to_all | solution.py:187
  40.8 0.9 %copy-start.2 = (bf16[128,512]{1,0:T(8,128)(2,1)S(1)}, bf16[128,512]{1,0:T(8,128)(2,1)}, u32[]{:S(2)}) copy-start(bf16[128,512]{1,0:T(8,128)(2,1)} %param.21) | copy-start | bytes 393220
  44.6 0.8 copy-start.9
  45.6 0.8 %copy-start.3 = (bf16[128,256]{1,0:T(8,128)(2,1)S(1)}, bf16[128,256]{1,0:T(8,128)(2,1)}, u32[]{:S(2)}) copy-start(bf16[128,256]{1,0:T(8,128)(2,1)} %param.25) | copy-start | bytes 196612
  45.6 0.9 %copy-start.4 = (bf16[128,256]{1,0:T(8,128)(2,1)S(1)}, bf16[128,256]{1,0:T(8,128)(2,1)}, u32[]{:S(2)}) copy-start(bf16[128,256]{1,0:T(8,128)(2,1)} %param.24) | copy-start | bytes 196612
  47.9 14.0 %all-to-all-start.2 = ((bf16[128,2,4,128]{3,2,1,0:T(4,128)(2,1)}), bf16[128,2,4,128]{3,2,1,0:T(4,128)(2,1)S(1)}, u32[]{:S(2)}, u32[]{:S(2)}) async-start(bf16[128,2,4,128]{3,2,1,0:T(4,128)(2,1)} %copy.191), calls=%async_computation.2 | async-start | bytes 524288 | tf_op jit(solution)/shard_map/all_to_all | solution.py:248
  64.0 15.7 %all-to-all-start.3 = ((f32[32,16,128]{2,1,0:T(8,128)}), f32[32,16,128]{2,1,0:T(8,128)S(1)}, u32[]{:S(2)}, u32[]{:S(2)}) async-start(f32[32,16,128]{2,1,0:T(8,128)} %reshape.442), calls=%async_computation.3 | async-start | bytes 524288 | tf_op jit(solution)/shard_map/all_to_all | solution.py:271
  66.8 4.9 %collective-permute-start = (bf16[16,4,128]{2,0,1:T(8,128)(2,1)S(1)}, bf16[16,4,128]{2,0,1:T(8,128)(2,1)S(1)}, u32[]{:S(2)}, u32[]{:S(2)}) collective-permute-start(bf16[16,4,128]{2,0,1:T(8,128)(2,1)S(1)} %get-tuple-element.17), channel_id=1, source_target_pairs={{0,4},{4,8},{8,12},{12,16},{16,20},{20,24},{24,28},{28,0},{1,5},{5... | collective-permute-start | bytes 49160 | tf_op jit(solution)/shard_map/ppermute | solution.py:266
  67.2 6.0 %collective-permute-start.1 = (bf16[16,4,128]{2,0,1:T(8,128)(2,1)S(1)}, bf16[16,4,128]{2,0,1:T(8,128)(2,1)S(1)}, u32[]{:S(2)}, u32[]{:S(2)}) collective-permute-start(bf16[16,4,128]{2,0,1:T(8,128)(2,1)S(1)} %get-tuple-element.16), channel_id=1, source_target_pairs={{0,8},{4,12},{8,16},{12,20},{16,24},{20,28},{24,0},{28,4},{1,9},{5... | collective-permute-start | bytes 49160 | tf_op jit(solution)/shard_map/ppermute | solution.py:266
  68.8 6.7 %collective-permute-start.2 = (bf16[16,4,128]{2,0,1:T(8,128)(2,1)S(1)}, bf16[16,4,128]{2,0,1:T(8,128)(2,1)S(1)}, u32[]{:S(2)}, u32[]{:S(2)}) collective-permute-start(bf16[16,4,128]{2,0,1:T(8,128)(2,1)S(1)} %get-tuple-element.15), channel_id=1, source_target_pairs={{0,12},{4,16},{8,20},{12,24},{16,28},{20,0},{24,4},{28,8},{1,13},{... | collective-permute-start | bytes 49160 | tf_op jit(solution)/shard_map/ppermute | solution.py:266
  71.0 4.4 %collective-permute-start.3 = (bf16[16,4,128]{2,0,1:T(8,128)(2,1)S(1)}, bf16[16,4,128]{2,0,1:T(8,128)(2,1)S(1)}, u32[]{:S(2)}, u32[]{:S(2)}) collective-permute-start(bf16[16,4,128]{2,0,1:T(8,128)(2,1)S(1)} %get-tuple-element.14), channel_id=1, source_target_pairs={{0,16},{4,20},{8,24},{12,28},{16,0},{20,4},{24,8},{28,12},{1,17},{... | collective-permute-start | bytes 49160 | tf_op jit(solution)/shard_map/ppermute | solution.py:266
  71.6 3.9 %collective-permute-start.4 = (bf16[16,4,128]{2,0,1:T(8,128)(2,1)S(1)}, bf16[16,4,128]{2,0,1:T(8,128)(2,1)S(1)}, u32[]{:S(2)}, u32[]{:S(2)}) collective-permute-start(bf16[16,4,128]{2,0,1:T(8,128)(2,1)S(1)} %get-tuple-element.19), channel_id=1, source_target_pairs={{0,20},{4,24},{8,28},{12,0},{16,4},{20,8},{24,12},{28,16},{1,21},{... | collective-permute-start | bytes 49160 | tf_op jit(solution)/shard_map/ppermute | solution.py:266
  71.7 3.8 %collective-permute-start.5 = (bf16[16,4,128]{2,0,1:T(8,128)(2,1)S(1)}, bf16[16,4,128]{2,0,1:T(8,128)(2,1)S(1)}, u32[]{:S(2)}, u32[]{:S(2)}) collective-permute-start(bf16[16,4,128]{2,0,1:T(8,128)(2,1)S(1)} %get-tuple-element.18), channel_id=1, source_target_pairs={{0,24},{4,28},{8,0},{12,4},{16,8},{20,12},{24,16},{28,20},{1,25},{... | collective-permute-start | bytes 49160 | tf_op jit(solution)/shard_map/ppermute | solution.py:266
  73.2 3.7 %collective-permute-start.6 = (bf16[16,4,128]{2,0,1:T(8,128)(2,1)S(1)}, bf16[16,4,128]{2,0,1:T(8,128)(2,1)S(1)}, u32[]{:S(2)}, u32[]{:S(2)}) collective-permute-start(bf16[16,4,128]{2,0,1:T(8,128)(2,1)S(1)} %get-tuple-element.13), channel_id=1, source_target_pairs={{0,28},{4,0},{8,4},{12,8},{16,12},{20,16},{24,20},{28,24},{1,29},{... | collective-permute-start | bytes 49160 | tf_op jit(solution)/shard_map/ppermute | solution.py:266
  78.6 0.8 copy-start.10
  80.4 0.8 copy-start.5

commit v16 on v15

--- a/solution.py
+++ b/solution.py
@@ -257,10 +257,12 @@
         .transpose(1, 3, 0, 2, 4)
         .reshape(device_count, channels_here, block_rows, block_cols)
     )
-    product_sent, second_pair = lax.optimization_barrier((product_sent, second_pair))
     raw_chunks = second_pair.reshape(rows_here, n_row, block_rows, channels).transpose(1, 2, 0, 3)
+    early = n_row // 2 - 1
     raw_pieces = [lax.dynamic_index_in_dim(raw_chunks, row_index, 0, keepdims=False)]
     for shift in range(1, n_row):
+        if shift == early + 1:
+            product_sent, raw_chunks = lax.optimization_barrier((product_sent, raw_chunks))
         piece = lax.dynamic_index_in_dim(raw_chunks, (row_index + shift) % n_row, 0, keepdims=False)
         raw_pieces.append(
             lax.ppermute(piece, "row", perm=[(r, (r + shift) % n_row) for r in range(n_row)])

time: 83 us -> 81.7 us (0.984)
  waiting for transfers between devices: 30.7 us -> 28.3 us
  starting transfers between devices: 25 us -> 26.4 us
    all_to_all x1, waiting for transfers between devices: 10.1 us -> 4.96 us  [shards(): edges_got = lax.all_to_all(edges, ('row', 'col'), 0, 2, tiled=True)]
    all_to_all x1, waiting for transfers between devices: 0.01 us -> 1.77 us  [shards(): lax.all_to_all(product_sent.reshape(device_count, -1, lanes), ('row', 'co...]
    ppermute x7, waiting for transfers between devices: 1.37 us -> 2.45 us  [shards(): lax.ppermute(piece, 'row', perm=[(r, (r + shift) % n_row) for r in range(...]
    ppermute x7, starting transfers between devices: 8.58 us -> 9.44 us  [shards(): lax.ppermute(piece, 'row', perm=[(r, (r + shift) % n_row) for r in range(...]
    unnamed x34 -> x38, local copies, waits for them, and re-layouts: 6.74 us -> 6.73 us
  transfers between devices with their start and end apart: 11 -> 11, of which waited for: 4 -> 8; matrix products, arithmetic and copies ran while one was open for 4% -> 6% of each run, Pallas kernels for 0% -> 0%
where the time goes in v16:
time: 81.7 us; the launch traced here: 80.9 us
  waiting for transfers between devices  28.3 us (35%)
  starting transfers between devices  26.4 us (32%)
  local copies, waits for them, and re-layouts  13.8 us (17%)
  matrix products  6.34 us (8%)
  other arithmetic  4.88 us (6%)
  between operations  1.34 us (2%)
    all_to_all x1, waiting for transfers between devices, shards(): lax.all_to_all(jnp.concatenate([pair_chunks, bias_chunks], axis=1), ('row...  11.6 us
    ppermute x7, starting transfers between devices, shards(): lax.ppermute(piece, 'row', perm=[(r, (r + shift) % n_row) for r in range(...  9.44 us
    all_to_all x1, waiting for transfers between devices, gather_lines(): got = lax.all_to_all(sent, ('row', 'col'), 0, 0, tiled=True)  7.48 us
    all_to_all x1, starting transfers between devices, gather_lines(): got = lax.all_to_all(sent, ('row', 'col'), 0, 0, tiled=True)  7.33 us
    unnamed x38, local copies, waits for them, and re-layouts  6.73 us
    all_to_all x1, waiting for transfers between devices, shards(): edges_got = lax.all_to_all(edges, ('row', 'col'), 0, 2, tiled=True)  4.96 us
    all_to_all x1, starting transfers between devices, shards(): edges_got = lax.all_to_all(edges, ('row', 'col'), 0, 2, tiled=True)  3.82 us
    all_to_all x1, starting transfers between devices, shards(): lax.all_to_all(product_sent.reshape(device_count, -1, lanes), ('row', 'co...  3.12 us
  transfers between devices with their start and end apart: 11, of which 8 were waited for; matrix products, arithmetic and copies ran while one was open for 6% of the time, Pallas kernels for 0%

profile of v16, /device:TPU:0, one launch (start us, length us, event | category | flops | bytes accessed | tf_op | source)
XLA Modules:
  0.0 80.9 jit_solution(560871823452249808)
XLA Ops:
  0.0 1.1 %convert_reduce_fusion = f32[4,128]{1,0:T(4,128)S(1)} fusion(bf16[4,128,128]{2,1,0:T(8,128)(2,1)} %param.14), kind=kLoop, calls=%fused_computation.39 | loop fusion | flops 130560 | bytes 133120 | tf_op jit(solution)/shard_map/reduce_sum | solution.py:9
  1.4 0.7 copy-done.13
  2.0 0.3 convolution_bitcast_fusion.1
  2.4 0.7 broadcast_in_dim.33
  3.1 7.3 %all-to-all-start = ((f32[32,4,4,128]{3,2,1,0:T(4,128)}), f32[32,4,4,128]{3,2,1,0:T(4,128)S(1)}, u32[]{:S(2)}, u32[]{:S(2)}) async-start(f32[32,4,4,128]{3,2,1,0:T(4,128)} %broadcast_in_dim.33), calls=%async_computation | async-start | bytes 524288 | tf_op jit(solution)/shard_map/all_to_all | solution.py:108
  11.1 0.4 fusion.64
  11.8 0.6 copy-done.9
  12.4 0.6 copy-done.8
  13.2 7.5 %all-to-all-done = f32[32,4,4,128]{3,2,1,0:T(4,128)S(1)} async-done(((f32[32,4,4,128]{3,2,1,0:T(4,128)}), f32[32,4,4,128]{3,2,1,0:T(4,128)S(1)}, u32[]{:S(2)}, u32[]{:S(2)}) %all-to-all-start) | async-done | bytes 262176 | tf_op jit(solution)/shard_map/all_to_all | solution.py:108
  20.9 0.4 fusion.7
  21.3 0.6 fusion.102
  21.9 0.3 fusion.18
  22.4 0.6 copy-done.10
  23.6 0.7 copy-done.14
  24.2 0.3 convert_bitcast_fusion.2
  24.7 0.8 pad_maximum_fusion
  25.4 2.7 %all-to-all-start.1 = ((bf16[32,48,128]{2,1,0:T(8,128)(2,1)}), bf16[32,48,128]{2,1,0:T(8,128)(2,1)S(1)}, u32[]{:S(2)}, u32[]{:S(2)}) async-start(bf16[32,48,128]{2,1,0:T(8,128)(2,1)} %pad_maximum_fusion), calls=%async_computation.1 | async-start | bytes 786432 | tf_op jit(solution)/shard_map/all_to_all | solution.py:187
  28.4 11.6 %all-to-all-done.1 = bf16[32,48,128]{2,1,0:T(8,128)(2,1)S(1)} async-done(((bf16[32,48,128]{2,1,0:T(8,128)(2,1)}), bf16[32,48,128]{2,1,0:T(8,128)(2,1)S(1)}, u32[]{:S(2)}, u32[]{:S(2)}) %all-to-all-start.1) | async-done | bytes 393248 | tf_op jit(solution)/shard_map/all_to_all | solution.py:187
  41.1 0.6 copy-done.2
  41.7 0.3 fusion.54
  43.2 0.4 fusion.9
  43.5 0.6 fusion.103
  44.1 0.3 fusion.19
  44.6 0.8 %copy-done.3 = f32[4,32,4,128]{3,2,1,0:T(4,128)S(1)} copy-done((f32[4,32,4,128]{3,2,1,0:T(4,128)S(1)}, f32[4,32,4,128]{3,2,1,0:T(4,128)}, u32[]{:S(2)}) %copy-start.3) | copy-done | bytes 262168
  45.4 0.3 convert_reduce_fusion.1
  46.0 0.6 copy-done.5
  46.6 0.4 fusion.58
  47.2 0.9 %copy.163 = bf16[128,2,4,128]{3,2,1,0:T(4,128)(2,1)} copy(bf16[128,2,4,128]{0,3,2,1:T(8,128)(2,1)S(1)} %maximum_bitcast_fusion) | data formatting | bytes 524288 | tf_op jit(solution)/shard_map/transpose | solution.py:247
  48.0 3.8 %all-to-all-start.2 = ((bf16[128,2,4,128]{3,2,1,0:T(4,128)(2,1)}), bf16[128,2,4,128]{3,2,1,0:T(4,128)(2,1)S(1)}, u32[]{:S(2)}, u32[]{:S(2)}) async-start(bf16[128,2,4,128]{3,2,1,0:T(4,128)(2,1)} %copy.163), calls=%async_computation.2 | async-start | bytes 524288 | tf_op jit(solution)/shard_map/all_to_all | solution.py:248
  51.9 0.3 collective-permute-start
  52.2 1.6 %collective-permute-start.1 = (bf16[16,4,128]{2,0,1:T(8,128)(2,1)S(1)}, bf16[16,4,128]{2,0,1:T(8,128)(2,1)S(1)}, u32[]{:S(2)}, u32[]{:S(2)}) collective-permute-start(bf16[16,4,128]{2,0,1:T(8,128)(2,1)S(1)} %get-tuple-element.18), channel_id=1, source_target_pairs={{0,8},{4,12},{8,16},{12,20},{16,24},{20,28},{24,0},{28,4},{1,9},{5... | collective-permute-start | bytes 49160 | tf_op jit(solution)/shard_map/ppermute | solution.py:268
  53.8 2.3 %collective-permute-start.2 = (bf16[16,4,128]{2,0,1:T(8,128)(2,1)S(1)}, bf16[16,4,128]{2,0,1:T(8,128)(2,1)S(1)}, u32[]{:S(2)}, u32[]{:S(2)}) collective-permute-start(bf16[16,4,128]{2,0,1:T(8,128)(2,1)S(1)} %get-tuple-element.17), channel_id=1, source_target_pairs={{0,12},{4,16},{8,20},{12,24},{16,28},{20,0},{24,4},{28,8},{1,13},{... | collective-permute-start | bytes 49160 | tf_op jit(solution)/shard_map/ppermute | solution.py:268
  56.2 0.9 %collective-permute-done.1 = bf16[16,4,128]{2,0,1:T(8,128)(2,1)S(1)} collective-permute-done((bf16[16,4,128]{2,0,1:T(8,128)(2,1)S(1)}, bf16[16,4,128]{2,0,1:T(8,128)(2,1)S(1)}, u32[]{:S(2)}, u32[]{:S(2)}) %collective-permute-start.1) | collective-permute-done | bytes 16416 | tf_op jit(solution)/shard_map/ppermute | solution.py:268
  57.1 5.0 %all-to-all-done.2 = bf16[128,2,4,128]{3,2,1,0:T(4,128)(2,1)S(1)} async-done(((bf16[128,2,4,128]{3,2,1,0:T(4,128)(2,1)}), bf16[128,2,4,128]{3,2,1,0:T(4,128)(2,1)S(1)}, u32[]{:S(2)}, u32[]{:S(2)}) %all-to-all-start.2) | async-done | bytes 262176 | tf_op jit(solution)/shard_map/all_to_all | solution.py:248
  62.6 0.4 reshape.439
  63.2 1.1 %collective-permute-start.3 = (bf16[16,4,128]{2,0,1:T(8,128)(2,1)S(1)}, bf16[16,4,128]{2,0,1:T(8,128)(2,1)S(1)}, u32[]{:S(2)}, u32[]{:S(2)}) collective-permute-start(bf16[16,4,128]{2,0,1:T(8,128)(2,1)S(1)} %get-tuple-element.16), channel_id=1, source_target_pairs={{0,16},{4,20},{8,24},{12,28},{16,0},{20,4},{24,8},{28,12},{1,17},{... | collective-permute-start | bytes 49160 | tf_op jit(solution)/shard_map/ppermute | solution.py:268
  64.3 1.0 %reshape.442 = f32[32,16,128]{2,1,0:T(8,128)} reshape(f32[32,4,16,32]{3,2,1,0:T(8,128)S(1)} %bitcast.214) | data formatting | bytes 524288 | tf_op jit(solution)/shard_map/reshape | solution.py:274
  65.2 3.1 %all-to-all-start.3 = ((f32[32,16,128]{2,1,0:T(8,128)}), f32[32,16,128]{2,1,0:T(8,128)S(1)}, u32[]{:S(2)}, u32[]{:S(2)}) async-start(f32[32,16,128]{2,1,0:T(8,128)} %reshape.442), calls=%async_computation.3 | async-start | bytes 524288 | tf_op jit(solution)/shard_map/all_to_all | solution.py:273
  68.4 1.5 %collective-permute-start.4 = (bf16[16,4,128]{2,0,1:T(8,128)(2,1)S(1)}, bf16[16,4,128]{2,0,1:T(8,128)(2,1)S(1)}, u32[]{:S(2)}, u32[]{:S(2)}) collective-permute-start(bf16[16,4,128]{2,0,1:T(8,128)(2,1)S(1)} %get-tuple-element.15), channel_id=1, source_target_pairs={{0,20},{4,24},{8,28},{12,0},{16,4},{20,8},{24,12},{28,16},{1,21},{... | collective-permute-start | bytes 49160 | tf_op jit(solution)/shard_map/ppermute | solution.py:268
  69.9 1.5 %collective-permute-start.5 = (bf16[16,4,128]{2,0,1:T(8,128)(2,1)S(1)}, bf16[16,4,128]{2,0,1:T(8,128)(2,1)S(1)}, u32[]{:S(2)}, u32[]{:S(2)}) collective-permute-start(bf16[16,4,128]{2,0,1:T(8,128)(2,1)S(1)} %get-tuple-element.14), channel_id=1, source_target_pairs={{0,24},{4,28},{8,0},{12,4},{16,8},{20,12},{24,16},{28,20},{1,25},{... | collective-permute-start | bytes 49160 | tf_op jit(solution)/shard_map/ppermute | solution.py:268
  71.4 1.2 %collective-permute-start.6 = (bf16[16,4,128]{2,0,1:T(8,128)(2,1)S(1)}, bf16[16,4,128]{2,0,1:T(8,128)(2,1)S(1)}, u32[]{:S(2)}, u32[]{:S(2)}) collective-permute-start(bf16[16,4,128]{2,0,1:T(8,128)(2,1)S(1)} %get-tuple-element.13), channel_id=1, source_target_pairs={{0,28},{4,0},{8,4},{12,8},{16,12},{20,16},{24,20},{28,24},{1,29},{... | collective-permute-start | bytes 49160 | tf_op jit(solution)/shard_map/ppermute | solution.py:268
  72.6 1.2 %collective-permute-done.5 = bf16[16,4,128]{2,0,1:T(8,128)(2,1)S(1)} collective-permute-done((bf16[16,4,128]{2,0,1:T(8,128)(2,1)S(1)}, bf16[16,4,128]{2,0,1:T(8,128)(2,1)S(1)}, u32[]{:S(2)}, u32[]{:S(2)}) %collective-permute-start.5) | collective-permute-done | bytes 16416 | tf_op jit(solution)/shard_map/ppermute | solution.py:268
  74.0 0.6 gather_fusion
  75.8 0.6 copy-done.12
  76.5 0.3 fusion.13
  76.8 1.8 %all-to-all-done.3 = f32[32,16,128]{2,1,0:T(8,128)S(1)} async-done(((f32[32,16,128]{2,1,0:T(8,128)}), f32[32,16,128]{2,1,0:T(8,128)S(1)}, u32[]{:S(2)}, u32[]{:S(2)}) %all-to-all-start.3) | async-done | bytes 262176 | tf_op jit(solution)/shard_map/all_to_all | solution.py:273
  79.3 0.6 copy-done.7
  80.0 1.0 %fusion.16 = bf16[16,32,128]{2,1,0:T(8,128)(2,1)} fusion(f32[16,32,128]{2,1,0:T(8,128)S(1)} %bitcast.227, f32[16,32,128]{2,1,0:T(8,128)S(1)} %bitcast.238, bf16[16,32,128]{1,0,2:T(8,128)(2,1)S(1)} %multiply_convert_fusion, bf16[128,128]{1,0:T(8,128)(2,1)S(1)} %copy-done.7), kind=kOutput, calls=%fused_computation.23 | convolution fusion | flops 16973824 | bytes 819200 | tf_op jit(solution)/shard_map/dot_general | solution.py:282
  (109 shorter events, 7.6 us)
Async XLA Ops:
  0.0 11.1 %copy-start = (bf16[128,512]{1,0:T(8,128)(2,1)S(1)}, bf16[128,512]{1,0:T(8,128)(2,1)}, u32[]{:S(2)}) copy-start(bf16[128,512]{1,0:T(8,128)(2,1)} %param.18) | copy-start | bytes 393220
  0.0 1.1 %copy-start.1 = (bf16[4,128,128]{2,1,0:T(8,128)(2,1)S(1)}, bf16[4,128,128]{2,1,0:T(8,128)(2,1)}, u32[]{:S(2)}) copy-start(bf16[4,128,128]{2,1,0:T(8,128)(2,1)} %param.14) | copy-start | bytes 393220
  1.4 0.7 copy-start.13
  3.1 17.6 %all-to-all-start = ((f32[32,4,4,128]{3,2,1,0:T(4,128)}), f32[32,4,4,128]{3,2,1,0:T(4,128)S(1)}, u32[]{:S(2)}, u32[]{:S(2)}) async-start(f32[32,4,4,128]{3,2,1,0:T(4,128)} %broadcast_in_dim.33), calls=%async_computation | async-start | bytes 524288 | tf_op jit(solution)/shard_map/all_to_all | solution.py:108
  11.8 0.7 copy-start.9
  12.4 0.7 copy-start.8
  22.2 0.8 copy-start.10
  23.5 0.7 copy-start.14
  25.4 14.5 %all-to-all-start.1 = ((bf16[32,48,128]{2,1,0:T(8,128)(2,1)}), bf16[32,48,128]{2,1,0:T(8,128)(2,1)S(1)}, u32[]{:S(2)}, u32[]{:S(2)}) async-start(bf16[32,48,128]{2,1,0:T(8,128)(2,1)} %pad_maximum_fusion), calls=%async_computation.1 | async-start | bytes 786432 | tf_op jit(solution)/shard_map/all_to_all | solution.py:187
  40.8 0.9 %copy-start.4 = (bf16[128,512]{1,0:T(8,128)(2,1)S(1)}, bf16[128,512]{1,0:T(8,128)(2,1)}, u32[]{:S(2)}) copy-start(bf16[128,512]{1,0:T(8,128)(2,1)} %param.21) | copy-start | bytes 393220
  41.0 0.7 copy-start.2
  44.4 1.0 %copy-start.3 = (f32[4,32,4,128]{3,2,1,0:T(4,128)S(1)}, f32[4,32,4,128]{3,2,1,0:T(4,128)}, u32[]{:S(2)}) copy-start(f32[4,32,4,128]{3,2,1,0:T(4,128)} %copy-done.2) | copy-start | bytes 786436
  44.4 1.0 %copy-start.11 = (bf16[128,128]{1,0:T(8,128)(2,1)S(1)}, bf16[128,128]{1,0:T(8,128)(2,1)}, u32[]{:S(2)}) copy-start(bf16[128,128]{1,0:T(8,128)(2,1)} %param.23) | copy-start | bytes 98308
  45.7 0.8 %copy-start.5 = (bf16[128,256]{1,0:T(8,128)(2,1)S(1)}, bf16[128,256]{1,0:T(8,128)(2,1)}, u32[]{:S(2)}) copy-start(bf16[128,256]{1,0:T(8,128)(2,1)} %param.25) | copy-start | bytes 196612
  45.7 0.9 %copy-start.6 = (bf16[128,256]{1,0:T(8,128)(2,1)S(1)}, bf16[128,256]{1,0:T(8,128)(2,1)}, u32[]{:S(2)}) copy-start(bf16[128,256]{1,0:T(8,128)(2,1)} %param.24) | copy-start | bytes 196612
  48.0 14.1 %all-to-all-start.2 = ((bf16[128,2,4,128]{3,2,1,0:T(4,128)(2,1)}), bf16[128,2,4,128]{3,2,1,0:T(4,128)(2,1)S(1)}, u32[]{:S(2)}, u32[]{:S(2)}) async-start(bf16[128,2,4,128]{3,2,1,0:T(4,128)(2,1)} %copy.163), calls=%async_computation.2 | async-start | bytes 524288 | tf_op jit(solution)/shard_map/all_to_all | solution.py:248
  51.9 4.3 %collective-permute-start = (bf16[16,4,128]{2,0,1:T(8,128)(2,1)S(1)}, bf16[16,4,128]{2,0,1:T(8,128)(2,1)S(1)}, u32[]{:S(2)}, u32[]{:S(2)}) collective-permute-start(bf16[16,4,128]{2,0,1:T(8,128)(2,1)S(1)} %get-tuple-element.19), channel_id=1, source_target_pairs={{0,4},{4,8},{8,12},{12,16},{16,20},{20,24},{24,28},{28,0},{1,5},{5... | collective-permute-start | bytes 49160 | tf_op jit(solution)/shard_map/ppermute | solution.py:268
  52.2 4.9 %collective-permute-start.1 = (bf16[16,4,128]{2,0,1:T(8,128)(2,1)S(1)}, bf16[16,4,128]{2,0,1:T(8,128)(2,1)S(1)}, u32[]{:S(2)}, u32[]{:S(2)}) collective-permute-start(bf16[16,4,128]{2,0,1:T(8,128)(2,1)S(1)} %get-tuple-element.18), channel_id=1, source_target_pairs={{0,8},{4,12},{8,16},{12,20},{16,24},{20,28},{24,0},{28,4},{1,9},{5... | collective-permute-start | bytes 49160 | tf_op jit(solution)/shard_map/ppermute | solution.py:268
  53.8 10.4 %collective-permute-start.2 = (bf16[16,4,128]{2,0,1:T(8,128)(2,1)S(1)}, bf16[16,4,128]{2,0,1:T(8,128)(2,1)S(1)}, u32[]{:S(2)}, u32[]{:S(2)}) collective-permute-start(bf16[16,4,128]{2,0,1:T(8,128)(2,1)S(1)} %get-tuple-element.17), channel_id=1, source_target_pairs={{0,12},{4,16},{8,20},{12,24},{16,28},{20,0},{24,4},{28,8},{1,13},{... | collective-permute-start | bytes 49160 | tf_op jit(solution)/shard_map/ppermute | solution.py:268
  63.2 9.4 %collective-permute-start.3 = (bf16[16,4,128]{2,0,1:T(8,128)(2,1)S(1)}, bf16[16,4,128]{2,0,1:T(8,128)(2,1)S(1)}, u32[]{:S(2)}, u32[]{:S(2)}) collective-permute-start(bf16[16,4,128]{2,0,1:T(8,128)(2,1)S(1)} %get-tuple-element.16), channel_id=1, source_target_pairs={{0,16},{4,20},{8,24},{12,28},{16,0},{20,4},{24,8},{28,12},{1,17},{... | collective-permute-start | bytes 49160 | tf_op jit(solution)/shard_map/ppermute | solution.py:268
  65.2 13.4 %all-to-all-start.3 = ((f32[32,16,128]{2,1,0:T(8,128)}), f32[32,16,128]{2,1,0:T(8,128)S(1)}, u32[]{:S(2)}, u32[]{:S(2)}) async-start(f32[32,16,128]{2,1,0:T(8,128)} %reshape.442), calls=%async_computation.3 | async-start | bytes 524288 | tf_op jit(solution)/shard_map/all_to_all | solution.py:273
  68.4 4.2 %collective-permute-start.4 = (bf16[16,4,128]{2,0,1:T(8,128)(2,1)S(1)}, bf16[16,4,128]{2,0,1:T(8,128)(2,1)S(1)}, u32[]{:S(2)}, u32[]{:S(2)}) collective-permute-start(bf16[16,4,128]{2,0,1:T(8,128)(2,1)S(1)} %get-tuple-element.15), channel_id=1, source_target_pairs={{0,20},{4,24},{8,28},{12,0},{16,4},{20,8},{24,12},{28,16},{1,21},{... | collective-permute-start | bytes 49160 | tf_op jit(solution)/shard_map/ppermute | solution.py:268
  69.9 3.9 %collective-permute-start.5 = (bf16[16,4,128]{2,0,1:T(8,128)(2,1)S(1)}, bf16[16,4,128]{2,0,1:T(8,128)(2,1)S(1)}, u32[]{:S(2)}, u32[]{:S(2)}) collective-permute-start(bf16[16,4,128]{2,0,1:T(8,128)(2,1)S(1)} %get-tuple-element.14), channel_id=1, source_target_pairs={{0,24},{4,28},{8,0},{12,4},{16,8},{20,12},{24,16},{28,20},{1,25},{... | collective-permute-start | bytes 49160 | tf_op jit(solution)/shard_map/ppermute | solution.py:268
  71.4 2.6 %collective-permute-start.6 = (bf16[16,4,128]{2,0,1:T(8,128)(2,1)S(1)}, bf16[16,4,128]{2,0,1:T(8,128)(2,1)S(1)}, u32[]{:S(2)}, u32[]{:S(2)}) collective-permute-start(bf16[16,4,128]{2,0,1:T(8,128)(2,1)S(1)} %get-tuple-element.13), channel_id=1, source_target_pairs={{0,28},{4,0},{8,4},{12,8},{16,12},{20,16},{24,20},{28,24},{1,29},{... | collective-permute-start | bytes 49160 | tf_op jit(solution)/shard_map/ppermute | solution.py:268
  75.7 0.8 copy-start.12
  79.2 0.8 copy-start.7

commit v17 on v16

--- a/solution.py
+++ b/solution.py
@@ -258,7 +258,7 @@
         .reshape(device_count, channels_here, block_rows, block_cols)
     )
     raw_chunks = second_pair.reshape(rows_here, n_row, block_rows, channels).transpose(1, 2, 0, 3)
-    early = n_row // 2 - 1
+    early = n_row // 2
     raw_pieces = [lax.dynamic_index_in_dim(raw_chunks, row_index, 0, keepdims=False)]
     for shift in range(1, n_row):
         if shift == early + 1:

time: 81.7 us -> 81.4 us (level)
  starting transfers between devices: 26.4 us -> 25.2 us
  waiting for transfers between devices: 28.3 us -> 29.2 us
    all_to_all x1, waiting for transfers between devices: 1.77 us -> 3.08 us  [shards(): lax.all_to_all(product_sent.reshape(device_count, -1, lanes), ('row', 'co...]
    ppermute x7, starting transfers between devices: 9.44 us -> 8.38 us  [shards(): lax.ppermute(piece, 'row', perm=[(r, (r + shift) % n_row) for r in range(...]
where the time goes in v17:
time: 81.4 us; the launch traced here: 80.6 us
  waiting for transfers between devices  29.2 us (36%)
  starting transfers between devices  25.2 us (31%)
  local copies, waits for them, and re-layouts  13.8 us (17%)
  matrix products  6.34 us (8%)
  other arithmetic  4.88 us (6%)
  between operations  1.33 us (2%)
    all_to_all x1, waiting for transfers between devices, shards(): lax.all_to_all(jnp.concatenate([pair_chunks, bias_chunks], axis=1), ('row...  11.6 us
    ppermute x7, starting transfers between devices, shards(): lax.ppermute(piece, 'row', perm=[(r, (r + shift) % n_row) for r in range(...  8.38 us
    all_to_all x1, waiting for transfers between devices, gather_lines(): got = lax.all_to_all(sent, ('row', 'col'), 0, 0, tiled=True)  7.48 us
    all_to_all x1, starting transfers between devices, gather_lines(): got = lax.all_to_all(sent, ('row', 'col'), 0, 0, tiled=True)  7.33 us
    unnamed x38, local copies, waits for them, and re-layouts  6.73 us
    all_to_all x1, waiting for transfers between devices, shards(): edges_got = lax.all_to_all(edges, ('row', 'col'), 0, 2, tiled=True)  4.28 us
    all_to_all x1, starting transfers between devices, shards(): edges_got = lax.all_to_all(edges, ('row', 'col'), 0, 2, tiled=True)  3.82 us
    all_to_all x1, waiting for transfers between devices, shards(): lax.all_to_all(product_sent.reshape(device_count, -1, lanes), ('row', 'co...  3.08 us
  transfers between devices with their start and end apart: 11, of which 8 were waited for; matrix products, arithmetic and copies ran while one was open for 6% of the time, Pallas kernels for 0%

profile of v17, /device:TPU:0, one launch (start us, length us, event | category | flops | bytes accessed | tf_op | source)
XLA Modules:
  0.0 80.6 jit_solution(5535929860434226173)
XLA Ops:
  0.0 1.1 %convert_reduce_fusion = f32[4,128]{1,0:T(4,128)S(1)} fusion(bf16[4,128,128]{2,1,0:T(8,128)(2,1)} %param.14), kind=kLoop, calls=%fused_computation.39 | loop fusion | flops 130560 | bytes 133120 | tf_op jit(solution)/shard_map/reduce_sum | solution.py:9
  1.4 0.7 copy-done.13
  2.0 0.3 convolution_bitcast_fusion.1
  2.4 0.7 broadcast_in_dim.33
  3.1 7.3 %all-to-all-start = ((f32[32,4,4,128]{3,2,1,0:T(4,128)}), f32[32,4,4,128]{3,2,1,0:T(4,128)S(1)}, u32[]{:S(2)}, u32[]{:S(2)}) async-start(f32[32,4,4,128]{3,2,1,0:T(4,128)} %broadcast_in_dim.33), calls=%async_computation | async-start | bytes 524288 | tf_op jit(solution)/shard_map/all_to_all | solution.py:108
  11.1 0.4 fusion.64
  11.8 0.6 copy-done.9
  12.4 0.6 copy-done.8
  13.2 7.5 %all-to-all-done = f32[32,4,4,128]{3,2,1,0:T(4,128)S(1)} async-done(((f32[32,4,4,128]{3,2,1,0:T(4,128)}), f32[32,4,4,128]{3,2,1,0:T(4,128)S(1)}, u32[]{:S(2)}, u32[]{:S(2)}) %all-to-all-start) | async-done | bytes 262176 | tf_op jit(solution)/shard_map/all_to_all | solution.py:108
  20.9 0.4 fusion.7
  21.3 0.6 fusion.102
  21.9 0.3 fusion.18
  22.4 0.6 copy-done.10
  23.6 0.7 copy-done.14
  24.2 0.3 convert_bitcast_fusion.2
  24.7 0.8 pad_maximum_fusion
  25.4 2.7 %all-to-all-start.1 = ((bf16[32,48,128]{2,1,0:T(8,128)(2,1)}), bf16[32,48,128]{2,1,0:T(8,128)(2,1)S(1)}, u32[]{:S(2)}, u32[]{:S(2)}) async-start(bf16[32,48,128]{2,1,0:T(8,128)(2,1)} %pad_maximum_fusion), calls=%async_computation.1 | async-start | bytes 786432 | tf_op jit(solution)/shard_map/all_to_all | solution.py:187
  28.4 11.6 %all-to-all-done.1 = bf16[32,48,128]{2,1,0:T(8,128)(2,1)S(1)} async-done(((bf16[32,48,128]{2,1,0:T(8,128)(2,1)}), bf16[32,48,128]{2,1,0:T(8,128)(2,1)S(1)}, u32[]{:S(2)}, u32[]{:S(2)}) %all-to-all-start.1) | async-done | bytes 393248 | tf_op jit(solution)/shard_map/all_to_all | solution.py:187
  41.1 0.6 copy-done.2
  41.7 0.3 fusion.54
  43.2 0.4 fusion.9
  43.5 0.6 fusion.103
  44.1 0.3 fusion.19
  44.6 0.8 %copy-done.3 = f32[4,32,4,128]{3,2,1,0:T(4,128)S(1)} copy-done((f32[4,32,4,128]{3,2,1,0:T(4,128)S(1)}, f32[4,32,4,128]{3,2,1,0:T(4,128)}, u32[]{:S(2)}) %copy-start.3) | copy-done | bytes 262168
  45.4 0.3 convert_reduce_fusion.1
  46.0 0.6 copy-done.5
  46.6 0.4 fusion.58
  47.2 0.9 %copy.168 = bf16[128,2,4,128]{3,2,1,0:T(4,128)(2,1)} copy(bf16[128,2,4,128]{0,3,2,1:T(8,128)(2,1)S(1)} %maximum_bitcast_fusion) | data formatting | bytes 524288 | tf_op jit(solution)/shard_map/transpose | solution.py:247
  48.0 3.8 %all-to-all-start.2 = ((bf16[128,2,4,128]{3,2,1,0:T(4,128)(2,1)}), bf16[128,2,4,128]{3,2,1,0:T(4,128)(2,1)S(1)}, u32[]{:S(2)}, u32[]{:S(2)}) async-start(bf16[128,2,4,128]{3,2,1,0:T(4,128)(2,1)} %copy.168), calls=%async_computation.2 | async-start | bytes 524288 | tf_op jit(solution)/shard_map/all_to_all | solution.py:248
  51.9 0.3 collective-permute-start
  52.2 1.6 %collective-permute-start.1 = (bf16[16,4,128]{2,0,1:T(8,128)(2,1)S(1)}, bf16[16,4,128]{2,0,1:T(8,128)(2,1)S(1)}, u32[]{:S(2)}, u32[]{:S(2)}) collective-permute-start(bf16[16,4,128]{2,0,1:T(8,128)(2,1)S(1)} %get-tuple-element.18), channel_id=1, source_target_pairs={{0,8},{4,12},{8,16},{12,20},{16,24},{20,28},{24,0},{28,4},{1,9},{5... | collective-permute-start | bytes 49160 | tf_op jit(solution)/shard_map/ppermute | solution.py:268
  53.8 2.3 %collective-permute-start.2 = (bf16[16,4,128]{2,0,1:T(8,128)(2,1)S(1)}, bf16[16,4,128]{2,0,1:T(8,128)(2,1)S(1)}, u32[]{:S(2)}, u32[]{:S(2)}) collective-permute-start(bf16[16,4,128]{2,0,1:T(8,128)(2,1)S(1)} %get-tuple-element.17), channel_id=1, source_target_pairs={{0,12},{4,16},{8,20},{12,24},{16,28},{20,0},{24,4},{28,8},{1,13},{... | collective-permute-start | bytes 49160 | tf_op jit(solution)/shard_map/ppermute | solution.py:268
  56.1 0.6 collective-permute-start.3
  56.6 0.3 collective-permute-done.1
  57.0 0.8 %collective-permute-done.2 = bf16[16,4,128]{2,0,1:T(8,128)(2,1)S(1)} collective-permute-done((bf16[16,4,128]{2,0,1:T(8,128)(2,1)S(1)}, bf16[16,4,128]{2,0,1:T(8,128)(2,1)S(1)}, u32[]{:S(2)}, u32[]{:S(2)}) %collective-permute-start.2) | collective-permute-done | bytes 16416 | tf_op jit(solution)/shard_map/ppermute | solution.py:268
  57.8 4.3 %all-to-all-done.2 = bf16[128,2,4,128]{3,2,1,0:T(4,128)(2,1)S(1)} async-done(((bf16[128,2,4,128]{3,2,1,0:T(4,128)(2,1)}), bf16[128,2,4,128]{3,2,1,0:T(4,128)(2,1)S(1)}, u32[]{:S(2)}, u32[]{:S(2)}) %all-to-all-start.2) | async-done | bytes 262176 | tf_op jit(solution)/shard_map/all_to_all | solution.py:248
  62.6 0.4 reshape.439
  63.2 0.9 %collective-permute-start.4 = (bf16[16,4,128]{2,0,1:T(8,128)(2,1)S(1)}, bf16[16,4,128]{2,0,1:T(8,128)(2,1)S(1)}, u32[]{:S(2)}, u32[]{:S(2)}) collective-permute-start(bf16[16,4,128]{2,0,1:T(8,128)(2,1)S(1)} %get-tuple-element.15), channel_id=1, source_target_pairs={{0,20},{4,24},{8,28},{12,0},{16,4},{20,8},{24,12},{28,16},{1,21},{... | collective-permute-start | bytes 49160 | tf_op jit(solution)/shard_map/ppermute | solution.py:268
  64.1 1.0 %reshape.442 = f32[32,16,128]{2,1,0:T(8,128)} reshape(f32[32,4,16,32]{3,2,1,0:T(8,128)S(1)} %bitcast.218) | data formatting | bytes 524288 | tf_op jit(solution)/shard_map/reshape | solution.py:274
  65.1 3.0 %all-to-all-start.3 = ((f32[32,16,128]{2,1,0:T(8,128)}), f32[32,16,128]{2,1,0:T(8,128)S(1)}, u32[]{:S(2)}, u32[]{:S(2)}) async-start(f32[32,16,128]{2,1,0:T(8,128)} %reshape.442), calls=%async_computation.3 | async-start | bytes 524288 | tf_op jit(solution)/shard_map/all_to_all | solution.py:273
  68.1 2.7 %collective-permute-start.5 = (bf16[16,4,128]{2,0,1:T(8,128)(2,1)S(1)}, bf16[16,4,128]{2,0,1:T(8,128)(2,1)S(1)}, u32[]{:S(2)}, u32[]{:S(2)}) collective-permute-start(bf16[16,4,128]{2,0,1:T(8,128)(2,1)S(1)} %get-tuple-element.14), channel_id=1, source_target_pairs={{0,24},{4,28},{8,0},{12,4},{16,8},{20,12},{24,16},{28,20},{1,25},{... | collective-permute-start | bytes 49160 | tf_op jit(solution)/shard_map/ppermute | solution.py:268
  70.8 1.4 %collective-permute-done.5 = bf16[16,4,128]{2,0,1:T(8,128)(2,1)S(1)} collective-permute-done((bf16[16,4,128]{2,0,1:T(8,128)(2,1)S(1)}, bf16[16,4,128]{2,0,1:T(8,128)(2,1)S(1)}, u32[]{:S(2)}, u32[]{:S(2)}) %collective-permute-start.5) | collective-permute-done | bytes 16416 | tf_op jit(solution)/shard_map/ppermute | solution.py:268
  72.4 0.6 gather_fusion
  74.2 0.6 copy-done.12
  74.9 0.3 fusion.13
  75.2 3.1 %all-to-all-done.3 = f32[32,16,128]{2,1,0:T(8,128)S(1)} async-done(((f32[32,16,128]{2,1,0:T(8,128)}), f32[32,16,128]{2,1,0:T(8,128)S(1)}, u32[]{:S(2)}, u32[]{:S(2)}) %all-to-all-start.3) | async-done | bytes 262176 | tf_op jit(solution)/shard_map/all_to_all | solution.py:273
  79.1 0.6 copy-done.7
  79.7 1.0 %fusion.16 = bf16[16,32,128]{2,1,0:T(8,128)(2,1)} fusion(f32[16,32,128]{2,1,0:T(8,128)S(1)} %bitcast.231, f32[16,32,128]{2,1,0:T(8,128)S(1)} %bitcast.242, bf16[16,32,128]{1,0,2:T(8,128)(2,1)S(1)} %multiply_convert_fusion, bf16[128,128]{1,0:T(8,128)(2,1)S(1)} %copy-done.7), kind=kOutput, calls=%fused_computation.23 | convolution fusion | flops 16973824 | bytes 819200 | tf_op jit(solution)/shard_map/dot_general | solution.py:282
  (109 shorter events, 7.4 us)
Async XLA Ops:
  0.0 11.1 %copy-start = (bf16[128,512]{1,0:T(8,128)(2,1)S(1)}, bf16[128,512]{1,0:T(8,128)(2,1)}, u32[]{:S(2)}) copy-start(bf16[128,512]{1,0:T(8,128)(2,1)} %param.18) | copy-start | bytes 393220
  0.0 1.1 %copy-start.1 = (bf16[4,128,128]{2,1,0:T(8,128)(2,1)S(1)}, bf16[4,128,128]{2,1,0:T(8,128)(2,1)}, u32[]{:S(2)}) copy-start(bf16[4,128,128]{2,1,0:T(8,128)(2,1)} %param.14) | copy-start | bytes 393220
  1.4 0.7 copy-start.13
  3.1 17.6 %all-to-all-start = ((f32[32,4,4,128]{3,2,1,0:T(4,128)}), f32[32,4,4,128]{3,2,1,0:T(4,128)S(1)}, u32[]{:S(2)}, u32[]{:S(2)}) async-start(f32[32,4,4,128]{3,2,1,0:T(4,128)} %broadcast_in_dim.33), calls=%async_computation | async-start | bytes 524288 | tf_op jit(solution)/shard_map/all_to_all | solution.py:108
  11.8 0.7 copy-start.9
  12.4 0.7 copy-start.8
  22.2 0.8 copy-start.10
  23.5 0.7 copy-start.14
  25.4 14.5 %all-to-all-start.1 = ((bf16[32,48,128]{2,1,0:T(8,128)(2,1)}), bf16[32,48,128]{2,1,0:T(8,128)(2,1)S(1)}, u32[]{:S(2)}, u32[]{:S(2)}) async-start(bf16[32,48,128]{2,1,0:T(8,128)(2,1)} %pad_maximum_fusion), calls=%async_computation.1 | async-start | bytes 786432 | tf_op jit(solution)/shard_map/all_to_all | solution.py:187
  40.8 0.9 %copy-start.4 = (bf16[128,512]{1,0:T(8,128)(2,1)S(1)}, bf16[128,512]{1,0:T(8,128)(2,1)}, u32[]{:S(2)}) copy-start(bf16[128,512]{1,0:T(8,128)(2,1)} %param.21) | copy-start | bytes 393220
  41.0 0.7 copy-start.2
  44.4 1.0 %copy-start.3 = (f32[4,32,4,128]{3,2,1,0:T(4,128)S(1)}, f32[4,32,4,128]{3,2,1,0:T(4,128)}, u32[]{:S(2)}) copy-start(f32[4,32,4,128]{3,2,1,0:T(4,128)} %copy-done.2) | copy-start | bytes 786436
  44.4 1.0 %copy-start.11 = (bf16[128,128]{1,0:T(8,128)(2,1)S(1)}, bf16[128,128]{1,0:T(8,128)(2,1)}, u32[]{:S(2)}) copy-start(bf16[128,128]{1,0:T(8,128)(2,1)} %param.23) | copy-start | bytes 98308
  45.7 0.8 %copy-start.5 = (bf16[128,256]{1,0:T(8,128)(2,1)S(1)}, bf16[128,256]{1,0:T(8,128)(2,1)}, u32[]{:S(2)}) copy-start(bf16[128,256]{1,0:T(8,128)(2,1)} %param.25) | copy-start | bytes 196612
  45.7 0.9 %copy-start.6 = (bf16[128,256]{1,0:T(8,128)(2,1)S(1)}, bf16[128,256]{1,0:T(8,128)(2,1)}, u32[]{:S(2)}) copy-start(bf16[128,256]{1,0:T(8,128)(2,1)} %param.24) | copy-start | bytes 196612
  48.0 14.1 %all-to-all-start.2 = ((bf16[128,2,4,128]{3,2,1,0:T(4,128)(2,1)}), bf16[128,2,4,128]{3,2,1,0:T(4,128)(2,1)S(1)}, u32[]{:S(2)}, u32[]{:S(2)}) async-start(bf16[128,2,4,128]{3,2,1,0:T(4,128)(2,1)} %copy.168), calls=%async_computation.2 | async-start | bytes 524288 | tf_op jit(solution)/shard_map/all_to_all | solution.py:248
  51.9 4.8 %collective-permute-start = (bf16[16,4,128]{2,0,1:T(8,128)(2,1)S(1)}, bf16[16,4,128]{2,0,1:T(8,128)(2,1)S(1)}, u32[]{:S(2)}, u32[]{:S(2)}) collective-permute-start(bf16[16,4,128]{2,0,1:T(8,128)(2,1)S(1)} %get-tuple-element.19), channel_id=1, source_target_pairs={{0,4},{4,8},{8,12},{12,16},{16,20},{20,24},{24,28},{28,0},{1,5},{5... | collective-permute-start | bytes 49160 | tf_op jit(solution)/shard_map/ppermute | solution.py:268
  52.2 4.8 %collective-permute-start.1 = (bf16[16,4,128]{2,0,1:T(8,128)(2,1)S(1)}, bf16[16,4,128]{2,0,1:T(8,128)(2,1)S(1)}, u32[]{:S(2)}, u32[]{:S(2)}) collective-permute-start(bf16[16,4,128]{2,0,1:T(8,128)(2,1)S(1)} %get-tuple-element.18), channel_id=1, source_target_pairs={{0,8},{4,12},{8,16},{12,20},{16,24},{20,28},{24,0},{28,4},{1,9},{5... | collective-permute-start | bytes 49160 | tf_op jit(solution)/shard_map/ppermute | solution.py:268
  53.8 4.0 %collective-permute-start.2 = (bf16[16,4,128]{2,0,1:T(8,128)(2,1)S(1)}, bf16[16,4,128]{2,0,1:T(8,128)(2,1)S(1)}, u32[]{:S(2)}, u32[]{:S(2)}) collective-permute-start(bf16[16,4,128]{2,0,1:T(8,128)(2,1)S(1)} %get-tuple-element.17), channel_id=1, source_target_pairs={{0,12},{4,16},{8,20},{12,24},{16,28},{20,0},{24,4},{28,8},{1,13},{... | collective-permute-start | bytes 49160 | tf_op jit(solution)/shard_map/ppermute | solution.py:268
  56.1 8.0 %collective-permute-start.3 = (bf16[16,4,128]{2,0,1:T(8,128)(2,1)S(1)}, bf16[16,4,128]{2,0,1:T(8,128)(2,1)S(1)}, u32[]{:S(2)}, u32[]{:S(2)}) collective-permute-start(bf16[16,4,128]{2,0,1:T(8,128)(2,1)S(1)} %get-tuple-element.16), channel_id=1, source_target_pairs={{0,16},{4,20},{8,24},{12,28},{16,0},{20,4},{24,8},{28,12},{1,17},{... | collective-permute-start | bytes 49160 | tf_op jit(solution)/shard_map/ppermute | solution.py:268
  63.2 7.6 %collective-permute-start.4 = (bf16[16,4,128]{2,0,1:T(8,128)(2,1)S(1)}, bf16[16,4,128]{2,0,1:T(8,128)(2,1)S(1)}, u32[]{:S(2)}, u32[]{:S(2)}) collective-permute-start(bf16[16,4,128]{2,0,1:T(8,128)(2,1)S(1)} %get-tuple-element.15), channel_id=1, source_target_pairs={{0,20},{4,24},{8,28},{12,0},{16,4},{20,8},{24,12},{28,16},{1,21},{... | collective-permute-start | bytes 49160 | tf_op jit(solution)/shard_map/ppermute | solution.py:268
  65.1 13.2 %all-to-all-start.3 = ((f32[32,16,128]{2,1,0:T(8,128)}), f32[32,16,128]{2,1,0:T(8,128)S(1)}, u32[]{:S(2)}, u32[]{:S(2)}) async-start(f32[32,16,128]{2,1,0:T(8,128)} %reshape.442), calls=%async_computation.3 | async-start | bytes 524288 | tf_op jit(solution)/shard_map/all_to_all | solution.py:273
  68.1 4.2 %collective-permute-start.5 = (bf16[16,4,128]{2,0,1:T(8,128)(2,1)S(1)}, bf16[16,4,128]{2,0,1:T(8,128)(2,1)S(1)}, u32[]{:S(2)}, u32[]{:S(2)}) collective-permute-start(bf16[16,4,128]{2,0,1:T(8,128)(2,1)S(1)} %get-tuple-element.14), channel_id=1, source_target_pairs={{0,24},{4,28},{8,0},{12,4},{16,8},{20,12},{24,16},{28,20},{1,25},{... | collective-permute-start | bytes 49160 | tf_op jit(solution)/shard_map/ppermute | solution.py:268
  70.8 1.6 %collective-permute-start.6 = (bf16[16,4,128]{2,0,1:T(8,128)(2,1)S(1)}, bf16[16,4,128]{2,0,1:T(8,128)(2,1)S(1)}, u32[]{:S(2)}, u32[]{:S(2)}) collective-permute-start(bf16[16,4,128]{2,0,1:T(8,128)(2,1)S(1)} %get-tuple-element.13), channel_id=1, source_target_pairs={{0,28},{4,0},{8,4},{12,8},{16,12},{20,16},{24,20},{28,24},{1,29},{... | collective-permute-start | bytes 49160 | tf_op jit(solution)/shard_map/ppermute | solution.py:268
  74.1 0.8 copy-start.12
  78.9 0.8 copy-start.7

commit v18 on v17

--- a/solution.py
+++ b/solution.py
@@ -258,7 +258,7 @@
         .reshape(device_count, channels_here, block_rows, block_cols)
     )
     raw_chunks = second_pair.reshape(rows_here, n_row, block_rows, channels).transpose(1, 2, 0, 3)
-    early = n_row // 2
+    early = n_row - 3
     raw_pieces = [lax.dynamic_index_in_dim(raw_chunks, row_index, 0, keepdims=False)]
     for shift in range(1, n_row):
         if shift == early + 1:

time: 81.4 us -> 81.7 us (level)
    all_to_all x1, waiting for transfers between devices: 4.28 us -> 2.17 us  [shards(): edges_got = lax.all_to_all(edges, ('row', 'col'), 0, 2, tiled=True)]
    ppermute x7, waiting for transfers between devices: 2.72 us -> 4.55 us  [shards(): lax.ppermute(piece, 'row', perm=[(r, (r + shift) % n_row) for r in range(...]
where the time goes in v18:
time: 81.7 us; the launch traced here: 80.9 us
  waiting for transfers between devices  29.3 us (36%)
  starting transfers between devices  25.3 us (31%)
  local copies, waits for them, and re-layouts  13.8 us (17%)
  matrix products  6.34 us (8%)
  other arithmetic  4.88 us (6%)
  between operations  1.33 us (2%)
    all_to_all x1, waiting for transfers between devices, shards(): lax.all_to_all(jnp.concatenate([pair_chunks, bias_chunks], axis=1), ('row...  11.6 us
    ppermute x7, starting transfers between devices, shards(): lax.ppermute(piece, 'row', perm=[(r, (r + shift) % n_row) for r in range(...  8.31 us
    all_to_all x1, waiting for transfers between devices, gather_lines(): got = lax.all_to_all(sent, ('row', 'col'), 0, 0, tiled=True)  7.48 us
    all_to_all x1, starting transfers between devices, gather_lines(): got = lax.all_to_all(sent, ('row', 'col'), 0, 0, tiled=True)  7.33 us
    unnamed x38, local copies, waits for them, and re-layouts  6.73 us
    ppermute x7, waiting for transfers between devices, shards(): lax.ppermute(piece, 'row', perm=[(r, (r + shift) % n_row) for r in range(...  4.55 us
    all_to_all x1, starting transfers between devices, shards(): edges_got = lax.all_to_all(edges, ('row', 'col'), 0, 2, tiled=True)  3.82 us
    all_to_all x1, waiting for transfers between devices, shards(): lax.all_to_all(product_sent.reshape(device_count, -1, lanes), ('row', 'co...  3.51 us
  transfers between devices with their start and end apart: 11, of which 8 were waited for; matrix products, arithmetic and copies ran while one was open for 6% of the time, Pallas kernels for 0%

profile of v18, /device:TPU:0, one launch (start us, length us, event | category | flops | bytes accessed | tf_op | source)
XLA Modules:
  0.0 80.9 jit_solution(17243219613448022681)
XLA Ops:
  0.0 1.1 %convert_reduce_fusion = f32[4,128]{1,0:T(4,128)S(1)} fusion(bf16[4,128,128]{2,1,0:T(8,128)(2,1)} %param.14), kind=kLoop, calls=%fused_computation.39 | loop fusion | flops 130560 | bytes 133120 | tf_op jit(solution)/shard_map/reduce_sum | solution.py:9
  1.4 0.7 copy-done.13
  2.0 0.3 convolution_bitcast_fusion.1
  2.4 0.7 broadcast_in_dim.33
  3.1 7.3 %all-to-all-start = ((f32[32,4,4,128]{3,2,1,0:T(4,128)}), f32[32,4,4,128]{3,2,1,0:T(4,128)S(1)}, u32[]{:S(2)}, u32[]{:S(2)}) async-start(f32[32,4,4,128]{3,2,1,0:T(4,128)} %broadcast_in_dim.33), calls=%async_computation | async-start | bytes 524288 | tf_op jit(solution)/shard_map/all_to_all | solution.py:108
  11.1 0.4 fusion.64
  11.8 0.6 copy-done.9
  12.4 0.6 copy-done.8
  13.2 7.5 %all-to-all-done = f32[32,4,4,128]{3,2,1,0:T(4,128)S(1)} async-done(((f32[32,4,4,128]{3,2,1,0:T(4,128)}), f32[32,4,4,128]{3,2,1,0:T(4,128)S(1)}, u32[]{:S(2)}, u32[]{:S(2)}) %all-to-all-start) | async-done | bytes 262176 | tf_op jit(solution)/shard_map/all_to_all | solution.py:108
  20.9 0.4 fusion.7
  21.3 0.6 fusion.102
  21.9 0.3 fusion.18
  22.4 0.6 copy-done.10
  23.6 0.7 copy-done.14
  24.2 0.3 convert_bitcast_fusion.2
  24.7 0.8 pad_maximum_fusion
  25.4 2.7 %all-to-all-start.1 = ((bf16[32,48,128]{2,1,0:T(8,128)(2,1)}), bf16[32,48,128]{2,1,0:T(8,128)(2,1)S(1)}, u32[]{:S(2)}, u32[]{:S(2)}) async-start(bf16[32,48,128]{2,1,0:T(8,128)(2,1)} %pad_maximum_fusion), calls=%async_computation.1 | async-start | bytes 786432 | tf_op jit(solution)/shard_map/all_to_all | solution.py:187
  28.4 11.6 %all-to-all-done.1 = bf16[32,48,128]{2,1,0:T(8,128)(2,1)S(1)} async-done(((bf16[32,48,128]{2,1,0:T(8,128)(2,1)}), bf16[32,48,128]{2,1,0:T(8,128)(2,1)S(1)}, u32[]{:S(2)}, u32[]{:S(2)}) %all-to-all-start.1) | async-done | bytes 393248 | tf_op jit(solution)/shard_map/all_to_all | solution.py:187
  41.1 0.6 copy-done.2
  41.7 0.3 fusion.54
  43.2 0.4 fusion.9
  43.5 0.6 fusion.103
  44.1 0.3 fusion.19
  44.6 0.8 %copy-done.3 = f32[4,32,4,128]{3,2,1,0:T(4,128)S(1)} copy-done((f32[4,32,4,128]{3,2,1,0:T(4,128)S(1)}, f32[4,32,4,128]{3,2,1,0:T(4,128)}, u32[]{:S(2)}) %copy-start.3) | copy-done | bytes 262168
  45.4 0.3 convert_reduce_fusion.1
  46.0 0.6 copy-done.5
  46.6 0.4 fusion.58
  47.2 0.9 %copy.173 = bf16[128,2,4,128]{3,2,1,0:T(4,128)(2,1)} copy(bf16[128,2,4,128]{0,3,2,1:T(8,128)(2,1)S(1)} %maximum_bitcast_fusion) | data formatting | bytes 524288 | tf_op jit(solution)/shard_map/transpose | solution.py:247
  48.0 3.8 %all-to-all-start.2 = ((bf16[128,2,4,128]{3,2,1,0:T(4,128)(2,1)}), bf16[128,2,4,128]{3,2,1,0:T(4,128)(2,1)S(1)}, u32[]{:S(2)}, u32[]{:S(2)}) async-start(bf16[128,2,4,128]{3,2,1,0:T(4,128)(2,1)} %copy.173), calls=%async_computation.2 | async-start | bytes 524288 | tf_op jit(solution)/shard_map/all_to_all | solution.py:248
  51.9 0.3 collective-permute-start
  52.2 1.6 %collective-permute-start.1 = (bf16[16,4,128]{2,0,1:T(8,128)(2,1)S(1)}, bf16[16,4,128]{2,0,1:T(8,128)(2,1)S(1)}, u32[]{:S(2)}, u32[]{:S(2)}) collective-permute-start(bf16[16,4,128]{2,0,1:T(8,128)(2,1)S(1)} %get-tuple-element.18), channel_id=1, source_target_pairs={{0,8},{4,12},{8,16},{12,20},{16,24},{20,28},{24,0},{28,4},{1,9},{5... | collective-permute-start | bytes 49160 | tf_op jit(solution)/shard_map/ppermute | solution.py:268
  53.8 2.3 %collective-permute-start.2 = (bf16[16,4,128]{2,0,1:T(8,128)(2,1)S(1)}, bf16[16,4,128]{2,0,1:T(8,128)(2,1)S(1)}, u32[]{:S(2)}, u32[]{:S(2)}) collective-permute-start(bf16[16,4,128]{2,0,1:T(8,128)(2,1)S(1)} %get-tuple-element.17), channel_id=1, source_target_pairs={{0,12},{4,16},{8,20},{12,24},{16,28},{20,0},{24,4},{28,8},{1,13},{... | collective-permute-start | bytes 49160 | tf_op jit(solution)/shard_map/ppermute | solution.py:268
  56.1 0.6 collective-permute-start.3
  57.0 0.8 %collective-permute-done.2 = bf16[16,4,128]{2,0,1:T(8,128)(2,1)S(1)} collective-permute-done((bf16[16,4,128]{2,0,1:T(8,128)(2,1)S(1)}, bf16[16,4,128]{2,0,1:T(8,128)(2,1)S(1)}, u32[]{:S(2)}, u32[]{:S(2)}) %collective-permute-start.2) | collective-permute-done | bytes 16416 | tf_op jit(solution)/shard_map/ppermute | solution.py:268
  57.8 2.1 %collective-permute-done.3 = bf16[16,4,128]{2,0,1:T(8,128)(2,1)S(1)} collective-permute-done((bf16[16,4,128]{2,0,1:T(8,128)(2,1)S(1)}, bf16[16,4,128]{2,0,1:T(8,128)(2,1)S(1)}, u32[]{:S(2)}, u32[]{:S(2)}) %collective-permute-start.3) | collective-permute-done | bytes 16416 | tf_op jit(solution)/shard_map/ppermute | solution.py:268
  59.9 2.2 %all-to-all-done.2 = bf16[128,2,4,128]{3,2,1,0:T(4,128)(2,1)S(1)} async-done(((bf16[128,2,4,128]{3,2,1,0:T(4,128)(2,1)}), bf16[128,2,4,128]{3,2,1,0:T(4,128)(2,1)S(1)}, u32[]{:S(2)}, u32[]{:S(2)}) %all-to-all-start.2) | async-done | bytes 262176 | tf_op jit(solution)/shard_map/all_to_all | solution.py:248
  62.6 0.4 reshape.439
  63.2 1.0 %collective-permute-start.5 = (bf16[16,4,128]{2,0,1:T(8,128)(2,1)S(1)}, bf16[16,4,128]{2,0,1:T(8,128)(2,1)S(1)}, u32[]{:S(2)}, u32[]{:S(2)}) collective-permute-start(bf16[16,4,128]{2,0,1:T(8,128)(2,1)S(1)} %get-tuple-element.14), channel_id=1, source_target_pairs={{0,24},{4,28},{8,0},{12,4},{16,8},{20,12},{24,16},{28,20},{1,25},{... | collective-permute-start | bytes 49160 | tf_op jit(solution)/shard_map/ppermute | solution.py:268
  64.2 1.0 %reshape.442 = f32[32,16,128]{2,1,0:T(8,128)} reshape(f32[32,4,16,32]{3,2,1,0:T(8,128)S(1)} %bitcast.222) | data formatting | bytes 524288 | tf_op jit(solution)/shard_map/reshape | solution.py:274
  65.2 3.2 %all-to-all-start.3 = ((f32[32,16,128]{2,1,0:T(8,128)}), f32[32,16,128]{2,1,0:T(8,128)S(1)}, u32[]{:S(2)}, u32[]{:S(2)}) async-start(f32[32,16,128]{2,1,0:T(8,128)} %reshape.442), calls=%async_computation.3 | async-start | bytes 524288 | tf_op jit(solution)/shard_map/all_to_all | solution.py:273
  68.3 2.4 %collective-permute-start.6 = (bf16[16,4,128]{2,0,1:T(8,128)(2,1)S(1)}, bf16[16,4,128]{2,0,1:T(8,128)(2,1)S(1)}, u32[]{:S(2)}, u32[]{:S(2)}) collective-permute-start(bf16[16,4,128]{2,0,1:T(8,128)(2,1)S(1)} %get-tuple-element.13), channel_id=1, source_target_pairs={{0,28},{4,0},{8,4},{12,8},{16,12},{20,16},{24,20},{28,24},{1,29},{... | collective-permute-start | bytes 49160 | tf_op jit(solution)/shard_map/ppermute | solution.py:268
  70.8 1.4 %collective-permute-done.6 = bf16[16,4,128]{2,0,1:T(8,128)(2,1)S(1)} collective-permute-done((bf16[16,4,128]{2,0,1:T(8,128)(2,1)S(1)}, bf16[16,4,128]{2,0,1:T(8,128)(2,1)S(1)}, u32[]{:S(2)}, u32[]{:S(2)}) %collective-permute-start.6) | collective-permute-done | bytes 16416 | tf_op jit(solution)/shard_map/ppermute | solution.py:268
  72.2 0.6 gather_fusion
  74.1 0.6 copy-done.12
  74.7 0.3 fusion.13
  75.1 3.5 %all-to-all-done.3 = f32[32,16,128]{2,1,0:T(8,128)S(1)} async-done(((f32[32,16,128]{2,1,0:T(8,128)}), f32[32,16,128]{2,1,0:T(8,128)S(1)}, u32[]{:S(2)}, u32[]{:S(2)}) %all-to-all-start.3) | async-done | bytes 262176 | tf_op jit(solution)/shard_map/all_to_all | solution.py:273
  79.3 0.6 copy-done.7
  80.0 1.0 %fusion.16 = bf16[16,32,128]{2,1,0:T(8,128)(2,1)} fusion(f32[16,32,128]{2,1,0:T(8,128)S(1)} %bitcast.235, f32[16,32,128]{2,1,0:T(8,128)S(1)} %bitcast.246, bf16[16,32,128]{1,0,2:T(8,128)(2,1)S(1)} %multiply_convert_fusion, bf16[128,128]{1,0:T(8,128)(2,1)S(1)} %copy-done.7), kind=kOutput, calls=%fused_computation.23 | convolution fusion | flops 16973824 | bytes 819200 | tf_op jit(solution)/shard_map/dot_general | solution.py:282
  (109 shorter events, 7.6 us)
Async XLA Ops:
  0.0 11.1 %copy-start = (bf16[128,512]{1,0:T(8,128)(2,1)S(1)}, bf16[128,512]{1,0:T(8,128)(2,1)}, u32[]{:S(2)}) copy-start(bf16[128,512]{1,0:T(8,128)(2,1)} %param.18) | copy-start | bytes 393220
  0.0 1.1 %copy-start.1 = (bf16[4,128,128]{2,1,0:T(8,128)(2,1)S(1)}, bf16[4,128,128]{2,1,0:T(8,128)(2,1)}, u32[]{:S(2)}) copy-start(bf16[4,128,128]{2,1,0:T(8,128)(2,1)} %param.14) | copy-start | bytes 393220
  1.4 0.7 copy-start.13
  3.1 17.6 %all-to-all-start = ((f32[32,4,4,128]{3,2,1,0:T(4,128)}), f32[32,4,4,128]{3,2,1,0:T(4,128)S(1)}, u32[]{:S(2)}, u32[]{:S(2)}) async-start(f32[32,4,4,128]{3,2,1,0:T(4,128)} %broadcast_in_dim.33), calls=%async_computation | async-start | bytes 524288 | tf_op jit(solution)/shard_map/all_to_all | solution.py:108
  11.8 0.7 copy-start.9
  12.4 0.7 copy-start.8
  22.2 0.8 copy-start.10
  23.5 0.7 copy-start.14
  25.4 14.5 %all-to-all-start.1 = ((bf16[32,48,128]{2,1,0:T(8,128)(2,1)}), bf16[32,48,128]{2,1,0:T(8,128)(2,1)S(1)}, u32[]{:S(2)}, u32[]{:S(2)}) async-start(bf16[32,48,128]{2,1,0:T(8,128)(2,1)} %pad_maximum_fusion), calls=%async_computation.1 | async-start | bytes 786432 | tf_op jit(solution)/shard_map/all_to_all | solution.py:187
  40.8 0.9 %copy-start.4 = (bf16[128,512]{1,0:T(8,128)(2,1)S(1)}, bf16[128,512]{1,0:T(8,128)(2,1)}, u32[]{:S(2)}) copy-start(bf16[128,512]{1,0:T(8,128)(2,1)} %param.21) | copy-start | bytes 393220
  41.0 0.7 copy-start.2
  44.4 1.0 %copy-start.3 = (f32[4,32,4,128]{3,2,1,0:T(4,128)S(1)}, f32[4,32,4,128]{3,2,1,0:T(4,128)}, u32[]{:S(2)}) copy-start(f32[4,32,4,128]{3,2,1,0:T(4,128)} %copy-done.2) | copy-start | bytes 786436
  44.4 1.0 %copy-start.11 = (bf16[128,128]{1,0:T(8,128)(2,1)S(1)}, bf16[128,128]{1,0:T(8,128)(2,1)}, u32[]{:S(2)}) copy-start(bf16[128,128]{1,0:T(8,128)(2,1)} %param.23) | copy-start | bytes 98308
  45.7 0.8 %copy-start.5 = (bf16[128,256]{1,0:T(8,128)(2,1)S(1)}, bf16[128,256]{1,0:T(8,128)(2,1)}, u32[]{:S(2)}) copy-start(bf16[128,256]{1,0:T(8,128)(2,1)} %param.25) | copy-start | bytes 196612
  45.7 0.9 %copy-start.6 = (bf16[128,256]{1,0:T(8,128)(2,1)S(1)}, bf16[128,256]{1,0:T(8,128)(2,1)}, u32[]{:S(2)}) copy-start(bf16[128,256]{1,0:T(8,128)(2,1)} %param.24) | copy-start | bytes 196612
  48.0 14.1 %all-to-all-start.2 = ((bf16[128,2,4,128]{3,2,1,0:T(4,128)(2,1)}), bf16[128,2,4,128]{3,2,1,0:T(4,128)(2,1)S(1)}, u32[]{:S(2)}, u32[]{:S(2)}) async-start(bf16[128,2,4,128]{3,2,1,0:T(4,128)(2,1)} %copy.173), calls=%async_computation.2 | async-start | bytes 524288 | tf_op jit(solution)/shard_map/all_to_all | solution.py:248
  51.9 4.9 %collective-permute-start = (bf16[16,4,128]{2,0,1:T(8,128)(2,1)S(1)}, bf16[16,4,128]{2,0,1:T(8,128)(2,1)S(1)}, u32[]{:S(2)}, u32[]{:S(2)}) collective-permute-start(bf16[16,4,128]{2,0,1:T(8,128)(2,1)S(1)} %get-tuple-element.19), channel_id=1, source_target_pairs={{0,4},{4,8},{8,12},{12,16},{16,20},{20,24},{24,28},{28,0},{1,5},{5... | collective-permute-start | bytes 49160 | tf_op jit(solution)/shard_map/ppermute | solution.py:268
  52.2 4.8 %collective-permute-start.1 = (bf16[16,4,128]{2,0,1:T(8,128)(2,1)S(1)}, bf16[16,4,128]{2,0,1:T(8,128)(2,1)S(1)}, u32[]{:S(2)}, u32[]{:S(2)}) collective-permute-start(bf16[16,4,128]{2,0,1:T(8,128)(2,1)S(1)} %get-tuple-element.18), channel_id=1, source_target_pairs={{0,8},{4,12},{8,16},{12,20},{16,24},{20,28},{24,0},{28,4},{1,9},{5... | collective-permute-start | bytes 49160 | tf_op jit(solution)/shard_map/ppermute | solution.py:268
  53.8 4.0 %collective-permute-start.2 = (bf16[16,4,128]{2,0,1:T(8,128)(2,1)S(1)}, bf16[16,4,128]{2,0,1:T(8,128)(2,1)S(1)}, u32[]{:S(2)}, u32[]{:S(2)}) collective-permute-start(bf16[16,4,128]{2,0,1:T(8,128)(2,1)S(1)} %get-tuple-element.17), channel_id=1, source_target_pairs={{0,12},{4,16},{8,20},{12,24},{16,28},{20,0},{24,4},{28,8},{1,13},{... | collective-permute-start | bytes 49160 | tf_op jit(solution)/shard_map/ppermute | solution.py:268
  56.1 3.8 %collective-permute-start.3 = (bf16[16,4,128]{2,0,1:T(8,128)(2,1)S(1)}, bf16[16,4,128]{2,0,1:T(8,128)(2,1)S(1)}, u32[]{:S(2)}, u32[]{:S(2)}) collective-permute-start(bf16[16,4,128]{2,0,1:T(8,128)(2,1)S(1)} %get-tuple-element.16), channel_id=1, source_target_pairs={{0,16},{4,20},{8,24},{12,28},{16,0},{20,4},{24,8},{28,12},{1,17},{... | collective-permute-start | bytes 49160 | tf_op jit(solution)/shard_map/ppermute | solution.py:268
  56.6 7.5 %collective-permute-start.4 = (bf16[16,4,128]{2,0,1:T(8,128)(2,1)S(1)}, bf16[16,4,128]{2,0,1:T(8,128)(2,1)S(1)}, u32[]{:S(2)}, u32[]{:S(2)}) collective-permute-start(bf16[16,4,128]{2,0,1:T(8,128)(2,1)S(1)} %get-tuple-element.15), channel_id=1, source_target_pairs={{0,20},{4,24},{8,28},{12,0},{16,4},{20,8},{24,12},{28,16},{1,21},{... | collective-permute-start | bytes 49160 | tf_op jit(solution)/shard_map/ppermute | solution.py:268
  63.2 7.6 %collective-permute-start.5 = (bf16[16,4,128]{2,0,1:T(8,128)(2,1)S(1)}, bf16[16,4,128]{2,0,1:T(8,128)(2,1)S(1)}, u32[]{:S(2)}, u32[]{:S(2)}) collective-permute-start(bf16[16,4,128]{2,0,1:T(8,128)(2,1)S(1)} %get-tuple-element.14), channel_id=1, source_target_pairs={{0,24},{4,28},{8,0},{12,4},{16,8},{20,12},{24,16},{28,20},{1,25},{... | collective-permute-start | bytes 49160 | tf_op jit(solution)/shard_map/ppermute | solution.py:268
  65.2 13.4 %all-to-all-start.3 = ((f32[32,16,128]{2,1,0:T(8,128)}), f32[32,16,128]{2,1,0:T(8,128)S(1)}, u32[]{:S(2)}, u32[]{:S(2)}) async-start(f32[32,16,128]{2,1,0:T(8,128)} %reshape.442), calls=%async_computation.3 | async-start | bytes 524288 | tf_op jit(solution)/shard_map/all_to_all | solution.py:273
  68.3 3.9 %collective-permute-start.6 = (bf16[16,4,128]{2,0,1:T(8,128)(2,1)S(1)}, bf16[16,4,128]{2,0,1:T(8,128)(2,1)S(1)}, u32[]{:S(2)}, u32[]{:S(2)}) collective-permute-start(bf16[16,4,128]{2,0,1:T(8,128)(2,1)S(1)} %get-tuple-element.13), channel_id=1, source_target_pairs={{0,28},{4,0},{8,4},{12,8},{16,12},{20,16},{24,20},{28,24},{1,29},{... | collective-permute-start | bytes 49160 | tf_op jit(solution)/shard_map/ppermute | solution.py:268
  74.0 0.8 copy-start.12
  79.2 0.8 copy-start.7

commit v19 on v17

--- a/solution.py
+++ b/solution.py
@@ -267,8 +267,8 @@
         raw_pieces.append(
             lax.ppermute(piece, "row", perm=[(r, (r + shift) % n_row) for r in range(n_row)])
         )
-    sources = (row_index - jnp.arange(n_row, dtype=jnp.int32)) % n_row
-    raw_got = jnp.take(jnp.stack(raw_pieces, axis=0), sources, axis=0)
+    doubled = jnp.stack(raw_pieces[::-1] + raw_pieces[::-1], axis=0)
+    raw_got = lax.dynamic_slice_in_dim(doubled, (n_row - 1 - row_index) % n_row, n_row, 0)
     own_pair = raw_got.transpose(1, 0, 2, 3).reshape(block_rows, block_cols, channels)
     product_got = lax.all_to_all(
         product_sent.reshape(device_count, -1, lanes), ("row", "col"), 0, 0, tiled=True

time: 81.4 us -> 85.3 us (1.048)
  waiting for transfers between devices: 29.2 us -> 34.2 us
    all_to_all x1, waiting for transfers between devices: 4.28 us -> 10.1 us  [shards(): edges_got = lax.all_to_all(edges, ('row', 'col'), 0, 2, tiled=True)]
    all_to_all x1, waiting for transfers between devices: 3.08 us -> 0.48 us  [shards(): lax.all_to_all(product_sent.reshape(device_count, -1, lanes), ('row', 'co...]
    ppermute x7, waiting for transfers between devices: 2.72 us -> 4.31 us  [shards(): lax.ppermute(piece, 'row', perm=[(r, (r + shift) % n_row) for r in range(...]
    ppermute x7, starting transfers between devices: 8.38 us -> 7.13 us  [shards(): lax.ppermute(piece, 'row', perm=[(r, (r + shift) % n_row) for r in range(...]
    unnamed x38 -> x50, local copies, waits for them, and re-layouts: 6.73 us -> 7.02 us
  transfers between devices with their start and end apart: 11 -> 11, of which waited for: 8 -> 6; matrix products, arithmetic and copies ran while one was open for 6% -> 4% of each run, Pallas kernels for 0% -> 0%
where the time goes in v19:
time: 85.3 us; the launch traced here: 84.5 us
  waiting for transfers between devices  34.2 us (40%)
  starting transfers between devices  24.6 us (29%)
  local copies, waits for them, and re-layouts  13.1 us (15%)
  matrix products  6.34 us (7%)
  other arithmetic  4.88 us (6%)
  between operations  1.46 us (2%)
    all_to_all x1, waiting for transfers between devices, shards(): lax.all_to_all(jnp.concatenate([pair_chunks, bias_chunks], axis=1), ('row...  11.8 us
    all_to_all x1, waiting for transfers between devices, shards(): edges_got = lax.all_to_all(edges, ('row', 'col'), 0, 2, tiled=True)  10.1 us
    all_to_all x1, waiting for transfers between devices, gather_lines(): got = lax.all_to_all(sent, ('row', 'col'), 0, 0, tiled=True)  7.48 us
    all_to_all x1, starting transfers between devices, gather_lines(): got = lax.all_to_all(sent, ('row', 'col'), 0, 0, tiled=True)  7.33 us
    ppermute x7, starting transfers between devices, shards(): lax.ppermute(piece, 'row', perm=[(r, (r + shift) % n_row) for r in range(...  7.13 us
    unnamed x50, local copies, waits for them, and re-layouts  7.02 us
    ppermute x7, waiting for transfers between devices, shards(): lax.ppermute(piece, 'row', perm=[(r, (r + shift) % n_row) for r in range(...  4.31 us
    all_to_all x1, starting transfers between devices, shards(): edges_got = lax.all_to_all(edges, ('row', 'col'), 0, 2, tiled=True)  3.82 us
  transfers between devices with their start and end apart: 11, of which 6 were waited for; matrix products, arithmetic and copies ran while one was open for 4% of the time, Pallas kernels for 0%

profile of v19, /device:TPU:0, one launch (start us, length us, event | category | flops | bytes accessed | tf_op | source)
XLA Modules:
  0.0 84.5 jit_solution(13482237584507607012)
XLA Ops:
  0.0 1.1 %convert_reduce_fusion = f32[4,128]{1,0:T(4,128)S(1)} fusion(bf16[4,128,128]{2,1,0:T(8,128)(2,1)} %param.14), kind=kLoop, calls=%fused_computation.38 | loop fusion | flops 130560 | bytes 133120 | tf_op jit(solution)/shard_map/reduce_sum | solution.py:9
  1.4 0.7 copy-done.13
  2.0 0.3 convolution_bitcast_fusion.1
  2.4 0.7 broadcast_in_dim.25
  3.1 7.3 %all-to-all-start = ((f32[32,4,4,128]{3,2,1,0:T(4,128)}), f32[32,4,4,128]{3,2,1,0:T(4,128)S(1)}, u32[]{:S(2)}, u32[]{:S(2)}) async-start(f32[32,4,4,128]{3,2,1,0:T(4,128)} %broadcast_in_dim.25), calls=%async_computation | async-start | bytes 524288 | tf_op jit(solution)/shard_map/all_to_all | solution.py:108
  11.1 0.4 fusion.65
  11.8 0.6 copy-done.9
  12.4 0.6 copy-done.8
  13.2 7.5 %all-to-all-done = f32[32,4,4,128]{3,2,1,0:T(4,128)S(1)} async-done(((f32[32,4,4,128]{3,2,1,0:T(4,128)}), f32[32,4,4,128]{3,2,1,0:T(4,128)S(1)}, u32[]{:S(2)}, u32[]{:S(2)}) %all-to-all-start) | async-done | bytes 262176 | tf_op jit(solution)/shard_map/all_to_all | solution.py:108
  20.9 0.4 fusion.7
  21.3 0.6 fusion.98
  21.9 0.3 fusion.18
  22.4 0.6 copy-done.10
  23.0 0.3 convert_reduce_fusion.2
  23.6 0.7 copy-done.14
  24.2 0.3 convert_bitcast_fusion.1
  24.7 0.8 pad_maximum_fusion
  25.4 2.7 %all-to-all-start.1 = ((bf16[32,48,128]{2,1,0:T(8,128)(2,1)}), bf16[32,48,128]{2,1,0:T(8,128)(2,1)S(1)}, u32[]{:S(2)}, u32[]{:S(2)}) async-start(bf16[32,48,128]{2,1,0:T(8,128)(2,1)} %pad_maximum_fusion), calls=%async_computation.1 | async-start | bytes 786432 | tf_op jit(solution)/shard_map/all_to_all | solution.py:187
  28.2 11.8 %all-to-all-done.1 = bf16[32,48,128]{2,1,0:T(8,128)(2,1)S(1)} async-done(((bf16[32,48,128]{2,1,0:T(8,128)(2,1)}), bf16[32,48,128]{2,1,0:T(8,128)(2,1)S(1)}, u32[]{:S(2)}, u32[]{:S(2)}) %all-to-all-start.1) | async-done | bytes 393248 | tf_op jit(solution)/shard_map/all_to_all | solution.py:187
  41.1 0.6 copy-done.2
  41.7 0.3 fusion.56
  43.2 0.4 fusion.9
  43.5 0.6 fusion.99
  44.1 0.3 fusion.19
  44.6 0.8 copy-done.3
  45.4 0.3 convert_reduce_fusion.1
  46.0 0.6 copy-done.5
  46.6 0.4 fusion.59
  47.2 0.9 %copy.127 = bf16[128,2,4,128]{3,2,1,0:T(4,128)(2,1)} copy(bf16[128,2,4,128]{0,3,2,1:T(8,128)(2,1)S(1)} %maximum_bitcast_fusion) | data formatting | bytes 524288 | tf_op jit(solution)/shard_map/transpose | solution.py:247
  48.0 3.8 %all-to-all-start.2 = ((bf16[128,2,4,128]{3,2,1,0:T(4,128)(2,1)}), bf16[128,2,4,128]{3,2,1,0:T(4,128)(2,1)S(1)}, u32[]{:S(2)}, u32[]{:S(2)}) async-start(bf16[128,2,4,128]{3,2,1,0:T(4,128)(2,1)} %copy.127), calls=%async_computation.2 | async-start | bytes 524288 | tf_op jit(solution)/shard_map/all_to_all | solution.py:248
  52.0 10.1 %all-to-all-done.2 = bf16[128,2,4,128]{3,2,1,0:T(4,128)(2,1)S(1)} async-done(((bf16[128,2,4,128]{3,2,1,0:T(4,128)(2,1)}), bf16[128,2,4,128]{3,2,1,0:T(4,128)(2,1)S(1)}, u32[]{:S(2)}, u32[]{:S(2)}) %all-to-all-start.2) | async-done | bytes 262176 | tf_op jit(solution)/shard_map/all_to_all | solution.py:248
  62.6 0.4 reshape.384
  63.2 0.9 %collective-permute-start = (bf16[16,4,128]{2,1,0:T(4,128)(2,1)S(1)}, bf16[16,4,128]{2,1,0:T(4,128)(2,1)S(1)}, u32[]{:S(2)}, u32[]{:S(2)}) collective-permute-start(bf16[16,4,128]{2,1,0:T(4,128)(2,1)S(1)} %bitcast.258), channel_id=1, source_target_pairs={{0,28},{4,0},{8,4},{12,8},{16,12},{20,16},{24,20},{28,24},{1,29},{... | collective-permute-start | bytes 49160 | tf_op jit(solution)/shard_map/ppermute | solution.py:268
  64.1 1.5 %collective-permute-start.3 = (bf16[16,4,128]{2,1,0:T(4,128)(2,1)S(1)}, bf16[16,4,128]{2,1,0:T(4,128)(2,1)S(1)}, u32[]{:S(2)}, u32[]{:S(2)}) collective-permute-start(bf16[16,4,128]{2,1,0:T(4,128)(2,1)S(1)} %bitcast.254), channel_id=1, source_target_pairs={{0,16},{4,20},{8,24},{12,28},{16,0},{20,4},{24,8},{28,12},{1,17},{... | collective-permute-start | bytes 49160 | tf_op jit(solution)/shard_map/ppermute | solution.py:268
  65.7 1.0 %collective-permute-start.5 = (bf16[16,4,128]{2,1,0:T(4,128)(2,1)S(1)}, bf16[16,4,128]{2,1,0:T(4,128)(2,1)S(1)}, u32[]{:S(2)}, u32[]{:S(2)}) collective-permute-start(bf16[16,4,128]{2,1,0:T(4,128)(2,1)S(1)} %bitcast.256), channel_id=1, source_target_pairs={{0,8},{4,12},{8,16},{12,20},{16,24},{20,28},{24,0},{28,4},{1,9},{5... | collective-permute-start | bytes 49160 | tf_op jit(solution)/shard_map/ppermute | solution.py:268
  66.8 0.6 collective-permute-start.6
  67.3 1.0 %reshape.388 = f32[32,16,128]{2,1,0:T(8,128)} reshape(f32[32,4,16,32]{3,2,1,0:T(8,128)S(1)} %bitcast.227) | data formatting | bytes 524288 | tf_op jit(solution)/shard_map/reshape | solution.py:274
  68.3 3.6 %all-to-all-start.3 = ((f32[32,16,128]{2,1,0:T(8,128)}), f32[32,16,128]{2,1,0:T(8,128)S(1)}, u32[]{:S(2)}, u32[]{:S(2)}) async-start(f32[32,16,128]{2,1,0:T(8,128)} %reshape.388), calls=%async_computation.3 | async-start | bytes 524288 | tf_op jit(solution)/shard_map/all_to_all | solution.py:273
  72.0 2.7 %collective-permute-start.1 = (bf16[16,4,128]{2,1,0:T(4,128)(2,1)S(1)}, bf16[16,4,128]{2,1,0:T(4,128)(2,1)S(1)}, u32[]{:S(2)}, u32[]{:S(2)}) collective-permute-start(bf16[16,4,128]{2,1,0:T(4,128)(2,1)S(1)} %bitcast.260), channel_id=1, source_target_pairs={{0,24},{4,28},{8,0},{12,4},{16,8},{20,12},{24,16},{28,20},{1,25},{... | collective-permute-start | bytes 49160 | tf_op jit(solution)/shard_map/ppermute | solution.py:268
  74.7 1.4 %collective-permute-done.1 = bf16[16,4,128]{2,1,0:T(4,128)(2,1)S(1)} collective-permute-done((bf16[16,4,128]{2,1,0:T(4,128)(2,1)S(1)}, bf16[16,4,128]{2,1,0:T(4,128)(2,1)S(1)}, u32[]{:S(2)}, u32[]{:S(2)}) %collective-permute-start.1) | collective-permute-done | bytes 16416 | tf_op jit(solution)/shard_map/ppermute | solution.py:268
  76.2 0.3 collective-permute-start.2
  76.5 2.9 %collective-permute-done.2 = bf16[16,4,128]{2,1,0:T(4,128)(2,1)S(1)} collective-permute-done((bf16[16,4,128]{2,1,0:T(4,128)(2,1)S(1)}, bf16[16,4,128]{2,1,0:T(4,128)(2,1)S(1)}, u32[]{:S(2)}, u32[]{:S(2)}) %collective-permute-start.2) | collective-permute-done | bytes 16416 | tf_op jit(solution)/shard_map/ppermute | solution.py:268
  80.0 0.4 fusion.52
  80.6 0.7 copy-done.12
  81.4 0.3 fusion.13
  81.7 0.5 all-to-all-done.3
  82.9 0.6 copy-done.7
  83.6 1.0 %fusion.16 = bf16[16,32,128]{2,1,0:T(8,128)(2,1)} fusion(f32[16,32,128]{2,1,0:T(8,128)S(1)} %bitcast.239, f32[16,32,128]{2,1,0:T(8,128)S(1)} %bitcast.250, bf16[16,32,128]{1,0,2:T(8,128)(2,1)S(1)} %multiply_convert_fusion, bf16[128,128]{1,0:T(8,128)(2,1)S(1)} %copy-done.7), kind=kOutput, calls=%fused_computation.22 | convolution fusion | flops 16973824 | bytes 819200 | tf_op jit(solution)/shard_map/dot_general | solution.py:282
  (116 shorter events, 6.5 us)
Async XLA Ops:
  0.0 11.1 %copy-start = (bf16[128,512]{1,0:T(8,128)(2,1)S(1)}, bf16[128,512]{1,0:T(8,128)(2,1)}, u32[]{:S(2)}) copy-start(bf16[128,512]{1,0:T(8,128)(2,1)} %param.18) | copy-start | bytes 393220
  0.0 1.1 %copy-start.1 = (bf16[4,128,128]{2,1,0:T(8,128)(2,1)S(1)}, bf16[4,128,128]{2,1,0:T(8,128)(2,1)}, u32[]{:S(2)}) copy-start(bf16[4,128,128]{2,1,0:T(8,128)(2,1)} %param.14) | copy-start | bytes 393220
  1.4 0.7 copy-start.13
  3.1 17.6 %all-to-all-start = ((f32[32,4,4,128]{3,2,1,0:T(4,128)}), f32[32,4,4,128]{3,2,1,0:T(4,128)S(1)}, u32[]{:S(2)}, u32[]{:S(2)}) async-start(f32[32,4,4,128]{3,2,1,0:T(4,128)} %broadcast_in_dim.25), calls=%async_computation | async-start | bytes 524288 | tf_op jit(solution)/shard_map/all_to_all | solution.py:108
  11.8 0.7 copy-start.9
  12.4 0.7 copy-start.8
  22.2 0.8 copy-start.10
  23.5 0.7 copy-start.14
  25.4 14.5 %all-to-all-start.1 = ((bf16[32,48,128]{2,1,0:T(8,128)(2,1)}), bf16[32,48,128]{2,1,0:T(8,128)(2,1)S(1)}, u32[]{:S(2)}, u32[]{:S(2)}) async-start(bf16[32,48,128]{2,1,0:T(8,128)(2,1)} %pad_maximum_fusion), calls=%async_computation.1 | async-start | bytes 786432 | tf_op jit(solution)/shard_map/all_to_all | solution.py:187
  40.8 0.9 %copy-start.4 = (bf16[128,512]{1,0:T(8,128)(2,1)S(1)}, bf16[128,512]{1,0:T(8,128)(2,1)}, u32[]{:S(2)}) copy-start(bf16[128,512]{1,0:T(8,128)(2,1)} %param.21) | copy-start | bytes 393220
  41.0 0.7 copy-start.2
  44.4 1.0 %copy-start.3 = (f32[4,32,4,128]{3,2,1,0:T(4,128)S(1)}, f32[4,32,4,128]{3,2,1,0:T(4,128)}, u32[]{:S(2)}) copy-start(f32[4,32,4,128]{3,2,1,0:T(4,128)} %copy-done.2) | copy-start | bytes 786436
  44.4 1.0 %copy-start.11 = (bf16[128,128]{1,0:T(8,128)(2,1)S(1)}, bf16[128,128]{1,0:T(8,128)(2,1)}, u32[]{:S(2)}) copy-start(bf16[128,128]{1,0:T(8,128)(2,1)} %param.23) | copy-start | bytes 98308
  45.7 0.8 copy-start.5
  45.7 0.9 %copy-start.6 = (bf16[128,256]{1,0:T(8,128)(2,1)S(1)}, bf16[128,256]{1,0:T(8,128)(2,1)}, u32[]{:S(2)}) copy-start(bf16[128,256]{1,0:T(8,128)(2,1)} %param.24) | copy-start | bytes 196612
  48.0 14.1 %all-to-all-start.2 = ((bf16[128,2,4,128]{3,2,1,0:T(4,128)(2,1)}), bf16[128,2,4,128]{3,2,1,0:T(4,128)(2,1)S(1)}, u32[]{:S(2)}, u32[]{:S(2)}) async-start(bf16[128,2,4,128]{3,2,1,0:T(4,128)(2,1)} %copy.127), calls=%async_computation.2 | async-start | bytes 524288 | tf_op jit(solution)/shard_map/all_to_all | solution.py:248
  63.2 8.8 %collective-permute-start = (bf16[16,4,128]{2,1,0:T(4,128)(2,1)S(1)}, bf16[16,4,128]{2,1,0:T(4,128)(2,1)S(1)}, u32[]{:S(2)}, u32[]{:S(2)}) collective-permute-start(bf16[16,4,128]{2,1,0:T(4,128)(2,1)S(1)} %bitcast.258), channel_id=1, source_target_pairs={{0,28},{4,0},{8,4},{12,8},{16,12},{20,16},{24,20},{28,24},{1,29},{... | collective-permute-start | bytes 49160 | tf_op jit(solution)/shard_map/ppermute | solution.py:268
  64.1 15.3 %collective-permute-start.3 = (bf16[16,4,128]{2,1,0:T(4,128)(2,1)S(1)}, bf16[16,4,128]{2,1,0:T(4,128)(2,1)S(1)}, u32[]{:S(2)}, u32[]{:S(2)}) collective-permute-start(bf16[16,4,128]{2,1,0:T(4,128)(2,1)S(1)} %bitcast.254), channel_id=1, source_target_pairs={{0,16},{4,20},{8,24},{12,28},{16,0},{20,4},{24,8},{28,12},{1,17},{... | collective-permute-start | bytes 49160 | tf_op jit(solution)/shard_map/ppermute | solution.py:268
  65.7 13.8 %collective-permute-start.4 = (bf16[16,4,128]{2,1,0:T(4,128)(2,1)S(1)}, bf16[16,4,128]{2,1,0:T(4,128)(2,1)S(1)}, u32[]{:S(2)}, u32[]{:S(2)}) collective-permute-start(bf16[16,4,128]{2,1,0:T(4,128)(2,1)S(1)} %bitcast.255), channel_id=1, source_target_pairs={{0,12},{4,16},{8,20},{12,24},{16,28},{20,0},{24,4},{28,8},{1,13},{... | collective-permute-start | bytes 49160 | tf_op jit(solution)/shard_map/ppermute | solution.py:268
  65.7 13.7 %collective-permute-start.5 = (bf16[16,4,128]{2,1,0:T(4,128)(2,1)S(1)}, bf16[16,4,128]{2,1,0:T(4,128)(2,1)S(1)}, u32[]{:S(2)}, u32[]{:S(2)}) collective-permute-start(bf16[16,4,128]{2,1,0:T(4,128)(2,1)S(1)} %bitcast.256), channel_id=1, source_target_pairs={{0,8},{4,12},{8,16},{12,20},{16,24},{20,28},{24,0},{28,4},{1,9},{5... | collective-permute-start | bytes 49160 | tf_op jit(solution)/shard_map/ppermute | solution.py:268
  66.8 12.7 %collective-permute-start.6 = (bf16[16,4,128]{2,1,0:T(4,128)(2,1)S(1)}, bf16[16,4,128]{2,1,0:T(4,128)(2,1)S(1)}, u32[]{:S(2)}, u32[]{:S(2)}) collective-permute-start(bf16[16,4,128]{2,1,0:T(4,128)(2,1)S(1)} %bitcast.257), channel_id=1, source_target_pairs={{0,4},{4,8},{8,12},{12,16},{16,20},{20,24},{24,28},{28,0},{1,5},{5... | collective-permute-start | bytes 49160 | tf_op jit(solution)/shard_map/ppermute | solution.py:268
  68.3 13.9 %all-to-all-start.3 = ((f32[32,16,128]{2,1,0:T(8,128)}), f32[32,16,128]{2,1,0:T(8,128)S(1)}, u32[]{:S(2)}, u32[]{:S(2)}) async-start(f32[32,16,128]{2,1,0:T(8,128)} %reshape.388), calls=%async_computation.3 | async-start | bytes 524288 | tf_op jit(solution)/shard_map/all_to_all | solution.py:273
  72.0 4.2 %collective-permute-start.1 = (bf16[16,4,128]{2,1,0:T(4,128)(2,1)S(1)}, bf16[16,4,128]{2,1,0:T(4,128)(2,1)S(1)}, u32[]{:S(2)}, u32[]{:S(2)}) collective-permute-start(bf16[16,4,128]{2,1,0:T(4,128)(2,1)S(1)} %bitcast.260), channel_id=1, source_target_pairs={{0,24},{4,28},{8,0},{12,4},{16,8},{20,12},{24,16},{28,20},{1,25},{... | collective-permute-start | bytes 49160 | tf_op jit(solution)/shard_map/ppermute | solution.py:268
  76.2 3.2 %collective-permute-start.2 = (bf16[16,4,128]{2,1,0:T(4,128)(2,1)S(1)}, bf16[16,4,128]{2,1,0:T(4,128)(2,1)S(1)}, u32[]{:S(2)}, u32[]{:S(2)}) collective-permute-start(bf16[16,4,128]{2,1,0:T(4,128)(2,1)S(1)} %bitcast.259), channel_id=1, source_target_pairs={{0,20},{4,24},{8,28},{12,0},{16,4},{20,8},{24,12},{28,16},{1,21},{... | collective-permute-start | bytes 49160 | tf_op jit(solution)/shard_map/ppermute | solution.py:268
  80.6 0.8 copy-start.12
  82.8 0.8 copy-start.7

commit v20 on v18

--- a/solution.py
+++ b/solution.py
@@ -258,7 +258,7 @@
         .reshape(device_count, channels_here, block_rows, block_cols)
     )
     raw_chunks = second_pair.reshape(rows_here, n_row, block_rows, channels).transpose(1, 2, 0, 3)
-    early = n_row - 3
+    early = n_row // 4
     raw_pieces = [lax.dynamic_index_in_dim(raw_chunks, row_index, 0, keepdims=False)]
     for shift in range(1, n_row):
         if shift == early + 1:

time: 81.7 us -> 81.4 us (level)
    all_to_all x1, waiting for transfers between devices: 2.17 us -> 5.87 us  [shards(): edges_got = lax.all_to_all(edges, ('row', 'col'), 0, 2, tiled=True)]
    all_to_all x1, waiting for transfers between devices: 3.51 us -> 0.29 us  [shards(): lax.all_to_all(product_sent.reshape(device_count, -1, lanes), ('row', 'co...]
  transfers between devices with their start and end apart: 11 -> 11, of which waited for: 8 -> 6; matrix products, arithmetic and copies ran while one was open for 6% -> 6% of each run, Pallas kernels for 0% -> 0%
where the time goes in v20:
time: 81.4 us; the launch traced here: 80.6 us
  waiting for transfers between devices  29 us (36%)
  starting transfers between devices  25.3 us (31%)
  local copies, waits for them, and re-layouts  13.8 us (17%)
  matrix products  6.34 us (8%)
  other arithmetic  4.87 us (6%)
  between operations  1.35 us (2%)
    all_to_all x1, waiting for transfers between devices, shards(): lax.all_to_all(jnp.concatenate([pair_chunks, bias_chunks], axis=1), ('row...  11.6 us
    ppermute x7, starting transfers between devices, shards(): lax.ppermute(piece, 'row', perm=[(r, (r + shift) % n_row) for r in range(...  8.49 us
    all_to_all x1, waiting for transfers between devices, gather_lines(): got = lax.all_to_all(sent, ('row', 'col'), 0, 0, tiled=True)  7.48 us
    all_to_all x1, starting transfers between devices, gather_lines(): got = lax.all_to_all(sent, ('row', 'col'), 0, 0, tiled=True)  7.33 us
    unnamed x38, local copies, waits for them, and re-layouts  6.73 us
    all_to_all x1, waiting for transfers between devices, shards(): edges_got = lax.all_to_all(edges, ('row', 'col'), 0, 2, tiled=True)  5.87 us
    all_to_all x1, starting transfers between devices, shards(): edges_got = lax.all_to_all(edges, ('row', 'col'), 0, 2, tiled=True)  3.81 us
    ppermute x7, waiting for transfers between devices, shards(): lax.ppermute(piece, 'row', perm=[(r, (r + shift) % n_row) for r in range(...  3.76 us
  transfers between devices with their start and end apart: 11, of which 6 were waited for; matrix products, arithmetic and copies ran while one was open for 6% of the time, Pallas kernels for 0%

profile of v20, /device:TPU:0, one launch (start us, length us, event | category | flops | bytes accessed | tf_op | source)
XLA Modules:
  0.0 80.6 jit_solution(5659049506177669306)
XLA Ops:
  0.0 1.1 %convert_reduce_fusion = f32[4,128]{1,0:T(4,128)S(1)} fusion(bf16[4,128,128]{2,1,0:T(8,128)(2,1)} %param.14), kind=kLoop, calls=%fused_computation.39 | loop fusion | flops 130560 | bytes 133120 | tf_op jit(solution)/shard_map/reduce_sum | solution.py:9
  1.4 0.7 copy-done.13
  2.0 0.3 convolution_bitcast_fusion.1
  2.4 0.7 broadcast_in_dim.33
  3.1 7.3 %all-to-all-start = ((f32[32,4,4,128]{3,2,1,0:T(4,128)}), f32[32,4,4,128]{3,2,1,0:T(4,128)S(1)}, u32[]{:S(2)}, u32[]{:S(2)}) async-start(f32[32,4,4,128]{3,2,1,0:T(4,128)} %broadcast_in_dim.33), calls=%async_computation | async-start | bytes 524288 | tf_op jit(solution)/shard_map/all_to_all | solution.py:108
  11.1 0.4 fusion.64
  11.8 0.6 copy-done.9
  12.4 0.6 copy-done.8
  13.2 7.5 %all-to-all-done = f32[32,4,4,128]{3,2,1,0:T(4,128)S(1)} async-done(((f32[32,4,4,128]{3,2,1,0:T(4,128)}), f32[32,4,4,128]{3,2,1,0:T(4,128)S(1)}, u32[]{:S(2)}, u32[]{:S(2)}) %all-to-all-start) | async-done | bytes 262176 | tf_op jit(solution)/shard_map/all_to_all | solution.py:108
  20.9 0.4 fusion.7
  21.3 0.6 fusion.102
  21.9 0.3 fusion.18
  22.4 0.6 copy-done.10
  23.0 0.3 convert_reduce_fusion.2
  23.6 0.7 copy-done.14
  24.2 0.3 convert_bitcast_fusion.2
  24.7 0.8 pad_maximum_fusion
  25.4 2.7 %all-to-all-start.1 = ((bf16[32,48,128]{2,1,0:T(8,128)(2,1)}), bf16[32,48,128]{2,1,0:T(8,128)(2,1)S(1)}, u32[]{:S(2)}, u32[]{:S(2)}) async-start(bf16[32,48,128]{2,1,0:T(8,128)(2,1)} %pad_maximum_fusion), calls=%async_computation.1 | async-start | bytes 786432 | tf_op jit(solution)/shard_map/all_to_all | solution.py:187
  28.3 11.6 %all-to-all-done.1 = bf16[32,48,128]{2,1,0:T(8,128)(2,1)S(1)} async-done(((bf16[32,48,128]{2,1,0:T(8,128)(2,1)}), bf16[32,48,128]{2,1,0:T(8,128)(2,1)S(1)}, u32[]{:S(2)}, u32[]{:S(2)}) %all-to-all-start.1) | async-done | bytes 393248 | tf_op jit(solution)/shard_map/all_to_all | solution.py:187
  41.1 0.6 copy-done.2
  41.7 0.3 fusion.54
  43.2 0.4 fusion.9
  43.5 0.6 fusion.103
  44.1 0.3 fusion.19
  44.6 0.8 %copy-done.3 = f32[4,32,4,128]{3,2,1,0:T(4,128)S(1)} copy-done((f32[4,32,4,128]{3,2,1,0:T(4,128)S(1)}, f32[4,32,4,128]{3,2,1,0:T(4,128)}, u32[]{:S(2)}) %copy-start.3) | copy-done | bytes 262168
  45.4 0.3 convert_reduce_fusion.1
  46.0 0.6 copy-done.5
  46.6 0.3 fusion.58
  47.2 0.9 %copy.158 = bf16[128,2,4,128]{3,2,1,0:T(4,128)(2,1)} copy(bf16[128,2,4,128]{0,3,2,1:T(8,128)(2,1)S(1)} %maximum_bitcast_fusion) | data formatting | bytes 524288 | tf_op jit(solution)/shard_map/transpose | solution.py:247
  48.0 3.8 %all-to-all-start.2 = ((bf16[128,2,4,128]{3,2,1,0:T(4,128)(2,1)}), bf16[128,2,4,128]{3,2,1,0:T(4,128)(2,1)S(1)}, u32[]{:S(2)}, u32[]{:S(2)}) async-start(bf16[128,2,4,128]{3,2,1,0:T(4,128)(2,1)} %copy.158), calls=%async_computation.2 | async-start | bytes 524288 | tf_op jit(solution)/shard_map/all_to_all | solution.py:248
  51.9 0.3 collective-permute-start
  52.2 1.6 %collective-permute-start.1 = (bf16[16,4,128]{2,0,1:T(8,128)(2,1)S(1)}, bf16[16,4,128]{2,0,1:T(8,128)(2,1)S(1)}, u32[]{:S(2)}, u32[]{:S(2)}) collective-permute-start(bf16[16,4,128]{2,0,1:T(8,128)(2,1)S(1)} %get-tuple-element.18), channel_id=1, source_target_pairs={{0,8},{4,12},{8,16},{12,20},{16,24},{20,28},{24,0},{28,4},{1,9},{5... | collective-permute-start | bytes 49160 | tf_op jit(solution)/shard_map/ppermute | solution.py:268
  53.8 2.4 %collective-permute-done = bf16[16,4,128]{2,0,1:T(8,128)(2,1)S(1)} collective-permute-done((bf16[16,4,128]{2,0,1:T(8,128)(2,1)S(1)}, bf16[16,4,128]{2,0,1:T(8,128)(2,1)S(1)}, u32[]{:S(2)}, u32[]{:S(2)}) %collective-permute-start) | collective-permute-done | bytes 16416 | tf_op jit(solution)/shard_map/ppermute | solution.py:268
  56.2 5.9 %all-to-all-done.2 = bf16[128,2,4,128]{3,2,1,0:T(4,128)(2,1)S(1)} async-done(((bf16[128,2,4,128]{3,2,1,0:T(4,128)(2,1)}), bf16[128,2,4,128]{3,2,1,0:T(4,128)(2,1)S(1)}, u32[]{:S(2)}, u32[]{:S(2)}) %all-to-all-start.2) | async-done | bytes 262176 | tf_op jit(solution)/shard_map/all_to_all | solution.py:248
  62.6 0.4 reshape.439
  63.2 0.9 %collective-permute-start.2 = (bf16[16,4,128]{2,0,1:T(8,128)(2,1)S(1)}, bf16[16,4,128]{2,0,1:T(8,128)(2,1)S(1)}, u32[]{:S(2)}, u32[]{:S(2)}) collective-permute-start(bf16[16,4,128]{2,0,1:T(8,128)(2,1)S(1)} %get-tuple-element.17), channel_id=1, source_target_pairs={{0,12},{4,16},{8,20},{12,24},{16,28},{20,0},{24,4},{28,8},{1,13},{... | collective-permute-start | bytes 49160 | tf_op jit(solution)/shard_map/ppermute | solution.py:268
  64.1 1.0 %reshape.442 = f32[32,16,128]{2,1,0:T(8,128)} reshape(f32[32,4,16,32]{3,2,1,0:T(8,128)S(1)} %bitcast.210) | data formatting | bytes 524288 | tf_op jit(solution)/shard_map/reshape | solution.py:274
  65.1 3.0 %all-to-all-start.3 = ((f32[32,16,128]{2,1,0:T(8,128)}), f32[32,16,128]{2,1,0:T(8,128)S(1)}, u32[]{:S(2)}, u32[]{:S(2)}) async-start(f32[32,16,128]{2,1,0:T(8,128)} %reshape.442), calls=%async_computation.3 | async-start | bytes 524288 | tf_op jit(solution)/shard_map/all_to_all | solution.py:273
  68.1 1.8 %collective-permute-start.3 = (bf16[16,4,128]{2,0,1:T(8,128)(2,1)S(1)}, bf16[16,4,128]{2,0,1:T(8,128)(2,1)S(1)}, u32[]{:S(2)}, u32[]{:S(2)}) collective-permute-start(bf16[16,4,128]{2,0,1:T(8,128)(2,1)S(1)} %get-tuple-element.16), channel_id=1, source_target_pairs={{0,16},{4,20},{8,24},{12,28},{16,0},{20,4},{24,8},{28,12},{1,17},{... | collective-permute-start | bytes 49160 | tf_op jit(solution)/shard_map/ppermute | solution.py:268
  69.9 2.4 %collective-permute-start.5 = (bf16[16,4,128]{2,0,1:T(8,128)(2,1)S(1)}, bf16[16,4,128]{2,0,1:T(8,128)(2,1)S(1)}, u32[]{:S(2)}, u32[]{:S(2)}) collective-permute-start(bf16[16,4,128]{2,0,1:T(8,128)(2,1)S(1)} %get-tuple-element.14), channel_id=1, source_target_pairs={{0,24},{4,28},{8,0},{12,4},{16,8},{20,12},{24,16},{28,20},{1,25},{... | collective-permute-start | bytes 49160 | tf_op jit(solution)/shard_map/ppermute | solution.py:268
  72.3 1.5 %collective-permute-start.6 = (bf16[16,4,128]{2,0,1:T(8,128)(2,1)S(1)}, bf16[16,4,128]{2,0,1:T(8,128)(2,1)S(1)}, u32[]{:S(2)}, u32[]{:S(2)}) collective-permute-start(bf16[16,4,128]{2,0,1:T(8,128)(2,1)S(1)} %get-tuple-element.13), channel_id=1, source_target_pairs={{0,28},{4,0},{8,4},{12,8},{16,12},{20,16},{24,20},{28,24},{1,29},{... | collective-permute-start | bytes 49160 | tf_op jit(solution)/shard_map/ppermute | solution.py:268
  73.8 1.4 %collective-permute-done.6 = bf16[16,4,128]{2,0,1:T(8,128)(2,1)S(1)} collective-permute-done((bf16[16,4,128]{2,0,1:T(8,128)(2,1)S(1)}, bf16[16,4,128]{2,0,1:T(8,128)(2,1)S(1)}, u32[]{:S(2)}, u32[]{:S(2)}) %collective-permute-start.6) | collective-permute-done | bytes 16416 | tf_op jit(solution)/shard_map/ppermute | solution.py:268
  75.2 0.6 gather_fusion
  77.0 0.6 copy-done.12
  77.7 0.3 fusion.13
  78.0 0.3 all-to-all-done.3
  79.1 0.6 copy-done.7
  79.7 1.0 %fusion.16 = bf16[16,32,128]{2,1,0:T(8,128)(2,1)} fusion(f32[16,32,128]{2,1,0:T(8,128)S(1)} %bitcast.223, f32[16,32,128]{2,1,0:T(8,128)S(1)} %bitcast.234, bf16[16,32,128]{1,0,2:T(8,128)(2,1)S(1)} %multiply_convert_fusion, bf16[128,128]{1,0:T(8,128)(2,1)S(1)} %copy-done.7), kind=kOutput, calls=%fused_computation.23 | convolution fusion | flops 16973824 | bytes 819200 | tf_op jit(solution)/shard_map/dot_general | solution.py:282
  (109 shorter events, 7.0 us)
Async XLA Ops:
  0.0 11.1 %copy-start = (bf16[128,512]{1,0:T(8,128)(2,1)S(1)}, bf16[128,512]{1,0:T(8,128)(2,1)}, u32[]{:S(2)}) copy-start(bf16[128,512]{1,0:T(8,128)(2,1)} %param.18) | copy-start | bytes 393220
  0.0 1.1 %copy-start.1 = (bf16[4,128,128]{2,1,0:T(8,128)(2,1)S(1)}, bf16[4,128,128]{2,1,0:T(8,128)(2,1)}, u32[]{:S(2)}) copy-start(bf16[4,128,128]{2,1,0:T(8,128)(2,1)} %param.14) | copy-start | bytes 393220
  1.4 0.7 copy-start.13
  3.1 17.6 %all-to-all-start = ((f32[32,4,4,128]{3,2,1,0:T(4,128)}), f32[32,4,4,128]{3,2,1,0:T(4,128)S(1)}, u32[]{:S(2)}, u32[]{:S(2)}) async-start(f32[32,4,4,128]{3,2,1,0:T(4,128)} %broadcast_in_dim.33), calls=%async_computation | async-start | bytes 524288 | tf_op jit(solution)/shard_map/all_to_all | solution.py:108
  11.8 0.7 copy-start.9
  12.4 0.7 copy-start.8
  22.2 0.8 copy-start.10
  23.5 0.7 copy-start.14
  25.4 14.5 %all-to-all-start.1 = ((bf16[32,48,128]{2,1,0:T(8,128)(2,1)}), bf16[32,48,128]{2,1,0:T(8,128)(2,1)S(1)}, u32[]{:S(2)}, u32[]{:S(2)}) async-start(bf16[32,48,128]{2,1,0:T(8,128)(2,1)} %pad_maximum_fusion), calls=%async_computation.1 | async-start | bytes 786432 | tf_op jit(solution)/shard_map/all_to_all | solution.py:187
  40.8 0.9 %copy-start.4 = (bf16[128,512]{1,0:T(8,128)(2,1)S(1)}, bf16[128,512]{1,0:T(8,128)(2,1)}, u32[]{:S(2)}) copy-start(bf16[128,512]{1,0:T(8,128)(2,1)} %param.21) | copy-start | bytes 393220
  41.0 0.7 copy-start.2
  44.4 1.0 %copy-start.3 = (f32[4,32,4,128]{3,2,1,0:T(4,128)S(1)}, f32[4,32,4,128]{3,2,1,0:T(4,128)}, u32[]{:S(2)}) copy-start(f32[4,32,4,128]{3,2,1,0:T(4,128)} %copy-done.2) | copy-start | bytes 786436
  44.4 1.0 %copy-start.11 = (bf16[128,128]{1,0:T(8,128)(2,1)S(1)}, bf16[128,128]{1,0:T(8,128)(2,1)}, u32[]{:S(2)}) copy-start(bf16[128,128]{1,0:T(8,128)(2,1)} %param.23) | copy-start | bytes 98308
  45.7 0.8 %copy-start.5 = (bf16[128,256]{1,0:T(8,128)(2,1)S(1)}, bf16[128,256]{1,0:T(8,128)(2,1)}, u32[]{:S(2)}) copy-start(bf16[128,256]{1,0:T(8,128)(2,1)} %param.25) | copy-start | bytes 196612
  45.7 0.9 %copy-start.6 = (bf16[128,256]{1,0:T(8,128)(2,1)S(1)}, bf16[128,256]{1,0:T(8,128)(2,1)}, u32[]{:S(2)}) copy-start(bf16[128,256]{1,0:T(8,128)(2,1)} %param.24) | copy-start | bytes 196612
  48.0 14.0 %all-to-all-start.2 = ((bf16[128,2,4,128]{3,2,1,0:T(4,128)(2,1)}), bf16[128,2,4,128]{3,2,1,0:T(4,128)(2,1)S(1)}, u32[]{:S(2)}, u32[]{:S(2)}) async-start(bf16[128,2,4,128]{3,2,1,0:T(4,128)(2,1)} %copy.158), calls=%async_computation.2 | async-start | bytes 524288 | tf_op jit(solution)/shard_map/all_to_all | solution.py:248
  51.9 4.3 %collective-permute-start = (bf16[16,4,128]{2,0,1:T(8,128)(2,1)S(1)}, bf16[16,4,128]{2,0,1:T(8,128)(2,1)S(1)}, u32[]{:S(2)}, u32[]{:S(2)}) collective-permute-start(bf16[16,4,128]{2,0,1:T(8,128)(2,1)S(1)} %get-tuple-element.19), channel_id=1, source_target_pairs={{0,4},{4,8},{8,12},{12,16},{16,20},{20,24},{24,28},{28,0},{1,5},{5... | collective-permute-start | bytes 49160 | tf_op jit(solution)/shard_map/ppermute | solution.py:268
  52.2 11.9 %collective-permute-start.1 = (bf16[16,4,128]{2,0,1:T(8,128)(2,1)S(1)}, bf16[16,4,128]{2,0,1:T(8,128)(2,1)S(1)}, u32[]{:S(2)}, u32[]{:S(2)}) collective-permute-start(bf16[16,4,128]{2,0,1:T(8,128)(2,1)S(1)} %get-tuple-element.18), channel_id=1, source_target_pairs={{0,8},{4,12},{8,16},{12,20},{16,24},{20,28},{24,0},{28,4},{1,9},{5... | collective-permute-start | bytes 49160 | tf_op jit(solution)/shard_map/ppermute | solution.py:268
  63.2 10.6 %collective-permute-start.2 = (bf16[16,4,128]{2,0,1:T(8,128)(2,1)S(1)}, bf16[16,4,128]{2,0,1:T(8,128)(2,1)S(1)}, u32[]{:S(2)}, u32[]{:S(2)}) collective-permute-start(bf16[16,4,128]{2,0,1:T(8,128)(2,1)S(1)} %get-tuple-element.17), channel_id=1, source_target_pairs={{0,12},{4,16},{8,20},{12,24},{16,28},{20,0},{24,4},{28,8},{1,13},{... | collective-permute-start | bytes 49160 | tf_op jit(solution)/shard_map/ppermute | solution.py:268
  65.1 13.2 %all-to-all-start.3 = ((f32[32,16,128]{2,1,0:T(8,128)}), f32[32,16,128]{2,1,0:T(8,128)S(1)}, u32[]{:S(2)}, u32[]{:S(2)}) async-start(f32[32,16,128]{2,1,0:T(8,128)} %reshape.442), calls=%async_computation.3 | async-start | bytes 524288 | tf_op jit(solution)/shard_map/all_to_all | solution.py:273
  68.1 5.7 %collective-permute-start.3 = (bf16[16,4,128]{2,0,1:T(8,128)(2,1)S(1)}, bf16[16,4,128]{2,0,1:T(8,128)(2,1)S(1)}, u32[]{:S(2)}, u32[]{:S(2)}) collective-permute-start(bf16[16,4,128]{2,0,1:T(8,128)(2,1)S(1)} %get-tuple-element.16), channel_id=1, source_target_pairs={{0,16},{4,20},{8,24},{12,28},{16,0},{20,4},{24,8},{28,12},{1,17},{... | collective-permute-start | bytes 49160 | tf_op jit(solution)/shard_map/ppermute | solution.py:268
  69.9 3.9 %collective-permute-start.4 = (bf16[16,4,128]{2,0,1:T(8,128)(2,1)S(1)}, bf16[16,4,128]{2,0,1:T(8,128)(2,1)S(1)}, u32[]{:S(2)}, u32[]{:S(2)}) collective-permute-start(bf16[16,4,128]{2,0,1:T(8,128)(2,1)S(1)} %get-tuple-element.15), channel_id=1, source_target_pairs={{0,20},{4,24},{8,28},{12,0},{16,4},{20,8},{24,12},{28,16},{1,21},{... | collective-permute-start | bytes 49160 | tf_op jit(solution)/shard_map/ppermute | solution.py:268
  69.9 3.9 %collective-permute-start.5 = (bf16[16,4,128]{2,0,1:T(8,128)(2,1)S(1)}, bf16[16,4,128]{2,0,1:T(8,128)(2,1)S(1)}, u32[]{:S(2)}, u32[]{:S(2)}) collective-permute-start(bf16[16,4,128]{2,0,1:T(8,128)(2,1)S(1)} %get-tuple-element.14), channel_id=1, source_target_pairs={{0,24},{4,28},{8,0},{12,4},{16,8},{20,12},{24,16},{28,20},{1,25},{... | collective-permute-start | bytes 49160 | tf_op jit(solution)/shard_map/ppermute | solution.py:268
  72.3 2.9 %collective-permute-start.6 = (bf16[16,4,128]{2,0,1:T(8,128)(2,1)S(1)}, bf16[16,4,128]{2,0,1:T(8,128)(2,1)S(1)}, u32[]{:S(2)}, u32[]{:S(2)}) collective-permute-start(bf16[16,4,128]{2,0,1:T(8,128)(2,1)S(1)} %get-tuple-element.13), channel_id=1, source_target_pairs={{0,28},{4,0},{8,4},{12,8},{16,12},{20,16},{24,20},{28,24},{1,29},{... | collective-permute-start | bytes 49160 | tf_op jit(solution)/shard_map/ppermute | solution.py:268
  76.9 0.8 copy-start.12
  78.9 0.8 copy-start.7
